TPU v7x, 512 devices: a whole 4x4x16 slice. The times are simulated.
512 devices in a mesh: seq: 32 (over z, core), fsdp: 16 (over x, y).
Axes of the slice: x: 4, y: 4, z: 16, core: 2. Of those that a mesh axis runs over, the one named last changes fastest.
Arguments:
- tokens: bfloat16 [12288, 2048], P('seq'), may hold values from -6 to 6
- w_query: bfloat16 [2048, 2048], P('seq', 'fsdp'), may hold values from -0.125 to 0.125
- w_key: bfloat16 [2048, 2048], P('seq', 'fsdp'), may hold values from -0.125 to 0.125
- w_value: bfloat16 [2048, 2048], P('seq', 'fsdp'), may hold values from -0.125 to 0.125
- norm_gain: float32 [2048], P('fsdp'), may hold values from 0.1 to 1.9
- block_mask: int32 [32, 3, 3], P('seq'), may hold values 0 or 1
- cotangent: bfloat16 [12288, 2048], P('seq', 'fsdp'), may hold values from -6 to 6
Outputs:
- attended: bfloat16 [12288, 2048], P('seq', 'fsdp')
- grad_tokens: bfloat16 [12288, 2048], P('seq', 'fsdp')
- grad_query: bfloat16 [2048, 2048], P('seq', 'fsdp')
- grad_key: bfloat16 [2048, 2048], P('seq', 'fsdp')
- grad_value: bfloat16 [2048, 2048], P('seq', 'fsdp')
All inputs are finite; a program needn't handle non-finite values. No bound on the sum of `block_mask` on one device may be relied on, other than what follows from the above.
Results may differ from a plain program's by a relative error of at most 0.035.
Values may be sent and summed in bfloat16 or wider, within the bound.
No kernel may reach another device: no remote copies, remote signals or barrier semaphores. Data moves between devices by JAX's collectives and lax.ppermute only.
A program may use at most 64 MiB of HBM per device.

v0:
```python
import math

import jax
import jax.numpy as jnp
from jax import lax
from jax.sharding import PartitionSpec as P

HDIM = 128
BLOCK = 128
SEG = 384
NB = 3


EPSILON = 1e-06


def entering(array, axis, join, neutral, backward):
    count = lax.axis_size(axis)
    place = lax.axis_index(axis)
    ahead = count - 1 - place if backward else place
    gathered = lax.all_gather(array.astype(jnp.bfloat16), axis)
    state = jnp.zeros_like(array) + jnp.asarray(neutral, array.dtype)

    def one(lap, state):
        source = count - 1 - lap if backward else lap
        return join(state, lax.dynamic_index_in_dim(gathered, source, 0, False).astype(array.dtype))

    return lax.fori_loop(0, ahead, one, state)


def allowed_pairs(pattern):
    positions = jnp.arange(SEG)
    block_ids = positions // BLOCK
    selector = (block_ids[:, None] == jnp.arange(NB)[None, :]).astype(jnp.float32)
    spread_out = jnp.dot(
        jnp.dot(selector, pattern.astype(jnp.float32), precision=lax.Precision.HIGHEST),
        selector.T,
        precision=lax.Precision.HIGHEST,
    )
    same_block = (block_ids[:, None] == block_ids[None, :]) & (
        positions[None, :] <= positions[:, None]
    )
    earlier_block = (block_ids[None, :] < block_ids[:, None]) & (spread_out > 0.5)
    return same_block | earlier_block


def add_states(first_term, second_term):
    return first_term + second_term


def shards(tokens, w_query, w_key, w_value, norm_gain, block_mask, cotangent):
    columns = w_query.shape[1]
    heads_here = columns // HDIM
    allowed = allowed_pairs(block_mask[0])
    full_query, full_key, full_value = (
        lax.all_gather(w_query, "seq", axis=0, tiled=True),
        lax.all_gather(w_key, "seq", axis=0, tiled=True),
        lax.all_gather(w_value, "seq", axis=0, tiled=True),
    )
    weight_cat = jnp.concatenate([full_query, full_key, full_value], axis=1)
    projected = jnp.dot(tokens, weight_cat, preferred_element_type=jnp.float32)
    projected = projected.astype(jnp.bfloat16)
    queries = projected[:, :columns].reshape(SEG, heads_here, HDIM)
    key_heads = projected[:, columns : 2 * columns].reshape(SEG, heads_here, HDIM)
    value_heads = projected[:, 2 * columns :].reshape(SEG, heads_here, HDIM)
    increment = jnp.einsum(
        "thd,the->hde", key_heads, value_heads, preferred_element_type=jnp.float32
    )
    state = entering(increment, "seq", add_states, jnp.zeros_like(increment), False)
    state_low = state.astype(jnp.bfloat16)
    scores = jnp.einsum("shd,thd->hst", queries, key_heads, preferred_element_type=jnp.float32)
    weights = jnp.where(allowed[None], scores, 0.0).astype(jnp.bfloat16)
    mixed = jnp.einsum("shd,hde->she", queries, state_low, preferred_element_type=jnp.float32)
    mixed = mixed + jnp.einsum(
        "hst,the->she", weights, value_heads, preferred_element_type=jnp.float32
    )
    scale = lax.rsqrt(jnp.mean(mixed * mixed, axis=-1, keepdims=True) + EPSILON)
    normed = mixed * scale
    gain_heads = norm_gain.reshape(heads_here, HDIM)
    attended = (normed * gain_heads).reshape(SEG, columns).astype(jnp.bfloat16)
    given = cotangent.reshape(SEG, heads_here, HDIM).astype(jnp.float32) * gain_heads
    d_mixed = (scale * (given - normed * jnp.mean(given * normed, axis=-1, keepdims=True))).astype(
        jnp.bfloat16
    )
    d_state = jnp.einsum("shd,she->hde", queries, d_mixed, preferred_element_type=jnp.float32)
    later = entering(d_state, "seq", add_states, jnp.zeros_like(d_state), True)
    later_low = later.astype(jnp.bfloat16)
    d_scores = jnp.einsum("she,the->hst", d_mixed, value_heads, preferred_element_type=jnp.float32)
    d_weights = jnp.where(allowed[None], d_scores, 0.0).astype(jnp.bfloat16)
    d_queries = jnp.einsum("she,hde->shd", d_mixed, state_low, preferred_element_type=jnp.float32)
    d_queries = d_queries + jnp.einsum(
        "hst,thd->shd", d_weights, key_heads, preferred_element_type=jnp.float32
    )
    d_keys = jnp.einsum("hst,shd->thd", d_weights, queries, preferred_element_type=jnp.float32)
    d_keys = d_keys + jnp.einsum(
        "the,hde->thd", value_heads, later_low, preferred_element_type=jnp.float32
    )
    d_values = jnp.einsum("hst,she->the", weights, d_mixed, preferred_element_type=jnp.float32)
    d_values = d_values + jnp.einsum(
        "thd,hde->the", key_heads, later_low, preferred_element_type=jnp.float32
    )
    grad_cat = jnp.concatenate(
        [part.reshape(SEG, columns).astype(jnp.bfloat16) for part in (d_queries, d_keys, d_values)],
        axis=1,
    )
    input_rows = lax.psum_scatter(
        lax.dot_general(
            weight_cat, grad_cat, (((1,), (1,)), ((), ())), preferred_element_type=jnp.float32
        ).astype(jnp.bfloat16),
        "fsdp",
        scatter_dimension=0,
        tiled=True,
    ).astype(jnp.float32)
    grad_tokens = input_rows.T.astype(jnp.bfloat16)
    weight_rows = lax.psum_scatter(
        lax.dot_general(
            tokens, grad_cat, (((0,), (0,)), ((), ())), preferred_element_type=jnp.float32
        ).astype(jnp.bfloat16),
        "seq",
        scatter_dimension=0,
        tiled=True,
    ).astype(jnp.float32)
    weight_rows = (weight_rows * (1.0 / math.sqrt(SEG * lax.axis_size("seq")))).astype(jnp.bfloat16)
    return (
        attended,
        grad_tokens,
        weight_rows[:, :columns],
        weight_rows[:, columns : 2 * columns],
        weight_rows[:, 2 * columns :],
    )


def solution(mesh):
    placed = (
        P("seq", None),
        P("seq", "fsdp"),
        P("seq", "fsdp"),
        P("seq", "fsdp"),
        P("fsdp"),
        P("seq", None, None),
        P("seq", "fsdp"),
    )
    return jax.shard_map(
        shards,
        mesh=mesh,
        in_specs=placed,
        out_specs=(
            P("seq", "fsdp"),
            P("seq", "fsdp"),
            P("seq", "fsdp"),
            P("seq", "fsdp"),
            P("seq", "fsdp"),
        ),
        check_vma=False,
    )
```

profile of v0, /device:TPU:6, one launch (start us, length us, event | category | flops | bytes accessed | tf_op | source)
XLA Modules:
  0.0 494.9 jit_solution(10688304476852029029)
XLA Ops:
  7.2 38.0 %all_gather.21 = bf16[2048,128]{1,0:T(8,128)(2,1)S(1)} all-gather(bf16[64,128]{1,0:T(8,128)(2,1)} %param.12), channel_id=1, replica_groups=mesh['seq'=32,'fsdp'=16] {'seq'}, dimensions={0}, use_global_device_ids=true | all-gather | bytes 540672 | tf_op jit(solution)/shard_map/all_gather | solution.py:56
  45.4 28.5 %all_gather.22 = bf16[2048,128]{1,0:T(8,128)(2,1)S(1)} all-gather(bf16[64,128]{1,0:T(8,128)(2,1)S(1)} %copy-done.9), channel_id=1, replica_groups=mesh['seq'=32,'fsdp'=16] {'seq'}, dimensions={0}, use_global_device_ids=true | all-gather | bytes 540672 | tf_op jit(solution)/shard_map/all_gather | solution.py:57
  73.9 29.8 %all_gather.23 = bf16[2048,128]{1,0:T(8,128)(2,1)S(1)} all-gather(bf16[64,128]{1,0:T(8,128)(2,1)S(1)} %copy-done.10), channel_id=1, replica_groups=mesh['seq'=32,'fsdp'=16] {'seq'}, dimensions={0}, use_global_device_ids=true | all-gather | bytes 540672 | tf_op jit(solution)/shard_map/all_gather | solution.py:58
  104.1 1.0 fusion.3
  105.2 0.8 convolution_convert_fusion.4
  107.6 65.1 %all-gather.5.cloned.1.call-done = bf16[4096,128]{1,0:T(8,128)(2,1)} async-done(((bf16[128,128]{1,0:T(8,128)(2,1)}), bf16[4096,128]{1,0:T(8,128)(2,1)}) %all-gather.5.cloned.1.call-update) | async-done | bytes 1048592 | tf_op jit(solution)/shard_map/all_gather | solution.py:21
  173.2 0.8 convolution_convert_fusion.3
  175.2 87.1 %all-gather.7.cloned.1.call-done = bf16[4096,128]{1,0:T(8,128)(2,1)} async-done(((bf16[128,128]{1,0:T(8,128)(2,1)}), bf16[4096,128]{1,0:T(8,128)(2,1)}) %all-gather.7.cloned.1.call-update) | async-done | bytes 1048592 | tf_op jit(solution)/shard_map/all_gather | solution.py:21
  262.3 24.6 %while.23 = (s32[]{:T(128)}, f32[1,128,128]{2,1,0:T(8,128)S(1)}, s32[]{:T(128)}, bf16[32,1,128,128]{3,2,1,0:T(8,128)(2,1)}, s32[]{:T(128)}, /*index=5*/s32[]{:T(128)}, s32[]{:T(128)}, s32[]{:T(128)}) while((s32[]{:T(128)}, f32[1,128,128]{2,1,0:T(8,128)S(1)}, s32[]{:T(128)}, bf16[32,1,128,128]{3,2,1,0:T(8,128)(2,1)}, s32[]{:T(128)}, ...), condition=%wide.region_5.6_spmd, body=%wide.region_4.5_spmd.sunk | while | flops 32774 | bytes 163983 | solution.py:28
  263.1 0.8 convert_add_fusion.5
  263.9 0.8 convert_add_fusion.5
  264.7 0.8 convert_add_fusion.5
  265.5 0.8 convert_add_fusion.5
  266.3 0.8 convert_add_fusion.5
  267.1 0.8 convert_add_fusion.5
  267.9 0.8 convert_add_fusion.5
  268.7 0.8 convert_add_fusion.5
  269.5 0.8 convert_add_fusion.5
  270.3 0.8 convert_add_fusion.5
  271.9 0.8 convert_add_fusion.5
  276.6 0.8 convert_add_fusion.5
  277.4 0.8 convert_add_fusion.5
  281.4 0.8 convert_add_fusion.5
  282.2 0.8 convert_add_fusion.5
  287.8 3.7 convolution_convert_fusion.1
  291.6 0.8 copy-done.3
  292.5 1.0 fusion
  293.5 1.6 copy.28
  295.8 76.5 %reduce-scatter.5.cloned.1.call-done = bf16[128,384]{1,0:T(8,128)(2,1)} async-done(((bf16[2048,384]{1,0:T(8,128)(2,1)}), bf16[128,384]{1,0:T(8,128)(2,1)}) %reduce-scatter.5.cloned.1.call-update) | async-done | bytes 98320 | tf_op jit(solution)/shard_map/reduce_scatter | solution.py:106
  372.3 1.6 copy.24
  374.0 111.3 %reduce-scatter.7.cloned.1.call-done = bf16[64,384]{1,0:T(8,128)(2,1)} async-done(((bf16[2048,384]{1,0:T(8,128)(2,1)}), bf16[64,384]{1,0:T(8,128)(2,1)}) %reduce-scatter.7.cloned.1.call-update) | async-done | bytes 49168
  485.3 0.9 copy.29
  (80 shorter events, 19.9 us)
Async XLA Ops:
  7.2 96.9 %copy-start = (bf16[384,2048]{1,0:T(8,128)(2,1)S(1)}, bf16[384,2048]{1,0:T(8,128)(2,1)}, u32[]{:S(2)}) copy-start(bf16[384,2048]{1,0:T(8,128)(2,1)} %param.11) | copy-start | bytes 4718596
  7.2 38.2 %copy-start.9 = (bf16[64,128]{1,0:T(8,128)(2,1)S(1)}, bf16[64,128]{1,0:T(8,128)(2,1)}, u32[]{:S(2)}) copy-start(bf16[64,128]{1,0:T(8,128)(2,1)} %param.13) | copy-start | bytes 49156
  7.2 66.7 %copy-start.10 = (bf16[64,128]{1,0:T(8,128)(2,1)S(1)}, bf16[64,128]{1,0:T(8,128)(2,1)}, u32[]{:S(2)}) copy-start(bf16[64,128]{1,0:T(8,128)(2,1)} %param.14) | copy-start | bytes 49156
  7.2 165.5 %all-gather.5.cloned.1.call-start = ((), (), s32[]{:S(2)}) async-start(), calls=%async_computation.3 | async-start | bytes 1081344 | tf_op jit(solution)/shard_map/all_gather | solution.py:21
  104.0 1.2 copy-start.1
  104.0 2.0 copy-start.12
  104.0 2.1 copy-start.8
  106.0 156.3 %all-gather.7.cloned.1.call-start = ((), (), s32[]{:S(2)}) async-start(), calls=%async_computation.4 | async-start | bytes 1081344 | tf_op jit(solution)/shard_map/all_gather | solution.py:21
  107.1 65.9 %copy-start.11 = (f32[128]{0:T(128)S(1)}, f32[128]{0:T(128)}, u32[]{:S(2)}) copy-start(f32[128]{0:T(128)} %param.15) | copy-start | bytes 1540
  174.1 198.3 %reduce-scatter.5.cloned.1.call-start = ((), (), s32[]{:S(2)}) async-start(), calls=%async_computation.2 | async-start | bytes 1671168 | tf_op jit(solution)/shard_map/reduce_scatter | solution.py:106
  174.8 112.6 %copy-start.2 = (bf16[384,128]{0,1:T(8,128)(2,1)}, bf16[384,128]{0,1:T(8,128)(2,1)S(1)}, u32[]{:S(2)}) copy-start(bf16[384,128]{0,1:T(8,128)(2,1)S(1)} %fusion.12) | copy-start | bytes 294916
  287.2 0.6 copy-start.4
  287.8 3.7 copy-start.6
  291.5 0.9 copy-start.3
  291.5 0.9 copy-start.5
  291.5 1.0 copy-start.7
  291.5 193.8 %reduce-scatter.7.cloned.1.call-start = ((), (), s32[]{:S(2)}) async-start(), calls=%async_computation.5 | async-start | bytes 1622016
Sparse Core Ops, SparseCore 0:
  106.1 66.5 all-gather.4
  175.4 86.8 all-gather.6
  291.7 80.6 reduce-scatter.4
  375.0 110.2 reduce-scatter.6
where the time goes:
time: 498 us; the launch traced here: 495 us
  waiting for transfers between devices  340 us (68%)
  blocking collectives  96.4 us (19%)
  other arithmetic  24.2 us (5%)
  between operations  14.1 us (3%)
  matrix products  10.3 us (2%)
  local copies, waits for them, and re-layouts  8.96 us (2%)
    all_gather x2, waiting for transfers between devices, entering(): gathered = lax.all_gather(array.astype(jnp.bfloat16), axis)  152 us
    unnamed x5, waiting for transfers between devices  111 us
    reduce_scatter x1, waiting for transfers between devices, shards(): lax.psum_scatter(lax.dot_general(weight_cat, grad_cat, (((1,), (1,)), (()...  76.5 us
    all_gather x1, blocking collectives, shards(): lax.all_gather(w_query, 'seq', axis=0, tiled=True)  38 us
    all_gather x1, blocking collectives, shards(): lax.all_gather(w_value, 'seq', axis=0, tiled=True)  29.8 us
    all_gather x1, blocking collectives, shards(): lax.all_gather(w_key, 'seq', axis=0, tiled=True)  28.5 us
    add x31, other arithmetic, add_states(): return first_term + second_term  23.9 us
  transfers between devices with their start and end apart: 4, of which 4 were waited for; matrix products, arithmetic and copies ran while one was open for 2% of the time, Pallas kernels for 0%

commit v1 on v0

--- a/solution.py
+++ b/solution.py
@@ -14,18 +14,15 @@
 EPSILON = 1e-06
 
 
-def entering(array, axis, join, neutral, backward):
+def entering(array, axis, backward):
     count = lax.axis_size(axis)
     place = lax.axis_index(axis)
-    ahead = count - 1 - place if backward else place
     gathered = lax.all_gather(array.astype(jnp.bfloat16), axis)
-    state = jnp.zeros_like(array) + jnp.asarray(neutral, array.dtype)
-
-    def one(lap, state):
-        source = count - 1 - lap if backward else lap
-        return join(state, lax.dynamic_index_in_dim(gathered, source, 0, False).astype(array.dtype))
-
-    return lax.fori_loop(0, ahead, one, state)
+    source = jnp.arange(count)
+    chosen = source > place if backward else source < place
+    flat = gathered.reshape(count, -1)
+    total = jnp.dot(chosen.astype(jnp.bfloat16), flat, preferred_element_type=jnp.float32)
+    return total.reshape(array.shape)
 
 
 def allowed_pairs(pattern):
@@ -52,12 +49,9 @@
     columns = w_query.shape[1]
     heads_here = columns // HDIM
     allowed = allowed_pairs(block_mask[0])
-    full_query, full_key, full_value = (
-        lax.all_gather(w_query, "seq", axis=0, tiled=True),
-        lax.all_gather(w_key, "seq", axis=0, tiled=True),
-        lax.all_gather(w_value, "seq", axis=0, tiled=True),
+    weight_cat = lax.all_gather(
+        jnp.concatenate([w_query, w_key, w_value], axis=1), "seq", axis=0, tiled=True
     )
-    weight_cat = jnp.concatenate([full_query, full_key, full_value], axis=1)
     projected = jnp.dot(tokens, weight_cat, preferred_element_type=jnp.float32)
     projected = projected.astype(jnp.bfloat16)
     queries = projected[:, :columns].reshape(SEG, heads_here, HDIM)
@@ -66,7 +60,7 @@
     increment = jnp.einsum(
         "thd,the->hde", key_heads, value_heads, preferred_element_type=jnp.float32
     )
-    state = entering(increment, "seq", add_states, jnp.zeros_like(increment), False)
+    state = entering(increment, "seq", False)
     state_low = state.astype(jnp.bfloat16)
     scores = jnp.einsum("shd,thd->hst", queries, key_heads, preferred_element_type=jnp.float32)
     weights = jnp.where(allowed[None], scores, 0.0).astype(jnp.bfloat16)
@@ -83,7 +77,7 @@
         jnp.bfloat16
     )
     d_state = jnp.einsum("shd,she->hde", queries, d_mixed, preferred_element_type=jnp.float32)
-    later = entering(d_state, "seq", add_states, jnp.zeros_like(d_state), True)
+    later = entering(d_state, "seq", True)
     later_low = later.astype(jnp.bfloat16)
     d_scores = jnp.einsum("she,the->hst", d_mixed, value_heads, preferred_element_type=jnp.float32)
     d_weights = jnp.where(allowed[None], d_scores, 0.0).astype(jnp.bfloat16)

time: 498 us -> 444 us (0.89)
  blocking collectives: 96.4 us -> 0 us
  waiting for transfers between devices: 340 us -> 403 us
  other arithmetic: 24.2 us -> 1.75 us
    all_gather x3 -> x0, blocking collectives: 96.4 us -> none  [the longest x1 38 us: shards(): lax.all_gather(w_query, 'seq', axis=0, tiled=True)]
    all_gather x0 -> x1, waiting for transfers between devices: none -> 77.4 us  [shards(): lax.all_gather(jnp.concatenate([w_query, w_key, w_value], axis=1), 'seq',...]
    add x31 -> x0, other arithmetic: 23.9 us -> none  [add_states(): return first_term + second_term]
    all_gather x2, waiting for transfers between devices: 152 us -> 132 us  [entering(): gathered = lax.all_gather(array.astype(jnp.bfloat16), axis)]
    reduce_scatter x1, waiting for transfers between devices: 76.5 us -> 81.9 us  [shards(): lax.psum_scatter(lax.dot_general(weight_cat, grad_cat, (((1,), (1,)), (()...]
    unnamed x5 -> x6, waiting for transfers between devices: 111 us -> 112 us
  transfers between devices with their start and end apart: 4 -> 5, of which waited for: 4 -> 5; matrix products, arithmetic and copies ran while one was open for 2% -> 2% of each run, Pallas kernels for 0% -> 0%
where the time goes in v1:
time: 444 us
  waiting for transfers between devices  403 us (91%)
  between operations  14.1 us (3%)
  matrix products  12.6 us (3%)
  local copies, waits for them, and re-layouts  12 us (3%)
    all_gather x2, waiting for transfers between devices, entering(): gathered = lax.all_gather(array.astype(jnp.bfloat16), axis)  132 us
    unnamed x6, waiting for transfers between devices  112 us
    reduce_scatter x1, waiting for transfers between devices, shards(): lax.psum_scatter(lax.dot_general(weight_cat, grad_cat, (((1,), (1,)), (()...  81.9 us
    all_gather x1, waiting for transfers between devices, shards(): lax.all_gather(jnp.concatenate([w_query, w_key, w_value], axis=1), 'seq',...  77.4 us
    unnamed x30, local copies, waits for them, and re-layouts  8.95 us
  transfers between devices with their start and end apart: 5, of which 5 were waited for; matrix products, arithmetic and copies ran while one was open for 2% of the time, Pallas kernels for 0%

profile of v1, /device:TPU:6, one launch (start us, length us, event | category | flops | bytes accessed | tf_op | source)
XLA Modules:
  0.0 443.8 jit_solution(17414190341026711263)
XLA Ops:
  7.2 1.5 pad_maximum_fusion.3
  8.8 77.4 %all-gather.6.cloned.1.call-done = bf16[2048,384]{1,0:T(8,128)(2,1)} async-done(((bf16[64,384]{1,0:T(8,128)(2,1)}), bf16[2048,384]{1,0:T(8,128)(2,1)}) %all-gather.6.cloned.1.call-update) | async-done | bytes 1572880 | tf_op jit(solution)/shard_map/all_gather | solution.py:52
  86.2 2.4 fusion.3
  88.6 0.8 convolution_convert_fusion.4
  89.7 0.3 fusion.24
  90.0 0.6 fusion.6
  90.5 0.3 fusion.1
  90.8 0.2 fusion.36
  91.2 66.2 %all-gather.8.cloned.1.call-done = bf16[4096,128]{1,0:T(8,128)(2,1)} async-done(((bf16[128,128]{1,0:T(8,128)(2,1)}), bf16[4096,128]{1,0:T(8,128)(2,1)}) %all-gather.8.cloned.1.call-update) | async-done | bytes 1048592 | tf_op jit(solution)/shard_map/all_gather | solution.py:20
  157.4 1.5 reshape.163
  159.0 0.3 fusion.16
  159.2 0.2 multiply_reduce_fusion
  159.9 0.8 convolution_convert_fusion.3
  160.7 0.3 fusion.2
  161.0 0.2 fusion.40
  161.2 1.0 fusion.12
  162.7 66.0 %all-gather.10.cloned.1.call-done = bf16[4096,128]{1,0:T(8,128)(2,1)} async-done(((bf16[128,128]{1,0:T(8,128)(2,1)}), bf16[4096,128]{1,0:T(8,128)(2,1)}) %all-gather.10.cloned.1.call-update) | async-done | bytes 1048592 | tf_op jit(solution)/shard_map/all_gather | solution.py:20
  228.7 1.5 reshape.165
  230.2 0.3 fusion.13
  230.9 0.7 copy-done.10
  231.6 2.3 convolution_convert_fusion.1
  234.0 0.8 copy-done.5
  234.8 1.9 fusion
  236.7 1.6 copy.28
  238.3 0.8 copy.19
  239.0 81.9 %reduce-scatter.5.cloned.1.call-done = bf16[128,384]{1,0:T(8,128)(2,1)} async-done(((bf16[2048,384]{1,0:T(8,128)(2,1)}), bf16[128,384]{1,0:T(8,128)(2,1)}) %reduce-scatter.5.cloned.1.call-update) | async-done | bytes 98320 | tf_op jit(solution)/shard_map/reduce_scatter | solution.py:100
  320.9 1.6 copy.20
  322.5 111.7 %reduce-scatter.7.cloned.1.call-done = bf16[64,384]{1,0:T(8,128)(2,1)} async-done(((bf16[2048,384]{1,0:T(8,128)(2,1)}), bf16[64,384]{1,0:T(8,128)(2,1)}) %reduce-scatter.7.cloned.1.call-update) | async-done | bytes 49168
  434.2 0.9 copy.29
  435.2 0.7 copy.23
  435.9 0.7 copy.22
  436.6 0.7 copy.21
  (43 shorter events, 1.8 us)
Async XLA Ops:
  7.2 79.0 %copy-start = (bf16[384,2048]{1,0:T(8,128)(2,1)S(1)}, bf16[384,2048]{1,0:T(8,128)(2,1)}, u32[]{:S(2)}) copy-start(bf16[384,2048]{1,0:T(8,128)(2,1)} %param.7) | copy-start | bytes 4718596
  7.2 79.0 %all-gather.6.cloned.1.call-start = ((), (), s32[]{:S(2)}) async-start(), calls=%async_computation.2 | async-start | bytes 1622016 | tf_op jit(solution)/shard_map/all_gather | solution.py:52
  8.7 80.8 %copy-start.9 = (s32[1,3,3]{2,0,1:T(1,128)S(1)}, s32[1,3,3]{2,0,1:T(1,128)}, u32[]{:S(2)}) copy-start(s32[1,3,3]{2,0,1:T(1,128)} %param.12) | copy-start | bytes 112
  8.8 80.8 %copy-start.7 = (bf16[384,128]{1,0:T(8,128)(2,1)S(1)}, bf16[384,128]{1,0:T(8,128)(2,1)}, u32[]{:S(2)}) copy-start(bf16[384,128]{1,0:T(8,128)(2,1)} %param.13) | copy-start | bytes 294916
  8.8 148.7 %all-gather.8.cloned.1.call-start = ((), (), s32[]{:S(2)}) async-start(), calls=%async_computation.4 | async-start | bytes 1081344 | tf_op jit(solution)/shard_map/all_gather | solution.py:20
  89.4 139.2 %all-gather.10.cloned.1.call-start = ((), (), s32[]{:S(2)}) async-start(), calls=%async_computation.5 | async-start | bytes 1081344 | tf_op jit(solution)/shard_map/all_gather | solution.py:20
  90.5 0.7 copy-start.1
  91.2 68.3 %copy-start.8 = (f32[128]{0:T(128)S(1)}, f32[128]{0:T(128)}, u32[]{:S(2)}) copy-start(f32[128]{0:T(128)} %param.11) | copy-start | bytes 1540
  159.2 0.6 copy-start.3
  159.2 1.5 copy-start.2
  160.7 160.2 %reduce-scatter.5.cloned.1.call-start = ((), (), s32[]{:S(2)}) async-start(), calls=%async_computation.3 | async-start | bytes 1671168 | tf_op jit(solution)/shard_map/reduce_scatter | solution.py:100
  230.2 1.4 copy-start.10
  230.7 3.2 copy-start.4
  231.6 2.3 copy-start.6
  233.9 0.9 copy-start.5
  233.9 200.3 %reduce-scatter.7.cloned.1.call-start = ((), (), s32[]{:S(2)}) async-start(), calls=%async_computation.6 | async-start | bytes 1622016
Sparse Core Ops, SparseCore 0:
  10.7 75.4 all-gather.5
  89.6 67.8 all-gather.7
  160.8 67.8 all-gather.9
  234.0 86.7 reduce-scatter.4
  323.5 110.6 reduce-scatter.6

commit v2 on v1

--- a/solution.py
+++ b/solution.py
@@ -16,13 +16,33 @@
 
 def entering(array, axis, backward):
     count = lax.axis_size(axis)
+    total = array
+    step = 1
+    while step < count:
+        if backward:
+            pairs = [(i, i - step) for i in range(step, count)]
+        else:
+            pairs = [(i, i + step) for i in range(count - step)]
+        total = total + lax.ppermute(total, axis, pairs)
+        step *= 2
+    return total - array
+
+
+def halving_scatter(term, axis):
+    count = lax.axis_size(axis)
     place = lax.axis_index(axis)
-    gathered = lax.all_gather(array.astype(jnp.bfloat16), axis)
-    source = jnp.arange(count)
-    chosen = source > place if backward else source < place
-    flat = gathered.reshape(count, -1)
-    total = jnp.dot(chosen.astype(jnp.bfloat16), flat, preferred_element_type=jnp.float32)
-    return total.reshape(array.shape)
+    rows = term.shape[0] // count
+    current = term.astype(jnp.float32).reshape(count, rows, term.shape[1])
+    bit = 0
+    while (1 << bit) < count:
+        mine = (place >> bit) & 1
+        split = current.reshape(current.shape[0] // 2, 2, rows, term.shape[1])
+        keep = lax.dynamic_index_in_dim(split, mine, 1, False)
+        away = lax.dynamic_index_in_dim(split, 1 - mine, 1, False)
+        pairs = [(i, i ^ (1 << bit)) for i in range(count)]
+        current = keep + lax.ppermute(away.astype(jnp.bfloat16), axis, pairs).astype(jnp.float32)
+        bit += 1
+    return current.reshape(rows, term.shape[1])
 
 
 def allowed_pairs(pattern):
@@ -106,14 +126,12 @@
         tiled=True,
     ).astype(jnp.float32)
     grad_tokens = input_rows.T.astype(jnp.bfloat16)
-    weight_rows = lax.psum_scatter(
+    weight_rows = halving_scatter(
         lax.dot_general(
             tokens, grad_cat, (((0,), (0,)), ((), ())), preferred_element_type=jnp.float32
         ).astype(jnp.bfloat16),
         "seq",
-        scatter_dimension=0,
-        tiled=True,
-    ).astype(jnp.float32)
+    )
     weight_rows = (weight_rows * (1.0 / math.sqrt(SEG * lax.axis_size("seq")))).astype(jnp.bfloat16)
     return (
         attended,

time: 444 us -> 292 us (0.66)
  waiting for transfers between devices: 403 us -> 189 us
  starting transfers between devices: 0.21 us -> 60.8 us
    all_gather x2 -> x0, waiting for transfers between devices: 132 us -> none  [entering(): gathered = lax.all_gather(array.astype(jnp.bfloat16), axis)]
    unnamed x6 -> x2, waiting for transfers between devices: 112 us -> 0.03 us
    ppermute x0 -> x15, waiting for transfers between devices: none -> 87 us  [the longest x10 45.6 us: entering(): total = total + lax.ppermute(total, axis, pairs)]
    ppermute x0 -> x15, starting transfers between devices: none -> 60.7 us  [the longest x10 41.3 us: entering(): total = total + lax.ppermute(total, axis, pairs)]
    reduce_scatter x1, waiting for transfers between devices: 81.9 us -> 25.7 us  [shards(): lax.psum_scatter(lax.dot_general(weight_cat, grad_cat, (((1,), (1,)), (()...]
    unnamed x30 -> x15, local copies, waits for them, and re-layouts: 8.95 us -> 3.4 us
  transfers between devices with their start and end apart: 5 -> 17, of which waited for: 5 -> 17; matrix products, arithmetic and copies ran while one was open for 2% -> 4% of each run, Pallas kernels for 0% -> 0%
where the time goes in v2:
time: 292 us
  waiting for transfers between devices  189 us (65%)
  starting transfers between devices  60.8 us (21%)
  between operations  14.5 us (5%)
  matrix products  10.8 us (4%)
  local copies, waits for them, and re-layouts  10.1 us (3%)
  other arithmetic  6.11 us (2%)
    all_gather x1, waiting for transfers between devices, shards(): lax.all_gather(jnp.concatenate([w_query, w_key, w_value], axis=1), 'seq',...  76.7 us
    ppermute x10, waiting for transfers between devices, entering(): total = total + lax.ppermute(total, axis, pairs)  45.6 us
    ppermute x5, waiting for transfers between devices, halving_scatter(): lax.ppermute(away.astype(jnp.bfloat16), axis, pairs).astype(jnp.float32)  41.4 us
    ppermute x10, starting transfers between devices, entering(): total = total + lax.ppermute(total, axis, pairs)  41.3 us
    reduce_scatter x1, waiting for transfers between devices, shards(): lax.psum_scatter(lax.dot_general(weight_cat, grad_cat, (((1,), (1,)), (()...  25.7 us
    ppermute x5, starting transfers between devices, halving_scatter(): lax.ppermute(away.astype(jnp.bfloat16), axis, pairs).astype(jnp.float32)  19.4 us
  transfers between devices with their start and end apart: 17, of which 17 were waited for; matrix products, arithmetic and copies ran while one was open for 4% of the time, Pallas kernels for 0%

profile of v2, /device:TPU:6, one launch (start us, length us, event | category | flops | bytes accessed | tf_op | source)
XLA Modules:
  0.0 291.7 jit_solution(16574468303862380254)
XLA Ops:
  7.2 1.5 pad_maximum_fusion.3
  9.5 76.7 %all-gather.2.cloned.1.call-done = bf16[2048,384]{1,0:T(8,128)(2,1)} async-done(((bf16[64,384]{1,0:T(8,128)(2,1)}), bf16[2048,384]{1,0:T(8,128)(2,1)}) %all-gather.2.cloned.1.call-update) | async-done | bytes 1572880 | tf_op jit(solution)/shard_map/all_gather | solution.py:72
  86.2 2.4 fusion.2
  88.8 2.1 collective-permute-start
  91.8 5.9 %collective-permute-start.1 = (f32[1,128,128]{2,1,0:T(8,128)S(1)}, f32[1,128,128]{2,1,0:T(8,128)S(1)}, u32[]{:S(2)}, u32[]{:S(2)}) collective-permute-start(f32[1,128,128]{2,1,0:T(8,128)S(1)} %add.129), channel_id=1, source_target_pairs={{0,32},{16,48},{32,64},{48,80},{64,96},{80,112},{96,128},{112,144}... | collective-permute-start | bytes 196616 | tf_op jit(solution)/shard_map/ppermute | solution.py:26
  98.0 1.6 collective-permute-done.1
  99.6 4.3 %collective-permute-start.2 = (f32[1,128,128]{2,1,0:T(8,128)S(1)}, f32[1,128,128]{2,1,0:T(8,128)S(1)}, u32[]{:S(2)}, u32[]{:S(2)}) collective-permute-start(f32[1,128,128]{2,1,0:T(8,128)S(1)} %add.130), channel_id=1, source_target_pairs={{0,64},{16,80},{32,96},{48,112},{64,128},{80,144},{96,160},{112,17... | collective-permute-start | bytes 196616 | tf_op jit(solution)/shard_map/ppermute | solution.py:26
  105.8 10.1 %collective-permute-start.3 = (f32[1,128,128]{2,1,0:T(8,128)S(1)}, f32[1,128,128]{2,1,0:T(8,128)S(1)}, u32[]{:S(2)}, u32[]{:S(2)}) collective-permute-start(f32[1,128,128]{2,1,0:T(8,128)S(1)} %add.131), channel_id=1, source_target_pairs={{0,128},{16,144},{32,160},{48,176},{64,192},{80,208},{96,224},{112... | collective-permute-start | bytes 196616 | tf_op jit(solution)/shard_map/ppermute | solution.py:26
  116.2 1.6 collective-permute-done.3
  117.9 12.4 %collective-permute-start.4 = (f32[1,128,128]{2,1,0:T(8,128)S(1)}, f32[1,128,128]{2,1,0:T(8,128)S(1)}, u32[]{:S(2)}, u32[]{:S(2)}) collective-permute-start(f32[1,128,128]{2,1,0:T(8,128)S(1)} %add.132), channel_id=1, source_target_pairs={{0,256},{16,272},{32,288},{48,304},{64,320},{80,336},{96,352},{112... | collective-permute-start | bytes 196616 | tf_op jit(solution)/shard_map/ppermute | solution.py:26
  130.5 1.6 collective-permute-done.4
  135.0 1.6 collective-permute-done.5
  138.3 4.6 %collective-permute-done.6 = f32[1,128,128]{2,1,0:T(8,128)S(1)} collective-permute-done((f32[1,128,128]{2,1,0:T(8,128)S(1)}, f32[1,128,128]{2,1,0:T(8,128)S(1)}, u32[]{:S(2)}, u32[]{:S(2)}) %collective-permute-start.6) | collective-permute-done | bytes 65568 | tf_op jit(solution)/shard_map/ppermute | solution.py:26
  144.4 5.6 %collective-permute-done.7 = f32[1,128,128]{2,1,0:T(8,128)S(1)} collective-permute-done((f32[1,128,128]{2,1,0:T(8,128)S(1)}, f32[1,128,128]{2,1,0:T(8,128)S(1)}, u32[]{:S(2)}, u32[]{:S(2)}) %collective-permute-start.7) | collective-permute-done | bytes 65568 | tf_op jit(solution)/shard_map/ppermute | solution.py:26
  151.5 8.9 %collective-permute-done.8 = f32[1,128,128]{2,1,0:T(8,128)S(1)} collective-permute-done((f32[1,128,128]{2,1,0:T(8,128)S(1)}, f32[1,128,128]{2,1,0:T(8,128)S(1)}, u32[]{:S(2)}, u32[]{:S(2)}) %collective-permute-start.8) | collective-permute-done | bytes 65568 | tf_op jit(solution)/shard_map/ppermute | solution.py:26
  161.9 18.0 %collective-permute-done.9 = f32[1,128,128]{2,1,0:T(8,128)S(1)} collective-permute-done((f32[1,128,128]{2,1,0:T(8,128)S(1)}, f32[1,128,128]{2,1,0:T(8,128)S(1)}, u32[]{:S(2)}, u32[]{:S(2)}) %collective-permute-start.9) | collective-permute-done | bytes 65568 | tf_op jit(solution)/shard_map/ppermute | solution.py:26
  180.3 2.7 convert_bitcast_fusion
  183.0 3.5 %copy.16 = f32[2048,384]{1,0:T(8,128)} copy(f32[2048,384]{0,1:T(8,128)} %convert_bitcast_fusion) | data formatting | bytes 6291456 | tf_op jit(solution)/shard_map/reshape;reshape | solution.py:39
  186.5 1.6 fusion.12
  188.2 1.9 collective-permute-start.10
  190.1 2.3 convolution_convert_fusion.1
  192.5 1.8 bitcast_add_fusion
  195.1 1.9 collective-permute-start.11
  197.1 11.6 %collective-permute-done.11 = bf16[8,64,384]{2,1,0:T(8,128)(2,1)S(1)} collective-permute-done((bf16[8,64,384]{2,1,0:T(8,128)(2,1)}, bf16[8,64,384]{2,1,0:T(8,128)(2,1)S(1)}, u32[]{:S(2)}, u32[]{:S(2)}) %collective-permute-start.11) | collective-permute-done | bytes 393248 | tf_op jit(solution)/shard_map/ppermute | solution.py:43
  209.7 7.0 %collective-permute-start.12 = (bf16[4,64,384]{2,1,0:T(8,128)(2,1)S(1)}, bf16[4,64,384]{2,1,0:T(8,128)(2,1)S(1)}, u32[]{:S(2)}, u32[]{:S(2)}) collective-permute-start(bf16[4,64,384]{2,1,0:T(8,128)(2,1)S(1)} %fusion.15), channel_id=1, source_target_pairs={{0,64},{16,80},{32,96},{48,112},{64,0},{80,16},{96,32},{112,48},{1... | collective-permute-start | bytes 589832 | tf_op jit(solution)/shard_map/ppermute | solution.py:43
  216.8 9.1 %collective-permute-done.12 = bf16[4,64,384]{2,1,0:T(8,128)(2,1)S(1)} collective-permute-done((bf16[4,64,384]{2,1,0:T(8,128)(2,1)S(1)}, bf16[4,64,384]{2,1,0:T(8,128)(2,1)S(1)}, u32[]{:S(2)}, u32[]{:S(2)}) %collective-permute-start.12) | collective-permute-done | bytes 196640 | tf_op jit(solution)/shard_map/ppermute | solution.py:43
  227.0 6.6 %collective-permute-start.13 = (bf16[2,64,384]{2,1,0:T(8,128)(2,1)S(1)}, bf16[2,64,384]{2,1,0:T(8,128)(2,1)S(1)}, u32[]{:S(2)}, u32[]{:S(2)}) collective-permute-start(bf16[2,64,384]{2,1,0:T(8,128)(2,1)S(1)} %fusion.21), channel_id=1, source_target_pairs={{0,128},{16,144},{32,160},{48,176},{64,192},{80,208},{96,224},{112... | collective-permute-start | bytes 294920 | tf_op jit(solution)/shard_map/ppermute | solution.py:43
  233.6 8.6 %collective-permute-done.13 = bf16[2,64,384]{2,1,0:T(8,128)(2,1)S(1)} collective-permute-done((bf16[2,64,384]{2,1,0:T(8,128)(2,1)S(1)}, bf16[2,64,384]{2,1,0:T(8,128)(2,1)S(1)}, u32[]{:S(2)}, u32[]{:S(2)}) %collective-permute-start.13) | collective-permute-done | bytes 98336 | tf_op jit(solution)/shard_map/ppermute | solution.py:43
  242.2 1.9 collective-permute-start.14
  244.9 12.0 %collective-permute-done.14 = bf16[1,64,384]{2,1,0:T(8,128)(2,1)S(1)} collective-permute-done((bf16[1,64,384]{2,1,0:T(8,128)(2,1)S(1)}, bf16[1,64,384]{2,1,0:T(8,128)(2,1)S(1)}, u32[]{:S(2)}, u32[]{:S(2)}) %collective-permute-start.14) | collective-permute-done | bytes 49184 | tf_op jit(solution)/shard_map/ppermute | solution.py:43
  257.5 25.7 %reduce-scatter.2.cloned.1.call-done = bf16[128,384]{1,0:T(8,128)(2,1)} async-done(((bf16[2048,384]{1,0:T(8,128)(2,1)}), bf16[128,384]{1,0:T(8,128)(2,1)}) %reduce-scatter.2.cloned.1.call-update) | async-done | bytes 98320 | tf_op jit(solution)/shard_map/reduce_scatter | solution.py:120
  283.2 1.6 copy.20
  (65 shorter events, 18.1 us)
Async XLA Ops:
  7.2 79.0 %copy-start = (bf16[384,2048]{1,0:T(8,128)(2,1)S(1)}, bf16[384,2048]{1,0:T(8,128)(2,1)}, u32[]{:S(2)}) copy-start(bf16[384,2048]{1,0:T(8,128)(2,1)} %param.7) | copy-start | bytes 4718596
  7.2 79.0 %all-gather.2.cloned.1.call-start = ((), (), s32[]{:S(2)}) async-start(), calls=%async_computation.1 | async-start | bytes 1622016 | tf_op jit(solution)/shard_map/all_gather | solution.py:72
  8.7 274.4 %reduce-scatter.2.cloned.1.call-start = ((), (), s32[]{:S(2)}) async-start(), calls=%async_computation.2 | async-start | bytes 1671168 | tf_op jit(solution)/shard_map/reduce_scatter | solution.py:120
  88.6 15.9 %copy-start.3 = (bf16[384,128]{1,0:T(8,128)(2,1)S(1)}, bf16[384,128]{1,0:T(8,128)(2,1)}, u32[]{:S(2)}) copy-start(bf16[384,128]{1,0:T(8,128)(2,1)} %param.13) | copy-start | bytes 294916
  88.8 3.0 %collective-permute-start = (f32[1,128,128]{2,1,0:T(8,128)S(1)}, f32[1,128,128]{2,1,0:T(8,128)S(1)}, u32[]{:S(2)}, u32[]{:S(2)}) collective-permute-start(f32[1,128,128]{2,1,0:T(8,128)S(1)} %convolution_bitcast_fusion.1), channel_id=1, source_target_pairs={{0,16},{16,32},{32,48},{48,64},{64,80},{80,96},{96,112},{112,128},... | collective-permute-start | bytes 196616 | tf_op jit(solution)/shard_map/ppermute | solution.py:26
  91.8 7.8 %collective-permute-start.1 = (f32[1,128,128]{2,1,0:T(8,128)S(1)}, f32[1,128,128]{2,1,0:T(8,128)S(1)}, u32[]{:S(2)}, u32[]{:S(2)}) collective-permute-start(f32[1,128,128]{2,1,0:T(8,128)S(1)} %add.129), channel_id=1, source_target_pairs={{0,32},{16,48},{32,64},{48,80},{64,96},{80,112},{96,128},{112,144}... | collective-permute-start | bytes 196616 | tf_op jit(solution)/shard_map/ppermute | solution.py:26
  99.6 6.2 %collective-permute-start.2 = (f32[1,128,128]{2,1,0:T(8,128)S(1)}, f32[1,128,128]{2,1,0:T(8,128)S(1)}, u32[]{:S(2)}, u32[]{:S(2)}) collective-permute-start(f32[1,128,128]{2,1,0:T(8,128)S(1)} %add.130), channel_id=1, source_target_pairs={{0,64},{16,80},{32,96},{48,112},{64,128},{80,144},{96,160},{112,17... | collective-permute-start | bytes 196616 | tf_op jit(solution)/shard_map/ppermute | solution.py:26
  104.5 27.9 %copy-start.4 = (f32[128]{0:T(128)S(1)}, f32[128]{0:T(128)}, u32[]{:S(2)}) copy-start(f32[128]{0:T(128)} %param.11) | copy-start | bytes 1540
  105.8 12.0 %collective-permute-start.3 = (f32[1,128,128]{2,1,0:T(8,128)S(1)}, f32[1,128,128]{2,1,0:T(8,128)S(1)}, u32[]{:S(2)}, u32[]{:S(2)}) collective-permute-start(f32[1,128,128]{2,1,0:T(8,128)S(1)} %add.131), channel_id=1, source_target_pairs={{0,128},{16,144},{32,160},{48,176},{64,192},{80,208},{96,224},{112... | collective-permute-start | bytes 196616 | tf_op jit(solution)/shard_map/ppermute | solution.py:26
  117.9 14.3 %collective-permute-start.4 = (f32[1,128,128]{2,1,0:T(8,128)S(1)}, f32[1,128,128]{2,1,0:T(8,128)S(1)}, u32[]{:S(2)}, u32[]{:S(2)}) collective-permute-start(f32[1,128,128]{2,1,0:T(8,128)S(1)} %add.132), channel_id=1, source_target_pairs={{0,256},{16,272},{32,288},{48,304},{64,320},{80,336},{96,352},{112... | collective-permute-start | bytes 196616 | tf_op jit(solution)/shard_map/ppermute | solution.py:26
  133.5 3.1 %collective-permute-start.5 = (f32[1,128,128]{2,1,0:T(8,128)S(1)}, f32[1,128,128]{2,1,0:T(8,128)S(1)}, u32[]{:S(2)}, u32[]{:S(2)}) collective-permute-start(f32[1,128,128]{2,1,0:T(8,128)S(1)} %convolution_bitcast_fusion), channel_id=1, source_target_pairs={{16,0},{32,16},{48,32},{64,48},{80,64},{96,80},{112,96},{128,112},... | collective-permute-start | bytes 196616 | tf_op jit(solution)/shard_map/ppermute | solution.py:26
  136.7 6.2 %collective-permute-start.6 = (f32[1,128,128]{2,1,0:T(8,128)S(1)}, f32[1,128,128]{2,1,0:T(8,128)S(1)}, u32[]{:S(2)}, u32[]{:S(2)}) collective-permute-start(f32[1,128,128]{2,1,0:T(8,128)S(1)} %add.139), channel_id=1, source_target_pairs={{32,0},{48,16},{64,32},{80,48},{96,64},{112,80},{128,96},{144,112}... | collective-permute-start | bytes 196616 | tf_op jit(solution)/shard_map/ppermute | solution.py:26
  142.9 7.1 %collective-permute-start.7 = (f32[1,128,128]{2,1,0:T(8,128)S(1)}, f32[1,128,128]{2,1,0:T(8,128)S(1)}, u32[]{:S(2)}, u32[]{:S(2)}) collective-permute-start(f32[1,128,128]{2,1,0:T(8,128)S(1)} %add.140), channel_id=1, source_target_pairs={{64,0},{80,16},{96,32},{112,48},{128,64},{144,80},{160,96},{176,11... | collective-permute-start | bytes 196616 | tf_op jit(solution)/shard_map/ppermute | solution.py:26
  150.0 10.5 %collective-permute-start.8 = (f32[1,128,128]{2,1,0:T(8,128)S(1)}, f32[1,128,128]{2,1,0:T(8,128)S(1)}, u32[]{:S(2)}, u32[]{:S(2)}) collective-permute-start(f32[1,128,128]{2,1,0:T(8,128)S(1)} %add.141), channel_id=1, source_target_pairs={{128,0},{144,16},{160,32},{176,48},{192,64},{208,80},{224,96},{240... | collective-permute-start | bytes 196616 | tf_op jit(solution)/shard_map/ppermute | solution.py:26
  160.4 19.5 %collective-permute-start.9 = (f32[1,128,128]{2,1,0:T(8,128)S(1)}, f32[1,128,128]{2,1,0:T(8,128)S(1)}, u32[]{:S(2)}, u32[]{:S(2)}) collective-permute-start(f32[1,128,128]{2,1,0:T(8,128)S(1)} %add.142), channel_id=1, source_target_pairs={{256,0},{272,16},{288,32},{304,48},{320,64},{336,80},{352,96},{368... | collective-permute-start | bytes 196616 | tf_op jit(solution)/shard_map/ppermute | solution.py:26
  186.5 3.6 %copy-start.5 = (bf16[2048,384]{1,0:T(8,128)(2,1)S(1)}, bf16[2048,384]{1,0:T(8,128)(2,1)}, u32[]{:S(2)}) copy-start(bf16[2048,384]{1,0:T(8,128)(2,1)} %all-gather.2.cloned.1.call-done) | copy-start | bytes 4718596
  188.2 4.3 %collective-permute-start.10 = (bf16[16,64,384]{2,1,0:T(8,128)(2,1)S(1)}, bf16[16,64,384]{2,1,0:T(8,128)(2,1)}, u32[]{:S(2)}, u32[]{:S(2)}) collective-permute-start(bf16[16,64,384]{2,1,0:T(8,128)(2,1)S(1)} %fusion.12), channel_id=1, source_target_pairs={{0,16},{16,0},{32,48},{48,32},{64,80},{80,64},{96,112},{112,96},{1... | collective-permute-start | bytes 2359304 | tf_op jit(solution)/shard_map/ppermute | solution.py:43
  195.1 13.6 %collective-permute-start.11 = (bf16[8,64,384]{2,1,0:T(8,128)(2,1)}, bf16[8,64,384]{2,1,0:T(8,128)(2,1)S(1)}, u32[]{:S(2)}, u32[]{:S(2)}) collective-permute-start(bf16[8,64,384]{2,1,0:T(8,128)(2,1)} %fusion.14), channel_id=1, source_target_pairs={{0,32},{16,48},{32,0},{48,16},{64,96},{80,112},{96,64},{112,80},{1... | collective-permute-start | bytes 1179656 | tf_op jit(solution)/shard_map/ppermute | solution.py:43
  208.8 0.9 copy-start.1
  208.8 35.3 %copy-start.2 = (bf16[384,128]{0,1:T(8,128)(2,1)S(1)}, bf16[384,128]{0,1:T(8,128)(2,1)}, u32[]{:S(2)}) copy-start(bf16[384,128]{0,1:T(8,128)(2,1)} %get-tuple-element.16) | copy-start | bytes 294916
  209.7 16.2 %collective-permute-start.12 = (bf16[4,64,384]{2,1,0:T(8,128)(2,1)S(1)}, bf16[4,64,384]{2,1,0:T(8,128)(2,1)S(1)}, u32[]{:S(2)}, u32[]{:S(2)}) collective-permute-start(bf16[4,64,384]{2,1,0:T(8,128)(2,1)S(1)} %fusion.15), channel_id=1, source_target_pairs={{0,64},{16,80},{32,96},{48,112},{64,0},{80,16},{96,32},{112,48},{1... | collective-permute-start | bytes 589832 | tf_op jit(solution)/shard_map/ppermute | solution.py:43
  227.0 15.2 %collective-permute-start.13 = (bf16[2,64,384]{2,1,0:T(8,128)(2,1)S(1)}, bf16[2,64,384]{2,1,0:T(8,128)(2,1)S(1)}, u32[]{:S(2)}, u32[]{:S(2)}) collective-permute-start(bf16[2,64,384]{2,1,0:T(8,128)(2,1)S(1)} %fusion.21), channel_id=1, source_target_pairs={{0,128},{16,144},{32,160},{48,176},{64,192},{80,208},{96,224},{112... | collective-permute-start | bytes 294920 | tf_op jit(solution)/shard_map/ppermute | solution.py:43
  242.2 14.7 %collective-permute-start.14 = (bf16[1,64,384]{2,1,0:T(8,128)(2,1)S(1)}, bf16[1,64,384]{2,1,0:T(8,128)(2,1)S(1)}, u32[]{:S(2)}, u32[]{:S(2)}) collective-permute-start(bf16[1,64,384]{2,1,0:T(8,128)(2,1)S(1)} %dynamic-slice_convert_fusion.2), channel_id=1, source_target_pairs={{0,256},{16,272},{32,288},{48,304},{64,320},{80,336},{96,352},{112... | collective-permute-start | bytes 147464 | tf_op jit(solution)/shard_map/ppermute | solution.py:43
Sparse Core Ops, SparseCore 0:
  10.7 75.4 all-gather.1
  192.6 90.5 reduce-scatter.1

commit v3 on v2

--- a/solution.py
+++ b/solution.py
@@ -3,7 +3,7 @@
 import jax
 import jax.numpy as jnp
 from jax import lax
-from jax.sharding import PartitionSpec as P
+from jax.sharding import Mesh, PartitionSpec as P
 
 HDIM = 128
 BLOCK = 128
@@ -12,24 +12,29 @@
 
 
 EPSILON = 1e-06
+SEQ = ("z", "core")
 
 
-def entering(array, axis, backward):
-    count = lax.axis_size(axis)
+def entering(array, axis, count, backward):
     total = array
     step = 1
     while step < count:
-        if backward:
-            pairs = [(i, i - step) for i in range(step, count)]
-        else:
-            pairs = [(i, i + step) for i in range(count - step)]
-        total = total + lax.ppermute(total, axis, pairs)
-        step *= 2
+        parts = [total]
+        for times in (1, 2, 3):
+            shift = step * times
+            if shift >= count:
+                break
+            if backward:
+                pairs = [(i, i - shift) for i in range(shift, count)]
+            else:
+                pairs = [(i, i + shift) for i in range(count - shift)]
+            parts.append(lax.ppermute(total, axis, pairs))
+        total = sum(parts[1:], parts[0])
+        step *= 4
     return total - array
 
 
-def halving_scatter(term, axis):
-    count = lax.axis_size(axis)
+def halving_scatter(term, axis, count):
     place = lax.axis_index(axis)
     rows = term.shape[0] // count
     current = term.astype(jnp.float32).reshape(count, rows, term.shape[1])
@@ -69,9 +74,12 @@
     columns = w_query.shape[1]
     heads_here = columns // HDIM
     allowed = allowed_pairs(block_mask[0])
-    weight_cat = lax.all_gather(
-        jnp.concatenate([w_query, w_key, w_value], axis=1), "seq", axis=0, tiled=True
+    seq_count = lax.axis_size("z") * lax.axis_size("core")
+    fsdp_count = lax.axis_size("fsdp")
+    pair_rows = lax.all_gather(
+        jnp.concatenate([w_query, w_key, w_value], axis=1), "core", axis=0, tiled=True
     )
+    weight_cat = lax.all_gather(pair_rows, "z", axis=0, tiled=True)
     projected = jnp.dot(tokens, weight_cat, preferred_element_type=jnp.float32)
     projected = projected.astype(jnp.bfloat16)
     queries = projected[:, :columns].reshape(SEG, heads_here, HDIM)
@@ -80,7 +88,7 @@
     increment = jnp.einsum(
         "thd,the->hde", key_heads, value_heads, preferred_element_type=jnp.float32
     )
-    state = entering(increment, "seq", False)
+    state = entering(increment, SEQ, seq_count, False)
     state_low = state.astype(jnp.bfloat16)
     scores = jnp.einsum("shd,thd->hst", queries, key_heads, preferred_element_type=jnp.float32)
     weights = jnp.where(allowed[None], scores, 0.0).astype(jnp.bfloat16)
@@ -97,7 +105,7 @@
         jnp.bfloat16
     )
     d_state = jnp.einsum("shd,she->hde", queries, d_mixed, preferred_element_type=jnp.float32)
-    later = entering(d_state, "seq", True)
+    later = entering(d_state, SEQ, seq_count, True)
     later_low = later.astype(jnp.bfloat16)
     d_scores = jnp.einsum("she,the->hst", d_mixed, value_heads, preferred_element_type=jnp.float32)
     d_weights = jnp.where(allowed[None], d_scores, 0.0).astype(jnp.bfloat16)
@@ -117,22 +125,22 @@
         [part.reshape(SEG, columns).astype(jnp.bfloat16) for part in (d_queries, d_keys, d_values)],
         axis=1,
     )
-    input_rows = lax.psum_scatter(
+    input_rows = halving_scatter(
         lax.dot_general(
             weight_cat, grad_cat, (((1,), (1,)), ((), ())), preferred_element_type=jnp.float32
         ).astype(jnp.bfloat16),
         "fsdp",
-        scatter_dimension=0,
-        tiled=True,
-    ).astype(jnp.float32)
+        fsdp_count,
+    )
     grad_tokens = input_rows.T.astype(jnp.bfloat16)
     weight_rows = halving_scatter(
         lax.dot_general(
             tokens, grad_cat, (((0,), (0,)), ((), ())), preferred_element_type=jnp.float32
         ).astype(jnp.bfloat16),
-        "seq",
+        SEQ,
+        seq_count,
     )
-    weight_rows = (weight_rows * (1.0 / math.sqrt(SEG * lax.axis_size("seq")))).astype(jnp.bfloat16)
+    weight_rows = (weight_rows * (1.0 / math.sqrt(SEG * seq_count))).astype(jnp.bfloat16)
     return (
         attended,
         grad_tokens,
@@ -143,25 +151,28 @@
 
 
 def solution(mesh):
+    split_mesh = Mesh(
+        mesh.devices.reshape(mesh.shape["seq"] // 2, 2, mesh.shape["fsdp"]), ("z", "core", "fsdp")
+    )
     placed = (
-        P("seq", None),
-        P("seq", "fsdp"),
-        P("seq", "fsdp"),
-        P("seq", "fsdp"),
+        P(SEQ, None),
+        P(SEQ, "fsdp"),
+        P(SEQ, "fsdp"),
+        P(SEQ, "fsdp"),
         P("fsdp"),
-        P("seq", None, None),
-        P("seq", "fsdp"),
+        P(SEQ, None, None),
+        P(SEQ, "fsdp"),
     )
     return jax.shard_map(
         shards,
-        mesh=mesh,
+        mesh=split_mesh,
         in_specs=placed,
         out_specs=(
-            P("seq", "fsdp"),
-            P("seq", "fsdp"),
-            P("seq", "fsdp"),
-            P("seq", "fsdp"),
-            P("seq", "fsdp"),
+            P(SEQ, "fsdp"),
+            P(SEQ, "fsdp"),
+            P(SEQ, "fsdp"),
+            P(SEQ, "fsdp"),
+            P(SEQ, "fsdp"),
         ),
         check_vma=False,
     )

time: 292 us -> 281 us (0.962)
  waiting for transfers between devices: 189 us -> 151 us
  starting transfers between devices: 60.8 us -> 81.7 us
  local copies, waits for them, and re-layouts: 10.1 us -> 13.9 us
    reduce_scatter x1 -> x0, waiting for transfers between devices: 25.7 us -> none  [shards(): lax.psum_scatter(lax.dot_general(weight_cat, grad_cat, (((1,), (1,)), (()...]
    ppermute x5 -> x9, starting transfers between devices: 19.4 us -> 32.6 us  [halving_scatter(): lax.ppermute(away.astype(jnp.bfloat16), axis, pairs).astype(jnp.float32)]
    ppermute x10 -> x14, starting transfers between devices: 41.3 us -> 49.1 us  [entering(): parts.append(lax.ppermute(total, axis, pairs))]
    ppermute x5 -> x9, waiting for transfers between devices: 41.4 us -> 35.1 us  [halving_scatter(): lax.ppermute(away.astype(jnp.bfloat16), axis, pairs).astype(jnp.float32)]
    ppermute x10 -> x14, waiting for transfers between devices: 45.6 us -> 40 us  [entering(): parts.append(lax.ppermute(total, axis, pairs))]
  transfers between devices with their start and end apart: 17 -> 24, of which waited for: 17 -> 13; matrix products, arithmetic and copies ran while one was open for 4% -> 5% of each run, Pallas kernels for 0% -> 0%
where the time goes in v3:
time: 281 us; the launch traced here: 280 us
  waiting for transfers between devices  151 us (54%)
  starting transfers between devices  81.7 us (29%)
  between operations  14.6 us (5%)
  local copies, waits for them, and re-layouts  13.9 us (5%)
  matrix products  9.68 us (3%)
  other arithmetic  7.42 us (3%)
    all_gather x1, waiting for transfers between devices, shards(): weight_cat = lax.all_gather(pair_rows, 'z', axis=0, tiled=True)  75.5 us
    ppermute x14, starting transfers between devices, entering(): parts.append(lax.ppermute(total, axis, pairs))  49.1 us
    ppermute x14, waiting for transfers between devices, entering(): parts.append(lax.ppermute(total, axis, pairs))  40 us
    ppermute x9, waiting for transfers between devices, halving_scatter(): lax.ppermute(away.astype(jnp.bfloat16), axis, pairs).astype(jnp.float32)  35.1 us
    ppermute x9, starting transfers between devices, halving_scatter(): lax.ppermute(away.astype(jnp.bfloat16), axis, pairs).astype(jnp.float32)  32.6 us
  transfers between devices with their start and end apart: 24, of which 13 were waited for; matrix products, arithmetic and copies ran while one was open for 5% of the time, Pallas kernels for 0%

profile of v3, /device:TPU:6, one launch (start us, length us, event | category | flops | bytes accessed | tf_op | source)
XLA Modules:
  0.0 279.9 jit_solution(7960701200601283070)
XLA Ops:
  8.1 2.0 all_gather.6
  11.1 75.5 %all-gather.2.cloned.1.call-done = bf16[2048,384]{1,0:T(8,128)(2,1)} async-done(((bf16[128,384]{1,0:T(8,128)(2,1)}), bf16[2048,384]{1,0:T(8,128)(2,1)}) %all-gather.2.cloned.1.call-update) | async-done | bytes 1572880 | tf_op jit(solution)/shard_map/all_gather | solution.py:82
  86.6 2.4 fusion.2
  90.5 3.3 %collective-permute-start.1 = (f32[1,128,128]{2,1,0:T(8,128)S(1)}, f32[1,128,128]{2,1,0:T(8,128)S(1)}, u32[]{:S(2)}, u32[]{:S(2)}) collective-permute-start(f32[1,128,128]{2,1,0:T(8,128)S(1)} %convolution_bitcast_fusion.1), channel_id=1, source_target_pairs={{0,32},{16,48},{32,64},{48,80},{64,96},{80,112},{96,128},{112,144}... | collective-permute-start | bytes 196616 | tf_op jit(solution)/shard_map/ppermute | solution.py:31
  93.8 3.8 %collective-permute-start = (f32[1,128,128]{2,1,0:T(8,128)S(1)}, f32[1,128,128]{2,1,0:T(8,128)S(1)}, u32[]{:S(2)}, u32[]{:S(2)}) collective-permute-start(f32[1,128,128]{2,1,0:T(8,128)S(1)} %convolution_bitcast_fusion.1), channel_id=1, source_target_pairs={{0,16},{16,32},{32,48},{48,64},{64,80},{80,96},{96,112},{112,128},... | collective-permute-start | bytes 196616 | tf_op jit(solution)/shard_map/ppermute | solution.py:31
  98.6 8.9 %collective-permute-start.5 = (f32[1,128,128]{2,1,0:T(8,128)S(1)}, f32[1,128,128]{2,1,0:T(8,128)S(1)}, u32[]{:S(2)}, u32[]{:S(2)}) collective-permute-start(f32[1,128,128]{2,1,0:T(8,128)S(1)} %add_add_fusion.3), channel_id=1, source_target_pairs={{0,192},{16,208},{32,224},{48,240},{64,256},{80,272},{96,288},{112... | collective-permute-start | bytes 196616 | tf_op jit(solution)/shard_map/ppermute | solution.py:31
  107.5 3.7 %collective-permute-start.4 = (f32[1,128,128]{2,1,0:T(8,128)S(1)}, f32[1,128,128]{2,1,0:T(8,128)S(1)}, u32[]{:S(2)}, u32[]{:S(2)}) collective-permute-start(f32[1,128,128]{2,1,0:T(8,128)S(1)} %add_add_fusion.3), channel_id=1, source_target_pairs={{0,128},{16,144},{32,160},{48,176},{64,192},{80,208},{96,224},{112... | collective-permute-start | bytes 196616 | tf_op jit(solution)/shard_map/ppermute | solution.py:31
  111.2 5.1 %collective-permute-start.3 = (f32[1,128,128]{2,1,0:T(8,128)S(1)}, f32[1,128,128]{2,1,0:T(8,128)S(1)}, u32[]{:S(2)}, u32[]{:S(2)}) collective-permute-start(f32[1,128,128]{2,1,0:T(8,128)S(1)} %add_add_fusion.3), channel_id=1, source_target_pairs={{0,64},{16,80},{32,96},{48,112},{64,128},{80,144},{96,160},{112,17... | collective-permute-start | bytes 196616 | tf_op jit(solution)/shard_map/ppermute | solution.py:31
  118.2 13.9 %collective-permute-start.6 = (f32[1,128,128]{2,1,0:T(8,128)S(1)}, f32[1,128,128]{2,1,0:T(8,128)S(1)}, u32[]{:S(2)}, u32[]{:S(2)}) collective-permute-start(f32[1,128,128]{2,1,0:T(8,128)S(1)} %add_add_fusion.2), channel_id=1, source_target_pairs={{0,256},{16,272},{32,288},{48,304},{64,320},{80,336},{96,352},{112... | collective-permute-start | bytes 196616 | tf_op jit(solution)/shard_map/ppermute | solution.py:31
  132.4 1.6 collective-permute-done.6
  141.4 2.4 collective-permute-done.8
  148.0 8.4 %collective-permute-done.12 = f32[1,128,128]{2,1,0:T(8,128)S(1)} collective-permute-done((f32[1,128,128]{2,1,0:T(8,128)S(1)}, f32[1,128,128]{2,1,0:T(8,128)S(1)}, u32[]{:S(2)}, u32[]{:S(2)}) %collective-permute-start.12) | collective-permute-done | bytes 65568 | tf_op jit(solution)/shard_map/ppermute | solution.py:31
  156.4 7.6 %collective-permute-done.11 = f32[1,128,128]{2,1,0:T(8,128)S(1)} collective-permute-done((f32[1,128,128]{2,1,0:T(8,128)S(1)}, f32[1,128,128]{2,1,0:T(8,128)S(1)}, u32[]{:S(2)}, u32[]{:S(2)}) %collective-permute-start.11) | collective-permute-done | bytes 65568 | tf_op jit(solution)/shard_map/ppermute | solution.py:31
  165.5 16.8 %collective-permute-done.13 = f32[1,128,128]{2,1,0:T(8,128)S(1)} collective-permute-done((f32[1,128,128]{2,1,0:T(8,128)S(1)}, f32[1,128,128]{2,1,0:T(8,128)S(1)}, u32[]{:S(2)}, u32[]{:S(2)}) %collective-permute-start.13) | collective-permute-done | bytes 65568 | tf_op jit(solution)/shard_map/ppermute | solution.py:31
  182.7 2.6 convert_bitcast_fusion
  185.3 3.6 %copy.22 = f32[2048,384]{1,0:T(8,128)} copy(f32[2048,384]{0,1:T(8,128)} %convert_bitcast_fusion) | data formatting | bytes 6291456 | tf_op jit(solution)/shard_map/reshape;reshape | solution.py:44
  188.9 1.6 fusion.12
  190.6 1.9 collective-permute-start.18
  196.6 3.4 %collective-permute-start.14 = (bf16[8,128,384]{2,1,0:T(8,128)(2,1)}, bf16[8,128,384]{2,1,0:T(8,128)(2,1)}, u32[]{:S(2)}, u32[]{:S(2)}) collective-permute-start(bf16[8,128,384]{2,1,0:T(8,128)(2,1)} %fusion.13), channel_id=1, source_target_pairs={{0,1},{1,0},{2,3},{3,2},{4,5},{5,4},{6,7},{7,6},{8,9},{9,8},{10,11... | collective-permute-start | bytes 2359304 | tf_op jit(solution)/shard_map/ppermute | solution.py:48
  200.0 2.0 bitcast_add_fusion
  202.8 1.9 collective-permute-start.19
  204.7 14.0 %collective-permute-done.14 = bf16[8,128,384]{2,1,0:T(8,128)(2,1)} collective-permute-done((bf16[8,128,384]{2,1,0:T(8,128)(2,1)}, bf16[8,128,384]{2,1,0:T(8,128)(2,1)}, u32[]{:S(2)}, u32[]{:S(2)}) %collective-permute-start.14) | collective-permute-done | bytes 786464 | tf_op jit(solution)/shard_map/ppermute | solution.py:48
  222.1 5.0 %collective-permute-start.15 = (bf16[4,128,384]{2,1,0:T(8,128)(2,1)}, bf16[4,128,384]{2,1,0:T(8,128)(2,1)}, u32[]{:S(2)}, u32[]{:S(2)}) collective-permute-start(bf16[4,128,384]{2,1,0:T(8,128)(2,1)} %fusion.15), channel_id=1, source_target_pairs={{0,2},{1,3},{2,0},{3,1},{4,6},{5,7},{6,4},{7,5},{8,10},{9,11},{10,... | collective-permute-start | bytes 1179656 | tf_op jit(solution)/shard_map/ppermute | solution.py:48
  228.8 4.6 %collective-permute-start.20 = (bf16[4,64,384]{2,1,0:T(8,128)(2,1)S(1)}, bf16[4,64,384]{2,1,0:T(8,128)(2,1)S(1)}, u32[]{:S(2)}, u32[]{:S(2)}) collective-permute-start(bf16[4,64,384]{2,1,0:T(8,128)(2,1)S(1)} %fusion.18), channel_id=1, source_target_pairs={{0,64},{16,80},{32,96},{48,112},{64,0},{80,16},{96,32},{112,48},{1... | collective-permute-start | bytes 589832 | tf_op jit(solution)/shard_map/ppermute | solution.py:48
  233.4 3.0 %collective-permute-done.15 = bf16[4,128,384]{2,1,0:T(8,128)(2,1)} collective-permute-done((bf16[4,128,384]{2,1,0:T(8,128)(2,1)}, bf16[4,128,384]{2,1,0:T(8,128)(2,1)}, u32[]{:S(2)}, u32[]{:S(2)}) %collective-permute-start.15) | collective-permute-done | bytes 393248 | tf_op jit(solution)/shard_map/ppermute | solution.py:48
  237.5 2.8 collective-permute-start.16
  240.3 1.8 collective-permute-done.20
  242.2 7.7 %collective-permute-start.21 = (bf16[2,64,384]{2,1,0:T(8,128)(2,1)S(1)}, bf16[2,64,384]{2,1,0:T(8,128)(2,1)S(1)}, u32[]{:S(2)}, u32[]{:S(2)}) collective-permute-start(bf16[2,64,384]{2,1,0:T(8,128)(2,1)S(1)} %fusion.25), channel_id=1, source_target_pairs={{0,128},{16,144},{32,160},{48,176},{64,192},{80,208},{96,224},{112... | collective-permute-start | bytes 294920 | tf_op jit(solution)/shard_map/ppermute | solution.py:48
  250.0 3.3 %collective-permute-start.17 = (bf16[1,128,384]{2,1,0:T(8,128)(2,1)S(1)}, bf16[1,128,384]{2,1,0:T(8,128)(2,1)S(1)}, u32[]{:S(2)}, u32[]{:S(2)}) collective-permute-start(bf16[1,128,384]{2,1,0:T(8,128)(2,1)S(1)} %dynamic-slice_convert_fusion.4), channel_id=1, source_target_pairs={{0,8},{1,9},{2,10},{3,11},{4,12},{5,13},{6,14},{7,15},{8,0},{9,1},... | collective-permute-start | bytes 294920 | tf_op jit(solution)/shard_map/ppermute | solution.py:48
  253.3 4.3 %collective-permute-done.21 = bf16[2,64,384]{2,1,0:T(8,128)(2,1)S(1)} collective-permute-done((bf16[2,64,384]{2,1,0:T(8,128)(2,1)S(1)}, bf16[2,64,384]{2,1,0:T(8,128)(2,1)S(1)}, u32[]{:S(2)}, u32[]{:S(2)}) %collective-permute-start.21) | collective-permute-done | bytes 98336 | tf_op jit(solution)/shard_map/ppermute | solution.py:48
  257.7 2.0 collective-permute-start.22
  260.6 11.9 %collective-permute-done.22 = bf16[1,64,384]{2,1,0:T(8,128)(2,1)S(1)} collective-permute-done((bf16[1,64,384]{2,1,0:T(8,128)(2,1)S(1)}, bf16[1,64,384]{2,1,0:T(8,128)(2,1)S(1)}, u32[]{:S(2)}, u32[]{:S(2)}) %collective-permute-start.22) | collective-permute-done | bytes 49184 | tf_op jit(solution)/shard_map/ppermute | solution.py:48
  (88 shorter events, 32.3 us)
Async XLA Ops:
  7.2 79.4 %copy-start = (bf16[384,2048]{1,0:T(8,128)(2,1)S(1)}, bf16[384,2048]{1,0:T(8,128)(2,1)}, u32[]{:S(2)}) copy-start(bf16[384,2048]{1,0:T(8,128)(2,1)} %param.7) | copy-start | bytes 4718596
  7.2 79.4 %all-gather.2.cloned.1.call-start = ((), (), s32[]{:S(2)}) async-start(), calls=%async_computation | async-start | bytes 1671168 | tf_op jit(solution)/shard_map/all_gather | solution.py:82
  89.0 9.3 %copy-start.5 = (bf16[384,128]{1,0:T(8,128)(2,1)S(1)}, bf16[384,128]{1,0:T(8,128)(2,1)}, u32[]{:S(2)}) copy-start(bf16[384,128]{1,0:T(8,128)(2,1)} %param.13) | copy-start | bytes 294916
  89.2 9.3 %collective-permute-start.2 = (f32[1,128,128]{2,1,0:T(8,128)S(1)}, f32[1,128,128]{2,1,0:T(8,128)S(1)}, u32[]{:S(2)}, u32[]{:S(2)}) collective-permute-start(f32[1,128,128]{2,1,0:T(8,128)S(1)} %convolution_bitcast_fusion.1), channel_id=1, source_target_pairs={{0,48},{16,64},{32,80},{48,96},{64,112},{80,128},{96,144},{112,160... | collective-permute-start | bytes 196616 | tf_op jit(solution)/shard_map/ppermute | solution.py:31
  90.5 8.0 %collective-permute-start.1 = (f32[1,128,128]{2,1,0:T(8,128)S(1)}, f32[1,128,128]{2,1,0:T(8,128)S(1)}, u32[]{:S(2)}, u32[]{:S(2)}) collective-permute-start(f32[1,128,128]{2,1,0:T(8,128)S(1)} %convolution_bitcast_fusion.1), channel_id=1, source_target_pairs={{0,32},{16,48},{32,64},{48,80},{64,96},{80,112},{96,128},{112,144}... | collective-permute-start | bytes 196616 | tf_op jit(solution)/shard_map/ppermute | solution.py:31
  93.8 4.7 %collective-permute-start = (f32[1,128,128]{2,1,0:T(8,128)S(1)}, f32[1,128,128]{2,1,0:T(8,128)S(1)}, u32[]{:S(2)}, u32[]{:S(2)}) collective-permute-start(f32[1,128,128]{2,1,0:T(8,128)S(1)} %convolution_bitcast_fusion.1), channel_id=1, source_target_pairs={{0,16},{16,32},{32,48},{48,64},{64,80},{80,96},{96,112},{112,128},... | collective-permute-start | bytes 196616 | tf_op jit(solution)/shard_map/ppermute | solution.py:31
  98.3 36.0 %copy-start.6 = (f32[128]{0:T(128)S(1)}, f32[128]{0:T(128)}, u32[]{:S(2)}) copy-start(f32[128]{0:T(128)} %param.11) | copy-start | bytes 1540
  98.6 18.0 %collective-permute-start.5 = (f32[1,128,128]{2,1,0:T(8,128)S(1)}, f32[1,128,128]{2,1,0:T(8,128)S(1)}, u32[]{:S(2)}, u32[]{:S(2)}) collective-permute-start(f32[1,128,128]{2,1,0:T(8,128)S(1)} %add_add_fusion.3), channel_id=1, source_target_pairs={{0,192},{16,208},{32,224},{48,240},{64,256},{80,272},{96,288},{112... | collective-permute-start | bytes 196616 | tf_op jit(solution)/shard_map/ppermute | solution.py:31
  107.5 9.1 %collective-permute-start.4 = (f32[1,128,128]{2,1,0:T(8,128)S(1)}, f32[1,128,128]{2,1,0:T(8,128)S(1)}, u32[]{:S(2)}, u32[]{:S(2)}) collective-permute-start(f32[1,128,128]{2,1,0:T(8,128)S(1)} %add_add_fusion.3), channel_id=1, source_target_pairs={{0,128},{16,144},{32,160},{48,176},{64,192},{80,208},{96,224},{112... | collective-permute-start | bytes 196616 | tf_op jit(solution)/shard_map/ppermute | solution.py:31
  111.2 7.0 %collective-permute-start.3 = (f32[1,128,128]{2,1,0:T(8,128)S(1)}, f32[1,128,128]{2,1,0:T(8,128)S(1)}, u32[]{:S(2)}, u32[]{:S(2)}) collective-permute-start(f32[1,128,128]{2,1,0:T(8,128)S(1)} %add_add_fusion.3), channel_id=1, source_target_pairs={{0,64},{16,80},{32,96},{48,112},{64,128},{80,144},{96,160},{112,17... | collective-permute-start | bytes 196616 | tf_op jit(solution)/shard_map/ppermute | solution.py:31
  118.2 15.8 %collective-permute-start.6 = (f32[1,128,128]{2,1,0:T(8,128)S(1)}, f32[1,128,128]{2,1,0:T(8,128)S(1)}, u32[]{:S(2)}, u32[]{:S(2)}) collective-permute-start(f32[1,128,128]{2,1,0:T(8,128)S(1)} %add_add_fusion.2), channel_id=1, source_target_pairs={{0,256},{16,272},{32,288},{48,304},{64,320},{80,336},{96,352},{112... | collective-permute-start | bytes 196616 | tf_op jit(solution)/shard_map/ppermute | solution.py:31
  135.6 5.8 %collective-permute-start.9 = (f32[1,128,128]{2,1,0:T(8,128)S(1)}, f32[1,128,128]{2,1,0:T(8,128)S(1)}, u32[]{:S(2)}, u32[]{:S(2)}) collective-permute-start(f32[1,128,128]{2,1,0:T(8,128)S(1)} %convolution_bitcast_fusion), channel_id=1, source_target_pairs={{48,0},{64,16},{80,32},{96,48},{112,64},{128,80},{144,96},{160,112... | collective-permute-start | bytes 196616 | tf_op jit(solution)/shard_map/ppermute | solution.py:31
  136.9 6.9 %collective-permute-start.8 = (f32[1,128,128]{2,1,0:T(8,128)S(1)}, f32[1,128,128]{2,1,0:T(8,128)S(1)}, u32[]{:S(2)}, u32[]{:S(2)}) collective-permute-start(f32[1,128,128]{2,1,0:T(8,128)S(1)} %convolution_bitcast_fusion), channel_id=1, source_target_pairs={{32,0},{48,16},{64,32},{80,48},{96,64},{112,80},{128,96},{144,112}... | collective-permute-start | bytes 196616 | tf_op jit(solution)/shard_map/ppermute | solution.py:31
  138.2 5.6 %collective-permute-start.7 = (f32[1,128,128]{2,1,0:T(8,128)S(1)}, f32[1,128,128]{2,1,0:T(8,128)S(1)}, u32[]{:S(2)}, u32[]{:S(2)}) collective-permute-start(f32[1,128,128]{2,1,0:T(8,128)S(1)} %convolution_bitcast_fusion), channel_id=1, source_target_pairs={{16,0},{32,16},{48,32},{64,48},{80,64},{96,80},{112,96},{128,112},... | collective-permute-start | bytes 196616 | tf_op jit(solution)/shard_map/ppermute | solution.py:31
  143.8 12.6 %collective-permute-start.12 = (f32[1,128,128]{2,1,0:T(8,128)S(1)}, f32[1,128,128]{2,1,0:T(8,128)S(1)}, u32[]{:S(2)}, u32[]{:S(2)}) collective-permute-start(f32[1,128,128]{2,1,0:T(8,128)S(1)} %add_add_fusion.1), channel_id=1, source_target_pairs={{192,0},{208,16},{224,32},{240,48},{256,64},{272,80},{288,96},{304... | collective-permute-start | bytes 196616 | tf_op jit(solution)/shard_map/ppermute | solution.py:31
  145.1 18.8 %collective-permute-start.11 = (f32[1,128,128]{2,1,0:T(8,128)S(1)}, f32[1,128,128]{2,1,0:T(8,128)S(1)}, u32[]{:S(2)}, u32[]{:S(2)}) collective-permute-start(f32[1,128,128]{2,1,0:T(8,128)S(1)} %add_add_fusion.1), channel_id=1, source_target_pairs={{128,0},{144,16},{160,32},{176,48},{192,64},{208,80},{224,96},{240... | collective-permute-start | bytes 196616 | tf_op jit(solution)/shard_map/ppermute | solution.py:31
  146.4 17.6 %collective-permute-start.10 = (f32[1,128,128]{2,1,0:T(8,128)S(1)}, f32[1,128,128]{2,1,0:T(8,128)S(1)}, u32[]{:S(2)}, u32[]{:S(2)}) collective-permute-start(f32[1,128,128]{2,1,0:T(8,128)S(1)} %add_add_fusion.1), channel_id=1, source_target_pairs={{64,0},{80,16},{96,32},{112,48},{128,64},{144,80},{160,96},{176,11... | collective-permute-start | bytes 196616 | tf_op jit(solution)/shard_map/ppermute | solution.py:31
  164.0 18.3 %collective-permute-start.13 = (f32[1,128,128]{2,1,0:T(8,128)S(1)}, f32[1,128,128]{2,1,0:T(8,128)S(1)}, u32[]{:S(2)}, u32[]{:S(2)}) collective-permute-start(f32[1,128,128]{2,1,0:T(8,128)S(1)} %add_add_fusion), channel_id=1, source_target_pairs={{256,0},{272,16},{288,32},{304,48},{320,64},{336,80},{352,96},{368... | collective-permute-start | bytes 196616 | tf_op jit(solution)/shard_map/ppermute | solution.py:31
  188.9 3.6 %copy-start.7 = (bf16[2048,384]{1,0:T(8,128)(2,1)S(1)}, bf16[2048,384]{1,0:T(8,128)(2,1)}, u32[]{:S(2)}) copy-start(bf16[2048,384]{1,0:T(8,128)(2,1)} %all-gather.2.cloned.1.call-done) | copy-start | bytes 4718596
  190.6 9.4 %collective-permute-start.18 = (bf16[16,64,384]{2,1,0:T(8,128)(2,1)S(1)}, bf16[16,64,384]{2,1,0:T(8,128)(2,1)}, u32[]{:S(2)}, u32[]{:S(2)}) collective-permute-start(bf16[16,64,384]{2,1,0:T(8,128)(2,1)S(1)} %fusion.12), channel_id=1, source_target_pairs={{0,16},{16,0},{32,48},{48,32},{64,80},{80,64},{96,112},{112,96},{1... | collective-permute-start | bytes 2359304 | tf_op jit(solution)/shard_map/ppermute | solution.py:48
  194.0 1.6 copy-start.1
  196.6 22.1 %collective-permute-start.14 = (bf16[8,128,384]{2,1,0:T(8,128)(2,1)}, bf16[8,128,384]{2,1,0:T(8,128)(2,1)}, u32[]{:S(2)}, u32[]{:S(2)}) collective-permute-start(bf16[8,128,384]{2,1,0:T(8,128)(2,1)} %fusion.13), channel_id=1, source_target_pairs={{0,1},{1,0},{2,3},{3,2},{4,5},{5,4},{6,7},{7,6},{8,9},{9,8},{10,11... | collective-permute-start | bytes 2359304 | tf_op jit(solution)/shard_map/ppermute | solution.py:48
  200.0 18.7 %copy-start.2 = (f32[8,2,128,384]{3,2,1,0:T(8,128)S(1)}, f32[8,2,128,384]{3,2,1,0:T(8,128)}, u32[]{:S(2)}) copy-start(f32[8,2,128,384]{3,2,1,0:T(8,128)} %copy-done.1) | copy-start | bytes 9437188
  202.8 25.9 %collective-permute-start.19 = (bf16[8,64,384]{2,1,0:T(8,128)(2,1)}, bf16[8,64,384]{2,1,0:T(8,128)(2,1)S(1)}, u32[]{:S(2)}, u32[]{:S(2)}) collective-permute-start(bf16[8,64,384]{2,1,0:T(8,128)(2,1)} %fusion.16), channel_id=1, source_target_pairs={{0,32},{16,48},{32,0},{48,16},{64,96},{80,112},{96,64},{112,80},{1... | collective-permute-start | bytes 1179656 | tf_op jit(solution)/shard_map/ppermute | solution.py:48
  220.1 1.2 copy-start.3
  222.1 14.4 %collective-permute-start.15 = (bf16[4,128,384]{2,1,0:T(8,128)(2,1)}, bf16[4,128,384]{2,1,0:T(8,128)(2,1)}, u32[]{:S(2)}, u32[]{:S(2)}) collective-permute-start(bf16[4,128,384]{2,1,0:T(8,128)(2,1)} %fusion.15), channel_id=1, source_target_pairs={{0,2},{1,3},{2,0},{3,1},{4,6},{5,7},{6,4},{7,5},{8,10},{9,11},{10,... | collective-permute-start | bytes 1179656 | tf_op jit(solution)/shard_map/ppermute | solution.py:48
  228.7 7.7 %copy-start.4 = (f32[8,128,384]{2,1,0:T(8,128)S(1)}, f32[8,128,384]{2,1,0:T(8,128)}, u32[]{:S(2)}) copy-start(f32[8,128,384]{2,1,0:T(8,128)} %copy-done.3) | copy-start | bytes 4718596
  228.8 13.3 %collective-permute-start.20 = (bf16[4,64,384]{2,1,0:T(8,128)(2,1)S(1)}, bf16[4,64,384]{2,1,0:T(8,128)(2,1)S(1)}, u32[]{:S(2)}, u32[]{:S(2)}) collective-permute-start(bf16[4,64,384]{2,1,0:T(8,128)(2,1)S(1)} %fusion.18), channel_id=1, source_target_pairs={{0,64},{16,80},{32,96},{48,112},{64,0},{80,16},{96,32},{112,48},{1... | collective-permute-start | bytes 589832 | tf_op jit(solution)/shard_map/ppermute | solution.py:48
  237.5 12.4 %collective-permute-start.16 = (bf16[2,128,384]{2,1,0:T(8,128)(2,1)S(1)}, bf16[2,128,384]{2,1,0:T(8,128)(2,1)S(1)}, u32[]{:S(2)}, u32[]{:S(2)}) collective-permute-start(bf16[2,128,384]{2,1,0:T(8,128)(2,1)S(1)} %fusion.17), channel_id=1, source_target_pairs={{0,4},{1,5},{2,6},{3,7},{4,0},{5,1},{6,2},{7,3},{8,12},{9,13},{10,... | collective-permute-start | bytes 589832 | tf_op jit(solution)/shard_map/ppermute | solution.py:48
  242.2 15.5 %collective-permute-start.21 = (bf16[2,64,384]{2,1,0:T(8,128)(2,1)S(1)}, bf16[2,64,384]{2,1,0:T(8,128)(2,1)S(1)}, u32[]{:S(2)}, u32[]{:S(2)}) collective-permute-start(bf16[2,64,384]{2,1,0:T(8,128)(2,1)S(1)} %fusion.25), channel_id=1, source_target_pairs={{0,128},{16,144},{32,160},{48,176},{64,192},{80,208},{96,224},{112... | collective-permute-start | bytes 294920 | tf_op jit(solution)/shard_map/ppermute | solution.py:48
  250.0 9.8 %collective-permute-start.17 = (bf16[1,128,384]{2,1,0:T(8,128)(2,1)S(1)}, bf16[1,128,384]{2,1,0:T(8,128)(2,1)S(1)}, u32[]{:S(2)}, u32[]{:S(2)}) collective-permute-start(bf16[1,128,384]{2,1,0:T(8,128)(2,1)S(1)} %dynamic-slice_convert_fusion.4), channel_id=1, source_target_pairs={{0,8},{1,9},{2,10},{3,11},{4,12},{5,13},{6,14},{7,15},{8,0},{9,1},... | collective-permute-start | bytes 294920 | tf_op jit(solution)/shard_map/ppermute | solution.py:48
  257.7 14.7 %collective-permute-start.22 = (bf16[1,64,384]{2,1,0:T(8,128)(2,1)S(1)}, bf16[1,64,384]{2,1,0:T(8,128)(2,1)S(1)}, u32[]{:S(2)}, u32[]{:S(2)}) collective-permute-start(bf16[1,64,384]{2,1,0:T(8,128)(2,1)S(1)} %dynamic-slice_convert_fusion.5), channel_id=1, source_target_pairs={{0,256},{16,272},{32,288},{48,304},{64,320},{80,336},{96,352},{112... | collective-permute-start | bytes 147464 | tf_op jit(solution)/shard_map/ppermute | solution.py:48
Sparse Core Ops, SparseCore 0:
  10.2 76.2 all-gather.1

commit v4 on v3

--- a/solution.py
+++ b/solution.py
@@ -32,6 +32,21 @@
         total = sum(parts[1:], parts[0])
         step *= 4
     return total - array
+
+
+def gathered_by_exchange(array, axis, count):
+    spread = jnp.broadcast_to(array[None], (count,) + array.shape)
+    return lax.all_to_all(spread, axis, 0, 0)
+
+
+def entering_exchange(array, axis, count, backward):
+    place = lax.axis_index(axis)
+    gathered = gathered_by_exchange(array.astype(jnp.bfloat16), axis, count)
+    source = jnp.arange(count)
+    chosen = source > place if backward else source < place
+    flat = gathered.reshape(count, -1)
+    total = jnp.dot(chosen.astype(jnp.bfloat16), flat, preferred_element_type=jnp.float32)
+    return total.reshape(array.shape)
 
 
 def halving_scatter(term, axis, count):
@@ -76,10 +91,9 @@
     allowed = allowed_pairs(block_mask[0])
     seq_count = lax.axis_size("z") * lax.axis_size("core")
     fsdp_count = lax.axis_size("fsdp")
-    pair_rows = lax.all_gather(
-        jnp.concatenate([w_query, w_key, w_value], axis=1), "core", axis=0, tiled=True
-    )
-    weight_cat = lax.all_gather(pair_rows, "z", axis=0, tiled=True)
+    weight_cat = gathered_by_exchange(
+        jnp.concatenate([w_query, w_key, w_value], axis=1), SEQ, seq_count
+    ).reshape(-1, 3 * columns)
     projected = jnp.dot(tokens, weight_cat, preferred_element_type=jnp.float32)
     projected = projected.astype(jnp.bfloat16)
     queries = projected[:, :columns].reshape(SEG, heads_here, HDIM)
@@ -88,7 +102,7 @@
     increment = jnp.einsum(
         "thd,the->hde", key_heads, value_heads, preferred_element_type=jnp.float32
     )
-    state = entering(increment, SEQ, seq_count, False)
+    state = entering_exchange(increment, SEQ, seq_count, False)
     state_low = state.astype(jnp.bfloat16)
     scores = jnp.einsum("shd,thd->hst", queries, key_heads, preferred_element_type=jnp.float32)
     weights = jnp.where(allowed[None], scores, 0.0).astype(jnp.bfloat16)

time: 281 us -> 301 us (1.071)
  blocking collectives: 2 us -> 94.1 us
  starting transfers between devices: 81.7 us -> 48.5 us
  waiting for transfers between devices: 151 us -> 124 us
  between operations: 14.6 us -> 1.19 us
    all_to_all x0 -> x1, blocking collectives: none -> 94.1 us  [gathered_by_exchange(): return lax.all_to_all(spread, axis, 0, 0)]
    all_gather x1 -> x0, waiting for transfers between devices: 75.5 us -> none  [shards(): weight_cat = lax.all_gather(pair_rows, 'z', axis=0, tiled=True)]
    all_to_all x0 -> x1, waiting for transfers between devices: none -> 54.4 us  [gathered_by_exchange(): return lax.all_to_all(spread, axis, 0, 0)]
    ppermute x14 -> x7, starting transfers between devices: 49.1 us -> 9.04 us  [entering(): parts.append(lax.ppermute(total, axis, pairs))]
    ppermute x14 -> x7, waiting for transfers between devices: 40 us -> 34.2 us  [entering(): parts.append(lax.ppermute(total, axis, pairs))]
    all_to_all x0 -> x1, starting transfers between devices: none -> 3.93 us  [gathered_by_exchange(): return lax.all_to_all(spread, axis, 0, 0)]
  transfers between devices with their start and end apart: 24 -> 17, of which waited for: 13 -> 11; matrix products, arithmetic and copies ran while one was open for 5% -> 5% of each run, Pallas kernels for 0% -> 0%
where the time goes in v4:
time: 301 us; the launch traced here: 299 us
  waiting for transfers between devices  124 us (41%)
  blocking collectives  94.1 us (31%)
  starting transfers between devices  48.5 us (16%)
  local copies, waits for them, and re-layouts  15.8 us (5%)
  matrix products  8.98 us (3%)
  other arithmetic  6.7 us (2%)
    all_to_all x1, blocking collectives, gathered_by_exchange(): return lax.all_to_all(spread, axis, 0, 0)  94.1 us
    all_to_all x1, waiting for transfers between devices, gathered_by_exchange(): return lax.all_to_all(spread, axis, 0, 0)  54.4 us
    ppermute x9, starting transfers between devices, halving_scatter(): lax.ppermute(away.astype(jnp.bfloat16), axis, pairs).astype(jnp.float32)  35.5 us
    ppermute x9, waiting for transfers between devices, halving_scatter(): lax.ppermute(away.astype(jnp.bfloat16), axis, pairs).astype(jnp.float32)  35.2 us
    ppermute x7, waiting for transfers between devices, entering(): parts.append(lax.ppermute(total, axis, pairs))  34.2 us
    ppermute x7, starting transfers between devices, entering(): parts.append(lax.ppermute(total, axis, pairs))  9.04 us
  transfers between devices with their start and end apart: 17, of which 11 were waited for; matrix products, arithmetic and copies ran while one was open for 5% of the time, Pallas kernels for 0%

profile of v4, /device:TPU:6, one launch (start us, length us, event | category | flops | bytes accessed | tf_op | source)
XLA Modules:
  0.0 299.0 jit_solution(16482997415922115089)
XLA Ops:
  1.8 94.1 %all_to_all.10 = bf16[32,64,384]{2,1,0:T(8,128)(2,1)S(1)} all-to-all(bf16[32,64,384]{2,1,0:T(8,128)(2,1)S(1)} %broadcast_in_dim.8), channel_id=1, replica_groups=mesh['z'=16,'core'=2,'fsdp'=16] {'z','core'}, dimensions={0} | all-to-all | bytes 3145728 | tf_op jit(solution)/shard_map/all_to_all | solution.py:39
  98.5 3.9 %all-to-all-start.1 = ((bf16[32,1,128,128]{3,2,1,0:T(8,128)(2,1)}), bf16[32,1,128,128]{3,2,1,0:T(8,128)(2,1)S(1)}, u32[]{:S(2)}, u32[]{:S(2)}) async-start(bf16[32,1,128,128]{3,2,1,0:T(8,128)(2,1)} %broadcast_in_dim.9), calls=%async_computation.1 | async-start | bytes 2097152 | tf_op jit(solution)/shard_map/all_to_all | solution.py:39
  104.4 54.4 %all-to-all-done.1 = bf16[32,1,128,128]{3,2,1,0:T(8,128)(2,1)S(1)} async-done(((bf16[32,1,128,128]{3,2,1,0:T(8,128)(2,1)}), bf16[32,1,128,128]{3,2,1,0:T(8,128)(2,1)S(1)}, u32[]{:S(2)}, u32[]{:S(2)}) %all-to-all-start.1) | async-done | bytes 1048608 | tf_op jit(solution)/shard_map/all_to_all | solution.py:39
  161.1 1.3 collective-permute-start.2
  162.4 1.3 collective-permute-start.1
  163.7 1.3 collective-permute-start
  165.5 1.9 collective-permute-done.2
  167.4 1.8 collective-permute-done.1
  169.2 1.3 collective-permute-start.5
  173.4 14.5 %collective-permute-done.5 = f32[1,128,128]{2,1,0:T(8,128)S(1)} collective-permute-done((f32[1,128,128]{2,1,0:T(8,128)S(1)}, f32[1,128,128]{2,1,0:T(8,128)S(1)}, u32[]{:S(2)}, u32[]{:S(2)}) %collective-permute-start.5) | collective-permute-done | bytes 65568 | tf_op jit(solution)/shard_map/ppermute | solution.py:31
  187.9 2.6 collective-permute-done.4
  191.9 13.4 %collective-permute-done.6 = f32[1,128,128]{2,1,0:T(8,128)S(1)} collective-permute-done((f32[1,128,128]{2,1,0:T(8,128)S(1)}, f32[1,128,128]{2,1,0:T(8,128)S(1)}, u32[]{:S(2)}, u32[]{:S(2)}) %collective-permute-start.6) | collective-permute-done | bytes 65568 | tf_op jit(solution)/shard_map/ppermute | solution.py:31
  205.7 2.6 convert_bitcast_fusion
  208.4 3.6 %copy.22 = f32[2048,384]{1,0:T(8,128)} copy(f32[2048,384]{0,1:T(8,128)} %convert_bitcast_fusion) | data formatting | bytes 6291456 | tf_op jit(solution)/shard_map/reshape;reshape | solution.py:59
  211.9 1.6 fusion.15
  213.6 1.9 collective-permute-start.11
  217.0 1.6 copy-done.1
  219.6 3.5 %collective-permute-start.7 = (bf16[8,128,384]{2,1,0:T(8,128)(2,1)}, bf16[8,128,384]{2,1,0:T(8,128)(2,1)}, u32[]{:S(2)}, u32[]{:S(2)}) collective-permute-start(bf16[8,128,384]{2,1,0:T(8,128)(2,1)} %fusion.16), channel_id=1, source_target_pairs={{0,1},{1,0},{2,3},{3,2},{4,5},{5,4},{6,7},{7,6},{8,9},{9,8},{10,11... | collective-permute-start | bytes 2359304 | tf_op jit(solution)/shard_map/ppermute | solution.py:63
  223.1 2.0 bitcast_add_fusion
  225.9 1.9 collective-permute-start.12
  227.8 13.9 %collective-permute-done.7 = bf16[8,128,384]{2,1,0:T(8,128)(2,1)} collective-permute-done((bf16[8,128,384]{2,1,0:T(8,128)(2,1)}, bf16[8,128,384]{2,1,0:T(8,128)(2,1)}, u32[]{:S(2)}, u32[]{:S(2)}) %collective-permute-start.7) | collective-permute-done | bytes 786464 | tf_op jit(solution)/shard_map/ppermute | solution.py:63
  241.7 1.3 bitcast_add_fusion.1
  245.0 5.1 %collective-permute-start.8 = (bf16[4,128,384]{2,1,0:T(8,128)(2,1)}, bf16[4,128,384]{2,1,0:T(8,128)(2,1)}, u32[]{:S(2)}, u32[]{:S(2)}) collective-permute-start(bf16[4,128,384]{2,1,0:T(8,128)(2,1)} %fusion.18), channel_id=1, source_target_pairs={{0,2},{1,3},{2,0},{3,1},{4,6},{5,7},{6,4},{7,5},{8,10},{9,11},{10,... | collective-permute-start | bytes 1179656 | tf_op jit(solution)/shard_map/ppermute | solution.py:63
  250.2 1.6 copy.25
  251.9 6.3 %collective-permute-start.13 = (bf16[4,64,384]{2,1,0:T(8,128)(2,1)S(1)}, bf16[4,64,384]{2,1,0:T(8,128)(2,1)S(1)}, u32[]{:S(2)}, u32[]{:S(2)}) collective-permute-start(bf16[4,64,384]{2,1,0:T(8,128)(2,1)S(1)} %fusion.21), channel_id=1, source_target_pairs={{0,64},{16,80},{32,96},{48,112},{64,0},{80,16},{96,32},{112,48},{1... | collective-permute-start | bytes 589832 | tf_op jit(solution)/shard_map/ppermute | solution.py:63
  260.5 2.7 collective-permute-start.9
  263.3 3.6 %collective-permute-done.13 = bf16[4,64,384]{2,1,0:T(8,128)(2,1)S(1)} collective-permute-done((bf16[4,64,384]{2,1,0:T(8,128)(2,1)S(1)}, bf16[4,64,384]{2,1,0:T(8,128)(2,1)S(1)}, u32[]{:S(2)}, u32[]{:S(2)}) %collective-permute-start.13) | collective-permute-done | bytes 196640 | tf_op jit(solution)/shard_map/ppermute | solution.py:63
  267.0 8.8 %collective-permute-start.14 = (bf16[2,64,384]{2,1,0:T(8,128)(2,1)S(1)}, bf16[2,64,384]{2,1,0:T(8,128)(2,1)S(1)}, u32[]{:S(2)}, u32[]{:S(2)}) collective-permute-start(bf16[2,64,384]{2,1,0:T(8,128)(2,1)S(1)} %fusion.28), channel_id=1, source_target_pairs={{0,128},{16,144},{32,160},{48,176},{64,192},{80,208},{96,224},{112... | collective-permute-start | bytes 294920 | tf_op jit(solution)/shard_map/ppermute | solution.py:63
  275.8 3.3 %collective-permute-start.10 = (bf16[1,128,384]{2,1,0:T(8,128)(2,1)S(1)}, bf16[1,128,384]{2,1,0:T(8,128)(2,1)S(1)}, u32[]{:S(2)}, u32[]{:S(2)}) collective-permute-start(bf16[1,128,384]{2,1,0:T(8,128)(2,1)S(1)} %dynamic-slice_convert_fusion.4), channel_id=1, source_target_pairs={{0,8},{1,9},{2,10},{3,11},{4,12},{5,13},{6,14},{7,15},{8,0},{9,1},... | collective-permute-start | bytes 294920 | tf_op jit(solution)/shard_map/ppermute | solution.py:63
  279.2 4.5 %collective-permute-done.14 = bf16[2,64,384]{2,1,0:T(8,128)(2,1)S(1)} collective-permute-done((bf16[2,64,384]{2,1,0:T(8,128)(2,1)S(1)}, bf16[2,64,384]{2,1,0:T(8,128)(2,1)S(1)}, u32[]{:S(2)}, u32[]{:S(2)}) %collective-permute-start.14) | collective-permute-done | bytes 98336 | tf_op jit(solution)/shard_map/ppermute | solution.py:63
  283.7 1.9 collective-permute-start.15
  286.4 12.0 %collective-permute-done.15 = bf16[1,64,384]{2,1,0:T(8,128)(2,1)S(1)} collective-permute-done((bf16[1,64,384]{2,1,0:T(8,128)(2,1)S(1)}, bf16[1,64,384]{2,1,0:T(8,128)(2,1)S(1)}, u32[]{:S(2)}, u32[]{:S(2)}) %collective-permute-start.15) | collective-permute-done | bytes 49184 | tf_op jit(solution)/shard_map/ppermute | solution.py:63
  (81 shorter events, 22.1 us)
Async XLA Ops:
  0.6 95.2 %copy-start = (bf16[384,2048]{1,0:T(8,128)(2,1)S(1)}, bf16[384,2048]{1,0:T(8,128)(2,1)}, u32[]{:S(2)}) copy-start(bf16[384,2048]{1,0:T(8,128)(2,1)} %param.7) | copy-start | bytes 4718596
  95.8 1.1 copy-start.5
  97.2 5.2 %copy-start.11 = (s32[1,3,3]{2,0,1:T(1,128)S(1)}, s32[1,3,3]{2,0,1:T(1,128)}, u32[]{:S(2)}) copy-start(s32[1,3,3]{2,0,1:T(1,128)} %param.12) | copy-start | bytes 112
  97.2 5.2 %copy-start.9 = (bf16[384,128]{1,0:T(8,128)(2,1)S(1)}, bf16[384,128]{1,0:T(8,128)(2,1)}, u32[]{:S(2)}) copy-start(bf16[384,128]{1,0:T(8,128)(2,1)} %param.13) | copy-start | bytes 294916
  98.5 60.4 %all-to-all-start.1 = ((bf16[32,1,128,128]{3,2,1,0:T(8,128)(2,1)}), bf16[32,1,128,128]{3,2,1,0:T(8,128)(2,1)S(1)}, u32[]{:S(2)}, u32[]{:S(2)}) async-start(bf16[32,1,128,128]{3,2,1,0:T(8,128)(2,1)} %broadcast_in_dim.9), calls=%async_computation.1 | async-start | bytes 2097152 | tf_op jit(solution)/shard_map/all_to_all | solution.py:39
  103.5 0.6 copy-start.7
  103.6 56.2 %copy-start.10 = (f32[128]{0:T(128)S(1)}, f32[128]{0:T(128)}, u32[]{:S(2)}) copy-start(f32[128]{0:T(128)} %param.11) | copy-start | bytes 1540
  158.9 6.1 %copy-start.8 = (pred[384,384]{1,0:T(32,128)(4,1)S(1)}, pred[384,384]{1,0:T(32,128)(4,1)}, u32[]{:S(2)}) copy-start(pred[384,384]{1,0:T(32,128)(4,1)} %copy-done.7) | copy-start | bytes 442372
  161.1 6.3 %collective-permute-start.2 = (f32[1,128,128]{2,1,0:T(8,128)S(1)}, f32[1,128,128]{2,1,0:T(8,128)S(1)}, u32[]{:S(2)}, u32[]{:S(2)}) collective-permute-start(f32[1,128,128]{2,1,0:T(8,128)S(1)} %convolution_bitcast_fusion), channel_id=1, source_target_pairs={{48,0},{64,16},{80,32},{96,48},{112,64},{128,80},{144,96},{160,112... | collective-permute-start | bytes 196616 | tf_op jit(solution)/shard_map/ppermute | solution.py:31
  162.4 6.8 %collective-permute-start.1 = (f32[1,128,128]{2,1,0:T(8,128)S(1)}, f32[1,128,128]{2,1,0:T(8,128)S(1)}, u32[]{:S(2)}, u32[]{:S(2)}) collective-permute-start(f32[1,128,128]{2,1,0:T(8,128)S(1)} %convolution_bitcast_fusion), channel_id=1, source_target_pairs={{32,0},{48,16},{64,32},{80,48},{96,64},{112,80},{128,96},{144,112}... | collective-permute-start | bytes 196616 | tf_op jit(solution)/shard_map/ppermute | solution.py:31
  163.7 5.5 %collective-permute-start = (f32[1,128,128]{2,1,0:T(8,128)S(1)}, f32[1,128,128]{2,1,0:T(8,128)S(1)}, u32[]{:S(2)}, u32[]{:S(2)}) collective-permute-start(f32[1,128,128]{2,1,0:T(8,128)S(1)} %convolution_bitcast_fusion), channel_id=1, source_target_pairs={{16,0},{32,16},{48,32},{64,48},{80,64},{96,80},{112,96},{128,112},... | collective-permute-start | bytes 196616 | tf_op jit(solution)/shard_map/ppermute | solution.py:31
  169.2 18.6 %collective-permute-start.5 = (f32[1,128,128]{2,1,0:T(8,128)S(1)}, f32[1,128,128]{2,1,0:T(8,128)S(1)}, u32[]{:S(2)}, u32[]{:S(2)}) collective-permute-start(f32[1,128,128]{2,1,0:T(8,128)S(1)} %add_add_fusion.1), channel_id=1, source_target_pairs={{192,0},{208,16},{224,32},{240,48},{256,64},{272,80},{288,96},{304... | collective-permute-start | bytes 196616 | tf_op jit(solution)/shard_map/ppermute | solution.py:31
  170.5 19.9 %collective-permute-start.4 = (f32[1,128,128]{2,1,0:T(8,128)S(1)}, f32[1,128,128]{2,1,0:T(8,128)S(1)}, u32[]{:S(2)}, u32[]{:S(2)}) collective-permute-start(f32[1,128,128]{2,1,0:T(8,128)S(1)} %add_add_fusion.1), channel_id=1, source_target_pairs={{128,0},{144,16},{160,32},{176,48},{192,64},{208,80},{224,96},{240... | collective-permute-start | bytes 196616 | tf_op jit(solution)/shard_map/ppermute | solution.py:31
  171.8 18.6 %collective-permute-start.3 = (f32[1,128,128]{2,1,0:T(8,128)S(1)}, f32[1,128,128]{2,1,0:T(8,128)S(1)}, u32[]{:S(2)}, u32[]{:S(2)}) collective-permute-start(f32[1,128,128]{2,1,0:T(8,128)S(1)} %add_add_fusion.1), channel_id=1, source_target_pairs={{64,0},{80,16},{96,32},{112,48},{128,64},{144,80},{160,96},{176,11... | collective-permute-start | bytes 196616 | tf_op jit(solution)/shard_map/ppermute | solution.py:31
  190.5 14.9 %collective-permute-start.6 = (f32[1,128,128]{2,1,0:T(8,128)S(1)}, f32[1,128,128]{2,1,0:T(8,128)S(1)}, u32[]{:S(2)}, u32[]{:S(2)}) collective-permute-start(f32[1,128,128]{2,1,0:T(8,128)S(1)} %add_add_fusion), channel_id=1, source_target_pairs={{256,0},{272,16},{288,32},{304,48},{320,64},{336,80},{352,96},{368... | collective-permute-start | bytes 196616 | tf_op jit(solution)/shard_map/ppermute | solution.py:31
  211.9 3.6 %copy-start.6 = (bf16[32,64,384]{2,1,0:T(8,128)(2,1)S(1)}, bf16[32,64,384]{2,1,0:T(8,128)(2,1)}, u32[]{:S(2)}) copy-start(bf16[32,64,384]{2,1,0:T(8,128)(2,1)} %copy-done.5) | copy-start | bytes 4718596
  213.6 9.5 %collective-permute-start.11 = (bf16[16,64,384]{2,1,0:T(8,128)(2,1)S(1)}, bf16[16,64,384]{2,1,0:T(8,128)(2,1)}, u32[]{:S(2)}, u32[]{:S(2)}) collective-permute-start(bf16[16,64,384]{2,1,0:T(8,128)(2,1)S(1)} %fusion.15), channel_id=1, source_target_pairs={{0,16},{16,0},{32,48},{48,32},{64,80},{80,64},{96,112},{112,96},{1... | collective-permute-start | bytes 2359304 | tf_op jit(solution)/shard_map/ppermute | solution.py:63
  217.0 1.6 copy-start.1
  219.6 22.1 %collective-permute-start.7 = (bf16[8,128,384]{2,1,0:T(8,128)(2,1)}, bf16[8,128,384]{2,1,0:T(8,128)(2,1)}, u32[]{:S(2)}, u32[]{:S(2)}) collective-permute-start(bf16[8,128,384]{2,1,0:T(8,128)(2,1)} %fusion.16), channel_id=1, source_target_pairs={{0,1},{1,0},{2,3},{3,2},{4,5},{5,4},{6,7},{7,6},{8,9},{9,8},{10,11... | collective-permute-start | bytes 2359304 | tf_op jit(solution)/shard_map/ppermute | solution.py:63
  223.1 18.7 %copy-start.2 = (f32[8,2,128,384]{3,2,1,0:T(8,128)S(1)}, f32[8,2,128,384]{3,2,1,0:T(8,128)}, u32[]{:S(2)}) copy-start(f32[8,2,128,384]{3,2,1,0:T(8,128)} %copy-done.1) | copy-start | bytes 9437188
  225.9 25.9 %collective-permute-start.12 = (bf16[8,64,384]{2,1,0:T(8,128)(2,1)}, bf16[8,64,384]{2,1,0:T(8,128)(2,1)S(1)}, u32[]{:S(2)}, u32[]{:S(2)}) collective-permute-start(bf16[8,64,384]{2,1,0:T(8,128)(2,1)} %fusion.19), channel_id=1, source_target_pairs={{0,32},{16,48},{32,0},{48,16},{64,96},{80,112},{96,64},{112,80},{1... | collective-permute-start | bytes 1179656 | tf_op jit(solution)/shard_map/ppermute | solution.py:63
  243.1 1.2 copy-start.3
  245.0 14.4 %collective-permute-start.8 = (bf16[4,128,384]{2,1,0:T(8,128)(2,1)}, bf16[4,128,384]{2,1,0:T(8,128)(2,1)}, u32[]{:S(2)}, u32[]{:S(2)}) collective-permute-start(bf16[4,128,384]{2,1,0:T(8,128)(2,1)} %fusion.18), channel_id=1, source_target_pairs={{0,2},{1,3},{2,0},{3,1},{4,6},{5,7},{6,4},{7,5},{8,10},{9,11},{10,... | collective-permute-start | bytes 1179656 | tf_op jit(solution)/shard_map/ppermute | solution.py:63
  251.8 7.6 %copy-start.4 = (f32[8,128,384]{2,1,0:T(8,128)S(1)}, f32[8,128,384]{2,1,0:T(8,128)}, u32[]{:S(2)}) copy-start(f32[8,128,384]{2,1,0:T(8,128)} %copy-done.3) | copy-start | bytes 4718596
  251.9 15.0 %collective-permute-start.13 = (bf16[4,64,384]{2,1,0:T(8,128)(2,1)S(1)}, bf16[4,64,384]{2,1,0:T(8,128)(2,1)S(1)}, u32[]{:S(2)}, u32[]{:S(2)}) collective-permute-start(bf16[4,64,384]{2,1,0:T(8,128)(2,1)S(1)} %fusion.21), channel_id=1, source_target_pairs={{0,64},{16,80},{32,96},{48,112},{64,0},{80,16},{96,32},{112,48},{1... | collective-permute-start | bytes 589832 | tf_op jit(solution)/shard_map/ppermute | solution.py:63
  260.5 15.2 %collective-permute-start.9 = (bf16[2,128,384]{2,1,0:T(8,128)(2,1)S(1)}, bf16[2,128,384]{2,1,0:T(8,128)(2,1)S(1)}, u32[]{:S(2)}, u32[]{:S(2)}) collective-permute-start(bf16[2,128,384]{2,1,0:T(8,128)(2,1)S(1)} %fusion.20), channel_id=1, source_target_pairs={{0,4},{1,5},{2,6},{3,7},{4,0},{5,1},{6,2},{7,3},{8,12},{9,13},{10,... | collective-permute-start | bytes 589832 | tf_op jit(solution)/shard_map/ppermute | solution.py:63
  267.0 16.7 %collective-permute-start.14 = (bf16[2,64,384]{2,1,0:T(8,128)(2,1)S(1)}, bf16[2,64,384]{2,1,0:T(8,128)(2,1)S(1)}, u32[]{:S(2)}, u32[]{:S(2)}) collective-permute-start(bf16[2,64,384]{2,1,0:T(8,128)(2,1)S(1)} %fusion.28), channel_id=1, source_target_pairs={{0,128},{16,144},{32,160},{48,176},{64,192},{80,208},{96,224},{112... | collective-permute-start | bytes 294920 | tf_op jit(solution)/shard_map/ppermute | solution.py:63
  275.8 9.8 %collective-permute-start.10 = (bf16[1,128,384]{2,1,0:T(8,128)(2,1)S(1)}, bf16[1,128,384]{2,1,0:T(8,128)(2,1)S(1)}, u32[]{:S(2)}, u32[]{:S(2)}) collective-permute-start(bf16[1,128,384]{2,1,0:T(8,128)(2,1)S(1)} %dynamic-slice_convert_fusion.4), channel_id=1, source_target_pairs={{0,8},{1,9},{2,10},{3,11},{4,12},{5,13},{6,14},{7,15},{8,0},{9,1},... | collective-permute-start | bytes 294920 | tf_op jit(solution)/shard_map/ppermute | solution.py:63
  283.7 14.7 %collective-permute-start.15 = (bf16[1,64,384]{2,1,0:T(8,128)(2,1)S(1)}, bf16[1,64,384]{2,1,0:T(8,128)(2,1)S(1)}, u32[]{:S(2)}, u32[]{:S(2)}) collective-permute-start(bf16[1,64,384]{2,1,0:T(8,128)(2,1)S(1)} %dynamic-slice_convert_fusion.5), channel_id=1, source_target_pairs={{0,256},{16,272},{32,288},{48,304},{64,320},{80,336},{96,352},{112... | collective-permute-start | bytes 147464 | tf_op jit(solution)/shard_map/ppermute | solution.py:63

commit v5 on v3

--- a/solution.py
+++ b/solution.py
@@ -15,8 +15,12 @@
 SEQ = ("z", "core")
 
 
-def entering(array, axis, count, backward):
-    total = array
+def entering(array, backward):
+    count = lax.axis_size("z")
+    core = lax.axis_index("core")
+    partner = lax.ppermute(array, "core", [(0, 1), (1, 0)])
+    pair_total = array + partner
+    total = pair_total
     step = 1
     while step < count:
         parts = [total]
@@ -28,10 +32,11 @@
                 pairs = [(i, i - shift) for i in range(shift, count)]
             else:
                 pairs = [(i, i + shift) for i in range(count - shift)]
-            parts.append(lax.ppermute(total, axis, pairs))
+            parts.append(lax.ppermute(total, "z", pairs))
         total = sum(parts[1:], parts[0])
         step *= 4
-    return total - array
+    inside = jnp.where(core == (0 if backward else 1), partner, jnp.zeros_like(partner))
+    return (total - pair_total) + inside
 
 
 def halving_scatter(term, axis, count):
@@ -88,7 +93,7 @@
     increment = jnp.einsum(
         "thd,the->hde", key_heads, value_heads, preferred_element_type=jnp.float32
     )
-    state = entering(increment, SEQ, seq_count, False)
+    state = entering(increment, False)
     state_low = state.astype(jnp.bfloat16)
     scores = jnp.einsum("shd,thd->hst", queries, key_heads, preferred_element_type=jnp.float32)
     weights = jnp.where(allowed[None], scores, 0.0).astype(jnp.bfloat16)
@@ -105,7 +110,7 @@
         jnp.bfloat16
     )
     d_state = jnp.einsum("shd,she->hde", queries, d_mixed, preferred_element_type=jnp.float32)
-    later = entering(d_state, SEQ, seq_count, True)
+    later = entering(d_state, True)
     later_low = later.astype(jnp.bfloat16)
     d_scores = jnp.einsum("she,the->hst", d_mixed, value_heads, preferred_element_type=jnp.float32)
     d_weights = jnp.where(allowed[None], d_scores, 0.0).astype(jnp.bfloat16)

time: 281 us -> 263 us (0.936)
  waiting for transfers between devices: 151 us -> 122 us
  starting transfers between devices: 81.7 us -> 91 us
    ppermute x9, starting transfers between devices: 32.6 us -> 52 us  [halving_scatter(): lax.ppermute(away.astype(jnp.bfloat16), axis, pairs).astype(jnp.float32)]
    ppermute x14, waiting for transfers between devices: 40 us -> 25 us  [the longest x12 23.6 us: entering(): parts.append(lax.ppermute(total, 'z', pairs))]
    ppermute x9, waiting for transfers between devices: 35.1 us -> 21.8 us  [halving_scatter(): lax.ppermute(away.astype(jnp.bfloat16), axis, pairs).astype(jnp.float32)]
    ppermute x14, starting transfers between devices: 49.1 us -> 38.9 us  [the longest x12 35.1 us: entering(): parts.append(lax.ppermute(total, 'z', pairs))]
  transfers between devices with their start and end apart: 24 -> 24, of which waited for: 13 -> 14; matrix products, arithmetic and copies ran while one was open for 5% -> 5% of each run, Pallas kernels for 0% -> 0%
where the time goes in v5:
time: 263 us; the launch traced here: 261 us
  waiting for transfers between devices  122 us (46%)
  starting transfers between devices  91 us (35%)
  between operations  14.6 us (6%)
  local copies, waits for them, and re-layouts  13.9 us (5%)
  matrix products  9.68 us (4%)
  other arithmetic  7.43 us (3%)
    all_gather x1, waiting for transfers between devices, shards(): weight_cat = lax.all_gather(pair_rows, 'z', axis=0, tiled=True)  75.5 us
    ppermute x9, starting transfers between devices, halving_scatter(): lax.ppermute(away.astype(jnp.bfloat16), axis, pairs).astype(jnp.float32)  52 us
    ppermute x12, starting transfers between devices, entering(): parts.append(lax.ppermute(total, 'z', pairs))  35.1 us
    ppermute x12, waiting for transfers between devices, entering(): parts.append(lax.ppermute(total, 'z', pairs))  23.6 us
    ppermute x9, waiting for transfers between devices, halving_scatter(): lax.ppermute(away.astype(jnp.bfloat16), axis, pairs).astype(jnp.float32)  21.8 us
    unnamed x19, local copies, waits for them, and re-layouts  5.37 us
  transfers between devices with their start and end apart: 24, of which 14 were waited for; matrix products, arithmetic and copies ran while one was open for 5% of the time, Pallas kernels for 0%

profile of v5, /device:TPU:6, one launch (start us, length us, event | category | flops | bytes accessed | tf_op | source)
XLA Modules:
  0.0 260.9 jit_solution(16503312570941527269)
XLA Ops:
  8.1 2.0 all_gather.6
  11.1 75.5 %all-gather.2.cloned.1.call-done = bf16[2048,384]{1,0:T(8,128)(2,1)} async-done(((bf16[128,384]{1,0:T(8,128)(2,1)}), bf16[2048,384]{1,0:T(8,128)(2,1)}) %all-gather.2.cloned.1.call-update) | async-done | bytes 1572880 | tf_op jit(solution)/shard_map/all_gather | solution.py:87
  86.6 2.4 fusion.2
  89.2 1.9 collective-permute-start
  92.4 4.2 %collective-permute-start.3 = (f32[1,128,128]{2,1,0:T(8,128)S(1)}, f32[1,128,128]{2,1,0:T(8,128)S(1)}, u32[]{:S(2)}, u32[]{:S(2)}) collective-permute-start(f32[1,128,128]{2,1,0:T(8,128)S(1)} %add.192), channel_id=1, source_target_pairs={{0,96},{32,128},{64,160},{96,192},{128,224},{160,256},{192,288},{2... | collective-permute-start | bytes 196616 | tf_op jit(solution)/shard_map/ppermute | solution.py:35
  96.6 3.5 %collective-permute-start.2 = (f32[1,128,128]{2,1,0:T(8,128)S(1)}, f32[1,128,128]{2,1,0:T(8,128)S(1)}, u32[]{:S(2)}, u32[]{:S(2)}) collective-permute-start(f32[1,128,128]{2,1,0:T(8,128)S(1)} %add.192), channel_id=1, source_target_pairs={{0,64},{32,96},{64,128},{96,160},{128,192},{160,224},{192,256},{22... | collective-permute-start | bytes 196616 | tf_op jit(solution)/shard_map/ppermute | solution.py:35
  100.1 3.7 %collective-permute-start.1 = (f32[1,128,128]{2,1,0:T(8,128)S(1)}, f32[1,128,128]{2,1,0:T(8,128)S(1)}, u32[]{:S(2)}, u32[]{:S(2)}) collective-permute-start(f32[1,128,128]{2,1,0:T(8,128)S(1)} %add.192), channel_id=1, source_target_pairs={{0,32},{32,64},{64,96},{96,128},{128,160},{160,192},{192,224},{224... | collective-permute-start | bytes 196616 | tf_op jit(solution)/shard_map/ppermute | solution.py:35
  105.7 7.3 %collective-permute-start.6 = (f32[1,128,128]{2,1,0:T(8,128)S(1)}, f32[1,128,128]{2,1,0:T(8,128)S(1)}, u32[]{:S(2)}, u32[]{:S(2)}) collective-permute-start(f32[1,128,128]{2,1,0:T(8,128)S(1)} %add_add_fusion.1), channel_id=1, source_target_pairs={{0,384},{32,416},{64,448},{96,480},{1,385},{33,417},{65,449},{97,4... | collective-permute-start | bytes 196616 | tf_op jit(solution)/shard_map/ppermute | solution.py:35
  113.1 3.4 %collective-permute-start.5 = (f32[1,128,128]{2,1,0:T(8,128)S(1)}, f32[1,128,128]{2,1,0:T(8,128)S(1)}, u32[]{:S(2)}, u32[]{:S(2)}) collective-permute-start(f32[1,128,128]{2,1,0:T(8,128)S(1)} %add_add_fusion.1), channel_id=1, source_target_pairs={{0,256},{32,288},{64,320},{96,352},{128,384},{160,416},{192,448},{... | collective-permute-start | bytes 196616 | tf_op jit(solution)/shard_map/ppermute | solution.py:35
  116.4 5.2 %collective-permute-start.4 = (f32[1,128,128]{2,1,0:T(8,128)S(1)}, f32[1,128,128]{2,1,0:T(8,128)S(1)}, u32[]{:S(2)}, u32[]{:S(2)}) collective-permute-start(f32[1,128,128]{2,1,0:T(8,128)S(1)} %add_add_fusion.1), channel_id=1, source_target_pairs={{0,128},{32,160},{64,192},{96,224},{128,256},{160,288},{192,320},{... | collective-permute-start | bytes 196616 | tf_op jit(solution)/shard_map/ppermute | solution.py:35
  125.4 1.9 collective-permute-start.7
  132.7 3.9 %collective-permute-done.10 = f32[1,128,128]{2,1,0:T(8,128)S(1)} collective-permute-done((f32[1,128,128]{2,1,0:T(8,128)S(1)}, f32[1,128,128]{2,1,0:T(8,128)S(1)}, u32[]{:S(2)}, u32[]{:S(2)}) %collective-permute-start.10) | collective-permute-done | bytes 65568 | tf_op jit(solution)/shard_map/ppermute | solution.py:35
  136.6 2.8 %collective-permute-done.9 = f32[1,128,128]{2,1,0:T(8,128)S(1)} collective-permute-done((f32[1,128,128]{2,1,0:T(8,128)S(1)}, f32[1,128,128]{2,1,0:T(8,128)S(1)}, u32[]{:S(2)}, u32[]{:S(2)}) %collective-permute-start.9) | collective-permute-done | bytes 65568 | tf_op jit(solution)/shard_map/ppermute | solution.py:35
  143.5 12.4 %collective-permute-done.13 = f32[1,128,128]{2,1,0:T(8,128)S(1)} collective-permute-done((f32[1,128,128]{2,1,0:T(8,128)S(1)}, f32[1,128,128]{2,1,0:T(8,128)S(1)}, u32[]{:S(2)}, u32[]{:S(2)}) %collective-permute-start.13) | collective-permute-done | bytes 65568 | tf_op jit(solution)/shard_map/ppermute | solution.py:35
  157.5 2.6 %convert_bitcast_fusion = f32[2048,384]{0,1:T(8,128)} fusion(bf16[384,2048]{1,0:T(8,128)(2,1)S(1)} %copy-done, bf16[384,128]{0,1:T(8,128)(2,1)S(1)} %fusion.9, bf16[384,128]{0,1:T(8,128)(2,1)S(1)} %fusion.10, bf16[384,128]{0,1:T(8,128)(2,1)S(1)} %fusion.11), kind=kOutput, calls=%fused_computation | convolution fusion | flops 606437376 | bytes 5013504 | tf_op jit(solution)/shard_map/dot_general | solution.py:142
  160.2 3.6 %copy.22 = f32[2048,384]{1,0:T(8,128)} copy(f32[2048,384]{0,1:T(8,128)} %convert_bitcast_fusion) | data formatting | bytes 6291456 | tf_op jit(solution)/shard_map/reshape;reshape | solution.py:49
  163.7 1.6 fusion.12
  165.4 1.9 collective-permute-start.18
  168.8 1.6 copy-done.1
  171.4 3.4 %collective-permute-start.14 = (bf16[8,128,384]{2,1,0:T(8,128)(2,1)}, bf16[8,128,384]{2,1,0:T(8,128)(2,1)}, u32[]{:S(2)}, u32[]{:S(2)}) collective-permute-start(bf16[8,128,384]{2,1,0:T(8,128)(2,1)} %fusion.13), channel_id=1, source_target_pairs={{0,1},{1,0},{2,3},{3,2},{4,5},{5,4},{6,7},{7,6},{8,9},{9,8},{10,11... | collective-permute-start | bytes 2359304 | tf_op jit(solution)/shard_map/ppermute | solution.py:53
  174.8 2.0 bitcast_add_fusion
  177.6 6.2 %collective-permute-start.19 = (bf16[8,64,384]{2,1,0:T(8,128)(2,1)}, bf16[8,64,384]{2,1,0:T(8,128)(2,1)S(1)}, u32[]{:S(2)}, u32[]{:S(2)}) collective-permute-start(bf16[8,64,384]{2,1,0:T(8,128)(2,1)} %fusion.16), channel_id=1, source_target_pairs={{0,32},{16,48},{32,0},{48,16},{64,96},{80,112},{96,64},{112,80},{1... | collective-permute-start | bytes 1179656 | tf_op jit(solution)/shard_map/ppermute | solution.py:53
  183.8 9.7 %collective-permute-done.14 = bf16[8,128,384]{2,1,0:T(8,128)(2,1)} collective-permute-done((bf16[8,128,384]{2,1,0:T(8,128)(2,1)}, bf16[8,128,384]{2,1,0:T(8,128)(2,1)}, u32[]{:S(2)}, u32[]{:S(2)}) %collective-permute-start.14) | collective-permute-done | bytes 786464 | tf_op jit(solution)/shard_map/ppermute | solution.py:53
  196.9 4.9 %collective-permute-start.15 = (bf16[4,128,384]{2,1,0:T(8,128)(2,1)}, bf16[4,128,384]{2,1,0:T(8,128)(2,1)}, u32[]{:S(2)}, u32[]{:S(2)}) collective-permute-start(bf16[4,128,384]{2,1,0:T(8,128)(2,1)} %fusion.15), channel_id=1, source_target_pairs={{0,2},{1,3},{2,0},{3,1},{4,6},{5,7},{6,4},{7,5},{8,10},{9,11},{10,... | collective-permute-start | bytes 1179656 | tf_op jit(solution)/shard_map/ppermute | solution.py:53
  201.8 1.6 copy.25
  203.6 10.5 %collective-permute-start.20 = (bf16[4,64,384]{2,1,0:T(8,128)(2,1)S(1)}, bf16[4,64,384]{2,1,0:T(8,128)(2,1)S(1)}, u32[]{:S(2)}, u32[]{:S(2)}) collective-permute-start(bf16[4,64,384]{2,1,0:T(8,128)(2,1)S(1)} %fusion.18), channel_id=1, source_target_pairs={{0,64},{16,80},{32,96},{48,112},{64,0},{80,16},{96,32},{112,48},{1... | collective-permute-start | bytes 589832 | tf_op jit(solution)/shard_map/ppermute | solution.py:53
  215.2 2.7 %collective-permute-start.16 = (bf16[2,128,384]{2,1,0:T(8,128)(2,1)S(1)}, bf16[2,128,384]{2,1,0:T(8,128)(2,1)S(1)}, u32[]{:S(2)}, u32[]{:S(2)}) collective-permute-start(bf16[2,128,384]{2,1,0:T(8,128)(2,1)S(1)} %fusion.17), channel_id=1, source_target_pairs={{0,4},{1,5},{2,6},{3,7},{4,0},{5,1},{6,2},{7,3},{8,12},{9,13},{10,... | collective-permute-start | bytes 589832 | tf_op jit(solution)/shard_map/ppermute | solution.py:53
  218.5 9.6 %collective-permute-start.21 = (bf16[2,64,384]{2,1,0:T(8,128)(2,1)S(1)}, bf16[2,64,384]{2,1,0:T(8,128)(2,1)S(1)}, u32[]{:S(2)}, u32[]{:S(2)}) collective-permute-start(bf16[2,64,384]{2,1,0:T(8,128)(2,1)S(1)} %fusion.25), channel_id=1, source_target_pairs={{0,128},{16,144},{32,160},{48,176},{64,192},{80,208},{96,224},{112... | collective-permute-start | bytes 294920 | tf_op jit(solution)/shard_map/ppermute | solution.py:53
  228.2 3.4 %collective-permute-start.17 = (bf16[1,128,384]{2,1,0:T(8,128)(2,1)S(1)}, bf16[1,128,384]{2,1,0:T(8,128)(2,1)S(1)}, u32[]{:S(2)}, u32[]{:S(2)}) collective-permute-start(bf16[1,128,384]{2,1,0:T(8,128)(2,1)S(1)} %dynamic-slice_convert_fusion.4), channel_id=1, source_target_pairs={{0,8},{1,9},{2,10},{3,11},{4,12},{5,13},{6,14},{7,15},{8,0},{9,1},... | collective-permute-start | bytes 294920 | tf_op jit(solution)/shard_map/ppermute | solution.py:53
  231.6 5.4 %collective-permute-done.21 = bf16[2,64,384]{2,1,0:T(8,128)(2,1)S(1)} collective-permute-done((bf16[2,64,384]{2,1,0:T(8,128)(2,1)S(1)}, bf16[2,64,384]{2,1,0:T(8,128)(2,1)S(1)}, u32[]{:S(2)}, u32[]{:S(2)}) %collective-permute-start.21) | collective-permute-done | bytes 98336 | tf_op jit(solution)/shard_map/ppermute | solution.py:53
  237.1 9.4 %collective-permute-start.22 = (bf16[1,64,384]{2,1,0:T(8,128)(2,1)S(1)}, bf16[1,64,384]{2,1,0:T(8,128)(2,1)S(1)}, u32[]{:S(2)}, u32[]{:S(2)}) collective-permute-start(bf16[1,64,384]{2,1,0:T(8,128)(2,1)S(1)} %dynamic-slice_convert_fusion.5), channel_id=1, source_target_pairs={{0,256},{16,272},{32,288},{48,304},{64,320},{80,336},{96,352},{112... | collective-permute-start | bytes 147464 | tf_op jit(solution)/shard_map/ppermute | solution.py:53
  247.3 6.0 %collective-permute-done.22 = bf16[1,64,384]{2,1,0:T(8,128)(2,1)S(1)} collective-permute-done((bf16[1,64,384]{2,1,0:T(8,128)(2,1)S(1)}, bf16[1,64,384]{2,1,0:T(8,128)(2,1)S(1)}, u32[]{:S(2)}, u32[]{:S(2)}) %collective-permute-start.22) | collective-permute-done | bytes 49184 | tf_op jit(solution)/shard_map/ppermute | solution.py:53
  (88 shorter events, 29.7 us)
Async XLA Ops:
  7.2 79.4 %copy-start = (bf16[384,2048]{1,0:T(8,128)(2,1)S(1)}, bf16[384,2048]{1,0:T(8,128)(2,1)}, u32[]{:S(2)}) copy-start(bf16[384,2048]{1,0:T(8,128)(2,1)} %param.7) | copy-start | bytes 4718596
  7.2 79.4 %all-gather.2.cloned.1.call-start = ((), (), s32[]{:S(2)}) async-start(), calls=%async_computation | async-start | bytes 1671168 | tf_op jit(solution)/shard_map/all_gather | solution.py:87
  89.0 2.8 %copy-start.5 = (bf16[384,128]{1,0:T(8,128)(2,1)S(1)}, bf16[384,128]{1,0:T(8,128)(2,1)}, u32[]{:S(2)}) copy-start(bf16[384,128]{1,0:T(8,128)(2,1)} %param.13) | copy-start | bytes 294916
  89.2 3.1 %collective-permute-start = (f32[1,128,128]{2,1,0:T(8,128)S(1)}, f32[1,128,128]{2,1,0:T(8,128)S(1)}, u32[]{:S(2)}, u32[]{:S(2)}) collective-permute-start(f32[1,128,128]{2,1,0:T(8,128)S(1)} %convolution_bitcast_fusion.1), channel_id=1, source_target_pairs={{0,16},{16,0},{1,17},{17,1},{2,18},{18,2},{3,19},{19,3},{4,20},{20... | collective-permute-start | bytes 196616 | tf_op jit(solution)/shard_map/ppermute | solution.py:21
  91.8 32.0 %copy-start.6 = (f32[128]{0:T(128)S(1)}, f32[128]{0:T(128)}, u32[]{:S(2)}) copy-start(f32[128]{0:T(128)} %param.11) | copy-start | bytes 1540
  92.4 11.7 %collective-permute-start.3 = (f32[1,128,128]{2,1,0:T(8,128)S(1)}, f32[1,128,128]{2,1,0:T(8,128)S(1)}, u32[]{:S(2)}, u32[]{:S(2)}) collective-permute-start(f32[1,128,128]{2,1,0:T(8,128)S(1)} %add.192), channel_id=1, source_target_pairs={{0,96},{32,128},{64,160},{96,192},{128,224},{160,256},{192,288},{2... | collective-permute-start | bytes 196616 | tf_op jit(solution)/shard_map/ppermute | solution.py:35
  96.6 7.5 %collective-permute-start.2 = (f32[1,128,128]{2,1,0:T(8,128)S(1)}, f32[1,128,128]{2,1,0:T(8,128)S(1)}, u32[]{:S(2)}, u32[]{:S(2)}) collective-permute-start(f32[1,128,128]{2,1,0:T(8,128)S(1)} %add.192), channel_id=1, source_target_pairs={{0,64},{32,96},{64,128},{96,160},{128,192},{160,224},{192,256},{22... | collective-permute-start | bytes 196616 | tf_op jit(solution)/shard_map/ppermute | solution.py:35
  100.1 5.6 %collective-permute-start.1 = (f32[1,128,128]{2,1,0:T(8,128)S(1)}, f32[1,128,128]{2,1,0:T(8,128)S(1)}, u32[]{:S(2)}, u32[]{:S(2)}) collective-permute-start(f32[1,128,128]{2,1,0:T(8,128)S(1)} %add.192), channel_id=1, source_target_pairs={{0,32},{32,64},{64,96},{96,128},{128,160},{160,192},{192,224},{224... | collective-permute-start | bytes 196616 | tf_op jit(solution)/shard_map/ppermute | solution.py:35
  105.7 17.1 %collective-permute-start.6 = (f32[1,128,128]{2,1,0:T(8,128)S(1)}, f32[1,128,128]{2,1,0:T(8,128)S(1)}, u32[]{:S(2)}, u32[]{:S(2)}) collective-permute-start(f32[1,128,128]{2,1,0:T(8,128)S(1)} %add_add_fusion.1), channel_id=1, source_target_pairs={{0,384},{32,416},{64,448},{96,480},{1,385},{33,417},{65,449},{97,4... | collective-permute-start | bytes 196616 | tf_op jit(solution)/shard_map/ppermute | solution.py:35
  113.1 9.8 %collective-permute-start.5 = (f32[1,128,128]{2,1,0:T(8,128)S(1)}, f32[1,128,128]{2,1,0:T(8,128)S(1)}, u32[]{:S(2)}, u32[]{:S(2)}) collective-permute-start(f32[1,128,128]{2,1,0:T(8,128)S(1)} %add_add_fusion.1), channel_id=1, source_target_pairs={{0,256},{32,288},{64,320},{96,352},{128,384},{160,416},{192,448},{... | collective-permute-start | bytes 196616 | tf_op jit(solution)/shard_map/ppermute | solution.py:35
  116.4 7.1 %collective-permute-start.4 = (f32[1,128,128]{2,1,0:T(8,128)S(1)}, f32[1,128,128]{2,1,0:T(8,128)S(1)}, u32[]{:S(2)}, u32[]{:S(2)}) collective-permute-start(f32[1,128,128]{2,1,0:T(8,128)S(1)} %add_add_fusion.1), channel_id=1, source_target_pairs={{0,128},{32,160},{64,192},{96,224},{128,256},{160,288},{192,320},{... | collective-permute-start | bytes 196616 | tf_op jit(solution)/shard_map/ppermute | solution.py:35
  125.4 3.1 %collective-permute-start.7 = (f32[1,128,128]{2,1,0:T(8,128)S(1)}, f32[1,128,128]{2,1,0:T(8,128)S(1)}, u32[]{:S(2)}, u32[]{:S(2)}) collective-permute-start(f32[1,128,128]{2,1,0:T(8,128)S(1)} %convolution_bitcast_fusion), channel_id=1, source_target_pairs={{0,16},{16,0},{1,17},{17,1},{2,18},{18,2},{3,19},{19,3},{4,20},{20... | collective-permute-start | bytes 196616 | tf_op jit(solution)/shard_map/ppermute | solution.py:21
  128.5 8.0 %collective-permute-start.10 = (f32[1,128,128]{2,1,0:T(8,128)S(1)}, f32[1,128,128]{2,1,0:T(8,128)S(1)}, u32[]{:S(2)}, u32[]{:S(2)}) collective-permute-start(f32[1,128,128]{2,1,0:T(8,128)S(1)} %add.205), channel_id=1, source_target_pairs={{96,0},{128,32},{160,64},{192,96},{224,128},{256,160},{288,192},{3... | collective-permute-start | bytes 196616 | tf_op jit(solution)/shard_map/ppermute | solution.py:35
  129.8 9.6 %collective-permute-start.9 = (f32[1,128,128]{2,1,0:T(8,128)S(1)}, f32[1,128,128]{2,1,0:T(8,128)S(1)}, u32[]{:S(2)}, u32[]{:S(2)}) collective-permute-start(f32[1,128,128]{2,1,0:T(8,128)S(1)} %add.205), channel_id=1, source_target_pairs={{64,0},{96,32},{128,64},{160,96},{192,128},{224,160},{256,192},{28... | collective-permute-start | bytes 196616 | tf_op jit(solution)/shard_map/ppermute | solution.py:35
  131.1 8.3 %collective-permute-start.8 = (f32[1,128,128]{2,1,0:T(8,128)S(1)}, f32[1,128,128]{2,1,0:T(8,128)S(1)}, u32[]{:S(2)}, u32[]{:S(2)}) collective-permute-start(f32[1,128,128]{2,1,0:T(8,128)S(1)} %add.205), channel_id=1, source_target_pairs={{32,0},{64,32},{96,64},{128,96},{160,128},{192,160},{224,192},{256... | collective-permute-start | bytes 196616 | tf_op jit(solution)/shard_map/ppermute | solution.py:35
  139.4 16.5 %collective-permute-start.13 = (f32[1,128,128]{2,1,0:T(8,128)S(1)}, f32[1,128,128]{2,1,0:T(8,128)S(1)}, u32[]{:S(2)}, u32[]{:S(2)}) collective-permute-start(f32[1,128,128]{2,1,0:T(8,128)S(1)} %add_add_fusion), channel_id=1, source_target_pairs={{384,0},{416,32},{448,64},{480,96},{385,1},{417,33},{449,65},{481,... | collective-permute-start | bytes 196616 | tf_op jit(solution)/shard_map/ppermute | solution.py:35
  140.7 16.4 %collective-permute-start.12 = (f32[1,128,128]{2,1,0:T(8,128)S(1)}, f32[1,128,128]{2,1,0:T(8,128)S(1)}, u32[]{:S(2)}, u32[]{:S(2)}) collective-permute-start(f32[1,128,128]{2,1,0:T(8,128)S(1)} %add_add_fusion), channel_id=1, source_target_pairs={{256,0},{288,32},{320,64},{352,96},{384,128},{416,160},{448,192},{... | collective-permute-start | bytes 196616 | tf_op jit(solution)/shard_map/ppermute | solution.py:35
  142.0 15.1 %collective-permute-start.11 = (f32[1,128,128]{2,1,0:T(8,128)S(1)}, f32[1,128,128]{2,1,0:T(8,128)S(1)}, u32[]{:S(2)}, u32[]{:S(2)}) collective-permute-start(f32[1,128,128]{2,1,0:T(8,128)S(1)} %add_add_fusion), channel_id=1, source_target_pairs={{128,0},{160,32},{192,64},{224,96},{256,128},{288,160},{320,192},{... | collective-permute-start | bytes 196616 | tf_op jit(solution)/shard_map/ppermute | solution.py:35
  163.7 3.6 %copy-start.7 = (bf16[2048,384]{1,0:T(8,128)(2,1)S(1)}, bf16[2048,384]{1,0:T(8,128)(2,1)}, u32[]{:S(2)}) copy-start(bf16[2048,384]{1,0:T(8,128)(2,1)} %all-gather.2.cloned.1.call-done) | copy-start | bytes 4718596
  165.4 9.4 %collective-permute-start.18 = (bf16[16,64,384]{2,1,0:T(8,128)(2,1)S(1)}, bf16[16,64,384]{2,1,0:T(8,128)(2,1)}, u32[]{:S(2)}, u32[]{:S(2)}) collective-permute-start(bf16[16,64,384]{2,1,0:T(8,128)(2,1)S(1)} %fusion.12), channel_id=1, source_target_pairs={{0,16},{16,0},{32,48},{48,32},{64,80},{80,64},{96,112},{112,96},{1... | collective-permute-start | bytes 2359304 | tf_op jit(solution)/shard_map/ppermute | solution.py:53
  168.8 1.6 copy-start.1
  171.4 22.1 %collective-permute-start.14 = (bf16[8,128,384]{2,1,0:T(8,128)(2,1)}, bf16[8,128,384]{2,1,0:T(8,128)(2,1)}, u32[]{:S(2)}, u32[]{:S(2)}) collective-permute-start(bf16[8,128,384]{2,1,0:T(8,128)(2,1)} %fusion.13), channel_id=1, source_target_pairs={{0,1},{1,0},{2,3},{3,2},{4,5},{5,4},{6,7},{7,6},{8,9},{9,8},{10,11... | collective-permute-start | bytes 2359304 | tf_op jit(solution)/shard_map/ppermute | solution.py:53
  174.8 18.7 %copy-start.2 = (f32[8,2,128,384]{3,2,1,0:T(8,128)S(1)}, f32[8,2,128,384]{3,2,1,0:T(8,128)}, u32[]{:S(2)}) copy-start(f32[8,2,128,384]{3,2,1,0:T(8,128)} %copy-done.1) | copy-start | bytes 9437188
  177.6 25.8 %collective-permute-start.19 = (bf16[8,64,384]{2,1,0:T(8,128)(2,1)}, bf16[8,64,384]{2,1,0:T(8,128)(2,1)S(1)}, u32[]{:S(2)}, u32[]{:S(2)}) collective-permute-start(bf16[8,64,384]{2,1,0:T(8,128)(2,1)} %fusion.16), channel_id=1, source_target_pairs={{0,32},{16,48},{32,0},{48,16},{64,96},{80,112},{96,64},{112,80},{1... | collective-permute-start | bytes 1179656 | tf_op jit(solution)/shard_map/ppermute | solution.py:53
  194.9 1.2 copy-start.3
  196.9 17.2 %collective-permute-start.15 = (bf16[4,128,384]{2,1,0:T(8,128)(2,1)}, bf16[4,128,384]{2,1,0:T(8,128)(2,1)}, u32[]{:S(2)}, u32[]{:S(2)}) collective-permute-start(bf16[4,128,384]{2,1,0:T(8,128)(2,1)} %fusion.15), channel_id=1, source_target_pairs={{0,2},{1,3},{2,0},{3,1},{4,6},{5,7},{6,4},{7,5},{8,10},{9,11},{10,... | collective-permute-start | bytes 1179656 | tf_op jit(solution)/shard_map/ppermute | solution.py:53
  203.4 10.6 %copy-start.4 = (f32[8,128,384]{2,1,0:T(8,128)S(1)}, f32[8,128,384]{2,1,0:T(8,128)}, u32[]{:S(2)}) copy-start(f32[8,128,384]{2,1,0:T(8,128)} %copy-done.3) | copy-start | bytes 4718596
  203.6 14.9 %collective-permute-start.20 = (bf16[4,64,384]{2,1,0:T(8,128)(2,1)S(1)}, bf16[4,64,384]{2,1,0:T(8,128)(2,1)S(1)}, u32[]{:S(2)}, u32[]{:S(2)}) collective-permute-start(bf16[4,64,384]{2,1,0:T(8,128)(2,1)S(1)} %fusion.18), channel_id=1, source_target_pairs={{0,64},{16,80},{32,96},{48,112},{64,0},{80,16},{96,32},{112,48},{1... | collective-permute-start | bytes 589832 | tf_op jit(solution)/shard_map/ppermute | solution.py:53
  215.2 13.0 %collective-permute-start.16 = (bf16[2,128,384]{2,1,0:T(8,128)(2,1)S(1)}, bf16[2,128,384]{2,1,0:T(8,128)(2,1)S(1)}, u32[]{:S(2)}, u32[]{:S(2)}) collective-permute-start(bf16[2,128,384]{2,1,0:T(8,128)(2,1)S(1)} %fusion.17), channel_id=1, source_target_pairs={{0,4},{1,5},{2,6},{3,7},{4,0},{5,1},{6,2},{7,3},{8,12},{9,13},{10,... | collective-permute-start | bytes 589832 | tf_op jit(solution)/shard_map/ppermute | solution.py:53
  218.5 18.5 %collective-permute-start.21 = (bf16[2,64,384]{2,1,0:T(8,128)(2,1)S(1)}, bf16[2,64,384]{2,1,0:T(8,128)(2,1)S(1)}, u32[]{:S(2)}, u32[]{:S(2)}) collective-permute-start(bf16[2,64,384]{2,1,0:T(8,128)(2,1)S(1)} %fusion.25), channel_id=1, source_target_pairs={{0,128},{16,144},{32,160},{48,176},{64,192},{80,208},{96,224},{112... | collective-permute-start | bytes 294920 | tf_op jit(solution)/shard_map/ppermute | solution.py:53
  228.2 18.3 %collective-permute-start.17 = (bf16[1,128,384]{2,1,0:T(8,128)(2,1)S(1)}, bf16[1,128,384]{2,1,0:T(8,128)(2,1)S(1)}, u32[]{:S(2)}, u32[]{:S(2)}) collective-permute-start(bf16[1,128,384]{2,1,0:T(8,128)(2,1)S(1)} %dynamic-slice_convert_fusion.4), channel_id=1, source_target_pairs={{0,8},{1,9},{2,10},{3,11},{4,12},{5,13},{6,14},{7,15},{8,0},{9,1},... | collective-permute-start | bytes 294920 | tf_op jit(solution)/shard_map/ppermute | solution.py:53
  237.1 16.3 %collective-permute-start.22 = (bf16[1,64,384]{2,1,0:T(8,128)(2,1)S(1)}, bf16[1,64,384]{2,1,0:T(8,128)(2,1)S(1)}, u32[]{:S(2)}, u32[]{:S(2)}) collective-permute-start(bf16[1,64,384]{2,1,0:T(8,128)(2,1)S(1)} %dynamic-slice_convert_fusion.5), channel_id=1, source_target_pairs={{0,256},{16,272},{32,288},{48,304},{64,320},{80,336},{96,352},{112... | collective-permute-start | bytes 147464 | tf_op jit(solution)/shard_map/ppermute | solution.py:53
Sparse Core Ops, SparseCore 0:
  10.2 76.2 all-gather.1

commit v6 on v5

--- a/solution.py
+++ b/solution.py
@@ -39,6 +39,21 @@
     return (total - pair_total) + inside
 
 
+def doubling_gather(block, axis, count):
+    place = lax.axis_index(axis)
+    current = block[None]
+    bit = count.bit_length() - 2
+    while bit >= 0:
+        pairs = [(i, i ^ (1 << bit)) for i in range(count)]
+        received = lax.ppermute(current, axis, pairs)
+        upper = ((place >> bit) & 1) == 1
+        low = jnp.where(upper, received, current)
+        high = jnp.where(upper, current, received)
+        current = jnp.stack([low, high], axis=1).reshape((-1,) + block.shape)
+        bit -= 1
+    return current
+
+
 def halving_scatter(term, axis, count):
     place = lax.axis_index(axis)
     rows = term.shape[0] // count
@@ -81,10 +96,17 @@
     allowed = allowed_pairs(block_mask[0])
     seq_count = lax.axis_size("z") * lax.axis_size("core")
     fsdp_count = lax.axis_size("fsdp")
-    pair_rows = lax.all_gather(
-        jnp.concatenate([w_query, w_key, w_value], axis=1), "core", axis=0, tiled=True
-    )
-    weight_cat = lax.all_gather(pair_rows, "z", axis=0, tiled=True)
+    own_rows = jnp.concatenate([w_query, w_key, w_value], axis=1)
+    chip_rows = doubling_gather(own_rows, "z", lax.axis_size("z"))
+    other_rows = lax.ppermute(chip_rows, "core", [(0, 1), (1, 0)])
+    second_core = lax.axis_index("core") == 1
+    weight_cat = jnp.stack(
+        [
+            jnp.where(second_core, other_rows, chip_rows),
+            jnp.where(second_core, chip_rows, other_rows),
+        ],
+        axis=1,
+    ).reshape(-1, 3 * columns)
     projected = jnp.dot(tokens, weight_cat, preferred_element_type=jnp.float32)
     projected = projected.astype(jnp.bfloat16)
     queries = projected[:, :columns].reshape(SEG, heads_here, HDIM)

time: 263 us -> 239 us (0.909)
  waiting for transfers between devices: 122 us -> 72.1 us
  starting transfers between devices: 91 us -> 126 us
  between operations: 14.6 us -> 1.39 us
  local copies, waits for them, and re-layouts: 13.9 us -> 17.1 us
    all_gather x1 -> x0, waiting for transfers between devices: 75.5 us -> none  [shards(): weight_cat = lax.all_gather(pair_rows, 'z', axis=0, tiled=True)]
    ppermute x0 -> x5, waiting for transfers between devices: none -> 30 us  [the longest x4 28.1 us: doubling_gather(): received = lax.ppermute(current, axis, pairs)]
    ppermute x0 -> x5, starting transfers between devices: none -> 29.1 us  [the longest x4 27.2 us: doubling_gather(): received = lax.ppermute(current, axis, pairs)]
    ppermute x12, starting transfers between devices: 35.1 us -> 40.4 us  [entering(): parts.append(lax.ppermute(total, 'z', pairs))]
    ppermute x9, waiting for transfers between devices: 21.8 us -> 17.4 us  [halving_scatter(): lax.ppermute(away.astype(jnp.bfloat16), axis, pairs).astype(jnp.float32)]
    unnamed x19 -> x27, local copies, waits for them, and re-layouts: 5.37 us -> 7.39 us
  transfers between devices with their start and end apart: 24 -> 28, of which waited for: 14 -> 18; matrix products, arithmetic and copies ran while one was open for 5% -> 7% of each run, Pallas kernels for 0% -> 0%
where the time goes in v6:
time: 239 us; the launch traced here: 237 us
  starting transfers between devices  126 us (53%)
  waiting for transfers between devices  72.1 us (30%)
  local copies, waits for them, and re-layouts  17.1 us (7%)
  matrix products  10.5 us (4%)
  other arithmetic  9.2 us (4%)
    ppermute x9, starting transfers between devices, halving_scatter(): lax.ppermute(away.astype(jnp.bfloat16), axis, pairs).astype(jnp.float32)  52.8 us
    ppermute x12, starting transfers between devices, entering(): parts.append(lax.ppermute(total, 'z', pairs))  40.4 us
    ppermute x4, waiting for transfers between devices, doubling_gather(): received = lax.ppermute(current, axis, pairs)  28.1 us
    ppermute x4, starting transfers between devices, doubling_gather(): received = lax.ppermute(current, axis, pairs)  27.2 us
    ppermute x12, waiting for transfers between devices, entering(): parts.append(lax.ppermute(total, 'z', pairs))  23.7 us
    ppermute x9, waiting for transfers between devices, halving_scatter(): lax.ppermute(away.astype(jnp.bfloat16), axis, pairs).astype(jnp.float32)  17.4 us
    unnamed x27, local copies, waits for them, and re-layouts  7.39 us
    convert_element_type x9, local copies, waits for them, and re-layouts, halving_scatter(): away.astype(jnp.bfloat16)  5.23 us
  transfers between devices with their start and end apart: 28, of which 18 were waited for; matrix products, arithmetic and copies ran while one was open for 7% of the time, Pallas kernels for 0%

profile of v6, /device:TPU:6, one launch (start us, length us, event | category | flops | bytes accessed | tf_op | source)
XLA Modules:
  0.0 236.6 jit_solution(4947370529556839497)
XLA Ops:
  1.5 15.7 %collective-permute-start = (bf16[1,64,384]{2,1,0:T(8,128)(2,1)S(1)}, bf16[1,64,384]{2,1,0:T(8,128)(2,1)S(1)}, u32[]{:S(2)}, u32[]{:S(2)}) collective-permute-start(bf16[1,64,384]{2,1,0:T(8,128)(2,1)S(1)} %maximum_bitcast_fusion.1), channel_id=1, source_target_pairs={{0,256},{32,288},{64,320},{96,352},{128,384},{160,416},{192,448},{... | collective-permute-start | bytes 147464 | tf_op jit(solution)/shard_map/ppermute | solution.py:48
  17.3 2.9 %collective-permute-done = bf16[1,64,384]{2,1,0:T(8,128)(2,1)S(1)} collective-permute-done((bf16[1,64,384]{2,1,0:T(8,128)(2,1)S(1)}, bf16[1,64,384]{2,1,0:T(8,128)(2,1)S(1)}, u32[]{:S(2)}, u32[]{:S(2)}) %collective-permute-start) | collective-permute-done | bytes 49184 | tf_op jit(solution)/shard_map/ppermute | solution.py:48
  21.0 7.0 %collective-permute-start.1 = (bf16[2,64,384]{2,1,0:T(8,128)(2,1)S(1)}, bf16[2,64,384]{2,1,0:T(8,128)(2,1)S(1)}, u32[]{:S(2)}, u32[]{:S(2)}) collective-permute-start(bf16[2,64,384]{2,1,0:T(8,128)(2,1)S(1)} %maximum_bitcast_fusion), channel_id=1, source_target_pairs={{0,128},{32,160},{64,192},{96,224},{128,0},{160,32},{192,64},{224,... | collective-permute-start | bytes 294920 | tf_op jit(solution)/shard_map/ppermute | solution.py:48
  28.0 8.1 %collective-permute-done.1 = bf16[2,64,384]{2,1,0:T(8,128)(2,1)S(1)} collective-permute-done((bf16[2,64,384]{2,1,0:T(8,128)(2,1)S(1)}, bf16[2,64,384]{2,1,0:T(8,128)(2,1)S(1)}, u32[]{:S(2)}, u32[]{:S(2)}) %collective-permute-start.1) | collective-permute-done | bytes 98336 | tf_op jit(solution)/shard_map/ppermute | solution.py:48
  38.1 7.8 %collective-permute-done.2 = bf16[4,64,384]{2,1,0:T(8,128)(2,1)S(1)} collective-permute-done((bf16[4,64,384]{2,1,0:T(8,128)(2,1)S(1)}, bf16[4,64,384]{2,1,0:T(8,128)(2,1)S(1)}, u32[]{:S(2)}, u32[]{:S(2)}) %collective-permute-start.2) | collective-permute-done | bytes 196640 | tf_op jit(solution)/shard_map/ppermute | solution.py:48
  46.0 2.6 %collective-permute-start.3 = (bf16[8,64,384]{2,1,0:T(8,128)(2,1)S(1)}, bf16[8,64,384]{2,1,0:T(8,128)(2,1)S(1)}, u32[]{:S(2)}, u32[]{:S(2)}) collective-permute-start(bf16[8,64,384]{2,1,0:T(8,128)(2,1)S(1)} %bitcast.190), channel_id=1, source_target_pairs={{0,32},{32,0},{64,96},{96,64},{128,160},{160,128},{192,224},{224,1... | collective-permute-start | bytes 1179656 | tf_op jit(solution)/shard_map/ppermute | solution.py:48
  48.6 9.3 %collective-permute-done.3 = bf16[8,64,384]{2,1,0:T(8,128)(2,1)S(1)} collective-permute-done((bf16[8,64,384]{2,1,0:T(8,128)(2,1)S(1)}, bf16[8,64,384]{2,1,0:T(8,128)(2,1)S(1)}, u32[]{:S(2)}, u32[]{:S(2)}) %collective-permute-start.3) | collective-permute-done | bytes 393248 | tf_op jit(solution)/shard_map/ppermute | solution.py:48
  64.9 2.0 collective-permute-start.5
  70.1 6.5 %collective-permute-start.8 = (f32[1,128,128]{2,1,0:T(8,128)S(1)}, f32[1,128,128]{2,1,0:T(8,128)S(1)}, u32[]{:S(2)}, u32[]{:S(2)}) collective-permute-start(f32[1,128,128]{2,1,0:T(8,128)S(1)} %add.192), channel_id=1, source_target_pairs={{0,96},{32,128},{64,160},{96,192},{128,224},{160,256},{192,288},{2... | collective-permute-start | bytes 196616 | tf_op jit(solution)/shard_map/ppermute | solution.py:35
  76.6 5.3 %collective-permute-start.7 = (f32[1,128,128]{2,1,0:T(8,128)S(1)}, f32[1,128,128]{2,1,0:T(8,128)S(1)}, u32[]{:S(2)}, u32[]{:S(2)}) collective-permute-start(f32[1,128,128]{2,1,0:T(8,128)S(1)} %add.192), channel_id=1, source_target_pairs={{0,64},{32,96},{64,128},{96,160},{128,192},{160,224},{192,256},{22... | collective-permute-start | bytes 196616 | tf_op jit(solution)/shard_map/ppermute | solution.py:35
  81.8 4.1 %collective-permute-start.6 = (f32[1,128,128]{2,1,0:T(8,128)S(1)}, f32[1,128,128]{2,1,0:T(8,128)S(1)}, u32[]{:S(2)}, u32[]{:S(2)}) collective-permute-start(f32[1,128,128]{2,1,0:T(8,128)S(1)} %add.192), channel_id=1, source_target_pairs={{0,32},{32,64},{64,96},{96,128},{128,160},{160,192},{192,224},{224... | collective-permute-start | bytes 196616 | tf_op jit(solution)/shard_map/ppermute | solution.py:35
  87.9 8.3 %collective-permute-start.11 = (f32[1,128,128]{2,1,0:T(8,128)S(1)}, f32[1,128,128]{2,1,0:T(8,128)S(1)}, u32[]{:S(2)}, u32[]{:S(2)}) collective-permute-start(f32[1,128,128]{2,1,0:T(8,128)S(1)} %add_add_fusion.1), channel_id=1, source_target_pairs={{0,384},{32,416},{64,448},{96,480},{1,385},{33,417},{65,449},{97,4... | collective-permute-start | bytes 196616 | tf_op jit(solution)/shard_map/ppermute | solution.py:35
  96.2 4.1 %collective-permute-start.10 = (f32[1,128,128]{2,1,0:T(8,128)S(1)}, f32[1,128,128]{2,1,0:T(8,128)S(1)}, u32[]{:S(2)}, u32[]{:S(2)}) collective-permute-start(f32[1,128,128]{2,1,0:T(8,128)S(1)} %add_add_fusion.1), channel_id=1, source_target_pairs={{0,256},{32,288},{64,320},{96,352},{128,384},{160,416},{192,448},{... | collective-permute-start | bytes 196616 | tf_op jit(solution)/shard_map/ppermute | solution.py:35
  100.2 4.5 %collective-permute-start.9 = (f32[1,128,128]{2,1,0:T(8,128)S(1)}, f32[1,128,128]{2,1,0:T(8,128)S(1)}, u32[]{:S(2)}, u32[]{:S(2)}) collective-permute-start(f32[1,128,128]{2,1,0:T(8,128)S(1)} %add_add_fusion.1), channel_id=1, source_target_pairs={{0,128},{32,160},{64,192},{96,224},{128,256},{160,288},{192,320},{... | collective-permute-start | bytes 196616 | tf_op jit(solution)/shard_map/ppermute | solution.py:35
  115.8 3.9 %collective-permute-done.15 = f32[1,128,128]{2,1,0:T(8,128)S(1)} collective-permute-done((f32[1,128,128]{2,1,0:T(8,128)S(1)}, f32[1,128,128]{2,1,0:T(8,128)S(1)}, u32[]{:S(2)}, u32[]{:S(2)}) %collective-permute-start.15) | collective-permute-done | bytes 65568 | tf_op jit(solution)/shard_map/ppermute | solution.py:35
  119.6 3.8 %collective-permute-done.14 = f32[1,128,128]{2,1,0:T(8,128)S(1)} collective-permute-done((f32[1,128,128]{2,1,0:T(8,128)S(1)}, f32[1,128,128]{2,1,0:T(8,128)S(1)}, u32[]{:S(2)}, u32[]{:S(2)}) %collective-permute-start.14) | collective-permute-done | bytes 65568 | tf_op jit(solution)/shard_map/ppermute | solution.py:35
  127.5 11.1 %collective-permute-done.18 = f32[1,128,128]{2,1,0:T(8,128)S(1)} collective-permute-done((f32[1,128,128]{2,1,0:T(8,128)S(1)}, f32[1,128,128]{2,1,0:T(8,128)S(1)}, u32[]{:S(2)}, u32[]{:S(2)}) %collective-permute-start.18) | collective-permute-done | bytes 65568 | tf_op jit(solution)/shard_map/ppermute | solution.py:35
  138.6 2.4 %collective-permute-done.17 = f32[1,128,128]{2,1,0:T(8,128)S(1)} collective-permute-done((f32[1,128,128]{2,1,0:T(8,128)S(1)}, f32[1,128,128]{2,1,0:T(8,128)S(1)}, u32[]{:S(2)}, u32[]{:S(2)}) %collective-permute-start.17) | collective-permute-done | bytes 65568 | tf_op jit(solution)/shard_map/ppermute | solution.py:35
  142.7 2.7 %convert_bitcast_fusion = f32[2048,384]{0,1:T(8,128)} fusion(bf16[384,2048]{1,0:T(8,128)(2,1)S(1)} %copy-done, bf16[384,128]{0,1:T(8,128)(2,1)S(1)} %fusion.9, bf16[384,128]{0,1:T(8,128)(2,1)S(1)} %fusion.10, bf16[384,128]{0,1:T(8,128)(2,1)S(1)} %fusion.11), kind=kOutput, calls=%fused_computation | convolution fusion | flops 606437376 | bytes 5013504 | tf_op jit(solution)/shard_map/dot_general | solution.py:164
  145.4 3.5 %copy.41 = f32[2048,384]{1,0:T(8,128)} copy(f32[2048,384]{0,1:T(8,128)} %convert_bitcast_fusion) | data formatting | bytes 6291456 | tf_op jit(solution)/shard_map/reshape;reshape | solution.py:64
  148.9 2.5 %fusion.12 = bf16[16,64,384]{2,1,0:T(8,128)(2,1)} fusion(f32[16,2,64,384]{3,2,1,0:T(8,128)} %bitcast.177, s32[]{:T(128)S(6)} %select_n.196), kind=kLoop, calls=%fused_computation.30 | loop fusion | bytes 1572868 | tf_op jit(solution)/shard_map/convert_element_type | solution.py:68
  157.5 3.5 %collective-permute-start.19 = (bf16[8,128,384]{2,1,0:T(8,128)(2,1)}, bf16[8,128,384]{2,1,0:T(8,128)(2,1)}, u32[]{:S(2)}, u32[]{:S(2)}) collective-permute-start(bf16[8,128,384]{2,1,0:T(8,128)(2,1)} %fusion.13), channel_id=1, source_target_pairs={{0,1},{1,0},{2,3},{3,2},{4,5},{5,4},{6,7},{7,6},{8,9},{9,8},{10,11... | collective-permute-start | bytes 2359304 | tf_op jit(solution)/shard_map/ppermute | solution.py:68
  163.8 5.5 %collective-permute-start.24 = (bf16[8,64,384]{2,1,0:T(8,128)(2,1)}, bf16[8,64,384]{2,1,0:T(8,128)(2,1)S(1)}, u32[]{:S(2)}, u32[]{:S(2)}) collective-permute-start(bf16[8,64,384]{2,1,0:T(8,128)(2,1)} %fusion.16), channel_id=1, source_target_pairs={{0,32},{16,48},{32,0},{48,16},{64,96},{80,112},{96,64},{112,80},{1... | collective-permute-start | bytes 1179656 | tf_op jit(solution)/shard_map/ppermute | solution.py:68
  169.3 10.3 %collective-permute-done.19 = bf16[8,128,384]{2,1,0:T(8,128)(2,1)} collective-permute-done((bf16[8,128,384]{2,1,0:T(8,128)(2,1)}, bf16[8,128,384]{2,1,0:T(8,128)(2,1)}, u32[]{:S(2)}, u32[]{:S(2)}) %collective-permute-start.19) | collective-permute-done | bytes 786464 | tf_op jit(solution)/shard_map/ppermute | solution.py:68
  183.0 5.1 %collective-permute-start.20 = (bf16[4,128,384]{2,1,0:T(8,128)(2,1)}, bf16[4,128,384]{2,1,0:T(8,128)(2,1)}, u32[]{:S(2)}, u32[]{:S(2)}) collective-permute-start(bf16[4,128,384]{2,1,0:T(8,128)(2,1)} %fusion.15), channel_id=1, source_target_pairs={{0,2},{1,3},{2,0},{3,1},{4,6},{5,7},{6,4},{7,5},{8,10},{9,11},{10,... | collective-permute-start | bytes 1179656 | tf_op jit(solution)/shard_map/ppermute | solution.py:68
  189.8 7.7 %collective-permute-start.25 = (bf16[4,64,384]{2,1,0:T(8,128)(2,1)S(1)}, bf16[4,64,384]{2,1,0:T(8,128)(2,1)S(1)}, u32[]{:S(2)}, u32[]{:S(2)}) collective-permute-start(bf16[4,64,384]{2,1,0:T(8,128)(2,1)S(1)} %fusion.18), channel_id=1, source_target_pairs={{0,64},{16,80},{32,96},{48,112},{64,0},{80,16},{96,32},{112,48},{1... | collective-permute-start | bytes 589832 | tf_op jit(solution)/shard_map/ppermute | solution.py:68
  198.7 2.8 %collective-permute-start.21 = (bf16[2,128,384]{2,1,0:T(8,128)(2,1)S(1)}, bf16[2,128,384]{2,1,0:T(8,128)(2,1)S(1)}, u32[]{:S(2)}, u32[]{:S(2)}) collective-permute-start(bf16[2,128,384]{2,1,0:T(8,128)(2,1)S(1)} %fusion.17), channel_id=1, source_target_pairs={{0,4},{1,5},{2,6},{3,7},{4,0},{5,1},{6,2},{7,3},{8,12},{9,13},{10,... | collective-permute-start | bytes 589832 | tf_op jit(solution)/shard_map/ppermute | solution.py:68
  202.0 12.3 %collective-permute-start.26 = (bf16[2,64,384]{2,1,0:T(8,128)(2,1)S(1)}, bf16[2,64,384]{2,1,0:T(8,128)(2,1)S(1)}, u32[]{:S(2)}, u32[]{:S(2)}) collective-permute-start(bf16[2,64,384]{2,1,0:T(8,128)(2,1)S(1)} %fusion.25), channel_id=1, source_target_pairs={{0,128},{16,144},{32,160},{48,176},{64,192},{80,208},{96,224},{112... | collective-permute-start | bytes 294920 | tf_op jit(solution)/shard_map/ppermute | solution.py:68
  214.4 3.4 %collective-permute-start.22 = (bf16[1,128,384]{2,1,0:T(8,128)(2,1)S(1)}, bf16[1,128,384]{2,1,0:T(8,128)(2,1)S(1)}, u32[]{:S(2)}, u32[]{:S(2)}) collective-permute-start(bf16[1,128,384]{2,1,0:T(8,128)(2,1)S(1)} %dynamic-slice_convert_fusion.4), channel_id=1, source_target_pairs={{0,8},{1,9},{2,10},{3,11},{4,12},{5,13},{6,14},{7,15},{8,0},{9,1},... | collective-permute-start | bytes 294920 | tf_op jit(solution)/shard_map/ppermute | solution.py:68
  217.8 3.4 %collective-permute-done.26 = bf16[2,64,384]{2,1,0:T(8,128)(2,1)S(1)} collective-permute-done((bf16[2,64,384]{2,1,0:T(8,128)(2,1)S(1)}, bf16[2,64,384]{2,1,0:T(8,128)(2,1)S(1)}, u32[]{:S(2)}, u32[]{:S(2)}) %collective-permute-start.26) | collective-permute-done | bytes 98336 | tf_op jit(solution)/shard_map/ppermute | solution.py:68
  221.2 10.7 %collective-permute-start.27 = (bf16[1,64,384]{2,1,0:T(8,128)(2,1)S(1)}, bf16[1,64,384]{2,1,0:T(8,128)(2,1)S(1)}, u32[]{:S(2)}, u32[]{:S(2)}) collective-permute-start(bf16[1,64,384]{2,1,0:T(8,128)(2,1)S(1)} %dynamic-slice_convert_fusion.5), channel_id=1, source_target_pairs={{0,256},{16,272},{32,288},{48,304},{64,320},{80,336},{96,352},{112... | collective-permute-start | bytes 147464 | tf_op jit(solution)/shard_map/ppermute | solution.py:68
  232.7 3.2 %collective-permute-done.27 = bf16[1,64,384]{2,1,0:T(8,128)(2,1)S(1)} collective-permute-done((bf16[1,64,384]{2,1,0:T(8,128)(2,1)S(1)}, bf16[1,64,384]{2,1,0:T(8,128)(2,1)S(1)}, u32[]{:S(2)}, u32[]{:S(2)}) %collective-permute-start.27) | collective-permute-done | bytes 49184 | tf_op jit(solution)/shard_map/ppermute | solution.py:68
  (115 shorter events, 49.5 us)
Async XLA Ops:
  0.6 62.4 %copy-start = (bf16[384,2048]{1,0:T(8,128)(2,1)S(1)}, bf16[384,2048]{1,0:T(8,128)(2,1)}, u32[]{:S(2)}) copy-start(bf16[384,2048]{1,0:T(8,128)(2,1)} %param.7) | copy-start | bytes 4718596
  1.5 18.7 %collective-permute-start = (bf16[1,64,384]{2,1,0:T(8,128)(2,1)S(1)}, bf16[1,64,384]{2,1,0:T(8,128)(2,1)S(1)}, u32[]{:S(2)}, u32[]{:S(2)}) collective-permute-start(bf16[1,64,384]{2,1,0:T(8,128)(2,1)S(1)} %maximum_bitcast_fusion.1), channel_id=1, source_target_pairs={{0,256},{32,288},{64,320},{96,352},{128,384},{160,416},{192,448},{... | collective-permute-start | bytes 147464 | tf_op jit(solution)/shard_map/ppermute | solution.py:48
  21.0 15.1 %collective-permute-start.1 = (bf16[2,64,384]{2,1,0:T(8,128)(2,1)S(1)}, bf16[2,64,384]{2,1,0:T(8,128)(2,1)S(1)}, u32[]{:S(2)}, u32[]{:S(2)}) collective-permute-start(bf16[2,64,384]{2,1,0:T(8,128)(2,1)S(1)} %maximum_bitcast_fusion), channel_id=1, source_target_pairs={{0,128},{32,160},{64,192},{96,224},{128,0},{160,32},{192,64},{224,... | collective-permute-start | bytes 294920 | tf_op jit(solution)/shard_map/ppermute | solution.py:48
  36.2 9.7 %collective-permute-start.2 = (bf16[4,64,384]{2,1,0:T(8,128)(2,1)S(1)}, bf16[4,64,384]{2,1,0:T(8,128)(2,1)S(1)}, u32[]{:S(2)}, u32[]{:S(2)}) collective-permute-start(bf16[4,64,384]{2,1,0:T(8,128)(2,1)S(1)} %bitcast.194), channel_id=1, source_target_pairs={{0,64},{32,96},{64,0},{96,32},{128,192},{160,224},{192,128},{224,1... | collective-permute-start | bytes 589832 | tf_op jit(solution)/shard_map/ppermute | solution.py:48
  46.0 11.9 %collective-permute-start.3 = (bf16[8,64,384]{2,1,0:T(8,128)(2,1)S(1)}, bf16[8,64,384]{2,1,0:T(8,128)(2,1)S(1)}, u32[]{:S(2)}, u32[]{:S(2)}) collective-permute-start(bf16[8,64,384]{2,1,0:T(8,128)(2,1)S(1)} %bitcast.190), channel_id=1, source_target_pairs={{0,32},{32,0},{64,96},{96,64},{128,160},{160,128},{192,224},{224,1... | collective-permute-start | bytes 1179656 | tf_op jit(solution)/shard_map/ppermute | solution.py:48
  58.2 4.2 %collective-permute-start.4 = (bf16[16,64,384]{2,1,0:T(8,128)(2,1)S(1)}, bf16[16,64,384]{2,1,0:T(8,128)(2,1)S(1)}, u32[]{:S(2)}, u32[]{:S(2)}) collective-permute-start(bf16[16,64,384]{2,1,0:T(8,128)(2,1)S(1)} %bitcast.183), channel_id=1, source_target_pairs={{0,16},{16,0},{1,17},{17,1},{2,18},{18,2},{3,19},{19,3},{4,20},{20... | collective-permute-start | bytes 2359304 | tf_op jit(solution)/shard_map/ppermute | solution.py:101
  64.9 4.4 %collective-permute-start.5 = (f32[1,128,128]{2,1,0:T(8,128)}, f32[1,128,128]{2,1,0:T(8,128)}, u32[]{:S(2)}, u32[]{:S(2)}) collective-permute-start(f32[1,128,128]{2,1,0:T(8,128)} %convolution_bitcast_fusion.1), channel_id=1, source_target_pairs={{0,16},{16,0},{1,17},{17,1},{2,18},{18,2},{3,19},{19,3},{4,20},{20... | collective-permute-start | bytes 196616 | tf_op jit(solution)/shard_map/ppermute | solution.py:21
  68.2 38.7 %copy-start.10 = (f32[128]{0:T(128)S(1)}, f32[128]{0:T(128)}, u32[]{:S(2)}) copy-start(f32[128]{0:T(128)} %param.11) | copy-start | bytes 1540
  70.1 17.0 %collective-permute-start.8 = (f32[1,128,128]{2,1,0:T(8,128)S(1)}, f32[1,128,128]{2,1,0:T(8,128)S(1)}, u32[]{:S(2)}, u32[]{:S(2)}) collective-permute-start(f32[1,128,128]{2,1,0:T(8,128)S(1)} %add.192), channel_id=1, source_target_pairs={{0,96},{32,128},{64,160},{96,192},{128,224},{160,256},{192,288},{2... | collective-permute-start | bytes 196616 | tf_op jit(solution)/shard_map/ppermute | solution.py:35
  76.6 10.6 %collective-permute-start.7 = (f32[1,128,128]{2,1,0:T(8,128)S(1)}, f32[1,128,128]{2,1,0:T(8,128)S(1)}, u32[]{:S(2)}, u32[]{:S(2)}) collective-permute-start(f32[1,128,128]{2,1,0:T(8,128)S(1)} %add.192), channel_id=1, source_target_pairs={{0,64},{32,96},{64,128},{96,160},{128,192},{160,224},{192,256},{22... | collective-permute-start | bytes 196616 | tf_op jit(solution)/shard_map/ppermute | solution.py:35
  81.8 6.0 %collective-permute-start.6 = (f32[1,128,128]{2,1,0:T(8,128)S(1)}, f32[1,128,128]{2,1,0:T(8,128)S(1)}, u32[]{:S(2)}, u32[]{:S(2)}) collective-permute-start(f32[1,128,128]{2,1,0:T(8,128)S(1)} %add.192), channel_id=1, source_target_pairs={{0,32},{32,64},{64,96},{96,128},{128,160},{160,192},{192,224},{224... | collective-permute-start | bytes 196616 | tf_op jit(solution)/shard_map/ppermute | solution.py:35
  87.9 20.3 %copy-start.5 = (pred[384,384]{1,0:T(32,128)(4,1)S(1)}, pred[384,384]{1,0:T(32,128)(4,1)}, u32[]{:S(2)}) copy-start(pred[384,384]{1,0:T(32,128)(4,1)} %fusion.5) | copy-start | bytes 442372
  87.9 18.4 %collective-permute-start.11 = (f32[1,128,128]{2,1,0:T(8,128)S(1)}, f32[1,128,128]{2,1,0:T(8,128)S(1)}, u32[]{:S(2)}, u32[]{:S(2)}) collective-permute-start(f32[1,128,128]{2,1,0:T(8,128)S(1)} %add_add_fusion.1), channel_id=1, source_target_pairs={{0,384},{32,416},{64,448},{96,480},{1,385},{33,417},{65,449},{97,4... | collective-permute-start | bytes 196616 | tf_op jit(solution)/shard_map/ppermute | solution.py:35
  96.2 10.1 %collective-permute-start.10 = (f32[1,128,128]{2,1,0:T(8,128)S(1)}, f32[1,128,128]{2,1,0:T(8,128)S(1)}, u32[]{:S(2)}, u32[]{:S(2)}) collective-permute-start(f32[1,128,128]{2,1,0:T(8,128)S(1)} %add_add_fusion.1), channel_id=1, source_target_pairs={{0,256},{32,288},{64,320},{96,352},{128,384},{160,416},{192,448},{... | collective-permute-start | bytes 196616 | tf_op jit(solution)/shard_map/ppermute | solution.py:35
  100.2 6.4 %collective-permute-start.9 = (f32[1,128,128]{2,1,0:T(8,128)S(1)}, f32[1,128,128]{2,1,0:T(8,128)S(1)}, u32[]{:S(2)}, u32[]{:S(2)}) collective-permute-start(f32[1,128,128]{2,1,0:T(8,128)S(1)} %add_add_fusion.1), channel_id=1, source_target_pairs={{0,128},{32,160},{64,192},{96,224},{128,256},{160,288},{192,320},{... | collective-permute-start | bytes 196616 | tf_op jit(solution)/shard_map/ppermute | solution.py:35
  108.5 3.1 %collective-permute-start.12 = (f32[1,128,128]{2,1,0:T(8,128)S(1)}, f32[1,128,128]{2,1,0:T(8,128)S(1)}, u32[]{:S(2)}, u32[]{:S(2)}) collective-permute-start(f32[1,128,128]{2,1,0:T(8,128)S(1)} %convolution_bitcast_fusion), channel_id=1, source_target_pairs={{0,16},{16,0},{1,17},{17,1},{2,18},{18,2},{3,19},{19,3},{4,20},{20... | collective-permute-start | bytes 196616 | tf_op jit(solution)/shard_map/ppermute | solution.py:21
  111.6 8.0 %collective-permute-start.15 = (f32[1,128,128]{2,1,0:T(8,128)S(1)}, f32[1,128,128]{2,1,0:T(8,128)S(1)}, u32[]{:S(2)}, u32[]{:S(2)}) collective-permute-start(f32[1,128,128]{2,1,0:T(8,128)S(1)} %add.205), channel_id=1, source_target_pairs={{96,0},{128,32},{160,64},{192,96},{224,128},{256,160},{288,192},{3... | collective-permute-start | bytes 196616 | tf_op jit(solution)/shard_map/ppermute | solution.py:35
  112.9 10.5 %collective-permute-start.14 = (f32[1,128,128]{2,1,0:T(8,128)S(1)}, f32[1,128,128]{2,1,0:T(8,128)S(1)}, u32[]{:S(2)}, u32[]{:S(2)}) collective-permute-start(f32[1,128,128]{2,1,0:T(8,128)S(1)} %add.205), channel_id=1, source_target_pairs={{64,0},{96,32},{128,64},{160,96},{192,128},{224,160},{256,192},{28... | collective-permute-start | bytes 196616 | tf_op jit(solution)/shard_map/ppermute | solution.py:35
  114.2 9.2 %collective-permute-start.13 = (f32[1,128,128]{2,1,0:T(8,128)S(1)}, f32[1,128,128]{2,1,0:T(8,128)S(1)}, u32[]{:S(2)}, u32[]{:S(2)}) collective-permute-start(f32[1,128,128]{2,1,0:T(8,128)S(1)} %add.205), channel_id=1, source_target_pairs={{32,0},{64,32},{96,64},{128,96},{160,128},{192,160},{224,192},{256... | collective-permute-start | bytes 196616 | tf_op jit(solution)/shard_map/ppermute | solution.py:35
  123.4 15.2 %collective-permute-start.18 = (f32[1,128,128]{2,1,0:T(8,128)S(1)}, f32[1,128,128]{2,1,0:T(8,128)S(1)}, u32[]{:S(2)}, u32[]{:S(2)}) collective-permute-start(f32[1,128,128]{2,1,0:T(8,128)S(1)} %add_add_fusion), channel_id=1, source_target_pairs={{384,0},{416,32},{448,64},{480,96},{385,1},{417,33},{449,65},{481,... | collective-permute-start | bytes 196616 | tf_op jit(solution)/shard_map/ppermute | solution.py:35
  124.7 16.3 %collective-permute-start.17 = (f32[1,128,128]{2,1,0:T(8,128)S(1)}, f32[1,128,128]{2,1,0:T(8,128)S(1)}, u32[]{:S(2)}, u32[]{:S(2)}) collective-permute-start(f32[1,128,128]{2,1,0:T(8,128)S(1)} %add_add_fusion), channel_id=1, source_target_pairs={{256,0},{288,32},{320,64},{352,96},{384,128},{416,160},{448,192},{... | collective-permute-start | bytes 196616 | tf_op jit(solution)/shard_map/ppermute | solution.py:35
  126.0 15.2 %collective-permute-start.16 = (f32[1,128,128]{2,1,0:T(8,128)S(1)}, f32[1,128,128]{2,1,0:T(8,128)S(1)}, u32[]{:S(2)}, u32[]{:S(2)}) collective-permute-start(f32[1,128,128]{2,1,0:T(8,128)S(1)} %add_add_fusion), channel_id=1, source_target_pairs={{128,0},{160,32},{192,64},{224,96},{256,128},{288,160},{320,192},{... | collective-permute-start | bytes 196616 | tf_op jit(solution)/shard_map/ppermute | solution.py:35
  151.4 9.6 %collective-permute-start.23 = (bf16[16,64,384]{2,1,0:T(8,128)(2,1)}, bf16[16,64,384]{2,1,0:T(8,128)(2,1)}, u32[]{:S(2)}, u32[]{:S(2)}) collective-permute-start(bf16[16,64,384]{2,1,0:T(8,128)(2,1)} %fusion.12), channel_id=1, source_target_pairs={{0,16},{16,0},{32,48},{48,32},{64,80},{80,64},{96,112},{112,96},{1... | collective-permute-start | bytes 2359304 | tf_op jit(solution)/shard_map/ppermute | solution.py:68
  157.5 22.1 %collective-permute-start.19 = (bf16[8,128,384]{2,1,0:T(8,128)(2,1)}, bf16[8,128,384]{2,1,0:T(8,128)(2,1)}, u32[]{:S(2)}, u32[]{:S(2)}) collective-permute-start(bf16[8,128,384]{2,1,0:T(8,128)(2,1)} %fusion.13), channel_id=1, source_target_pairs={{0,1},{1,0},{2,3},{3,2},{4,5},{5,4},{6,7},{7,6},{8,9},{9,8},{10,11... | collective-permute-start | bytes 2359304 | tf_op jit(solution)/shard_map/ppermute | solution.py:68
  161.0 18.7 %copy-start.2 = (f32[8,2,128,384]{3,2,1,0:T(8,128)S(1)}, f32[8,2,128,384]{3,2,1,0:T(8,128)}, u32[]{:S(2)}) copy-start(f32[8,2,128,384]{3,2,1,0:T(8,128)} %copy-done.1) | copy-start | bytes 9437188
  163.8 25.9 %collective-permute-start.24 = (bf16[8,64,384]{2,1,0:T(8,128)(2,1)}, bf16[8,64,384]{2,1,0:T(8,128)(2,1)S(1)}, u32[]{:S(2)}, u32[]{:S(2)}) collective-permute-start(bf16[8,64,384]{2,1,0:T(8,128)(2,1)} %fusion.16), channel_id=1, source_target_pairs={{0,32},{16,48},{32,0},{48,16},{64,96},{80,112},{96,64},{112,80},{1... | collective-permute-start | bytes 1179656 | tf_op jit(solution)/shard_map/ppermute | solution.py:68
  183.0 14.6 %collective-permute-start.20 = (bf16[4,128,384]{2,1,0:T(8,128)(2,1)}, bf16[4,128,384]{2,1,0:T(8,128)(2,1)}, u32[]{:S(2)}, u32[]{:S(2)}) collective-permute-start(bf16[4,128,384]{2,1,0:T(8,128)(2,1)} %fusion.15), channel_id=1, source_target_pairs={{0,2},{1,3},{2,0},{3,1},{4,6},{5,7},{6,4},{7,5},{8,10},{9,11},{10,... | collective-permute-start | bytes 1179656 | tf_op jit(solution)/shard_map/ppermute | solution.py:68
  189.8 12.1 %collective-permute-start.25 = (bf16[4,64,384]{2,1,0:T(8,128)(2,1)S(1)}, bf16[4,64,384]{2,1,0:T(8,128)(2,1)S(1)}, u32[]{:S(2)}, u32[]{:S(2)}) collective-permute-start(bf16[4,64,384]{2,1,0:T(8,128)(2,1)S(1)} %fusion.18), channel_id=1, source_target_pairs={{0,64},{16,80},{32,96},{48,112},{64,0},{80,16},{96,32},{112,48},{1... | collective-permute-start | bytes 589832 | tf_op jit(solution)/shard_map/ppermute | solution.py:68
  198.7 15.6 %collective-permute-start.21 = (bf16[2,128,384]{2,1,0:T(8,128)(2,1)S(1)}, bf16[2,128,384]{2,1,0:T(8,128)(2,1)S(1)}, u32[]{:S(2)}, u32[]{:S(2)}) collective-permute-start(bf16[2,128,384]{2,1,0:T(8,128)(2,1)S(1)} %fusion.17), channel_id=1, source_target_pairs={{0,4},{1,5},{2,6},{3,7},{4,0},{5,1},{6,2},{7,3},{8,12},{9,13},{10,... | collective-permute-start | bytes 589832 | tf_op jit(solution)/shard_map/ppermute | solution.py:68
  202.0 19.1 %collective-permute-start.26 = (bf16[2,64,384]{2,1,0:T(8,128)(2,1)S(1)}, bf16[2,64,384]{2,1,0:T(8,128)(2,1)S(1)}, u32[]{:S(2)}, u32[]{:S(2)}) collective-permute-start(bf16[2,64,384]{2,1,0:T(8,128)(2,1)S(1)} %fusion.25), channel_id=1, source_target_pairs={{0,128},{16,144},{32,160},{48,176},{64,192},{80,208},{96,224},{112... | collective-permute-start | bytes 294920 | tf_op jit(solution)/shard_map/ppermute | solution.py:68
  214.4 17.5 %collective-permute-start.22 = (bf16[1,128,384]{2,1,0:T(8,128)(2,1)S(1)}, bf16[1,128,384]{2,1,0:T(8,128)(2,1)S(1)}, u32[]{:S(2)}, u32[]{:S(2)}) collective-permute-start(bf16[1,128,384]{2,1,0:T(8,128)(2,1)S(1)} %dynamic-slice_convert_fusion.4), channel_id=1, source_target_pairs={{0,8},{1,9},{2,10},{3,11},{4,12},{5,13},{6,14},{7,15},{8,0},{9,1},... | collective-permute-start | bytes 294920 | tf_op jit(solution)/shard_map/ppermute | solution.py:68
  221.2 14.7 %collective-permute-start.27 = (bf16[1,64,384]{2,1,0:T(8,128)(2,1)S(1)}, bf16[1,64,384]{2,1,0:T(8,128)(2,1)S(1)}, u32[]{:S(2)}, u32[]{:S(2)}) collective-permute-start(bf16[1,64,384]{2,1,0:T(8,128)(2,1)S(1)} %dynamic-slice_convert_fusion.5), channel_id=1, source_target_pairs={{0,256},{16,272},{32,288},{48,304},{64,320},{80,336},{96,352},{112... | collective-permute-start | bytes 147464 | tf_op jit(solution)/shard_map/ppermute | solution.py:68
  (8 other events, 22.9 us)

commit v7 on v6

--- a/solution.py
+++ b/solution.py
@@ -54,6 +54,66 @@
     return current
 
 
+def radices_for(count):
+    radices = []
+    while count % 4 == 0:
+        radices.append(4)
+        count //= 4
+    if count > 1:
+        radices.append(count)
+    return tuple(radices)
+
+
+def digit_pairs(count, stride, radix, offset):
+    pairs = []
+    for i in range(count):
+        digit = (i // stride) % radix
+        pairs.append((i, i + ((digit + offset) % radix - digit) * stride))
+    return pairs
+
+
+def exchange_gather(block, axis, radices):
+    count = math.prod(radices)
+    place = lax.axis_index(axis)
+    strides = [math.prod(radices[:k]) for k in range(len(radices))]
+    current = block[None]
+    for radix, stride in reversed(list(zip(radices, strides))):
+        digit = (place // stride) % radix
+        got = [current]
+        for offset in range(1, radix):
+            got.append(lax.ppermute(current, axis, digit_pairs(count, stride, radix, offset)))
+        blocks = []
+        for value in range(radix):
+            pick = got[0]
+            for offset in range(1, radix):
+                pick = jnp.where((digit - value) % radix == offset, got[offset], pick)
+            blocks.append(pick)
+        current = jnp.stack(blocks, axis=1).reshape((-1,) + block.shape)
+    return current
+
+
+def exchange_scatter(term, axis, radices):
+    count = math.prod(radices)
+    place = lax.axis_index(axis)
+    rows = term.shape[0] // count
+    cols = term.shape[1]
+    current = term.astype(jnp.float32).reshape(count, rows, cols)
+    stride = 1
+    for radix in radices:
+        digit = (place // stride) % radix
+        split = current.reshape(-1, radix, rows, cols)
+        total = lax.dynamic_index_in_dim(split, digit, 1, False)
+        for offset in range(1, radix):
+            away = lax.dynamic_index_in_dim(split, (digit + offset) % radix, 1, False)
+            moved = lax.ppermute(
+                away.astype(jnp.bfloat16), axis, digit_pairs(count, stride, radix, offset)
+            )
+            total = total + moved.astype(jnp.float32)
+        current = total
+        stride *= radix
+    return current.reshape(rows, cols)
+
+
 def halving_scatter(term, axis, count):
     place = lax.axis_index(axis)
     rows = term.shape[0] // count
@@ -96,16 +156,10 @@
     allowed = allowed_pairs(block_mask[0])
     seq_count = lax.axis_size("z") * lax.axis_size("core")
     fsdp_count = lax.axis_size("fsdp")
-    own_rows = jnp.concatenate([w_query, w_key, w_value], axis=1)
-    chip_rows = doubling_gather(own_rows, "z", lax.axis_size("z"))
-    other_rows = lax.ppermute(chip_rows, "core", [(0, 1), (1, 0)])
-    second_core = lax.axis_index("core") == 1
-    weight_cat = jnp.stack(
-        [
-            jnp.where(second_core, other_rows, chip_rows),
-            jnp.where(second_core, chip_rows, other_rows),
-        ],
-        axis=1,
+    seq_radices = (lax.axis_size("core"),) + radices_for(lax.axis_size("z"))
+    fsdp_radices = radices_for(fsdp_count)
+    weight_cat = exchange_gather(
+        jnp.concatenate([w_query, w_key, w_value], axis=1), SEQ, seq_radices
     ).reshape(-1, 3 * columns)
     projected = jnp.dot(tokens, weight_cat, preferred_element_type=jnp.float32)
     projected = projected.astype(jnp.bfloat16)
@@ -152,20 +206,20 @@
         [part.reshape(SEG, columns).astype(jnp.bfloat16) for part in (d_queries, d_keys, d_values)],
         axis=1,
     )
-    input_rows = halving_scatter(
+    input_rows = exchange_scatter(
         lax.dot_general(
             weight_cat, grad_cat, (((1,), (1,)), ((), ())), preferred_element_type=jnp.float32
         ).astype(jnp.bfloat16),
         "fsdp",
-        fsdp_count,
+        fsdp_radices,
     )
     grad_tokens = input_rows.T.astype(jnp.bfloat16)
-    weight_rows = halving_scatter(
+    weight_rows = exchange_scatter(
         lax.dot_general(
             tokens, grad_cat, (((0,), (0,)), ((), ())), preferred_element_type=jnp.float32
         ).astype(jnp.bfloat16),
         SEQ,
-        seq_count,
+        seq_radices,
     )
     weight_rows = (weight_rows * (1.0 / math.sqrt(SEG * seq_count))).astype(jnp.bfloat16)
     return (

time: 239 us -> 225 us (0.941)
  waiting for transfers between devices: 72.1 us -> 46.7 us
  starting transfers between devices: 126 us -> 139 us
    ppermute x14 -> x20, waiting for transfers between devices: 47.4 us -> 22.5 us  [the longest x7 19.3 us: exchange_gather(): lax.ppermute(current, axis, digit_pairs(count, stride, radix, offset))]
    ppermute x14 -> x20, starting transfers between devices: 81.9 us -> 99.3 us  [the longest x13 61.6 us: exchange_scatter(): lax.ppermute(away.astype(jnp.bfloat16), axis, digit_pairs(count, stride,...]
    ppermute x12, starting transfers between devices: 40.4 us -> 35.4 us  [entering(): parts.append(lax.ppermute(total, 'z', pairs))]
    convert_element_type x9 -> x4, local copies, waits for them, and re-layouts: 5.23 us -> 2.69 us  [exchange_scatter(): away.astype(jnp.bfloat16)]
    unnamed x27 -> x25, local copies, waits for them, and re-layouts: 7.39 us -> 5.92 us
  transfers between devices with their start and end apart: 28 -> 34, of which waited for: 18 -> 15; matrix products, arithmetic and copies ran while one was open for 7% -> 6% of each run, Pallas kernels for 0% -> 0%
where the time goes in v7:
time: 225 us; the launch traced here: 222 us
  starting transfers between devices  139 us (62%)
  waiting for transfers between devices  46.7 us (21%)
  local copies, waits for them, and re-layouts  15 us (7%)
  matrix products  10.4 us (5%)
  other arithmetic  9.32 us (4%)
    ppermute x13, starting transfers between devices, exchange_scatter(): lax.ppermute(away.astype(jnp.bfloat16), axis, digit_pairs(count, stride,...  61.6 us
    ppermute x7, starting transfers between devices, exchange_gather(): lax.ppermute(current, axis, digit_pairs(count, stride, radix, offset))  37.7 us
    ppermute x12, starting transfers between devices, entering(): parts.append(lax.ppermute(total, 'z', pairs))  35.4 us
    ppermute x12, waiting for transfers between devices, entering(): parts.append(lax.ppermute(total, 'z', pairs))  23.2 us
    ppermute x7, waiting for transfers between devices, exchange_gather(): lax.ppermute(current, axis, digit_pairs(count, stride, radix, offset))  19.3 us
    unnamed x25, local copies, waits for them, and re-layouts  5.92 us
  transfers between devices with their start and end apart: 34, of which 15 were waited for; matrix products, arithmetic and copies ran while one was open for 6% of the time, Pallas kernels for 0%

profile of v7, /device:TPU:6, one launch (start us, length us, event | category | flops | bytes accessed | tf_op | source)
XLA Modules:
  0.0 222.0 jit_solution(5375282381562393552)
XLA Ops:
  1.5 12.7 %collective-permute-start = (bf16[1,64,384]{2,1,0:T(8,128)(2,1)S(1)}, bf16[1,64,384]{2,1,0:T(8,128)(2,1)S(1)}, u32[]{:S(2)}, u32[]{:S(2)}) collective-permute-start(bf16[1,64,384]{2,1,0:T(8,128)(2,1)S(1)} %maximum_bitcast_fusion.1), channel_id=1, source_target_pairs={{0,384},{16,400},{32,416},{48,432},{64,448},{80,464},{96,480},{112... | collective-permute-start | bytes 147464 | tf_op jit(solution)/shard_map/ppermute | solution.py:84
  14.3 4.9 %collective-permute-start.1 = (bf16[1,64,384]{2,1,0:T(8,128)(2,1)S(1)}, bf16[1,64,384]{2,1,0:T(8,128)(2,1)S(1)}, u32[]{:S(2)}, u32[]{:S(2)}) collective-permute-start(bf16[1,64,384]{2,1,0:T(8,128)(2,1)S(1)} %maximum_bitcast_fusion.1), channel_id=1, source_target_pairs={{0,256},{16,272},{32,288},{48,304},{64,320},{80,336},{96,352},{112... | collective-permute-start | bytes 147464 | tf_op jit(solution)/shard_map/ppermute | solution.py:84
  19.2 7.8 %collective-permute-start.2 = (bf16[1,64,384]{2,1,0:T(8,128)(2,1)S(1)}, bf16[1,64,384]{2,1,0:T(8,128)(2,1)S(1)}, u32[]{:S(2)}, u32[]{:S(2)}) collective-permute-start(bf16[1,64,384]{2,1,0:T(8,128)(2,1)S(1)} %maximum_bitcast_fusion.1), channel_id=1, source_target_pairs={{0,128},{16,144},{32,160},{48,176},{64,192},{80,208},{96,224},{112... | collective-permute-start | bytes 147464 | tf_op jit(solution)/shard_map/ppermute | solution.py:84
  27.1 2.2 %collective-permute-done.1 = bf16[1,64,384]{2,1,0:T(8,128)(2,1)S(1)} collective-permute-done((bf16[1,64,384]{2,1,0:T(8,128)(2,1)S(1)}, bf16[1,64,384]{2,1,0:T(8,128)(2,1)S(1)}, u32[]{:S(2)}, u32[]{:S(2)}) %collective-permute-start.1) | collective-permute-done | bytes 49184 | tf_op jit(solution)/shard_map/ppermute | solution.py:84
  29.4 2.3 %collective-permute-done.2 = bf16[1,64,384]{2,1,0:T(8,128)(2,1)S(1)} collective-permute-done((bf16[1,64,384]{2,1,0:T(8,128)(2,1)S(1)}, bf16[1,64,384]{2,1,0:T(8,128)(2,1)S(1)}, u32[]{:S(2)}, u32[]{:S(2)}) %collective-permute-start.2) | collective-permute-done | bytes 49184 | tf_op jit(solution)/shard_map/ppermute | solution.py:84
  33.3 5.9 %collective-permute-start.3 = (bf16[4,64,384]{2,1,0:T(8,128)(2,1)S(1)}, bf16[4,64,384]{2,1,0:T(8,128)(2,1)S(1)}, u32[]{:S(2)}, u32[]{:S(2)}) collective-permute-start(bf16[4,64,384]{2,1,0:T(8,128)(2,1)S(1)} %maximum_bitcast_fusion), channel_id=1, source_target_pairs={{0,96},{16,112},{32,0},{48,16},{64,32},{80,48},{96,64},{112,80},{1... | collective-permute-start | bytes 589832 | tf_op jit(solution)/shard_map/ppermute | solution.py:84
  41.2 2.5 %collective-permute-start.5 = (bf16[4,64,384]{2,1,0:T(8,128)(2,1)S(1)}, bf16[4,64,384]{2,1,0:T(8,128)(2,1)S(1)}, u32[]{:S(2)}, u32[]{:S(2)}) collective-permute-start(bf16[4,64,384]{2,1,0:T(8,128)(2,1)S(1)} %maximum_bitcast_fusion), channel_id=1, source_target_pairs={{0,32},{16,48},{32,64},{48,80},{64,96},{80,112},{96,0},{112,16},{1... | collective-permute-start | bytes 589832 | tf_op jit(solution)/shard_map/ppermute | solution.py:84
  44.6 12.1 %collective-permute-done.4 = bf16[4,64,384]{2,1,0:T(8,128)(2,1)S(1)} collective-permute-done((bf16[4,64,384]{2,1,0:T(8,128)(2,1)S(1)}, bf16[4,64,384]{2,1,0:T(8,128)(2,1)S(1)}, u32[]{:S(2)}, u32[]{:S(2)}) %collective-permute-start.4) | collective-permute-done | bytes 196640 | tf_op jit(solution)/shard_map/ppermute | solution.py:84
  63.6 2.0 collective-permute-start.7
  70.7 4.3 %collective-permute-start.9 = (f32[1,128,128]{2,1,0:T(8,128)S(1)}, f32[1,128,128]{2,1,0:T(8,128)S(1)}, u32[]{:S(2)}, u32[]{:S(2)}) collective-permute-start(f32[1,128,128]{2,1,0:T(8,128)S(1)} %add.361), channel_id=1, source_target_pairs={{0,64},{32,96},{64,128},{96,160},{128,192},{160,224},{192,256},{22... | collective-permute-start | bytes 196616 | tf_op jit(solution)/shard_map/ppermute | solution.py:35
  75.0 3.4 %collective-permute-start.8 = (f32[1,128,128]{2,1,0:T(8,128)S(1)}, f32[1,128,128]{2,1,0:T(8,128)S(1)}, u32[]{:S(2)}, u32[]{:S(2)}) collective-permute-start(f32[1,128,128]{2,1,0:T(8,128)S(1)} %add.361), channel_id=1, source_target_pairs={{0,32},{32,64},{64,96},{96,128},{128,160},{160,192},{192,224},{224... | collective-permute-start | bytes 196616 | tf_op jit(solution)/shard_map/ppermute | solution.py:35
  80.3 9.5 %collective-permute-start.13 = (f32[1,128,128]{2,1,0:T(8,128)S(1)}, f32[1,128,128]{2,1,0:T(8,128)S(1)}, u32[]{:S(2)}, u32[]{:S(2)}) collective-permute-start(f32[1,128,128]{2,1,0:T(8,128)S(1)} %add_add_fusion.1), channel_id=1, source_target_pairs={{0,384},{32,416},{64,448},{96,480},{1,385},{33,417},{65,449},{97,4... | collective-permute-start | bytes 196616 | tf_op jit(solution)/shard_map/ppermute | solution.py:35
  89.8 3.2 %collective-permute-start.12 = (f32[1,128,128]{2,1,0:T(8,128)S(1)}, f32[1,128,128]{2,1,0:T(8,128)S(1)}, u32[]{:S(2)}, u32[]{:S(2)}) collective-permute-start(f32[1,128,128]{2,1,0:T(8,128)S(1)} %add_add_fusion.1), channel_id=1, source_target_pairs={{0,256},{32,288},{64,320},{96,352},{128,384},{160,416},{192,448},{... | collective-permute-start | bytes 196616 | tf_op jit(solution)/shard_map/ppermute | solution.py:35
  93.1 5.4 %collective-permute-start.11 = (f32[1,128,128]{2,1,0:T(8,128)S(1)}, f32[1,128,128]{2,1,0:T(8,128)S(1)}, u32[]{:S(2)}, u32[]{:S(2)}) collective-permute-start(f32[1,128,128]{2,1,0:T(8,128)S(1)} %add_add_fusion.1), channel_id=1, source_target_pairs={{0,128},{32,160},{64,192},{96,224},{128,256},{160,288},{192,320},{... | collective-permute-start | bytes 196616 | tf_op jit(solution)/shard_map/ppermute | solution.py:35
  109.5 3.9 %collective-permute-done.17 = f32[1,128,128]{2,1,0:T(8,128)S(1)} collective-permute-done((f32[1,128,128]{2,1,0:T(8,128)S(1)}, f32[1,128,128]{2,1,0:T(8,128)S(1)}, u32[]{:S(2)}, u32[]{:S(2)}) %collective-permute-start.17) | collective-permute-done | bytes 65568 | tf_op jit(solution)/shard_map/ppermute | solution.py:35
  113.4 3.6 %collective-permute-done.16 = f32[1,128,128]{2,1,0:T(8,128)S(1)} collective-permute-done((f32[1,128,128]{2,1,0:T(8,128)S(1)}, f32[1,128,128]{2,1,0:T(8,128)S(1)}, u32[]{:S(2)}, u32[]{:S(2)}) %collective-permute-start.16) | collective-permute-done | bytes 65568 | tf_op jit(solution)/shard_map/ppermute | solution.py:35
  121.1 11.3 %collective-permute-done.20 = f32[1,128,128]{2,1,0:T(8,128)S(1)} collective-permute-done((f32[1,128,128]{2,1,0:T(8,128)S(1)}, f32[1,128,128]{2,1,0:T(8,128)S(1)}, u32[]{:S(2)}, u32[]{:S(2)}) %collective-permute-start.20) | collective-permute-done | bytes 65568 | tf_op jit(solution)/shard_map/ppermute | solution.py:35
  132.4 2.0 collective-permute-done.19
  135.9 2.7 %convert_bitcast_fusion = f32[2048,384]{0,1:T(8,128)} fusion(bf16[384,2048]{1,0:T(8,128)(2,1)S(1)} %copy-done, bf16[384,128]{0,1:T(8,128)(2,1)S(1)} %fusion.9, bf16[384,128]{0,1:T(8,128)(2,1)S(1)} %fusion.10, bf16[384,128]{0,1:T(8,128)(2,1)S(1)} %fusion.11), kind=kOutput, calls=%fused_computation | convolution fusion | flops 606437376 | bytes 5013504 | tf_op jit(solution)/shard_map/dot_general | solution.py:218
  138.6 3.5 %copy.27 = f32[2048,384]{1,0:T(8,128)} copy(f32[2048,384]{0,1:T(8,128)} %convert_bitcast_fusion) | data formatting | bytes 6291456 | tf_op jit(solution)/shard_map/reshape;reshape | solution.py:104
  142.1 2.5 %fusion.12 = bf16[16,64,384]{2,1,0:T(8,128)(2,1)} fusion(f32[16,2,64,384]{3,2,1,0:T(8,128)} %bitcast.178, s32[]{:T(128)S(6)} %select_n.524), kind=kLoop, calls=%fused_computation.28 | loop fusion | bytes 1572868 | tf_op jit(solution)/shard_map/convert_element_type | solution.py:109
  153.7 4.9 %collective-permute-start.23 = (bf16[4,128,384]{1,2,0:T(8,128)(2,1)}, bf16[4,128,384]{1,2,0:T(8,128)(2,1)}, u32[]{:S(2)}, u32[]{:S(2)}) collective-permute-start(bf16[4,128,384]{1,2,0:T(8,128)(2,1)} %bitcast.187), channel_id=1, source_target_pairs={{0,3},{1,0},{2,1},{3,2},{4,7},{5,4},{6,5},{7,6},{8,11},{9,8},{10,9... | collective-permute-start | bytes 1179656 | tf_op jit(solution)/shard_map/ppermute | solution.py:108
  158.9 2.5 %collective-permute-start.22 = (bf16[4,128,384]{1,2,0:T(8,128)(2,1)S(1)}, bf16[4,128,384]{1,2,0:T(8,128)(2,1)}, u32[]{:S(2)}, u32[]{:S(2)}) collective-permute-start(bf16[4,128,384]{1,2,0:T(8,128)(2,1)S(1)} %bitcast.186), channel_id=1, source_target_pairs={{0,2},{1,3},{2,0},{3,1},{4,6},{5,7},{6,4},{7,5},{8,10},{9,11},{10,... | collective-permute-start | bytes 1179656 | tf_op jit(solution)/shard_map/ppermute | solution.py:108
  161.7 2.9 %collective-permute-start.21 = (bf16[4,128,384]{1,2,0:T(8,128)(2,1)S(1)}, bf16[4,128,384]{1,2,0:T(8,128)(2,1)S(1)}, u32[]{:S(2)}, u32[]{:S(2)}) collective-permute-start(bf16[4,128,384]{1,2,0:T(8,128)(2,1)S(1)} %bitcast.188), channel_id=1, source_target_pairs={{0,1},{1,2},{2,3},{3,0},{4,5},{5,6},{6,7},{7,4},{8,9},{9,10},{10,1... | collective-permute-start | bytes 1179656 | tf_op jit(solution)/shard_map/ppermute | solution.py:108
  166.5 12.9 %collective-permute-start.30 = (bf16[4,64,384]{2,1,0:T(8,128)(2,1)S(1)}, bf16[4,64,384]{2,1,0:T(8,128)(2,1)S(1)}, u32[]{:S(2)}, u32[]{:S(2)}) collective-permute-start(bf16[4,64,384]{2,1,0:T(8,128)(2,1)S(1)} %get-tuple-element.19), channel_id=1, source_target_pairs={{0,96},{16,112},{32,0},{48,16},{64,32},{80,48},{96,64},{112,80},{1... | collective-permute-start | bytes 589832 | tf_op jit(solution)/shard_map/ppermute | solution.py:108
  181.3 2.5 %collective-permute-start.28 = (bf16[4,64,384]{2,1,0:T(8,128)(2,1)S(1)}, bf16[4,64,384]{2,1,0:T(8,128)(2,1)S(1)}, u32[]{:S(2)}, u32[]{:S(2)}) collective-permute-start(bf16[4,64,384]{2,1,0:T(8,128)(2,1)S(1)} %get-tuple-element.18), channel_id=1, source_target_pairs={{0,32},{16,48},{32,64},{48,80},{64,96},{80,112},{96,0},{112,16},{1... | collective-permute-start | bytes 589832 | tf_op jit(solution)/shard_map/ppermute | solution.py:108
  185.2 2.8 %collective-permute-start.26 = (bf16[1,128,384]{1,2,0:T(8,128)(2,1)S(1)}, bf16[1,128,384]{1,2,0:T(8,128)(2,1)S(1)}, u32[]{:S(2)}, u32[]{:S(2)}) collective-permute-start(bf16[1,128,384]{1,2,0:T(8,128)(2,1)S(1)} %get-tuple-element.24), channel_id=1, source_target_pairs={{0,12},{1,13},{2,14},{3,15},{4,0},{5,1},{6,2},{7,3},{8,4},{9,5},{1... | collective-permute-start | bytes 294920 | tf_op jit(solution)/shard_map/ppermute | solution.py:108
  187.9 3.0 %collective-permute-start.25 = (bf16[1,128,384]{1,2,0:T(8,128)(2,1)S(1)}, bf16[1,128,384]{1,2,0:T(8,128)(2,1)S(1)}, u32[]{:S(2)}, u32[]{:S(2)}) collective-permute-start(bf16[1,128,384]{1,2,0:T(8,128)(2,1)S(1)} %get-tuple-element.25), channel_id=1, source_target_pairs={{0,8},{1,9},{2,10},{3,11},{4,12},{5,13},{6,14},{7,15},{8,0},{9,1},... | collective-permute-start | bytes 294920 | tf_op jit(solution)/shard_map/ppermute | solution.py:108
  191.0 4.0 %collective-permute-start.24 = (bf16[1,128,384]{1,2,0:T(8,128)(2,1)S(1)}, bf16[1,128,384]{1,2,0:T(8,128)(2,1)S(1)}, u32[]{:S(2)}, u32[]{:S(2)}) collective-permute-start(bf16[1,128,384]{1,2,0:T(8,128)(2,1)S(1)} %get-tuple-element.23), channel_id=1, source_target_pairs={{0,4},{1,5},{2,6},{3,7},{4,8},{5,9},{6,10},{7,11},{8,12},{9,13},{1... | collective-permute-start | bytes 294920 | tf_op jit(solution)/shard_map/ppermute | solution.py:108
  196.4 6.7 %collective-permute-start.33 = (bf16[1,64,384]{2,1,0:T(8,128)(2,1)S(1)}, bf16[1,64,384]{2,1,0:T(8,128)(2,1)S(1)}, u32[]{:S(2)}, u32[]{:S(2)}) collective-permute-start(bf16[1,64,384]{2,1,0:T(8,128)(2,1)S(1)} %get-tuple-element.31), channel_id=1, source_target_pairs={{0,384},{16,400},{32,416},{48,432},{64,448},{80,464},{96,480},{112... | collective-permute-start | bytes 147464 | tf_op jit(solution)/shard_map/ppermute | solution.py:108
  203.1 7.8 %collective-permute-start.32 = (bf16[1,64,384]{2,1,0:T(8,128)(2,1)S(1)}, bf16[1,64,384]{2,1,0:T(8,128)(2,1)S(1)}, u32[]{:S(2)}, u32[]{:S(2)}) collective-permute-start(bf16[1,64,384]{2,1,0:T(8,128)(2,1)S(1)} %get-tuple-element.32), channel_id=1, source_target_pairs={{0,256},{16,272},{32,288},{48,304},{64,320},{80,336},{96,352},{112... | collective-permute-start | bytes 147464 | tf_op jit(solution)/shard_map/ppermute | solution.py:108
  210.9 7.8 %collective-permute-start.31 = (bf16[1,64,384]{2,1,0:T(8,128)(2,1)S(1)}, bf16[1,64,384]{2,1,0:T(8,128)(2,1)S(1)}, u32[]{:S(2)}, u32[]{:S(2)}) collective-permute-start(bf16[1,64,384]{2,1,0:T(8,128)(2,1)S(1)} %get-tuple-element.30), channel_id=1, source_target_pairs={{0,128},{16,144},{32,160},{48,176},{64,192},{80,208},{96,224},{112... | collective-permute-start | bytes 147464 | tf_op jit(solution)/shard_map/ppermute | solution.py:108
  (115 shorter events, 54.5 us)
Async XLA Ops:
  1.5 25.6 %collective-permute-start = (bf16[1,64,384]{2,1,0:T(8,128)(2,1)S(1)}, bf16[1,64,384]{2,1,0:T(8,128)(2,1)S(1)}, u32[]{:S(2)}, u32[]{:S(2)}) collective-permute-start(bf16[1,64,384]{2,1,0:T(8,128)(2,1)S(1)} %maximum_bitcast_fusion.1), channel_id=1, source_target_pairs={{0,384},{16,400},{32,416},{48,432},{64,448},{80,464},{96,480},{112... | collective-permute-start | bytes 147464 | tf_op jit(solution)/shard_map/ppermute | solution.py:84
  14.3 15.1 %collective-permute-start.1 = (bf16[1,64,384]{2,1,0:T(8,128)(2,1)S(1)}, bf16[1,64,384]{2,1,0:T(8,128)(2,1)S(1)}, u32[]{:S(2)}, u32[]{:S(2)}) collective-permute-start(bf16[1,64,384]{2,1,0:T(8,128)(2,1)S(1)} %maximum_bitcast_fusion.1), channel_id=1, source_target_pairs={{0,256},{16,272},{32,288},{48,304},{64,320},{80,336},{96,352},{112... | collective-permute-start | bytes 147464 | tf_op jit(solution)/shard_map/ppermute | solution.py:84
  19.2 12.5 %collective-permute-start.2 = (bf16[1,64,384]{2,1,0:T(8,128)(2,1)S(1)}, bf16[1,64,384]{2,1,0:T(8,128)(2,1)S(1)}, u32[]{:S(2)}, u32[]{:S(2)}) collective-permute-start(bf16[1,64,384]{2,1,0:T(8,128)(2,1)S(1)} %maximum_bitcast_fusion.1), channel_id=1, source_target_pairs={{0,128},{16,144},{32,160},{48,176},{64,192},{80,208},{96,224},{112... | collective-permute-start | bytes 147464 | tf_op jit(solution)/shard_map/ppermute | solution.py:84
  33.3 11.3 %collective-permute-start.3 = (bf16[4,64,384]{2,1,0:T(8,128)(2,1)S(1)}, bf16[4,64,384]{2,1,0:T(8,128)(2,1)S(1)}, u32[]{:S(2)}, u32[]{:S(2)}) collective-permute-start(bf16[4,64,384]{2,1,0:T(8,128)(2,1)S(1)} %maximum_bitcast_fusion), channel_id=1, source_target_pairs={{0,96},{16,112},{32,0},{48,16},{64,32},{80,48},{96,64},{112,80},{1... | collective-permute-start | bytes 589832 | tf_op jit(solution)/shard_map/ppermute | solution.py:84
  39.3 17.4 %collective-permute-start.4 = (bf16[4,64,384]{2,1,0:T(8,128)(2,1)S(1)}, bf16[4,64,384]{2,1,0:T(8,128)(2,1)S(1)}, u32[]{:S(2)}, u32[]{:S(2)}) collective-permute-start(bf16[4,64,384]{2,1,0:T(8,128)(2,1)S(1)} %maximum_bitcast_fusion), channel_id=1, source_target_pairs={{0,64},{16,80},{32,96},{48,112},{64,0},{80,16},{96,32},{112,48},{1... | collective-permute-start | bytes 589832 | tf_op jit(solution)/shard_map/ppermute | solution.py:84
  41.2 15.5 %collective-permute-start.5 = (bf16[4,64,384]{2,1,0:T(8,128)(2,1)S(1)}, bf16[4,64,384]{2,1,0:T(8,128)(2,1)S(1)}, u32[]{:S(2)}, u32[]{:S(2)}) collective-permute-start(bf16[4,64,384]{2,1,0:T(8,128)(2,1)S(1)} %maximum_bitcast_fusion), channel_id=1, source_target_pairs={{0,32},{16,48},{32,64},{48,80},{64,96},{80,112},{96,0},{112,16},{1... | collective-permute-start | bytes 589832 | tf_op jit(solution)/shard_map/ppermute | solution.py:84
  63.6 4.3 %collective-permute-start.7 = (f32[1,128,128]{2,1,0:T(8,128)}, f32[1,128,128]{2,1,0:T(8,128)}, u32[]{:S(2)}, u32[]{:S(2)}) collective-permute-start(f32[1,128,128]{2,1,0:T(8,128)} %convolution_bitcast_fusion.1), channel_id=1, source_target_pairs={{0,16},{16,0},{1,17},{17,1},{2,18},{18,2},{3,19},{19,3},{4,20},{20... | collective-permute-start | bytes 196616 | tf_op jit(solution)/shard_map/ppermute | solution.py:21
  68.8 10.8 %collective-permute-start.10 = (f32[1,128,128]{2,1,0:T(8,128)S(1)}, f32[1,128,128]{2,1,0:T(8,128)S(1)}, u32[]{:S(2)}, u32[]{:S(2)}) collective-permute-start(f32[1,128,128]{2,1,0:T(8,128)S(1)} %add.361), channel_id=1, source_target_pairs={{0,96},{32,128},{64,160},{96,192},{128,224},{160,256},{192,288},{2... | collective-permute-start | bytes 196616 | tf_op jit(solution)/shard_map/ppermute | solution.py:35
  70.7 8.8 %collective-permute-start.9 = (f32[1,128,128]{2,1,0:T(8,128)S(1)}, f32[1,128,128]{2,1,0:T(8,128)S(1)}, u32[]{:S(2)}, u32[]{:S(2)}) collective-permute-start(f32[1,128,128]{2,1,0:T(8,128)S(1)} %add.361), channel_id=1, source_target_pairs={{0,64},{32,96},{64,128},{96,160},{128,192},{160,224},{192,256},{22... | collective-permute-start | bytes 196616 | tf_op jit(solution)/shard_map/ppermute | solution.py:35
  75.0 5.3 %collective-permute-start.8 = (f32[1,128,128]{2,1,0:T(8,128)S(1)}, f32[1,128,128]{2,1,0:T(8,128)S(1)}, u32[]{:S(2)}, u32[]{:S(2)}) collective-permute-start(f32[1,128,128]{2,1,0:T(8,128)S(1)} %add.361), channel_id=1, source_target_pairs={{0,32},{32,64},{64,96},{96,128},{128,160},{160,192},{192,224},{224... | collective-permute-start | bytes 196616 | tf_op jit(solution)/shard_map/ppermute | solution.py:35
  80.3 18.5 %collective-permute-start.13 = (f32[1,128,128]{2,1,0:T(8,128)S(1)}, f32[1,128,128]{2,1,0:T(8,128)S(1)}, u32[]{:S(2)}, u32[]{:S(2)}) collective-permute-start(f32[1,128,128]{2,1,0:T(8,128)S(1)} %add_add_fusion.1), channel_id=1, source_target_pairs={{0,384},{32,416},{64,448},{96,480},{1,385},{33,417},{65,449},{97,4... | collective-permute-start | bytes 196616 | tf_op jit(solution)/shard_map/ppermute | solution.py:35
  89.8 9.0 %collective-permute-start.12 = (f32[1,128,128]{2,1,0:T(8,128)S(1)}, f32[1,128,128]{2,1,0:T(8,128)S(1)}, u32[]{:S(2)}, u32[]{:S(2)}) collective-permute-start(f32[1,128,128]{2,1,0:T(8,128)S(1)} %add_add_fusion.1), channel_id=1, source_target_pairs={{0,256},{32,288},{64,320},{96,352},{128,384},{160,416},{192,448},{... | collective-permute-start | bytes 196616 | tf_op jit(solution)/shard_map/ppermute | solution.py:35
  93.1 7.2 %collective-permute-start.11 = (f32[1,128,128]{2,1,0:T(8,128)S(1)}, f32[1,128,128]{2,1,0:T(8,128)S(1)}, u32[]{:S(2)}, u32[]{:S(2)}) collective-permute-start(f32[1,128,128]{2,1,0:T(8,128)S(1)} %add_add_fusion.1), channel_id=1, source_target_pairs={{0,128},{32,160},{64,192},{96,224},{128,256},{160,288},{192,320},{... | collective-permute-start | bytes 196616 | tf_op jit(solution)/shard_map/ppermute | solution.py:35
  105.3 8.1 %collective-permute-start.17 = (f32[1,128,128]{2,1,0:T(8,128)S(1)}, f32[1,128,128]{2,1,0:T(8,128)S(1)}, u32[]{:S(2)}, u32[]{:S(2)}) collective-permute-start(f32[1,128,128]{2,1,0:T(8,128)S(1)} %add.374), channel_id=1, source_target_pairs={{96,0},{128,32},{160,64},{192,96},{224,128},{256,160},{288,192},{3... | collective-permute-start | bytes 196616 | tf_op jit(solution)/shard_map/ppermute | solution.py:35
  106.6 10.4 %collective-permute-start.16 = (f32[1,128,128]{2,1,0:T(8,128)S(1)}, f32[1,128,128]{2,1,0:T(8,128)S(1)}, u32[]{:S(2)}, u32[]{:S(2)}) collective-permute-start(f32[1,128,128]{2,1,0:T(8,128)S(1)} %add.374), channel_id=1, source_target_pairs={{64,0},{96,32},{128,64},{160,96},{192,128},{224,160},{256,192},{28... | collective-permute-start | bytes 196616 | tf_op jit(solution)/shard_map/ppermute | solution.py:35
  107.9 9.1 %collective-permute-start.15 = (f32[1,128,128]{2,1,0:T(8,128)S(1)}, f32[1,128,128]{2,1,0:T(8,128)S(1)}, u32[]{:S(2)}, u32[]{:S(2)}) collective-permute-start(f32[1,128,128]{2,1,0:T(8,128)S(1)} %add.374), channel_id=1, source_target_pairs={{32,0},{64,32},{96,64},{128,96},{160,128},{192,160},{224,192},{256... | collective-permute-start | bytes 196616 | tf_op jit(solution)/shard_map/ppermute | solution.py:35
  117.1 15.4 %collective-permute-start.20 = (f32[1,128,128]{2,1,0:T(8,128)S(1)}, f32[1,128,128]{2,1,0:T(8,128)S(1)}, u32[]{:S(2)}, u32[]{:S(2)}) collective-permute-start(f32[1,128,128]{2,1,0:T(8,128)S(1)} %add_add_fusion), channel_id=1, source_target_pairs={{384,0},{416,32},{448,64},{480,96},{385,1},{417,33},{449,65},{481,... | collective-permute-start | bytes 196616 | tf_op jit(solution)/shard_map/ppermute | solution.py:35
  118.4 16.0 %collective-permute-start.19 = (f32[1,128,128]{2,1,0:T(8,128)S(1)}, f32[1,128,128]{2,1,0:T(8,128)S(1)}, u32[]{:S(2)}, u32[]{:S(2)}) collective-permute-start(f32[1,128,128]{2,1,0:T(8,128)S(1)} %add_add_fusion), channel_id=1, source_target_pairs={{256,0},{288,32},{320,64},{352,96},{384,128},{416,160},{448,192},{... | collective-permute-start | bytes 196616 | tf_op jit(solution)/shard_map/ppermute | solution.py:35
  119.7 14.8 %collective-permute-start.18 = (f32[1,128,128]{2,1,0:T(8,128)S(1)}, f32[1,128,128]{2,1,0:T(8,128)S(1)}, u32[]{:S(2)}, u32[]{:S(2)}) collective-permute-start(f32[1,128,128]{2,1,0:T(8,128)S(1)} %add_add_fusion), channel_id=1, source_target_pairs={{128,0},{160,32},{192,64},{224,96},{256,128},{288,160},{320,192},{... | collective-permute-start | bytes 196616 | tf_op jit(solution)/shard_map/ppermute | solution.py:35
  144.6 19.9 %collective-permute-start.27 = (bf16[16,64,384]{2,1,0:T(8,128)(2,1)}, bf16[16,64,384]{2,1,0:T(8,128)(2,1)}, u32[]{:S(2)}, u32[]{:S(2)}) collective-permute-start(bf16[16,64,384]{2,1,0:T(8,128)(2,1)} %fusion.12), channel_id=1, source_target_pairs={{0,16},{16,0},{32,48},{48,32},{64,80},{80,64},{96,112},{112,96},{1... | collective-permute-start | bytes 2359304 | tf_op jit(solution)/shard_map/ppermute | solution.py:108
  153.7 27.6 %collective-permute-start.23 = (bf16[4,128,384]{1,2,0:T(8,128)(2,1)}, bf16[4,128,384]{1,2,0:T(8,128)(2,1)}, u32[]{:S(2)}, u32[]{:S(2)}) collective-permute-start(bf16[4,128,384]{1,2,0:T(8,128)(2,1)} %bitcast.187), channel_id=1, source_target_pairs={{0,3},{1,0},{2,1},{3,2},{4,7},{5,4},{6,5},{7,6},{8,11},{9,8},{10,9... | collective-permute-start | bytes 1179656 | tf_op jit(solution)/shard_map/ppermute | solution.py:108
  158.9 24.9 %collective-permute-start.22 = (bf16[4,128,384]{1,2,0:T(8,128)(2,1)S(1)}, bf16[4,128,384]{1,2,0:T(8,128)(2,1)}, u32[]{:S(2)}, u32[]{:S(2)}) collective-permute-start(bf16[4,128,384]{1,2,0:T(8,128)(2,1)S(1)} %bitcast.186), channel_id=1, source_target_pairs={{0,2},{1,3},{2,0},{3,1},{4,6},{5,7},{6,4},{7,5},{8,10},{9,11},{10,... | collective-permute-start | bytes 1179656 | tf_op jit(solution)/shard_map/ppermute | solution.py:108
  161.7 22.2 %collective-permute-start.21 = (bf16[4,128,384]{1,2,0:T(8,128)(2,1)S(1)}, bf16[4,128,384]{1,2,0:T(8,128)(2,1)S(1)}, u32[]{:S(2)}, u32[]{:S(2)}) collective-permute-start(bf16[4,128,384]{1,2,0:T(8,128)(2,1)S(1)} %bitcast.188), channel_id=1, source_target_pairs={{0,1},{1,2},{2,3},{3,0},{4,5},{5,6},{6,7},{7,4},{8,9},{9,10},{10,1... | collective-permute-start | bytes 1179656 | tf_op jit(solution)/shard_map/ppermute | solution.py:108
  166.5 24.5 %collective-permute-start.30 = (bf16[4,64,384]{2,1,0:T(8,128)(2,1)S(1)}, bf16[4,64,384]{2,1,0:T(8,128)(2,1)S(1)}, u32[]{:S(2)}, u32[]{:S(2)}) collective-permute-start(bf16[4,64,384]{2,1,0:T(8,128)(2,1)S(1)} %get-tuple-element.19), channel_id=1, source_target_pairs={{0,96},{16,112},{32,0},{48,16},{64,32},{80,48},{96,64},{112,80},{1... | collective-permute-start | bytes 589832 | tf_op jit(solution)/shard_map/ppermute | solution.py:108
  179.4 16.9 %collective-permute-start.29 = (bf16[4,64,384]{2,1,0:T(8,128)(2,1)S(1)}, bf16[4,64,384]{2,1,0:T(8,128)(2,1)S(1)}, u32[]{:S(2)}, u32[]{:S(2)}) collective-permute-start(bf16[4,64,384]{2,1,0:T(8,128)(2,1)S(1)} %get-tuple-element.20), channel_id=1, source_target_pairs={{0,64},{16,80},{32,96},{48,112},{64,0},{80,16},{96,32},{112,48},{1... | collective-permute-start | bytes 589832 | tf_op jit(solution)/shard_map/ppermute | solution.py:108
  181.3 14.9 %collective-permute-start.28 = (bf16[4,64,384]{2,1,0:T(8,128)(2,1)S(1)}, bf16[4,64,384]{2,1,0:T(8,128)(2,1)S(1)}, u32[]{:S(2)}, u32[]{:S(2)}) collective-permute-start(bf16[4,64,384]{2,1,0:T(8,128)(2,1)S(1)} %get-tuple-element.18), channel_id=1, source_target_pairs={{0,32},{16,48},{32,64},{48,80},{64,96},{80,112},{96,0},{112,16},{1... | collective-permute-start | bytes 589832 | tf_op jit(solution)/shard_map/ppermute | solution.py:108
  185.2 25.7 %collective-permute-start.26 = (bf16[1,128,384]{1,2,0:T(8,128)(2,1)S(1)}, bf16[1,128,384]{1,2,0:T(8,128)(2,1)S(1)}, u32[]{:S(2)}, u32[]{:S(2)}) collective-permute-start(bf16[1,128,384]{1,2,0:T(8,128)(2,1)S(1)} %get-tuple-element.24), channel_id=1, source_target_pairs={{0,12},{1,13},{2,14},{3,15},{4,0},{5,1},{6,2},{7,3},{8,4},{9,5},{1... | collective-permute-start | bytes 294920 | tf_op jit(solution)/shard_map/ppermute | solution.py:108
  187.9 30.8 %collective-permute-start.25 = (bf16[1,128,384]{1,2,0:T(8,128)(2,1)S(1)}, bf16[1,128,384]{1,2,0:T(8,128)(2,1)S(1)}, u32[]{:S(2)}, u32[]{:S(2)}) collective-permute-start(bf16[1,128,384]{1,2,0:T(8,128)(2,1)S(1)} %get-tuple-element.25), channel_id=1, source_target_pairs={{0,8},{1,9},{2,10},{3,11},{4,12},{5,13},{6,14},{7,15},{8,0},{9,1},... | collective-permute-start | bytes 294920 | tf_op jit(solution)/shard_map/ppermute | solution.py:108
  191.0 27.8 %collective-permute-start.24 = (bf16[1,128,384]{1,2,0:T(8,128)(2,1)S(1)}, bf16[1,128,384]{1,2,0:T(8,128)(2,1)S(1)}, u32[]{:S(2)}, u32[]{:S(2)}) collective-permute-start(bf16[1,128,384]{1,2,0:T(8,128)(2,1)S(1)} %get-tuple-element.23), channel_id=1, source_target_pairs={{0,4},{1,5},{2,6},{3,7},{4,8},{5,9},{6,10},{7,11},{8,12},{9,13},{1... | collective-permute-start | bytes 294920 | tf_op jit(solution)/shard_map/ppermute | solution.py:108
  196.4 23.1 %collective-permute-start.33 = (bf16[1,64,384]{2,1,0:T(8,128)(2,1)S(1)}, bf16[1,64,384]{2,1,0:T(8,128)(2,1)S(1)}, u32[]{:S(2)}, u32[]{:S(2)}) collective-permute-start(bf16[1,64,384]{2,1,0:T(8,128)(2,1)S(1)} %get-tuple-element.31), channel_id=1, source_target_pairs={{0,384},{16,400},{32,416},{48,432},{64,448},{80,464},{96,480},{112... | collective-permute-start | bytes 147464 | tf_op jit(solution)/shard_map/ppermute | solution.py:108
  203.1 16.4 %collective-permute-start.32 = (bf16[1,64,384]{2,1,0:T(8,128)(2,1)S(1)}, bf16[1,64,384]{2,1,0:T(8,128)(2,1)S(1)}, u32[]{:S(2)}, u32[]{:S(2)}) collective-permute-start(bf16[1,64,384]{2,1,0:T(8,128)(2,1)S(1)} %get-tuple-element.32), channel_id=1, source_target_pairs={{0,256},{16,272},{32,288},{48,304},{64,320},{80,336},{96,352},{112... | collective-permute-start | bytes 147464 | tf_op jit(solution)/shard_map/ppermute | solution.py:108
  210.9 10.5 %collective-permute-start.31 = (bf16[1,64,384]{2,1,0:T(8,128)(2,1)S(1)}, bf16[1,64,384]{2,1,0:T(8,128)(2,1)S(1)}, u32[]{:S(2)}, u32[]{:S(2)}) collective-permute-start(bf16[1,64,384]{2,1,0:T(8,128)(2,1)S(1)} %get-tuple-element.30), channel_id=1, source_target_pairs={{0,128},{16,144},{32,160},{48,176},{64,192},{80,208},{96,224},{112... | collective-permute-start | bytes 147464 | tf_op jit(solution)/shard_map/ppermute | solution.py:108
  (12 other events, 144.6 us)

commit v8 on v7

--- a/solution.py
+++ b/solution.py
@@ -97,12 +97,12 @@
     place = lax.axis_index(axis)
     rows = term.shape[0] // count
     cols = term.shape[1]
-    current = term.astype(jnp.float32).reshape(count, rows, cols)
+    current = term.reshape(count, rows, cols)
     stride = 1
     for radix in radices:
         digit = (place // stride) % radix
         split = current.reshape(-1, radix, rows, cols)
-        total = lax.dynamic_index_in_dim(split, digit, 1, False)
+        total = lax.dynamic_index_in_dim(split, digit, 1, False).astype(jnp.float32)
         for offset in range(1, radix):
             away = lax.dynamic_index_in_dim(split, (digit + offset) % radix, 1, False)
             moved = lax.ppermute(

time: 225 us -> 218 us (0.969)
  local copies, waits for them, and re-layouts: 15 us -> 11.9 us
    unnamed x25 -> x13, local copies, waits for them, and re-layouts: 5.92 us -> 2.21 us
    another operation x1 -> x0, local copies, waits for them, and re-layouts: 3.51 us -> none  [exchange_scatter(): split = current.reshape(-1, radix, rows, cols)]
    dynamic_slice x1 -> x3, local copies, waits for them, and re-layouts: 1.78 us -> 4.79 us  [exchange_scatter(): away = lax.dynamic_index_in_dim(split, (digit + offset) % radix, 1, False)]
    convert_element_type x4 -> x3, local copies, waits for them, and re-layouts: 2.69 us -> 0.17 us  [exchange_scatter(): away.astype(jnp.bfloat16)]
  transfers between devices with their start and end apart: 34 -> 34, of which waited for: 15 -> 16; matrix products, arithmetic and copies ran while one was open for 6% -> 7% of each run, Pallas kernels for 0% -> 0%
where the time goes in v8:
time: 218 us; the launch traced here: 215 us
  starting transfers between devices  138 us (63%)
  waiting for transfers between devices  47.1 us (22%)
  local copies, waits for them, and re-layouts  11.9 us (5%)
  matrix products  9.11 us (4%)
  other arithmetic  7.11 us (3%)
    ppermute x13, starting transfers between devices, exchange_scatter(): lax.ppermute(away.astype(jnp.bfloat16), axis, digit_pairs(count, stride,...  60.8 us
    ppermute x7, starting transfers between devices, exchange_gather(): lax.ppermute(current, axis, digit_pairs(count, stride, radix, offset))  37.7 us
    ppermute x12, starting transfers between devices, entering(): parts.append(lax.ppermute(total, 'z', pairs))  35.1 us
    ppermute x12, waiting for transfers between devices, entering(): parts.append(lax.ppermute(total, 'z', pairs))  23.8 us
    ppermute x7, waiting for transfers between devices, exchange_gather(): lax.ppermute(current, axis, digit_pairs(count, stride, radix, offset))  19.3 us
    dynamic_slice x3, local copies, waits for them, and re-layouts, exchange_scatter(): away = lax.dynamic_index_in_dim(split, (digit + offset) % radix, 1, False)  4.79 us
  transfers between devices with their start and end apart: 34, of which 16 were waited for; matrix products, arithmetic and copies ran while one was open for 7% of the time, Pallas kernels for 0%

profile of v8, /device:TPU:6, one launch (start us, length us, event | category | flops | bytes accessed | tf_op | source)
XLA Modules:
  0.0 214.8 jit_solution(11692773755355941026)
XLA Ops:
  1.5 12.7 %collective-permute-start = (bf16[1,64,384]{2,1,0:T(8,128)(2,1)S(1)}, bf16[1,64,384]{2,1,0:T(8,128)(2,1)S(1)}, u32[]{:S(2)}, u32[]{:S(2)}) collective-permute-start(bf16[1,64,384]{2,1,0:T(8,128)(2,1)S(1)} %maximum_bitcast_fusion.1), channel_id=1, source_target_pairs={{0,384},{16,400},{32,416},{48,432},{64,448},{80,464},{96,480},{112... | collective-permute-start | bytes 147464 | tf_op jit(solution)/shard_map/ppermute | solution.py:84
  14.3 4.9 %collective-permute-start.1 = (bf16[1,64,384]{2,1,0:T(8,128)(2,1)S(1)}, bf16[1,64,384]{2,1,0:T(8,128)(2,1)S(1)}, u32[]{:S(2)}, u32[]{:S(2)}) collective-permute-start(bf16[1,64,384]{2,1,0:T(8,128)(2,1)S(1)} %maximum_bitcast_fusion.1), channel_id=1, source_target_pairs={{0,256},{16,272},{32,288},{48,304},{64,320},{80,336},{96,352},{112... | collective-permute-start | bytes 147464 | tf_op jit(solution)/shard_map/ppermute | solution.py:84
  19.2 7.8 %collective-permute-start.2 = (bf16[1,64,384]{2,1,0:T(8,128)(2,1)S(1)}, bf16[1,64,384]{2,1,0:T(8,128)(2,1)S(1)}, u32[]{:S(2)}, u32[]{:S(2)}) collective-permute-start(bf16[1,64,384]{2,1,0:T(8,128)(2,1)S(1)} %maximum_bitcast_fusion.1), channel_id=1, source_target_pairs={{0,128},{16,144},{32,160},{48,176},{64,192},{80,208},{96,224},{112... | collective-permute-start | bytes 147464 | tf_op jit(solution)/shard_map/ppermute | solution.py:84
  27.1 2.2 %collective-permute-done.1 = bf16[1,64,384]{2,1,0:T(8,128)(2,1)S(1)} collective-permute-done((bf16[1,64,384]{2,1,0:T(8,128)(2,1)S(1)}, bf16[1,64,384]{2,1,0:T(8,128)(2,1)S(1)}, u32[]{:S(2)}, u32[]{:S(2)}) %collective-permute-start.1) | collective-permute-done | bytes 49184 | tf_op jit(solution)/shard_map/ppermute | solution.py:84
  29.4 2.3 %collective-permute-done.2 = bf16[1,64,384]{2,1,0:T(8,128)(2,1)S(1)} collective-permute-done((bf16[1,64,384]{2,1,0:T(8,128)(2,1)S(1)}, bf16[1,64,384]{2,1,0:T(8,128)(2,1)S(1)}, u32[]{:S(2)}, u32[]{:S(2)}) %collective-permute-start.2) | collective-permute-done | bytes 49184 | tf_op jit(solution)/shard_map/ppermute | solution.py:84
  33.3 5.9 %collective-permute-start.3 = (bf16[4,64,384]{2,1,0:T(8,128)(2,1)S(1)}, bf16[4,64,384]{2,1,0:T(8,128)(2,1)S(1)}, u32[]{:S(2)}, u32[]{:S(2)}) collective-permute-start(bf16[4,64,384]{2,1,0:T(8,128)(2,1)S(1)} %maximum_bitcast_fusion), channel_id=1, source_target_pairs={{0,96},{16,112},{32,0},{48,16},{64,32},{80,48},{96,64},{112,80},{1... | collective-permute-start | bytes 589832 | tf_op jit(solution)/shard_map/ppermute | solution.py:84
  41.2 2.5 %collective-permute-start.5 = (bf16[4,64,384]{2,1,0:T(8,128)(2,1)S(1)}, bf16[4,64,384]{2,1,0:T(8,128)(2,1)S(1)}, u32[]{:S(2)}, u32[]{:S(2)}) collective-permute-start(bf16[4,64,384]{2,1,0:T(8,128)(2,1)S(1)} %maximum_bitcast_fusion), channel_id=1, source_target_pairs={{0,32},{16,48},{32,64},{48,80},{64,96},{80,112},{96,0},{112,16},{1... | collective-permute-start | bytes 589832 | tf_op jit(solution)/shard_map/ppermute | solution.py:84
  44.6 12.1 %collective-permute-done.4 = bf16[4,64,384]{2,1,0:T(8,128)(2,1)S(1)} collective-permute-done((bf16[4,64,384]{2,1,0:T(8,128)(2,1)S(1)}, bf16[4,64,384]{2,1,0:T(8,128)(2,1)S(1)}, u32[]{:S(2)}, u32[]{:S(2)}) %collective-permute-start.4) | collective-permute-done | bytes 196640 | tf_op jit(solution)/shard_map/ppermute | solution.py:84
  63.2 2.0 collective-permute-start.7
  68.2 4.3 %collective-permute-start.9 = (f32[1,128,128]{2,1,0:T(8,128)S(1)}, f32[1,128,128]{2,1,0:T(8,128)S(1)}, u32[]{:S(2)}, u32[]{:S(2)}) collective-permute-start(f32[1,128,128]{2,1,0:T(8,128)S(1)} %add.361), channel_id=1, source_target_pairs={{0,64},{32,96},{64,128},{96,160},{128,192},{160,224},{192,256},{22... | collective-permute-start | bytes 196616 | tf_op jit(solution)/shard_map/ppermute | solution.py:35
  72.5 3.4 %collective-permute-start.8 = (f32[1,128,128]{2,1,0:T(8,128)S(1)}, f32[1,128,128]{2,1,0:T(8,128)S(1)}, u32[]{:S(2)}, u32[]{:S(2)}) collective-permute-start(f32[1,128,128]{2,1,0:T(8,128)S(1)} %add.361), channel_id=1, source_target_pairs={{0,32},{32,64},{64,96},{96,128},{128,160},{160,192},{192,224},{224... | collective-permute-start | bytes 196616 | tf_op jit(solution)/shard_map/ppermute | solution.py:35
  77.8 9.2 %collective-permute-start.13 = (f32[1,128,128]{2,1,0:T(8,128)S(1)}, f32[1,128,128]{2,1,0:T(8,128)S(1)}, u32[]{:S(2)}, u32[]{:S(2)}) collective-permute-start(f32[1,128,128]{2,1,0:T(8,128)S(1)} %add_add_fusion.1), channel_id=1, source_target_pairs={{0,384},{32,416},{64,448},{96,480},{1,385},{33,417},{65,449},{97,4... | collective-permute-start | bytes 196616 | tf_op jit(solution)/shard_map/ppermute | solution.py:35
  87.0 3.2 %collective-permute-start.12 = (f32[1,128,128]{2,1,0:T(8,128)S(1)}, f32[1,128,128]{2,1,0:T(8,128)S(1)}, u32[]{:S(2)}, u32[]{:S(2)}) collective-permute-start(f32[1,128,128]{2,1,0:T(8,128)S(1)} %add_add_fusion.1), channel_id=1, source_target_pairs={{0,256},{32,288},{64,320},{96,352},{128,384},{160,416},{192,448},{... | collective-permute-start | bytes 196616 | tf_op jit(solution)/shard_map/ppermute | solution.py:35
  90.2 5.4 %collective-permute-start.11 = (f32[1,128,128]{2,1,0:T(8,128)S(1)}, f32[1,128,128]{2,1,0:T(8,128)S(1)}, u32[]{:S(2)}, u32[]{:S(2)}) collective-permute-start(f32[1,128,128]{2,1,0:T(8,128)S(1)} %add_add_fusion.1), channel_id=1, source_target_pairs={{0,128},{32,160},{64,192},{96,224},{128,256},{160,288},{192,320},{... | collective-permute-start | bytes 196616 | tf_op jit(solution)/shard_map/ppermute | solution.py:35
  98.7 1.9 collective-permute-start.14
  106.0 3.9 %collective-permute-done.17 = f32[1,128,128]{2,1,0:T(8,128)S(1)} collective-permute-done((f32[1,128,128]{2,1,0:T(8,128)S(1)}, f32[1,128,128]{2,1,0:T(8,128)S(1)}, u32[]{:S(2)}, u32[]{:S(2)}) %collective-permute-start.17) | collective-permute-done | bytes 65568 | tf_op jit(solution)/shard_map/ppermute | solution.py:35
  109.9 3.8 %collective-permute-done.16 = f32[1,128,128]{2,1,0:T(8,128)S(1)} collective-permute-done((f32[1,128,128]{2,1,0:T(8,128)S(1)}, f32[1,128,128]{2,1,0:T(8,128)S(1)}, u32[]{:S(2)}, u32[]{:S(2)}) %collective-permute-start.16) | collective-permute-done | bytes 65568 | tf_op jit(solution)/shard_map/ppermute | solution.py:35
  117.7 11.2 %collective-permute-done.20 = f32[1,128,128]{2,1,0:T(8,128)S(1)} collective-permute-done((f32[1,128,128]{2,1,0:T(8,128)S(1)}, f32[1,128,128]{2,1,0:T(8,128)S(1)}, u32[]{:S(2)}, u32[]{:S(2)}) %collective-permute-start.20) | collective-permute-done | bytes 65568 | tf_op jit(solution)/shard_map/ppermute | solution.py:35
  131.0 2.2 %fusion = bf16[2048,384]{0,1:T(8,128)(2,1)} fusion(bf16[384,2048]{1,0:T(8,128)(2,1)S(1)} %copy-done, bf16[384,128]{0,1:T(8,128)(2,1)S(1)} %fusion.10, bf16[384,128]{0,1:T(8,128)(2,1)S(1)} %fusion.11, bf16[384,128]{0,1:T(8,128)(2,1)S(1)} %fusion.12), kind=kOutput, calls=%fused_computation.2 | convolution fusion | flops 605650944 | bytes 3440640 | tf_op jit(solution)/shard_map/dot_general | solution.py:218
  139.0 2.5 %convolution_convert_fusion.1 = bf16[2048,384]{1,0:T(8,128)(2,1)S(1)} fusion(bf16[2048,384]{1,0:T(8,128)(2,1)} %bitcast.175, bf16[384,128]{0,1:T(8,128)(2,1)S(1)} %fusion.10, bf16[384,128]{0,1:T(8,128)(2,1)S(1)} %fusion.11, bf16[384,128]{0,1:T(8,128)(2,1)S(1)} %fusion.12), kind=kOutput, calls=%fused_computation.1 | convolution fusion | flops 605650944 | bytes 3440640 | tf_op jit(solution)/shard_map/dot_general | solution.py:210
  142.6 1.9 copy.26
  144.5 4.9 %collective-permute-start.23 = (bf16[4,128,384]{1,2,0:T(8,128)(2,1)}, bf16[4,128,384]{1,2,0:T(8,128)(2,1)}, u32[]{:S(2)}, u32[]{:S(2)}) collective-permute-start(bf16[4,128,384]{1,2,0:T(8,128)(2,1)} %bitcast.179), channel_id=1, source_target_pairs={{0,3},{1,0},{2,1},{3,2},{4,7},{5,4},{6,5},{7,6},{8,11},{9,8},{10,9... | collective-permute-start | bytes 1179656 | tf_op jit(solution)/shard_map/ppermute | solution.py:108
  149.5 1.9 copy.25
  151.4 2.5 %collective-permute-start.22 = (bf16[4,128,384]{1,2,0:T(8,128)(2,1)}, bf16[4,128,384]{1,2,0:T(8,128)(2,1)}, u32[]{:S(2)}, u32[]{:S(2)}) collective-permute-start(bf16[4,128,384]{1,2,0:T(8,128)(2,1)} %bitcast.177), channel_id=1, source_target_pairs={{0,2},{1,3},{2,0},{3,1},{4,6},{5,7},{6,4},{7,5},{8,10},{9,11},{10,... | collective-permute-start | bytes 1179656 | tf_op jit(solution)/shard_map/ppermute | solution.py:108
  154.8 2.9 %collective-permute-start.21 = (bf16[4,128,384]{1,2,0:T(8,128)(2,1)}, bf16[4,128,384]{1,2,0:T(8,128)(2,1)}, u32[]{:S(2)}, u32[]{:S(2)}) collective-permute-start(bf16[4,128,384]{1,2,0:T(8,128)(2,1)} %bitcast.178), channel_id=1, source_target_pairs={{0,1},{1,2},{2,3},{3,0},{4,5},{5,6},{6,7},{7,4},{8,9},{9,10},{10,1... | collective-permute-start | bytes 1179656 | tf_op jit(solution)/shard_map/ppermute | solution.py:108
  160.4 14.6 %collective-permute-start.30 = (bf16[4,64,384]{2,1,0:T(8,128)(2,1)S(1)}, bf16[4,64,384]{2,1,0:T(8,128)(2,1)S(1)}, u32[]{:S(2)}, u32[]{:S(2)}) collective-permute-start(bf16[4,64,384]{2,1,0:T(8,128)(2,1)S(1)} %get-tuple-element.16), channel_id=1, source_target_pairs={{0,96},{16,112},{32,0},{48,16},{64,32},{80,48},{96,64},{112,80},{1... | collective-permute-start | bytes 589832 | tf_op jit(solution)/shard_map/ppermute | solution.py:108
  177.0 2.5 %collective-permute-start.28 = (bf16[4,64,384]{2,1,0:T(8,128)(2,1)S(1)}, bf16[4,64,384]{2,1,0:T(8,128)(2,1)S(1)}, u32[]{:S(2)}, u32[]{:S(2)}) collective-permute-start(bf16[4,64,384]{2,1,0:T(8,128)(2,1)S(1)} %get-tuple-element.15), channel_id=1, source_target_pairs={{0,32},{16,48},{32,64},{48,80},{64,96},{80,112},{96,0},{112,16},{1... | collective-permute-start | bytes 589832 | tf_op jit(solution)/shard_map/ppermute | solution.py:108
  181.0 2.7 %collective-permute-start.26 = (bf16[1,128,384]{1,2,0:T(8,128)(2,1)S(1)}, bf16[1,128,384]{1,2,0:T(8,128)(2,1)S(1)}, u32[]{:S(2)}, u32[]{:S(2)}) collective-permute-start(bf16[1,128,384]{1,2,0:T(8,128)(2,1)S(1)} %get-tuple-element.25), channel_id=1, source_target_pairs={{0,12},{1,13},{2,14},{3,15},{4,0},{5,1},{6,2},{7,3},{8,4},{9,5},{1... | collective-permute-start | bytes 294920 | tf_op jit(solution)/shard_map/ppermute | solution.py:108
  183.7 3.0 %collective-permute-start.25 = (bf16[1,128,384]{1,2,0:T(8,128)(2,1)S(1)}, bf16[1,128,384]{1,2,0:T(8,128)(2,1)S(1)}, u32[]{:S(2)}, u32[]{:S(2)}) collective-permute-start(bf16[1,128,384]{1,2,0:T(8,128)(2,1)S(1)} %get-tuple-element.26), channel_id=1, source_target_pairs={{0,8},{1,9},{2,10},{3,11},{4,12},{5,13},{6,14},{7,15},{8,0},{9,1},... | collective-permute-start | bytes 294920 | tf_op jit(solution)/shard_map/ppermute | solution.py:108
  186.7 4.0 %collective-permute-start.24 = (bf16[1,128,384]{1,2,0:T(8,128)(2,1)S(1)}, bf16[1,128,384]{1,2,0:T(8,128)(2,1)S(1)}, u32[]{:S(2)}, u32[]{:S(2)}) collective-permute-start(bf16[1,128,384]{1,2,0:T(8,128)(2,1)S(1)} %get-tuple-element.24), channel_id=1, source_target_pairs={{0,4},{1,5},{2,6},{3,7},{4,8},{5,9},{6,10},{7,11},{8,12},{9,13},{1... | collective-permute-start | bytes 294920 | tf_op jit(solution)/shard_map/ppermute | solution.py:108
  194.0 10.0 %collective-permute-start.32 = (bf16[1,64,384]{2,1,0:T(8,128)(2,1)S(1)}, bf16[1,64,384]{2,1,0:T(8,128)(2,1)S(1)}, u32[]{:S(2)}, u32[]{:S(2)}) collective-permute-start(bf16[1,64,384]{2,1,0:T(8,128)(2,1)S(1)} %get-tuple-element.33), channel_id=1, source_target_pairs={{0,256},{16,272},{32,288},{48,304},{64,320},{80,336},{96,352},{112... | collective-permute-start | bytes 147464 | tf_op jit(solution)/shard_map/ppermute | solution.py:108
  204.0 7.8 %collective-permute-start.31 = (bf16[1,64,384]{2,1,0:T(8,128)(2,1)S(1)}, bf16[1,64,384]{2,1,0:T(8,128)(2,1)S(1)}, u32[]{:S(2)}, u32[]{:S(2)}) collective-permute-start(bf16[1,64,384]{2,1,0:T(8,128)(2,1)S(1)} %get-tuple-element.31), channel_id=1, source_target_pairs={{0,128},{16,144},{32,160},{48,176},{64,192},{80,208},{96,224},{112... | collective-permute-start | bytes 147464 | tf_op jit(solution)/shard_map/ppermute | solution.py:108
  (103 shorter events, 50.6 us)
Async XLA Ops:
  1.5 25.6 %collective-permute-start = (bf16[1,64,384]{2,1,0:T(8,128)(2,1)S(1)}, bf16[1,64,384]{2,1,0:T(8,128)(2,1)S(1)}, u32[]{:S(2)}, u32[]{:S(2)}) collective-permute-start(bf16[1,64,384]{2,1,0:T(8,128)(2,1)S(1)} %maximum_bitcast_fusion.1), channel_id=1, source_target_pairs={{0,384},{16,400},{32,416},{48,432},{64,448},{80,464},{96,480},{112... | collective-permute-start | bytes 147464 | tf_op jit(solution)/shard_map/ppermute | solution.py:84
  14.3 15.1 %collective-permute-start.1 = (bf16[1,64,384]{2,1,0:T(8,128)(2,1)S(1)}, bf16[1,64,384]{2,1,0:T(8,128)(2,1)S(1)}, u32[]{:S(2)}, u32[]{:S(2)}) collective-permute-start(bf16[1,64,384]{2,1,0:T(8,128)(2,1)S(1)} %maximum_bitcast_fusion.1), channel_id=1, source_target_pairs={{0,256},{16,272},{32,288},{48,304},{64,320},{80,336},{96,352},{112... | collective-permute-start | bytes 147464 | tf_op jit(solution)/shard_map/ppermute | solution.py:84
  19.2 12.5 %collective-permute-start.2 = (bf16[1,64,384]{2,1,0:T(8,128)(2,1)S(1)}, bf16[1,64,384]{2,1,0:T(8,128)(2,1)S(1)}, u32[]{:S(2)}, u32[]{:S(2)}) collective-permute-start(bf16[1,64,384]{2,1,0:T(8,128)(2,1)S(1)} %maximum_bitcast_fusion.1), channel_id=1, source_target_pairs={{0,128},{16,144},{32,160},{48,176},{64,192},{80,208},{96,224},{112... | collective-permute-start | bytes 147464 | tf_op jit(solution)/shard_map/ppermute | solution.py:84
  33.3 11.3 %collective-permute-start.3 = (bf16[4,64,384]{2,1,0:T(8,128)(2,1)S(1)}, bf16[4,64,384]{2,1,0:T(8,128)(2,1)S(1)}, u32[]{:S(2)}, u32[]{:S(2)}) collective-permute-start(bf16[4,64,384]{2,1,0:T(8,128)(2,1)S(1)} %maximum_bitcast_fusion), channel_id=1, source_target_pairs={{0,96},{16,112},{32,0},{48,16},{64,32},{80,48},{96,64},{112,80},{1... | collective-permute-start | bytes 589832 | tf_op jit(solution)/shard_map/ppermute | solution.py:84
  39.3 17.4 %collective-permute-start.4 = (bf16[4,64,384]{2,1,0:T(8,128)(2,1)S(1)}, bf16[4,64,384]{2,1,0:T(8,128)(2,1)S(1)}, u32[]{:S(2)}, u32[]{:S(2)}) collective-permute-start(bf16[4,64,384]{2,1,0:T(8,128)(2,1)S(1)} %maximum_bitcast_fusion), channel_id=1, source_target_pairs={{0,64},{16,80},{32,96},{48,112},{64,0},{80,16},{96,32},{112,48},{1... | collective-permute-start | bytes 589832 | tf_op jit(solution)/shard_map/ppermute | solution.py:84
  41.2 15.5 %collective-permute-start.5 = (bf16[4,64,384]{2,1,0:T(8,128)(2,1)S(1)}, bf16[4,64,384]{2,1,0:T(8,128)(2,1)S(1)}, u32[]{:S(2)}, u32[]{:S(2)}) collective-permute-start(bf16[4,64,384]{2,1,0:T(8,128)(2,1)S(1)} %maximum_bitcast_fusion), channel_id=1, source_target_pairs={{0,32},{16,48},{32,64},{48,80},{64,96},{80,112},{96,0},{112,16},{1... | collective-permute-start | bytes 589832 | tf_op jit(solution)/shard_map/ppermute | solution.py:84
  57.0 4.2 %collective-permute-start.6 = (bf16[16,64,384]{2,1,0:T(8,128)(2,1)S(1)}, bf16[16,64,384]{2,1,0:T(8,128)(2,1)S(1)}, u32[]{:S(2)}, u32[]{:S(2)}) collective-permute-start(bf16[16,64,384]{2,1,0:T(8,128)(2,1)S(1)} %bitcast.173), channel_id=1, source_target_pairs={{0,16},{16,0},{32,48},{48,32},{64,80},{80,64},{96,112},{112,96},{1... | collective-permute-start | bytes 2359304 | tf_op jit(solution)/shard_map/ppermute | solution.py:84
  66.3 9.8 %collective-permute-start.10 = (f32[1,128,128]{2,1,0:T(8,128)S(1)}, f32[1,128,128]{2,1,0:T(8,128)S(1)}, u32[]{:S(2)}, u32[]{:S(2)}) collective-permute-start(f32[1,128,128]{2,1,0:T(8,128)S(1)} %add.361), channel_id=1, source_target_pairs={{0,96},{32,128},{64,160},{96,192},{128,224},{160,256},{192,288},{2... | collective-permute-start | bytes 196616 | tf_op jit(solution)/shard_map/ppermute | solution.py:35
  68.2 7.9 %collective-permute-start.9 = (f32[1,128,128]{2,1,0:T(8,128)S(1)}, f32[1,128,128]{2,1,0:T(8,128)S(1)}, u32[]{:S(2)}, u32[]{:S(2)}) collective-permute-start(f32[1,128,128]{2,1,0:T(8,128)S(1)} %add.361), channel_id=1, source_target_pairs={{0,64},{32,96},{64,128},{96,160},{128,192},{160,224},{192,256},{22... | collective-permute-start | bytes 196616 | tf_op jit(solution)/shard_map/ppermute | solution.py:35
  72.5 5.3 %collective-permute-start.8 = (f32[1,128,128]{2,1,0:T(8,128)S(1)}, f32[1,128,128]{2,1,0:T(8,128)S(1)}, u32[]{:S(2)}, u32[]{:S(2)}) collective-permute-start(f32[1,128,128]{2,1,0:T(8,128)S(1)} %add.361), channel_id=1, source_target_pairs={{0,32},{32,64},{64,96},{96,128},{128,160},{160,192},{192,224},{224... | collective-permute-start | bytes 196616 | tf_op jit(solution)/shard_map/ppermute | solution.py:35
  77.8 18.2 %collective-permute-start.13 = (f32[1,128,128]{2,1,0:T(8,128)S(1)}, f32[1,128,128]{2,1,0:T(8,128)S(1)}, u32[]{:S(2)}, u32[]{:S(2)}) collective-permute-start(f32[1,128,128]{2,1,0:T(8,128)S(1)} %add_add_fusion.1), channel_id=1, source_target_pairs={{0,384},{32,416},{64,448},{96,480},{1,385},{33,417},{65,449},{97,4... | collective-permute-start | bytes 196616 | tf_op jit(solution)/shard_map/ppermute | solution.py:35
  87.0 9.0 %collective-permute-start.12 = (f32[1,128,128]{2,1,0:T(8,128)S(1)}, f32[1,128,128]{2,1,0:T(8,128)S(1)}, u32[]{:S(2)}, u32[]{:S(2)}) collective-permute-start(f32[1,128,128]{2,1,0:T(8,128)S(1)} %add_add_fusion.1), channel_id=1, source_target_pairs={{0,256},{32,288},{64,320},{96,352},{128,384},{160,416},{192,448},{... | collective-permute-start | bytes 196616 | tf_op jit(solution)/shard_map/ppermute | solution.py:35
  90.2 7.3 %collective-permute-start.11 = (f32[1,128,128]{2,1,0:T(8,128)S(1)}, f32[1,128,128]{2,1,0:T(8,128)S(1)}, u32[]{:S(2)}, u32[]{:S(2)}) collective-permute-start(f32[1,128,128]{2,1,0:T(8,128)S(1)} %add_add_fusion.1), channel_id=1, source_target_pairs={{0,128},{32,160},{64,192},{96,224},{128,256},{160,288},{192,320},{... | collective-permute-start | bytes 196616 | tf_op jit(solution)/shard_map/ppermute | solution.py:35
  101.8 8.0 %collective-permute-start.17 = (f32[1,128,128]{2,1,0:T(8,128)S(1)}, f32[1,128,128]{2,1,0:T(8,128)S(1)}, u32[]{:S(2)}, u32[]{:S(2)}) collective-permute-start(f32[1,128,128]{2,1,0:T(8,128)S(1)} %add.374), channel_id=1, source_target_pairs={{96,0},{128,32},{160,64},{192,96},{224,128},{256,160},{288,192},{3... | collective-permute-start | bytes 196616 | tf_op jit(solution)/shard_map/ppermute | solution.py:35
  103.1 10.5 %collective-permute-start.16 = (f32[1,128,128]{2,1,0:T(8,128)S(1)}, f32[1,128,128]{2,1,0:T(8,128)S(1)}, u32[]{:S(2)}, u32[]{:S(2)}) collective-permute-start(f32[1,128,128]{2,1,0:T(8,128)S(1)} %add.374), channel_id=1, source_target_pairs={{64,0},{96,32},{128,64},{160,96},{192,128},{224,160},{256,192},{28... | collective-permute-start | bytes 196616 | tf_op jit(solution)/shard_map/ppermute | solution.py:35
  104.4 9.2 %collective-permute-start.15 = (f32[1,128,128]{2,1,0:T(8,128)S(1)}, f32[1,128,128]{2,1,0:T(8,128)S(1)}, u32[]{:S(2)}, u32[]{:S(2)}) collective-permute-start(f32[1,128,128]{2,1,0:T(8,128)S(1)} %add.374), channel_id=1, source_target_pairs={{32,0},{64,32},{96,64},{128,96},{160,128},{192,160},{224,192},{256... | collective-permute-start | bytes 196616 | tf_op jit(solution)/shard_map/ppermute | solution.py:35
  113.6 15.3 %collective-permute-start.20 = (f32[1,128,128]{2,1,0:T(8,128)S(1)}, f32[1,128,128]{2,1,0:T(8,128)S(1)}, u32[]{:S(2)}, u32[]{:S(2)}) collective-permute-start(f32[1,128,128]{2,1,0:T(8,128)S(1)} %add_add_fusion), channel_id=1, source_target_pairs={{384,0},{416,32},{448,64},{480,96},{385,1},{417,33},{449,65},{481,... | collective-permute-start | bytes 196616 | tf_op jit(solution)/shard_map/ppermute | solution.py:35
  114.9 15.7 %collective-permute-start.19 = (f32[1,128,128]{2,1,0:T(8,128)S(1)}, f32[1,128,128]{2,1,0:T(8,128)S(1)}, u32[]{:S(2)}, u32[]{:S(2)}) collective-permute-start(f32[1,128,128]{2,1,0:T(8,128)S(1)} %add_add_fusion), channel_id=1, source_target_pairs={{256,0},{288,32},{320,64},{352,96},{384,128},{416,160},{448,192},{... | collective-permute-start | bytes 196616 | tf_op jit(solution)/shard_map/ppermute | solution.py:35
  116.2 14.4 %collective-permute-start.18 = (f32[1,128,128]{2,1,0:T(8,128)S(1)}, f32[1,128,128]{2,1,0:T(8,128)S(1)}, u32[]{:S(2)}, u32[]{:S(2)}) collective-permute-start(f32[1,128,128]{2,1,0:T(8,128)S(1)} %add_add_fusion), channel_id=1, source_target_pairs={{128,0},{160,32},{192,64},{224,96},{256,128},{288,160},{320,192},{... | collective-permute-start | bytes 196616 | tf_op jit(solution)/shard_map/ppermute | solution.py:35
  136.1 22.9 %collective-permute-start.27 = (bf16[16,64,384]{2,1,0:T(8,128)(2,1)}, bf16[16,64,384]{2,1,0:T(8,128)(2,1)}, u32[]{:S(2)}, u32[]{:S(2)}) collective-permute-start(bf16[16,64,384]{2,1,0:T(8,128)(2,1)} %dynamic-slice_bitcast_fusion), channel_id=1, source_target_pairs={{0,16},{16,0},{32,48},{48,32},{64,80},{80,64},{96,112},{112,96},{1... | collective-permute-start | bytes 2359304 | tf_op jit(solution)/shard_map/ppermute | solution.py:108
  144.5 32.4 %collective-permute-start.23 = (bf16[4,128,384]{1,2,0:T(8,128)(2,1)}, bf16[4,128,384]{1,2,0:T(8,128)(2,1)}, u32[]{:S(2)}, u32[]{:S(2)}) collective-permute-start(bf16[4,128,384]{1,2,0:T(8,128)(2,1)} %bitcast.179), channel_id=1, source_target_pairs={{0,3},{1,0},{2,1},{3,2},{4,7},{5,4},{6,5},{7,6},{8,11},{9,8},{10,9... | collective-permute-start | bytes 1179656 | tf_op jit(solution)/shard_map/ppermute | solution.py:108
  151.4 28.1 %collective-permute-start.22 = (bf16[4,128,384]{1,2,0:T(8,128)(2,1)}, bf16[4,128,384]{1,2,0:T(8,128)(2,1)}, u32[]{:S(2)}, u32[]{:S(2)}) collective-permute-start(bf16[4,128,384]{1,2,0:T(8,128)(2,1)} %bitcast.177), channel_id=1, source_target_pairs={{0,2},{1,3},{2,0},{3,1},{4,6},{5,7},{6,4},{7,5},{8,10},{9,11},{10,... | collective-permute-start | bytes 1179656 | tf_op jit(solution)/shard_map/ppermute | solution.py:108
  154.8 24.6 %collective-permute-start.21 = (bf16[4,128,384]{1,2,0:T(8,128)(2,1)}, bf16[4,128,384]{1,2,0:T(8,128)(2,1)}, u32[]{:S(2)}, u32[]{:S(2)}) collective-permute-start(bf16[4,128,384]{1,2,0:T(8,128)(2,1)} %bitcast.178), channel_id=1, source_target_pairs={{0,1},{1,2},{2,3},{3,0},{4,5},{5,6},{6,7},{7,4},{8,9},{9,10},{10,1... | collective-permute-start | bytes 1179656 | tf_op jit(solution)/shard_map/ppermute | solution.py:108
  160.4 26.3 %collective-permute-start.30 = (bf16[4,64,384]{2,1,0:T(8,128)(2,1)S(1)}, bf16[4,64,384]{2,1,0:T(8,128)(2,1)S(1)}, u32[]{:S(2)}, u32[]{:S(2)}) collective-permute-start(bf16[4,64,384]{2,1,0:T(8,128)(2,1)S(1)} %get-tuple-element.16), channel_id=1, source_target_pairs={{0,96},{16,112},{32,0},{48,16},{64,32},{80,48},{96,64},{112,80},{1... | collective-permute-start | bytes 589832 | tf_op jit(solution)/shard_map/ppermute | solution.py:108
  175.0 16.9 %collective-permute-start.29 = (bf16[4,64,384]{2,1,0:T(8,128)(2,1)S(1)}, bf16[4,64,384]{2,1,0:T(8,128)(2,1)S(1)}, u32[]{:S(2)}, u32[]{:S(2)}) collective-permute-start(bf16[4,64,384]{2,1,0:T(8,128)(2,1)S(1)} %get-tuple-element.17), channel_id=1, source_target_pairs={{0,64},{16,80},{32,96},{48,112},{64,0},{80,16},{96,32},{112,48},{1... | collective-permute-start | bytes 589832 | tf_op jit(solution)/shard_map/ppermute | solution.py:108
  177.0 14.9 %collective-permute-start.28 = (bf16[4,64,384]{2,1,0:T(8,128)(2,1)S(1)}, bf16[4,64,384]{2,1,0:T(8,128)(2,1)S(1)}, u32[]{:S(2)}, u32[]{:S(2)}) collective-permute-start(bf16[4,64,384]{2,1,0:T(8,128)(2,1)S(1)} %get-tuple-element.15), channel_id=1, source_target_pairs={{0,32},{16,48},{32,64},{48,80},{64,96},{80,112},{96,0},{112,16},{1... | collective-permute-start | bytes 589832 | tf_op jit(solution)/shard_map/ppermute | solution.py:108
  181.0 23.0 %collective-permute-start.26 = (bf16[1,128,384]{1,2,0:T(8,128)(2,1)S(1)}, bf16[1,128,384]{1,2,0:T(8,128)(2,1)S(1)}, u32[]{:S(2)}, u32[]{:S(2)}) collective-permute-start(bf16[1,128,384]{1,2,0:T(8,128)(2,1)S(1)} %get-tuple-element.25), channel_id=1, source_target_pairs={{0,12},{1,13},{2,14},{3,15},{4,0},{5,1},{6,2},{7,3},{8,4},{9,5},{1... | collective-permute-start | bytes 294920 | tf_op jit(solution)/shard_map/ppermute | solution.py:108
  183.7 28.1 %collective-permute-start.25 = (bf16[1,128,384]{1,2,0:T(8,128)(2,1)S(1)}, bf16[1,128,384]{1,2,0:T(8,128)(2,1)S(1)}, u32[]{:S(2)}, u32[]{:S(2)}) collective-permute-start(bf16[1,128,384]{1,2,0:T(8,128)(2,1)S(1)} %get-tuple-element.26), channel_id=1, source_target_pairs={{0,8},{1,9},{2,10},{3,11},{4,12},{5,13},{6,14},{7,15},{8,0},{9,1},... | collective-permute-start | bytes 294920 | tf_op jit(solution)/shard_map/ppermute | solution.py:108
  186.7 25.1 %collective-permute-start.24 = (bf16[1,128,384]{1,2,0:T(8,128)(2,1)S(1)}, bf16[1,128,384]{1,2,0:T(8,128)(2,1)S(1)}, u32[]{:S(2)}, u32[]{:S(2)}) collective-permute-start(bf16[1,128,384]{1,2,0:T(8,128)(2,1)S(1)} %get-tuple-element.24), channel_id=1, source_target_pairs={{0,4},{1,5},{2,6},{3,7},{4,8},{5,9},{6,10},{7,11},{8,12},{9,13},{1... | collective-permute-start | bytes 294920 | tf_op jit(solution)/shard_map/ppermute | solution.py:108
  192.0 20.5 %collective-permute-start.33 = (bf16[1,64,384]{2,1,0:T(8,128)(2,1)S(1)}, bf16[1,64,384]{2,1,0:T(8,128)(2,1)S(1)}, u32[]{:S(2)}, u32[]{:S(2)}) collective-permute-start(bf16[1,64,384]{2,1,0:T(8,128)(2,1)S(1)} %get-tuple-element.32), channel_id=1, source_target_pairs={{0,384},{16,400},{32,416},{48,432},{64,448},{80,464},{96,480},{112... | collective-permute-start | bytes 147464 | tf_op jit(solution)/shard_map/ppermute | solution.py:108
  194.0 18.6 %collective-permute-start.32 = (bf16[1,64,384]{2,1,0:T(8,128)(2,1)S(1)}, bf16[1,64,384]{2,1,0:T(8,128)(2,1)S(1)}, u32[]{:S(2)}, u32[]{:S(2)}) collective-permute-start(bf16[1,64,384]{2,1,0:T(8,128)(2,1)S(1)} %get-tuple-element.33), channel_id=1, source_target_pairs={{0,256},{16,272},{32,288},{48,304},{64,320},{80,336},{96,352},{112... | collective-permute-start | bytes 147464 | tf_op jit(solution)/shard_map/ppermute | solution.py:108
  204.0 10.1 %collective-permute-start.31 = (bf16[1,64,384]{2,1,0:T(8,128)(2,1)S(1)}, bf16[1,64,384]{2,1,0:T(8,128)(2,1)S(1)}, u32[]{:S(2)}, u32[]{:S(2)}) collective-permute-start(bf16[1,64,384]{2,1,0:T(8,128)(2,1)S(1)} %get-tuple-element.31), channel_id=1, source_target_pairs={{0,128},{16,144},{32,160},{48,176},{64,192},{80,208},{96,224},{112... | collective-permute-start | bytes 147464 | tf_op jit(solution)/shard_map/ppermute | solution.py:108
  (7 other events, 105.7 us)

commit v9 on v8

--- a/solution.py
+++ b/solution.py
@@ -158,17 +158,21 @@
     fsdp_count = lax.axis_size("fsdp")
     seq_radices = (lax.axis_size("core"),) + radices_for(lax.axis_size("z"))
     fsdp_radices = radices_for(fsdp_count)
-    weight_cat = exchange_gather(
-        jnp.concatenate([w_query, w_key, w_value], axis=1), SEQ, seq_radices
-    ).reshape(-1, 3 * columns)
-    projected = jnp.dot(tokens, weight_cat, preferred_element_type=jnp.float32)
-    projected = projected.astype(jnp.bfloat16)
-    queries = projected[:, :columns].reshape(SEG, heads_here, HDIM)
-    key_heads = projected[:, columns : 2 * columns].reshape(SEG, heads_here, HDIM)
-    value_heads = projected[:, 2 * columns :].reshape(SEG, heads_here, HDIM)
+    pair_cat = exchange_gather(
+        jnp.concatenate([w_key, w_value], axis=1), SEQ, seq_radices
+    ).reshape(-1, 2 * columns)
+    pair_projected = jnp.dot(tokens, pair_cat, preferred_element_type=jnp.float32)
+    pair_projected = pair_projected.astype(jnp.bfloat16)
+    key_heads = pair_projected[:, :columns].reshape(SEG, heads_here, HDIM)
+    value_heads = pair_projected[:, columns:].reshape(SEG, heads_here, HDIM)
     increment = jnp.einsum(
         "thd,the->hde", key_heads, value_heads, preferred_element_type=jnp.float32
     )
+    query_rows, increment = lax.optimization_barrier((w_query, increment))
+    query_cat = exchange_gather(query_rows, SEQ, seq_radices).reshape(-1, columns)
+    queries = jnp.dot(tokens, query_cat, preferred_element_type=jnp.float32)
+    queries = queries.astype(jnp.bfloat16).reshape(SEG, heads_here, HDIM)
+    weight_cat = jnp.concatenate([query_cat, pair_cat], axis=1)
     state = entering(increment, False)
     state_low = state.astype(jnp.bfloat16)
     scores = jnp.einsum("shd,thd->hst", queries, key_heads, preferred_element_type=jnp.float32)

time: 218 us -> 237 us (1.087)
  starting transfers between devices: 138 us -> 163 us
  waiting for transfers between devices: 47.1 us -> 40.7 us
    ppermute x7 -> x14, starting transfers between devices: 37.7 us -> 64.2 us  [exchange_gather(): lax.ppermute(current, axis, digit_pairs(count, stride, radix, offset))]
    ppermute x7 -> x14, waiting for transfers between devices: 19.3 us -> 15.9 us  [exchange_gather(): lax.ppermute(current, axis, digit_pairs(count, stride, radix, offset))]
    ppermute x12, waiting for transfers between devices: 23.8 us -> 20.7 us  [entering(): parts.append(lax.ppermute(total, 'z', pairs))]
  transfers between devices with their start and end apart: 34 -> 41, of which waited for: 16 -> 15; matrix products, arithmetic and copies ran while one was open for 7% -> 7% of each run, Pallas kernels for 0% -> 0%
where the time goes in v9:
time: 237 us; the launch traced here: 233 us
  starting transfers between devices  163 us (69%)
  waiting for transfers between devices  40.7 us (17%)
  local copies, waits for them, and re-layouts  11.8 us (5%)
  matrix products  9.39 us (4%)
  other arithmetic  6.92 us (3%)
    ppermute x14, starting transfers between devices, exchange_gather(): lax.ppermute(current, axis, digit_pairs(count, stride, radix, offset))  64.2 us
    ppermute x13, starting transfers between devices, exchange_scatter(): lax.ppermute(away.astype(jnp.bfloat16), axis, digit_pairs(count, stride,...  61.1 us
    ppermute x12, starting transfers between devices, entering(): parts.append(lax.ppermute(total, 'z', pairs))  33.3 us
    ppermute x12, waiting for transfers between devices, entering(): parts.append(lax.ppermute(total, 'z', pairs))  20.7 us
    ppermute x14, waiting for transfers between devices, exchange_gather(): lax.ppermute(current, axis, digit_pairs(count, stride, radix, offset))  15.9 us
    dynamic_slice x3, local copies, waits for them, and re-layouts, exchange_scatter(): away = lax.dynamic_index_in_dim(split, (digit + offset) % radix, 1, False)  4.78 us
  transfers between devices with their start and end apart: 41, of which 15 were waited for; matrix products, arithmetic and copies ran while one was open for 7% of the time, Pallas kernels for 0%

profile of v9, /device:TPU:6, one launch (start us, length us, event | category | flops | bytes accessed | tf_op | source)
XLA Modules:
  0.0 233.5 jit_solution(16326509103012734991)
XLA Ops:
  1.5 12.7 %collective-permute-start = (bf16[1,64,256]{2,1,0:T(8,128)(2,1)S(1)}, bf16[1,64,256]{2,1,0:T(8,128)(2,1)S(1)}, u32[]{:S(2)}, u32[]{:S(2)}) collective-permute-start(bf16[1,64,256]{2,1,0:T(8,128)(2,1)S(1)} %maximum_bitcast_fusion.2), channel_id=1, source_target_pairs={{0,384},{16,400},{32,416},{48,432},{64,448},{80,464},{96,480},{112... | collective-permute-start | bytes 98312 | tf_op jit(solution)/shard_map/ppermute | solution.py:84
  14.2 4.9 %collective-permute-start.1 = (bf16[1,64,256]{2,1,0:T(8,128)(2,1)S(1)}, bf16[1,64,256]{2,1,0:T(8,128)(2,1)S(1)}, u32[]{:S(2)}, u32[]{:S(2)}) collective-permute-start(bf16[1,64,256]{2,1,0:T(8,128)(2,1)S(1)} %maximum_bitcast_fusion.2), channel_id=1, source_target_pairs={{0,256},{16,272},{32,288},{48,304},{64,320},{80,336},{96,352},{112... | collective-permute-start | bytes 98312 | tf_op jit(solution)/shard_map/ppermute | solution.py:84
  19.2 7.8 %collective-permute-start.2 = (bf16[1,64,256]{2,1,0:T(8,128)(2,1)S(1)}, bf16[1,64,256]{2,1,0:T(8,128)(2,1)S(1)}, u32[]{:S(2)}, u32[]{:S(2)}) collective-permute-start(bf16[1,64,256]{2,1,0:T(8,128)(2,1)S(1)} %maximum_bitcast_fusion.2), channel_id=1, source_target_pairs={{0,128},{16,144},{32,160},{48,176},{64,192},{80,208},{96,224},{112... | collective-permute-start | bytes 98312 | tf_op jit(solution)/shard_map/ppermute | solution.py:84
  32.0 4.6 %collective-permute-start.3 = (bf16[4,64,256]{2,1,0:T(8,128)(2,1)S(1)}, bf16[4,64,256]{2,1,0:T(8,128)(2,1)S(1)}, u32[]{:S(2)}, u32[]{:S(2)}) collective-permute-start(bf16[4,64,256]{2,1,0:T(8,128)(2,1)S(1)} %maximum_bitcast_fusion), channel_id=1, source_target_pairs={{0,96},{16,112},{32,0},{48,16},{64,32},{80,48},{96,64},{112,80},{1... | collective-permute-start | bytes 393224 | tf_op jit(solution)/shard_map/ppermute | solution.py:84
  41.2 7.5 %collective-permute-done.4 = bf16[4,64,256]{2,1,0:T(8,128)(2,1)S(1)} collective-permute-done((bf16[4,64,256]{2,1,0:T(8,128)(2,1)S(1)}, bf16[4,64,256]{2,1,0:T(8,128)(2,1)S(1)}, u32[]{:S(2)}, u32[]{:S(2)}) %collective-permute-start.4) | collective-permute-done | bytes 131104 | tf_op jit(solution)/shard_map/ppermute | solution.py:84
  54.0 4.7 %collective-permute-start.14 = (bf16[1,64,128]{2,1,0:T(8,128)(2,1)S(1)}, bf16[1,64,128]{2,1,0:T(8,128)(2,1)S(1)}, u32[]{:S(2)}, u32[]{:S(2)}) collective-permute-start(bf16[1,64,128]{2,1,0:T(8,128)(2,1)S(1)} %bitcast.233), channel_id=1, source_target_pairs={{0,384},{16,400},{32,416},{48,432},{64,448},{80,464},{96,480},{112... | collective-permute-start | bytes 49160 | tf_op jit(solution)/shard_map/ppermute | solution.py:84
  58.7 8.0 %collective-permute-start.15 = (bf16[1,64,128]{2,1,0:T(8,128)(2,1)S(1)}, bf16[1,64,128]{2,1,0:T(8,128)(2,1)S(1)}, u32[]{:S(2)}, u32[]{:S(2)}) collective-permute-start(bf16[1,64,128]{2,1,0:T(8,128)(2,1)S(1)} %bitcast.234), channel_id=1, source_target_pairs={{0,256},{16,272},{32,288},{48,304},{64,320},{80,336},{96,352},{112... | collective-permute-start | bytes 49160 | tf_op jit(solution)/shard_map/ppermute | solution.py:84
  66.7 4.3 %collective-permute-start.16 = (bf16[1,64,128]{2,1,0:T(8,128)(2,1)S(1)}, bf16[1,64,128]{2,1,0:T(8,128)(2,1)S(1)}, u32[]{:S(2)}, u32[]{:S(2)}) collective-permute-start(bf16[1,64,128]{2,1,0:T(8,128)(2,1)S(1)} %bitcast.235), channel_id=1, source_target_pairs={{0,128},{16,144},{32,160},{48,176},{64,192},{80,208},{96,224},{112... | collective-permute-start | bytes 49160 | tf_op jit(solution)/shard_map/ppermute | solution.py:84
  73.1 3.2 %collective-permute-done.16 = bf16[1,64,128]{2,1,0:T(8,128)(2,1)S(1)} collective-permute-done((bf16[1,64,128]{2,1,0:T(8,128)(2,1)S(1)}, bf16[1,64,128]{2,1,0:T(8,128)(2,1)S(1)}, u32[]{:S(2)}, u32[]{:S(2)}) %collective-permute-start.16) | collective-permute-done | bytes 16416 | tf_op jit(solution)/shard_map/ppermute | solution.py:84
  76.3 2.8 %collective-permute-start.17 = (bf16[4,64,128]{2,1,0:T(8,128)(2,1)S(1)}, bf16[4,64,128]{2,1,0:T(8,128)(2,1)S(1)}, u32[]{:S(2)}, u32[]{:S(2)}) collective-permute-start(bf16[4,64,128]{2,1,0:T(8,128)(2,1)S(1)} %maximum_bitcast_fusion.1), channel_id=1, source_target_pairs={{0,96},{16,112},{32,0},{48,16},{64,32},{80,48},{96,64},{112,80},{1... | collective-permute-start | bytes 196616 | tf_op jit(solution)/shard_map/ppermute | solution.py:84
  79.1 2.3 collective-permute-start.18
  81.3 3.9 %collective-permute-start.19 = (bf16[4,64,128]{2,1,0:T(8,128)(2,1)S(1)}, bf16[4,64,128]{2,1,0:T(8,128)(2,1)S(1)}, u32[]{:S(2)}, u32[]{:S(2)}) collective-permute-start(bf16[4,64,128]{2,1,0:T(8,128)(2,1)S(1)} %maximum_bitcast_fusion.1), channel_id=1, source_target_pairs={{0,32},{16,48},{32,64},{48,80},{64,96},{80,112},{96,0},{112,16},{1... | collective-permute-start | bytes 196616 | tf_op jit(solution)/shard_map/ppermute | solution.py:84
  85.6 3.7 %collective-permute-start.10 = (f32[1,128,128]{2,1,0:T(8,128)S(1)}, f32[1,128,128]{2,1,0:T(8,128)S(1)}, u32[]{:S(2)}, u32[]{:S(2)}) collective-permute-start(f32[1,128,128]{2,1,0:T(8,128)S(1)} %add.391), channel_id=1, source_target_pairs={{0,96},{32,128},{64,160},{96,192},{128,224},{160,256},{192,288},{2... | collective-permute-start | bytes 196616 | tf_op jit(solution)/shard_map/ppermute | solution.py:35
  89.3 4.1 %collective-permute-start.9 = (f32[1,128,128]{2,1,0:T(8,128)S(1)}, f32[1,128,128]{2,1,0:T(8,128)S(1)}, u32[]{:S(2)}, u32[]{:S(2)}) collective-permute-start(f32[1,128,128]{2,1,0:T(8,128)S(1)} %add.391), channel_id=1, source_target_pairs={{0,64},{32,96},{64,128},{96,160},{128,192},{160,224},{192,256},{22... | collective-permute-start | bytes 196616 | tf_op jit(solution)/shard_map/ppermute | solution.py:35
  93.5 2.6 %collective-permute-start.8 = (f32[1,128,128]{2,1,0:T(8,128)S(1)}, f32[1,128,128]{2,1,0:T(8,128)S(1)}, u32[]{:S(2)}, u32[]{:S(2)}) collective-permute-start(f32[1,128,128]{2,1,0:T(8,128)S(1)} %add.391), channel_id=1, source_target_pairs={{0,32},{32,64},{64,96},{96,128},{128,160},{160,192},{192,224},{224... | collective-permute-start | bytes 196616 | tf_op jit(solution)/shard_map/ppermute | solution.py:35
  98.2 6.6 %collective-permute-start.13 = (f32[1,128,128]{2,1,0:T(8,128)S(1)}, f32[1,128,128]{2,1,0:T(8,128)S(1)}, u32[]{:S(2)}, u32[]{:S(2)}) collective-permute-start(f32[1,128,128]{2,1,0:T(8,128)S(1)} %add_add_fusion.1), channel_id=1, source_target_pairs={{0,384},{32,416},{64,448},{96,480},{1,385},{33,417},{65,449},{97,4... | collective-permute-start | bytes 196616 | tf_op jit(solution)/shard_map/ppermute | solution.py:35
  104.8 4.9 %collective-permute-start.12 = (f32[1,128,128]{2,1,0:T(8,128)S(1)}, f32[1,128,128]{2,1,0:T(8,128)S(1)}, u32[]{:S(2)}, u32[]{:S(2)}) collective-permute-start(f32[1,128,128]{2,1,0:T(8,128)S(1)} %add_add_fusion.1), channel_id=1, source_target_pairs={{0,256},{32,288},{64,320},{96,352},{128,384},{160,416},{192,448},{... | collective-permute-start | bytes 196616 | tf_op jit(solution)/shard_map/ppermute | solution.py:35
  109.7 3.7 %collective-permute-start.11 = (f32[1,128,128]{2,1,0:T(8,128)S(1)}, f32[1,128,128]{2,1,0:T(8,128)S(1)}, u32[]{:S(2)}, u32[]{:S(2)}) collective-permute-start(f32[1,128,128]{2,1,0:T(8,128)S(1)} %add_add_fusion.1), channel_id=1, source_target_pairs={{0,128},{32,160},{64,192},{96,224},{128,256},{160,288},{192,320},{... | collective-permute-start | bytes 196616 | tf_op jit(solution)/shard_map/ppermute | solution.py:35
  125.1 3.9 %collective-permute-done.24 = f32[1,128,128]{2,1,0:T(8,128)S(1)} collective-permute-done((f32[1,128,128]{2,1,0:T(8,128)S(1)}, f32[1,128,128]{2,1,0:T(8,128)S(1)}, u32[]{:S(2)}, u32[]{:S(2)}) %collective-permute-start.24) | collective-permute-done | bytes 65568 | tf_op jit(solution)/shard_map/ppermute | solution.py:35
  135.7 12.1 %collective-permute-done.27 = f32[1,128,128]{2,1,0:T(8,128)S(1)} collective-permute-done((f32[1,128,128]{2,1,0:T(8,128)S(1)}, f32[1,128,128]{2,1,0:T(8,128)S(1)}, u32[]{:S(2)}, u32[]{:S(2)}) %collective-permute-start.27) | collective-permute-done | bytes 65568 | tf_op jit(solution)/shard_map/ppermute | solution.py:35
  157.2 2.5 %convolution_convert_fusion.1 = bf16[2048,384]{1,0:T(8,128)(2,1)S(1)} fusion(bf16[2048,256]{1,0:T(8,128)(2,1)} %bitcast.229, bf16[2048,128]{1,0:T(8,128)(2,1)} %bitcast.224, bf16[384,128]{0,1:T(8,128)(2,1)S(1)} %fusion.13, bf16[384,128]{0,1:T(8,128)(2,1)S(1)} %fusion.14, bf16[384,128]{0,1:T(8,128)(2,1)S(1)} %fusion.15), kind=kOutput, calls=%fused_computation.1 | convolution fusion | flops 608796672 | bytes 3440640 | tf_op jit(solution)/shard_map/dot_general | solution.py:214
  162.6 4.8 %collective-permute-start.30 = (bf16[4,128,384]{1,2,0:T(8,128)(2,1)}, bf16[4,128,384]{1,2,0:T(8,128)(2,1)}, u32[]{:S(2)}, u32[]{:S(2)}) collective-permute-start(bf16[4,128,384]{1,2,0:T(8,128)(2,1)} %bitcast.232), channel_id=1, source_target_pairs={{0,3},{1,0},{2,1},{3,2},{4,7},{5,4},{6,5},{7,6},{8,11},{9,8},{10,9... | collective-permute-start | bytes 1179656 | tf_op jit(solution)/shard_map/ppermute | solution.py:108
  169.4 2.6 %collective-permute-start.29 = (bf16[4,128,384]{1,2,0:T(8,128)(2,1)}, bf16[4,128,384]{1,2,0:T(8,128)(2,1)}, u32[]{:S(2)}, u32[]{:S(2)}) collective-permute-start(bf16[4,128,384]{1,2,0:T(8,128)(2,1)} %bitcast.230), channel_id=1, source_target_pairs={{0,2},{1,3},{2,0},{3,1},{4,6},{5,7},{6,4},{7,5},{8,10},{9,11},{10,... | collective-permute-start | bytes 1179656 | tf_op jit(solution)/shard_map/ppermute | solution.py:108
  172.9 2.8 %collective-permute-start.28 = (bf16[4,128,384]{1,2,0:T(8,128)(2,1)}, bf16[4,128,384]{1,2,0:T(8,128)(2,1)}, u32[]{:S(2)}, u32[]{:S(2)}) collective-permute-start(bf16[4,128,384]{1,2,0:T(8,128)(2,1)} %bitcast.231), channel_id=1, source_target_pairs={{0,1},{1,2},{2,3},{3,0},{4,5},{5,6},{6,7},{7,4},{8,9},{9,10},{10,1... | collective-permute-start | bytes 1179656 | tf_op jit(solution)/shard_map/ppermute | solution.py:108
  178.4 13.4 %collective-permute-start.37 = (bf16[4,64,384]{2,1,0:T(8,128)(2,1)S(1)}, bf16[4,64,384]{2,1,0:T(8,128)(2,1)S(1)}, u32[]{:S(2)}, u32[]{:S(2)}) collective-permute-start(bf16[4,64,384]{2,1,0:T(8,128)(2,1)S(1)} %get-tuple-element.20), channel_id=1, source_target_pairs={{0,96},{16,112},{32,0},{48,16},{64,32},{80,48},{96,64},{112,80},{1... | collective-permute-start | bytes 589832 | tf_op jit(solution)/shard_map/ppermute | solution.py:108
  193.8 2.5 %collective-permute-start.35 = (bf16[4,64,384]{2,1,0:T(8,128)(2,1)S(1)}, bf16[4,64,384]{2,1,0:T(8,128)(2,1)S(1)}, u32[]{:S(2)}, u32[]{:S(2)}) collective-permute-start(bf16[4,64,384]{2,1,0:T(8,128)(2,1)S(1)} %get-tuple-element.19), channel_id=1, source_target_pairs={{0,32},{16,48},{32,64},{48,80},{64,96},{80,112},{96,0},{112,16},{1... | collective-permute-start | bytes 589832 | tf_op jit(solution)/shard_map/ppermute | solution.py:108
  197.8 2.8 %collective-permute-start.33 = (bf16[1,128,384]{1,2,0:T(8,128)(2,1)S(1)}, bf16[1,128,384]{1,2,0:T(8,128)(2,1)S(1)}, u32[]{:S(2)}, u32[]{:S(2)}) collective-permute-start(bf16[1,128,384]{1,2,0:T(8,128)(2,1)S(1)} %get-tuple-element.29), channel_id=1, source_target_pairs={{0,12},{1,13},{2,14},{3,15},{4,0},{5,1},{6,2},{7,3},{8,4},{9,5},{1... | collective-permute-start | bytes 294920 | tf_op jit(solution)/shard_map/ppermute | solution.py:108
  200.6 3.0 %collective-permute-start.32 = (bf16[1,128,384]{1,2,0:T(8,128)(2,1)S(1)}, bf16[1,128,384]{1,2,0:T(8,128)(2,1)S(1)}, u32[]{:S(2)}, u32[]{:S(2)}) collective-permute-start(bf16[1,128,384]{1,2,0:T(8,128)(2,1)S(1)} %get-tuple-element.30), channel_id=1, source_target_pairs={{0,8},{1,9},{2,10},{3,11},{4,12},{5,13},{6,14},{7,15},{8,0},{9,1},... | collective-permute-start | bytes 294920 | tf_op jit(solution)/shard_map/ppermute | solution.py:108
  203.6 4.0 %collective-permute-start.31 = (bf16[1,128,384]{1,2,0:T(8,128)(2,1)S(1)}, bf16[1,128,384]{1,2,0:T(8,128)(2,1)S(1)}, u32[]{:S(2)}, u32[]{:S(2)}) collective-permute-start(bf16[1,128,384]{1,2,0:T(8,128)(2,1)S(1)} %get-tuple-element.28), channel_id=1, source_target_pairs={{0,4},{1,5},{2,6},{3,7},{4,8},{5,9},{6,10},{7,11},{8,12},{9,13},{1... | collective-permute-start | bytes 294920 | tf_op jit(solution)/shard_map/ppermute | solution.py:108
  208.8 5.7 %collective-permute-start.40 = (bf16[1,64,384]{2,1,0:T(8,128)(2,1)S(1)}, bf16[1,64,384]{2,1,0:T(8,128)(2,1)S(1)}, u32[]{:S(2)}, u32[]{:S(2)}) collective-permute-start(bf16[1,64,384]{2,1,0:T(8,128)(2,1)S(1)} %get-tuple-element.38), channel_id=1, source_target_pairs={{0,384},{16,400},{32,416},{48,432},{64,448},{80,464},{96,480},{112... | collective-permute-start | bytes 147464 | tf_op jit(solution)/shard_map/ppermute | solution.py:108
  214.5 7.8 %collective-permute-start.39 = (bf16[1,64,384]{2,1,0:T(8,128)(2,1)S(1)}, bf16[1,64,384]{2,1,0:T(8,128)(2,1)S(1)}, u32[]{:S(2)}, u32[]{:S(2)}) collective-permute-start(bf16[1,64,384]{2,1,0:T(8,128)(2,1)S(1)} %get-tuple-element.39), channel_id=1, source_target_pairs={{0,256},{16,272},{32,288},{48,304},{64,320},{80,336},{96,352},{112... | collective-permute-start | bytes 147464 | tf_op jit(solution)/shard_map/ppermute | solution.py:108
  222.3 7.8 %collective-permute-start.38 = (bf16[1,64,384]{2,1,0:T(8,128)(2,1)S(1)}, bf16[1,64,384]{2,1,0:T(8,128)(2,1)S(1)}, u32[]{:S(2)}, u32[]{:S(2)}) collective-permute-start(bf16[1,64,384]{2,1,0:T(8,128)(2,1)S(1)} %get-tuple-element.37), channel_id=1, source_target_pairs={{0,128},{16,144},{32,160},{48,176},{64,192},{80,208},{96,224},{112... | collective-permute-start | bytes 147464 | tf_op jit(solution)/shard_map/ppermute | solution.py:108
  (130 shorter events, 63.4 us)
Async XLA Ops:
  1.5 25.6 %collective-permute-start = (bf16[1,64,256]{2,1,0:T(8,128)(2,1)S(1)}, bf16[1,64,256]{2,1,0:T(8,128)(2,1)S(1)}, u32[]{:S(2)}, u32[]{:S(2)}) collective-permute-start(bf16[1,64,256]{2,1,0:T(8,128)(2,1)S(1)} %maximum_bitcast_fusion.2), channel_id=1, source_target_pairs={{0,384},{16,400},{32,416},{48,432},{64,448},{80,464},{96,480},{112... | collective-permute-start | bytes 98312 | tf_op jit(solution)/shard_map/ppermute | solution.py:84
  14.2 14.7 %collective-permute-start.1 = (bf16[1,64,256]{2,1,0:T(8,128)(2,1)S(1)}, bf16[1,64,256]{2,1,0:T(8,128)(2,1)S(1)}, u32[]{:S(2)}, u32[]{:S(2)}) collective-permute-start(bf16[1,64,256]{2,1,0:T(8,128)(2,1)S(1)} %maximum_bitcast_fusion.2), channel_id=1, source_target_pairs={{0,256},{16,272},{32,288},{48,304},{64,320},{80,336},{96,352},{112... | collective-permute-start | bytes 98312 | tf_op jit(solution)/shard_map/ppermute | solution.py:84
  19.2 11.3 %collective-permute-start.2 = (bf16[1,64,256]{2,1,0:T(8,128)(2,1)S(1)}, bf16[1,64,256]{2,1,0:T(8,128)(2,1)S(1)}, u32[]{:S(2)}, u32[]{:S(2)}) collective-permute-start(bf16[1,64,256]{2,1,0:T(8,128)(2,1)S(1)} %maximum_bitcast_fusion.2), channel_id=1, source_target_pairs={{0,128},{16,144},{32,160},{48,176},{64,192},{80,208},{96,224},{112... | collective-permute-start | bytes 98312 | tf_op jit(solution)/shard_map/ppermute | solution.py:84
  36.6 12.1 %collective-permute-start.4 = (bf16[4,64,256]{2,1,0:T(8,128)(2,1)S(1)}, bf16[4,64,256]{2,1,0:T(8,128)(2,1)S(1)}, u32[]{:S(2)}, u32[]{:S(2)}) collective-permute-start(bf16[4,64,256]{2,1,0:T(8,128)(2,1)S(1)} %maximum_bitcast_fusion), channel_id=1, source_target_pairs={{0,64},{16,80},{32,96},{48,112},{64,0},{80,16},{96,32},{112,48},{1... | collective-permute-start | bytes 393224 | tf_op jit(solution)/shard_map/ppermute | solution.py:84
  38.8 9.8 %collective-permute-start.5 = (bf16[4,64,256]{2,1,0:T(8,128)(2,1)S(1)}, bf16[4,64,256]{2,1,0:T(8,128)(2,1)S(1)}, u32[]{:S(2)}, u32[]{:S(2)}) collective-permute-start(bf16[4,64,256]{2,1,0:T(8,128)(2,1)S(1)} %maximum_bitcast_fusion), channel_id=1, source_target_pairs={{0,32},{16,48},{32,64},{48,80},{64,96},{80,112},{96,0},{112,16},{1... | collective-permute-start | bytes 393224 | tf_op jit(solution)/shard_map/ppermute | solution.py:84
  54.0 19.0 %collective-permute-start.14 = (bf16[1,64,128]{2,1,0:T(8,128)(2,1)S(1)}, bf16[1,64,128]{2,1,0:T(8,128)(2,1)S(1)}, u32[]{:S(2)}, u32[]{:S(2)}) collective-permute-start(bf16[1,64,128]{2,1,0:T(8,128)(2,1)S(1)} %bitcast.233), channel_id=1, source_target_pairs={{0,384},{16,400},{32,416},{48,432},{64,448},{80,464},{96,480},{112... | collective-permute-start | bytes 49160 | tf_op jit(solution)/shard_map/ppermute | solution.py:84
  58.7 14.4 %collective-permute-start.15 = (bf16[1,64,128]{2,1,0:T(8,128)(2,1)S(1)}, bf16[1,64,128]{2,1,0:T(8,128)(2,1)S(1)}, u32[]{:S(2)}, u32[]{:S(2)}) collective-permute-start(bf16[1,64,128]{2,1,0:T(8,128)(2,1)S(1)} %bitcast.234), channel_id=1, source_target_pairs={{0,256},{16,272},{32,288},{48,304},{64,320},{80,336},{96,352},{112... | collective-permute-start | bytes 49160 | tf_op jit(solution)/shard_map/ppermute | solution.py:84
  66.7 9.5 %collective-permute-start.16 = (bf16[1,64,128]{2,1,0:T(8,128)(2,1)S(1)}, bf16[1,64,128]{2,1,0:T(8,128)(2,1)S(1)}, u32[]{:S(2)}, u32[]{:S(2)}) collective-permute-start(bf16[1,64,128]{2,1,0:T(8,128)(2,1)S(1)} %bitcast.235), channel_id=1, source_target_pairs={{0,128},{16,144},{32,160},{48,176},{64,192},{80,208},{96,224},{112... | collective-permute-start | bytes 49160 | tf_op jit(solution)/shard_map/ppermute | solution.py:84
  71.0 14.6 %collective-permute-start.7 = (f32[1,128,128]{2,1,0:T(8,128)S(1)}, f32[1,128,128]{2,1,0:T(8,128)S(1)}, u32[]{:S(2)}, u32[]{:S(2)}) collective-permute-start(f32[1,128,128]{2,1,0:T(8,128)S(1)} %convolution_bitcast_fusion.1), channel_id=1, source_target_pairs={{0,16},{16,0},{1,17},{17,1},{2,18},{18,2},{3,19},{19,3},{4,20},{20... | collective-permute-start | bytes 196616 | tf_op jit(solution)/shard_map/ppermute | solution.py:21
  76.3 17.2 %collective-permute-start.17 = (bf16[4,64,128]{2,1,0:T(8,128)(2,1)S(1)}, bf16[4,64,128]{2,1,0:T(8,128)(2,1)S(1)}, u32[]{:S(2)}, u32[]{:S(2)}) collective-permute-start(bf16[4,64,128]{2,1,0:T(8,128)(2,1)S(1)} %maximum_bitcast_fusion.1), channel_id=1, source_target_pairs={{0,96},{16,112},{32,0},{48,16},{64,32},{80,48},{96,64},{112,80},{1... | collective-permute-start | bytes 196616 | tf_op jit(solution)/shard_map/ppermute | solution.py:84
  79.1 17.0 %collective-permute-start.18 = (bf16[4,64,128]{2,1,0:T(8,128)(2,1)S(1)}, bf16[4,64,128]{2,1,0:T(8,128)(2,1)S(1)}, u32[]{:S(2)}, u32[]{:S(2)}) collective-permute-start(bf16[4,64,128]{2,1,0:T(8,128)(2,1)S(1)} %maximum_bitcast_fusion.1), channel_id=1, source_target_pairs={{0,64},{16,80},{32,96},{48,112},{64,0},{80,16},{96,32},{112,48},{1... | collective-permute-start | bytes 196616 | tf_op jit(solution)/shard_map/ppermute | solution.py:84
  81.3 14.7 %collective-permute-start.19 = (bf16[4,64,128]{2,1,0:T(8,128)(2,1)S(1)}, bf16[4,64,128]{2,1,0:T(8,128)(2,1)S(1)}, u32[]{:S(2)}, u32[]{:S(2)}) collective-permute-start(bf16[4,64,128]{2,1,0:T(8,128)(2,1)S(1)} %maximum_bitcast_fusion.1), channel_id=1, source_target_pairs={{0,32},{16,48},{32,64},{48,80},{64,96},{80,112},{96,0},{112,16},{1... | collective-permute-start | bytes 196616 | tf_op jit(solution)/shard_map/ppermute | solution.py:84
  85.6 12.5 %collective-permute-start.10 = (f32[1,128,128]{2,1,0:T(8,128)S(1)}, f32[1,128,128]{2,1,0:T(8,128)S(1)}, u32[]{:S(2)}, u32[]{:S(2)}) collective-permute-start(f32[1,128,128]{2,1,0:T(8,128)S(1)} %add.391), channel_id=1, source_target_pairs={{0,96},{32,128},{64,160},{96,192},{128,224},{160,256},{192,288},{2... | collective-permute-start | bytes 196616 | tf_op jit(solution)/shard_map/ppermute | solution.py:35
  96.2 19.1 %collective-permute-start.20 = (bf16[16,64,128]{2,1,0:T(8,128)(2,1)S(1)}, bf16[16,64,128]{2,1,0:T(8,128)(2,1)S(1)}, u32[]{:S(2)}, u32[]{:S(2)}) collective-permute-start(bf16[16,64,128]{2,1,0:T(8,128)(2,1)S(1)} %bitcast.227), channel_id=1, source_target_pairs={{0,16},{16,0},{32,48},{48,32},{64,80},{80,64},{96,112},{112,96},{1... | collective-permute-start | bytes 786440 | tf_op jit(solution)/shard_map/ppermute | solution.py:84
  98.2 15.9 %collective-permute-start.13 = (f32[1,128,128]{2,1,0:T(8,128)S(1)}, f32[1,128,128]{2,1,0:T(8,128)S(1)}, u32[]{:S(2)}, u32[]{:S(2)}) collective-permute-start(f32[1,128,128]{2,1,0:T(8,128)S(1)} %add_add_fusion.1), channel_id=1, source_target_pairs={{0,384},{32,416},{64,448},{96,480},{1,385},{33,417},{65,449},{97,4... | collective-permute-start | bytes 196616 | tf_op jit(solution)/shard_map/ppermute | solution.py:35
  104.8 9.3 %collective-permute-start.12 = (f32[1,128,128]{2,1,0:T(8,128)S(1)}, f32[1,128,128]{2,1,0:T(8,128)S(1)}, u32[]{:S(2)}, u32[]{:S(2)}) collective-permute-start(f32[1,128,128]{2,1,0:T(8,128)S(1)} %add_add_fusion.1), channel_id=1, source_target_pairs={{0,256},{32,288},{64,320},{96,352},{128,384},{160,416},{192,448},{... | collective-permute-start | bytes 196616 | tf_op jit(solution)/shard_map/ppermute | solution.py:35
  131.6 16.2 %collective-permute-start.27 = (f32[1,128,128]{2,1,0:T(8,128)S(1)}, f32[1,128,128]{2,1,0:T(8,128)S(1)}, u32[]{:S(2)}, u32[]{:S(2)}) collective-permute-start(f32[1,128,128]{2,1,0:T(8,128)S(1)} %add_add_fusion), channel_id=1, source_target_pairs={{384,0},{416,32},{448,64},{480,96},{385,1},{417,33},{449,65},{481,... | collective-permute-start | bytes 196616 | tf_op jit(solution)/shard_map/ppermute | solution.py:35
  132.9 15.8 %collective-permute-start.26 = (f32[1,128,128]{2,1,0:T(8,128)S(1)}, f32[1,128,128]{2,1,0:T(8,128)S(1)}, u32[]{:S(2)}, u32[]{:S(2)}) collective-permute-start(f32[1,128,128]{2,1,0:T(8,128)S(1)} %add_add_fusion), channel_id=1, source_target_pairs={{256,0},{288,32},{320,64},{352,96},{384,128},{416,160},{448,192},{... | collective-permute-start | bytes 196616 | tf_op jit(solution)/shard_map/ppermute | solution.py:35
  134.2 14.5 %collective-permute-start.25 = (f32[1,128,128]{2,1,0:T(8,128)S(1)}, f32[1,128,128]{2,1,0:T(8,128)S(1)}, u32[]{:S(2)}, u32[]{:S(2)}) collective-permute-start(f32[1,128,128]{2,1,0:T(8,128)S(1)} %add_add_fusion), channel_id=1, source_target_pairs={{128,0},{160,32},{192,64},{224,96},{256,128},{288,160},{320,192},{... | collective-permute-start | bytes 196616 | tf_op jit(solution)/shard_map/ppermute | solution.py:35
  154.2 22.8 %collective-permute-start.34 = (bf16[16,64,384]{2,1,0:T(8,128)(2,1)}, bf16[16,64,384]{2,1,0:T(8,128)(2,1)}, u32[]{:S(2)}, u32[]{:S(2)}) collective-permute-start(bf16[16,64,384]{2,1,0:T(8,128)(2,1)} %dynamic-slice_bitcast_fusion), channel_id=1, source_target_pairs={{0,16},{16,0},{32,48},{48,32},{64,80},{80,64},{96,112},{112,96},{1... | collective-permute-start | bytes 2359304 | tf_op jit(solution)/shard_map/ppermute | solution.py:108
  162.6 31.2 %collective-permute-start.30 = (bf16[4,128,384]{1,2,0:T(8,128)(2,1)}, bf16[4,128,384]{1,2,0:T(8,128)(2,1)}, u32[]{:S(2)}, u32[]{:S(2)}) collective-permute-start(bf16[4,128,384]{1,2,0:T(8,128)(2,1)} %bitcast.232), channel_id=1, source_target_pairs={{0,3},{1,0},{2,1},{3,2},{4,7},{5,4},{6,5},{7,6},{8,11},{9,8},{10,9... | collective-permute-start | bytes 1179656 | tf_op jit(solution)/shard_map/ppermute | solution.py:108
  169.4 26.9 %collective-permute-start.29 = (bf16[4,128,384]{1,2,0:T(8,128)(2,1)}, bf16[4,128,384]{1,2,0:T(8,128)(2,1)}, u32[]{:S(2)}, u32[]{:S(2)}) collective-permute-start(bf16[4,128,384]{1,2,0:T(8,128)(2,1)} %bitcast.230), channel_id=1, source_target_pairs={{0,2},{1,3},{2,0},{3,1},{4,6},{5,7},{6,4},{7,5},{8,10},{9,11},{10,... | collective-permute-start | bytes 1179656 | tf_op jit(solution)/shard_map/ppermute | solution.py:108
  172.9 23.4 %collective-permute-start.28 = (bf16[4,128,384]{1,2,0:T(8,128)(2,1)}, bf16[4,128,384]{1,2,0:T(8,128)(2,1)}, u32[]{:S(2)}, u32[]{:S(2)}) collective-permute-start(bf16[4,128,384]{1,2,0:T(8,128)(2,1)} %bitcast.231), channel_id=1, source_target_pairs={{0,1},{1,2},{2,3},{3,0},{4,5},{5,6},{6,7},{7,4},{8,9},{9,10},{10,1... | collective-permute-start | bytes 1179656 | tf_op jit(solution)/shard_map/ppermute | solution.py:108
  178.4 25.2 %collective-permute-start.37 = (bf16[4,64,384]{2,1,0:T(8,128)(2,1)S(1)}, bf16[4,64,384]{2,1,0:T(8,128)(2,1)S(1)}, u32[]{:S(2)}, u32[]{:S(2)}) collective-permute-start(bf16[4,64,384]{2,1,0:T(8,128)(2,1)S(1)} %get-tuple-element.20), channel_id=1, source_target_pairs={{0,96},{16,112},{32,0},{48,16},{64,32},{80,48},{96,64},{112,80},{1... | collective-permute-start | bytes 589832 | tf_op jit(solution)/shard_map/ppermute | solution.py:108
  191.8 16.9 %collective-permute-start.36 = (bf16[4,64,384]{2,1,0:T(8,128)(2,1)S(1)}, bf16[4,64,384]{2,1,0:T(8,128)(2,1)S(1)}, u32[]{:S(2)}, u32[]{:S(2)}) collective-permute-start(bf16[4,64,384]{2,1,0:T(8,128)(2,1)S(1)} %get-tuple-element.21), channel_id=1, source_target_pairs={{0,64},{16,80},{32,96},{48,112},{64,0},{80,16},{96,32},{112,48},{1... | collective-permute-start | bytes 589832 | tf_op jit(solution)/shard_map/ppermute | solution.py:108
  193.8 14.9 %collective-permute-start.35 = (bf16[4,64,384]{2,1,0:T(8,128)(2,1)S(1)}, bf16[4,64,384]{2,1,0:T(8,128)(2,1)S(1)}, u32[]{:S(2)}, u32[]{:S(2)}) collective-permute-start(bf16[4,64,384]{2,1,0:T(8,128)(2,1)S(1)} %get-tuple-element.19), channel_id=1, source_target_pairs={{0,32},{16,48},{32,64},{48,80},{64,96},{80,112},{96,0},{112,16},{1... | collective-permute-start | bytes 589832 | tf_op jit(solution)/shard_map/ppermute | solution.py:108
  197.8 24.5 %collective-permute-start.33 = (bf16[1,128,384]{1,2,0:T(8,128)(2,1)S(1)}, bf16[1,128,384]{1,2,0:T(8,128)(2,1)S(1)}, u32[]{:S(2)}, u32[]{:S(2)}) collective-permute-start(bf16[1,128,384]{1,2,0:T(8,128)(2,1)S(1)} %get-tuple-element.29), channel_id=1, source_target_pairs={{0,12},{1,13},{2,14},{3,15},{4,0},{5,1},{6,2},{7,3},{8,4},{9,5},{1... | collective-permute-start | bytes 294920 | tf_op jit(solution)/shard_map/ppermute | solution.py:108
  200.6 29.5 %collective-permute-start.32 = (bf16[1,128,384]{1,2,0:T(8,128)(2,1)S(1)}, bf16[1,128,384]{1,2,0:T(8,128)(2,1)S(1)}, u32[]{:S(2)}, u32[]{:S(2)}) collective-permute-start(bf16[1,128,384]{1,2,0:T(8,128)(2,1)S(1)} %get-tuple-element.30), channel_id=1, source_target_pairs={{0,8},{1,9},{2,10},{3,11},{4,12},{5,13},{6,14},{7,15},{8,0},{9,1},... | collective-permute-start | bytes 294920 | tf_op jit(solution)/shard_map/ppermute | solution.py:108
  203.6 26.5 %collective-permute-start.31 = (bf16[1,128,384]{1,2,0:T(8,128)(2,1)S(1)}, bf16[1,128,384]{1,2,0:T(8,128)(2,1)S(1)}, u32[]{:S(2)}, u32[]{:S(2)}) collective-permute-start(bf16[1,128,384]{1,2,0:T(8,128)(2,1)S(1)} %get-tuple-element.28), channel_id=1, source_target_pairs={{0,4},{1,5},{2,6},{3,7},{4,8},{5,9},{6,10},{7,11},{8,12},{9,13},{1... | collective-permute-start | bytes 294920 | tf_op jit(solution)/shard_map/ppermute | solution.py:108
  208.8 22.0 %collective-permute-start.40 = (bf16[1,64,384]{2,1,0:T(8,128)(2,1)S(1)}, bf16[1,64,384]{2,1,0:T(8,128)(2,1)S(1)}, u32[]{:S(2)}, u32[]{:S(2)}) collective-permute-start(bf16[1,64,384]{2,1,0:T(8,128)(2,1)S(1)} %get-tuple-element.38), channel_id=1, source_target_pairs={{0,384},{16,400},{32,416},{48,432},{64,448},{80,464},{96,480},{112... | collective-permute-start | bytes 147464 | tf_op jit(solution)/shard_map/ppermute | solution.py:108
  214.5 16.4 %collective-permute-start.39 = (bf16[1,64,384]{2,1,0:T(8,128)(2,1)S(1)}, bf16[1,64,384]{2,1,0:T(8,128)(2,1)S(1)}, u32[]{:S(2)}, u32[]{:S(2)}) collective-permute-start(bf16[1,64,384]{2,1,0:T(8,128)(2,1)S(1)} %get-tuple-element.39), channel_id=1, source_target_pairs={{0,256},{16,272},{32,288},{48,304},{64,320},{80,336},{96,352},{112... | collective-permute-start | bytes 147464 | tf_op jit(solution)/shard_map/ppermute | solution.py:108
  222.3 10.5 %collective-permute-start.38 = (bf16[1,64,384]{2,1,0:T(8,128)(2,1)S(1)}, bf16[1,64,384]{2,1,0:T(8,128)(2,1)S(1)}, u32[]{:S(2)}, u32[]{:S(2)}) collective-permute-start(bf16[1,64,384]{2,1,0:T(8,128)(2,1)S(1)} %get-tuple-element.37), channel_id=1, source_target_pairs={{0,128},{16,144},{32,160},{48,176},{64,192},{80,208},{96,224},{112... | collective-permute-start | bytes 147464 | tf_op jit(solution)/shard_map/ppermute | solution.py:108
  (16 other events, 152.2 us)

commit v10 on v8

--- a/solution.py
+++ b/solution.py
@@ -92,25 +92,33 @@
     return current
 
 
-def exchange_scatter(term, axis, radices):
+def digit_major(array, radices, order):
+    rows = array.shape[-1] // math.prod(radices)
+    spread = array.reshape(array.shape[:-1] + tuple(reversed(radices)) + (rows,))
+    lead = array.ndim - 1
+    axes = list(range(lead)) + [lead + len(radices) - 1 - d for d in order] + [lead + len(radices)]
+    return spread.transpose(axes).reshape(array.shape)
+
+
+def exchange_scatter(term, axis, radices, order):
     count = math.prod(radices)
     place = lax.axis_index(axis)
     rows = term.shape[0] // count
     cols = term.shape[1]
     current = term.reshape(count, rows, cols)
-    stride = 1
-    for radix in radices:
+    for position in order:
+        radix = radices[position]
+        stride = math.prod(radices[:position])
         digit = (place // stride) % radix
-        split = current.reshape(-1, radix, rows, cols)
-        total = lax.dynamic_index_in_dim(split, digit, 1, False).astype(jnp.float32)
+        split = current.reshape(radix, -1, rows, cols)
+        total = lax.dynamic_index_in_dim(split, digit, 0, False).astype(jnp.float32)
         for offset in range(1, radix):
-            away = lax.dynamic_index_in_dim(split, (digit + offset) % radix, 1, False)
+            away = lax.dynamic_index_in_dim(split, (digit + offset) % radix, 0, False)
             moved = lax.ppermute(
                 away.astype(jnp.bfloat16), axis, digit_pairs(count, stride, radix, offset)
             )
             total = total + moved.astype(jnp.float32)
         current = total
-        stride *= radix
     return current.reshape(rows, cols)
 
 
@@ -212,14 +220,20 @@
         ).astype(jnp.bfloat16),
         "fsdp",
         fsdp_radices,
+        tuple(reversed(range(len(fsdp_radices)))),
     )
     grad_tokens = input_rows.T.astype(jnp.bfloat16)
+    seq_order = tuple(range(len(seq_radices)))
     weight_rows = exchange_scatter(
         lax.dot_general(
-            tokens, grad_cat, (((0,), (0,)), ((), ())), preferred_element_type=jnp.float32
+            digit_major(tokens, seq_radices, seq_order),
+            grad_cat,
+            (((0,), (0,)), ((), ())),
+            preferred_element_type=jnp.float32,
         ).astype(jnp.bfloat16),
         SEQ,
         seq_radices,
+        seq_order,
     )
     weight_rows = (weight_rows * (1.0 / math.sqrt(SEG * seq_count))).astype(jnp.bfloat16)
     return (

time: 218 us -> 217 us (level)
  the two profiles are of different devices: /device:TPU:6 before, /device:TPU:104 now
where the time goes in v10:
time: 217 us; the launch traced here: 215 us
  starting transfers between devices  117 us (54%)
  waiting for transfers between devices  70 us (32%)
  local copies, waits for them, and re-layouts  11.3 us (5%)
  matrix products  8.76 us (4%)
  other arithmetic  6.63 us (3%)
    ppermute x13, starting transfers between devices, exchange_scatter(): lax.ppermute(away.astype(jnp.bfloat16), axis, digit_pairs(count, stride,...  45.1 us
    ppermute x12, waiting for transfers between devices, entering(): parts.append(lax.ppermute(total, 'z', pairs))  38 us
    ppermute x7, starting transfers between devices, exchange_gather(): lax.ppermute(current, axis, digit_pairs(count, stride, radix, offset))  34.2 us
    ppermute x12, starting transfers between devices, entering(): parts.append(lax.ppermute(total, 'z', pairs))  33.3 us
    ppermute x7, waiting for transfers between devices, exchange_gather(): lax.ppermute(current, axis, digit_pairs(count, stride, radix, offset))  18.1 us
    ppermute x13, waiting for transfers between devices, exchange_scatter(): lax.ppermute(away.astype(jnp.bfloat16), axis, digit_pairs(count, stride,...  12.8 us
    unnamed x28, local copies, waits for them, and re-layouts  5.28 us
  transfers between devices with their start and end apart: 34, of which 17 were waited for; matrix products, arithmetic and copies ran while one was open for 6% of the time, Pallas kernels for 0%

profile of v10, /device:TPU:104, one launch (start us, length us, event | category | flops | bytes accessed | tf_op | source)
XLA Modules:
  0.0 215.3 jit_solution(506705944410037802)
XLA Ops:
  1.4 10.0 %collective-permute-start = (bf16[1,64,384]{2,1,0:T(8,128)(2,1)S(1)}, bf16[1,64,384]{2,1,0:T(8,128)(2,1)S(1)}, u32[]{:S(2)}, u32[]{:S(2)}) collective-permute-start(bf16[1,64,384]{2,1,0:T(8,128)(2,1)S(1)} %maximum_bitcast_fusion.1), channel_id=1, source_target_pairs={{0,384},{16,400},{32,416},{48,432},{64,448},{80,464},{96,480},{112... | collective-permute-start | bytes 147464 | tf_op jit(solution)/shard_map/ppermute | solution.py:84
  11.4 6.3 %collective-permute-start.1 = (bf16[1,64,384]{2,1,0:T(8,128)(2,1)S(1)}, bf16[1,64,384]{2,1,0:T(8,128)(2,1)S(1)}, u32[]{:S(2)}, u32[]{:S(2)}) collective-permute-start(bf16[1,64,384]{2,1,0:T(8,128)(2,1)S(1)} %maximum_bitcast_fusion.1), channel_id=1, source_target_pairs={{0,256},{16,272},{32,288},{48,304},{64,320},{80,336},{96,352},{112... | collective-permute-start | bytes 147464 | tf_op jit(solution)/shard_map/ppermute | solution.py:84
  17.8 6.4 %collective-permute-start.2 = (bf16[1,64,384]{2,1,0:T(8,128)(2,1)S(1)}, bf16[1,64,384]{2,1,0:T(8,128)(2,1)S(1)}, u32[]{:S(2)}, u32[]{:S(2)}) collective-permute-start(bf16[1,64,384]{2,1,0:T(8,128)(2,1)S(1)} %maximum_bitcast_fusion.1), channel_id=1, source_target_pairs={{0,128},{16,144},{32,160},{48,176},{64,192},{80,208},{96,224},{112... | collective-permute-start | bytes 147464 | tf_op jit(solution)/shard_map/ppermute | solution.py:84
  24.3 2.5 %collective-permute-done.1 = bf16[1,64,384]{2,1,0:T(8,128)(2,1)S(1)} collective-permute-done((bf16[1,64,384]{2,1,0:T(8,128)(2,1)S(1)}, bf16[1,64,384]{2,1,0:T(8,128)(2,1)S(1)}, u32[]{:S(2)}, u32[]{:S(2)}) %collective-permute-start.1) | collective-permute-done | bytes 49184 | tf_op jit(solution)/shard_map/ppermute | solution.py:84
  26.8 4.1 %collective-permute-done.2 = bf16[1,64,384]{2,1,0:T(8,128)(2,1)S(1)} collective-permute-done((bf16[1,64,384]{2,1,0:T(8,128)(2,1)S(1)}, bf16[1,64,384]{2,1,0:T(8,128)(2,1)S(1)}, u32[]{:S(2)}, u32[]{:S(2)}) %collective-permute-start.2) | collective-permute-done | bytes 49184 | tf_op jit(solution)/shard_map/ppermute | solution.py:84
  32.6 1.9 collective-permute-start.3
  34.5 2.3 %collective-permute-start.4 = (bf16[4,64,384]{2,1,0:T(8,128)(2,1)S(1)}, bf16[4,64,384]{2,1,0:T(8,128)(2,1)S(1)}, u32[]{:S(2)}, u32[]{:S(2)}) collective-permute-start(bf16[4,64,384]{2,1,0:T(8,128)(2,1)S(1)} %maximum_bitcast_fusion), channel_id=1, source_target_pairs={{0,64},{16,80},{32,96},{48,112},{64,0},{80,16},{96,32},{112,48},{1... | collective-permute-start | bytes 589832 | tf_op jit(solution)/shard_map/ppermute | solution.py:84
  36.8 5.4 %collective-permute-start.5 = (bf16[4,64,384]{2,1,0:T(8,128)(2,1)S(1)}, bf16[4,64,384]{2,1,0:T(8,128)(2,1)S(1)}, u32[]{:S(2)}, u32[]{:S(2)}) collective-permute-start(bf16[4,64,384]{2,1,0:T(8,128)(2,1)S(1)} %maximum_bitcast_fusion), channel_id=1, source_target_pairs={{0,32},{16,48},{32,64},{48,80},{64,96},{80,112},{96,0},{112,16},{1... | collective-permute-start | bytes 589832 | tf_op jit(solution)/shard_map/ppermute | solution.py:84
  44.2 7.5 %collective-permute-done.4 = bf16[4,64,384]{2,1,0:T(8,128)(2,1)S(1)} collective-permute-done((bf16[4,64,384]{2,1,0:T(8,128)(2,1)S(1)}, bf16[4,64,384]{2,1,0:T(8,128)(2,1)S(1)}, u32[]{:S(2)}, u32[]{:S(2)}) %collective-permute-start.4) | collective-permute-done | bytes 196640 | tf_op jit(solution)/shard_map/ppermute | solution.py:84
  52.2 1.9 collective-permute-start.6
  60.7 2.0 collective-permute-start.7
  67.0 5.2 %collective-permute-start.10 = (f32[1,128,128]{2,1,0:T(8,128)S(1)}, f32[1,128,128]{2,1,0:T(8,128)S(1)}, u32[]{:S(2)}, u32[]{:S(2)}) collective-permute-start(f32[1,128,128]{2,1,0:T(8,128)S(1)} %add.361), channel_id=1, source_target_pairs={{0,96},{32,128},{64,160},{96,192},{128,224},{160,256},{192,288},{2... | collective-permute-start | bytes 196616 | tf_op jit(solution)/shard_map/ppermute | solution.py:35
  72.1 5.1 %collective-permute-start.9 = (f32[1,128,128]{2,1,0:T(8,128)S(1)}, f32[1,128,128]{2,1,0:T(8,128)S(1)}, u32[]{:S(2)}, u32[]{:S(2)}) collective-permute-start(f32[1,128,128]{2,1,0:T(8,128)S(1)} %add.361), channel_id=1, source_target_pairs={{0,64},{32,96},{64,128},{96,160},{128,192},{160,224},{192,256},{22... | collective-permute-start | bytes 196616 | tf_op jit(solution)/shard_map/ppermute | solution.py:35
  77.3 3.1 %collective-permute-start.8 = (f32[1,128,128]{2,1,0:T(8,128)S(1)}, f32[1,128,128]{2,1,0:T(8,128)S(1)}, u32[]{:S(2)}, u32[]{:S(2)}) collective-permute-start(f32[1,128,128]{2,1,0:T(8,128)S(1)} %add.361), channel_id=1, source_target_pairs={{0,32},{32,64},{64,96},{96,128},{128,160},{160,192},{192,224},{224... | collective-permute-start | bytes 196616 | tf_op jit(solution)/shard_map/ppermute | solution.py:35
  84.9 7.3 %collective-permute-start.12 = (f32[1,128,128]{2,1,0:T(8,128)S(1)}, f32[1,128,128]{2,1,0:T(8,128)S(1)}, u32[]{:S(2)}, u32[]{:S(2)}) collective-permute-start(f32[1,128,128]{2,1,0:T(8,128)S(1)} %add_add_fusion.1), channel_id=1, source_target_pairs={{0,256},{32,288},{64,320},{96,352},{128,384},{160,416},{192,448},{... | collective-permute-start | bytes 196616 | tf_op jit(solution)/shard_map/ppermute | solution.py:35
  94.1 7.9 %collective-permute-done.11 = f32[1,128,128]{2,1,0:T(8,128)S(1)} collective-permute-done((f32[1,128,128]{2,1,0:T(8,128)S(1)}, f32[1,128,128]{2,1,0:T(8,128)S(1)}, u32[]{:S(2)}, u32[]{:S(2)}) %collective-permute-start.11) | collective-permute-done | bytes 65568 | tf_op jit(solution)/shard_map/ppermute | solution.py:35
  106.4 2.2 %collective-permute-start.17 = (f32[1,128,128]{2,1,0:T(8,128)S(1)}, f32[1,128,128]{2,1,0:T(8,128)S(1)}, u32[]{:S(2)}, u32[]{:S(2)}) collective-permute-start(f32[1,128,128]{2,1,0:T(8,128)S(1)} %add.374), channel_id=1, source_target_pairs={{96,0},{128,32},{160,64},{192,96},{224,128},{256,160},{288,192},{3... | collective-permute-start | bytes 196616 | tf_op jit(solution)/shard_map/ppermute | solution.py:35
  112.6 3.0 %collective-permute-done.17 = f32[1,128,128]{2,1,0:T(8,128)S(1)} collective-permute-done((f32[1,128,128]{2,1,0:T(8,128)S(1)}, f32[1,128,128]{2,1,0:T(8,128)S(1)}, u32[]{:S(2)}, u32[]{:S(2)}) %collective-permute-start.17) | collective-permute-done | bytes 65568 | tf_op jit(solution)/shard_map/ppermute | solution.py:35
  115.6 5.6 %collective-permute-done.16 = f32[1,128,128]{2,1,0:T(8,128)S(1)} collective-permute-done((f32[1,128,128]{2,1,0:T(8,128)S(1)}, f32[1,128,128]{2,1,0:T(8,128)S(1)}, u32[]{:S(2)}, u32[]{:S(2)}) %collective-permute-start.16) | collective-permute-done | bytes 65568 | tf_op jit(solution)/shard_map/ppermute | solution.py:35
  125.3 14.7 %collective-permute-done.20 = f32[1,128,128]{2,1,0:T(8,128)S(1)} collective-permute-done((f32[1,128,128]{2,1,0:T(8,128)S(1)}, f32[1,128,128]{2,1,0:T(8,128)S(1)}, u32[]{:S(2)}, u32[]{:S(2)}) %collective-permute-start.20) | collective-permute-done | bytes 65568 | tf_op jit(solution)/shard_map/ppermute | solution.py:35
  140.0 4.6 %collective-permute-done.19 = f32[1,128,128]{2,1,0:T(8,128)S(1)} collective-permute-done((f32[1,128,128]{2,1,0:T(8,128)S(1)}, f32[1,128,128]{2,1,0:T(8,128)S(1)}, u32[]{:S(2)}, u32[]{:S(2)}) %collective-permute-start.19) | collective-permute-done | bytes 65568 | tf_op jit(solution)/shard_map/ppermute | solution.py:35
  153.9 2.9 %collective-permute-start.23 = (bf16[4,128,384]{1,2,0:T(8,128)(2,1)}, bf16[4,128,384]{1,2,0:T(8,128)(2,1)S(1)}, u32[]{:S(2)}, u32[]{:S(2)}) collective-permute-start(bf16[4,128,384]{1,2,0:T(8,128)(2,1)} %bitcast.40), channel_id=1, source_target_pairs={{0,12},{1,13},{2,14},{3,15},{4,0},{5,1},{6,2},{7,3},{8,4},{9,5},{1... | collective-permute-start | bytes 1179656 | tf_op jit(solution)/shard_map/ppermute | solution.py:117
  157.7 2.7 %collective-permute-start.22 = (bf16[4,128,384]{1,2,0:T(8,128)(2,1)}, bf16[4,128,384]{1,2,0:T(8,128)(2,1)S(1)}, u32[]{:S(2)}, u32[]{:S(2)}) collective-permute-start(bf16[4,128,384]{1,2,0:T(8,128)(2,1)} %bitcast.39), channel_id=1, source_target_pairs={{0,8},{1,9},{2,10},{3,11},{4,12},{5,13},{6,14},{7,15},{8,0},{9,1},... | collective-permute-start | bytes 1179656 | tf_op jit(solution)/shard_map/ppermute | solution.py:117
  161.4 2.8 %collective-permute-start.21 = (bf16[4,128,384]{1,2,0:T(8,128)(2,1)}, bf16[4,128,384]{1,2,0:T(8,128)(2,1)S(1)}, u32[]{:S(2)}, u32[]{:S(2)}) collective-permute-start(bf16[4,128,384]{1,2,0:T(8,128)(2,1)} %bitcast.38), channel_id=1, source_target_pairs={{0,4},{1,5},{2,6},{3,7},{4,8},{5,9},{6,10},{7,11},{8,12},{9,13},{1... | collective-permute-start | bytes 1179656 | tf_op jit(solution)/shard_map/ppermute | solution.py:117
  169.7 5.7 %collective-permute-start.28 = (bf16[4,64,384]{2,1,0:T(8,128)(2,1)S(1)}, bf16[4,64,384]{2,1,0:T(8,128)(2,1)S(1)}, u32[]{:S(2)}, u32[]{:S(2)}) collective-permute-start(bf16[4,64,384]{2,1,0:T(8,128)(2,1)S(1)} %get-tuple-element.15), channel_id=1, source_target_pairs={{0,32},{16,48},{32,64},{48,80},{64,96},{80,112},{96,0},{112,16},{1... | collective-permute-start | bytes 589832 | tf_op jit(solution)/shard_map/ppermute | solution.py:117
  175.4 5.6 %collective-permute-done.21 = bf16[4,128,384]{1,2,0:T(8,128)(2,1)S(1)} collective-permute-done((bf16[4,128,384]{1,2,0:T(8,128)(2,1)}, bf16[4,128,384]{1,2,0:T(8,128)(2,1)S(1)}, u32[]{:S(2)}, u32[]{:S(2)}) %collective-permute-start.21) | collective-permute-done | bytes 393248 | tf_op jit(solution)/shard_map/ppermute | solution.py:117
  181.2 4.1 %collective-permute-start.26 = (bf16[1,128,384]{1,2,0:T(8,128)(2,1)S(1)}, bf16[1,128,384]{1,2,0:T(8,128)(2,1)S(1)}, u32[]{:S(2)}, u32[]{:S(2)}) collective-permute-start(bf16[1,128,384]{1,2,0:T(8,128)(2,1)S(1)} %get-tuple-element.25), channel_id=1, source_target_pairs={{0,3},{1,0},{2,1},{3,2},{4,7},{5,4},{6,5},{7,6},{8,11},{9,8},{10,9... | collective-permute-start | bytes 294920 | tf_op jit(solution)/shard_map/ppermute | solution.py:117
  185.3 2.8 %collective-permute-start.25 = (bf16[1,128,384]{1,2,0:T(8,128)(2,1)S(1)}, bf16[1,128,384]{1,2,0:T(8,128)(2,1)S(1)}, u32[]{:S(2)}, u32[]{:S(2)}) collective-permute-start(bf16[1,128,384]{1,2,0:T(8,128)(2,1)S(1)} %get-tuple-element.26), channel_id=1, source_target_pairs={{0,2},{1,3},{2,0},{3,1},{4,6},{5,7},{6,4},{7,5},{8,10},{9,11},{10,... | collective-permute-start | bytes 294920 | tf_op jit(solution)/shard_map/ppermute | solution.py:117
  188.1 3.8 %collective-permute-start.24 = (bf16[1,128,384]{1,2,0:T(8,128)(2,1)S(1)}, bf16[1,128,384]{1,2,0:T(8,128)(2,1)S(1)}, u32[]{:S(2)}, u32[]{:S(2)}) collective-permute-start(bf16[1,128,384]{1,2,0:T(8,128)(2,1)S(1)} %get-tuple-element.24), channel_id=1, source_target_pairs={{0,1},{1,2},{2,3},{3,0},{4,5},{5,6},{6,7},{7,4},{8,9},{9,10},{10,1... | collective-permute-start | bytes 294920 | tf_op jit(solution)/shard_map/ppermute | solution.py:117
  194.0 10.8 %collective-permute-start.32 = (bf16[1,64,384]{2,1,0:T(8,128)(2,1)S(1)}, bf16[1,64,384]{2,1,0:T(8,128)(2,1)S(1)}, u32[]{:S(2)}, u32[]{:S(2)}) collective-permute-start(bf16[1,64,384]{2,1,0:T(8,128)(2,1)S(1)} %get-tuple-element.33), channel_id=1, source_target_pairs={{0,256},{16,272},{32,288},{48,304},{64,320},{80,336},{96,352},{112... | collective-permute-start | bytes 147464 | tf_op jit(solution)/shard_map/ppermute | solution.py:117
  204.8 1.9 collective-permute-start.31
  208.7 6.0 %collective-permute-done.31 = bf16[1,64,384]{2,1,0:T(8,128)(2,1)S(1)} collective-permute-done((bf16[1,64,384]{2,1,0:T(8,128)(2,1)S(1)}, bf16[1,64,384]{2,1,0:T(8,128)(2,1)S(1)}, u32[]{:S(2)}, u32[]{:S(2)}) %collective-permute-start.31) | collective-permute-done | bytes 49184 | tf_op jit(solution)/shard_map/ppermute | solution.py:117
  (119 shorter events, 55.2 us)
Async XLA Ops:
  1.4 22.9 %collective-permute-start = (bf16[1,64,384]{2,1,0:T(8,128)(2,1)S(1)}, bf16[1,64,384]{2,1,0:T(8,128)(2,1)S(1)}, u32[]{:S(2)}, u32[]{:S(2)}) collective-permute-start(bf16[1,64,384]{2,1,0:T(8,128)(2,1)S(1)} %maximum_bitcast_fusion.1), channel_id=1, source_target_pairs={{0,384},{16,400},{32,416},{48,432},{64,448},{80,464},{96,480},{112... | collective-permute-start | bytes 147464 | tf_op jit(solution)/shard_map/ppermute | solution.py:84
  11.4 15.4 %collective-permute-start.1 = (bf16[1,64,384]{2,1,0:T(8,128)(2,1)S(1)}, bf16[1,64,384]{2,1,0:T(8,128)(2,1)S(1)}, u32[]{:S(2)}, u32[]{:S(2)}) collective-permute-start(bf16[1,64,384]{2,1,0:T(8,128)(2,1)S(1)} %maximum_bitcast_fusion.1), channel_id=1, source_target_pairs={{0,256},{16,272},{32,288},{48,304},{64,320},{80,336},{96,352},{112... | collective-permute-start | bytes 147464 | tf_op jit(solution)/shard_map/ppermute | solution.py:84
  17.8 13.2 %collective-permute-start.2 = (bf16[1,64,384]{2,1,0:T(8,128)(2,1)S(1)}, bf16[1,64,384]{2,1,0:T(8,128)(2,1)S(1)}, u32[]{:S(2)}, u32[]{:S(2)}) collective-permute-start(bf16[1,64,384]{2,1,0:T(8,128)(2,1)S(1)} %maximum_bitcast_fusion.1), channel_id=1, source_target_pairs={{0,128},{16,144},{32,160},{48,176},{64,192},{80,208},{96,224},{112... | collective-permute-start | bytes 147464 | tf_op jit(solution)/shard_map/ppermute | solution.py:84
  32.6 11.6 %collective-permute-start.3 = (bf16[4,64,384]{2,1,0:T(8,128)(2,1)S(1)}, bf16[4,64,384]{2,1,0:T(8,128)(2,1)S(1)}, u32[]{:S(2)}, u32[]{:S(2)}) collective-permute-start(bf16[4,64,384]{2,1,0:T(8,128)(2,1)S(1)} %maximum_bitcast_fusion), channel_id=1, source_target_pairs={{0,96},{16,112},{32,0},{48,16},{64,32},{80,48},{96,64},{112,80},{1... | collective-permute-start | bytes 589832 | tf_op jit(solution)/shard_map/ppermute | solution.py:84
  34.5 17.1 %collective-permute-start.4 = (bf16[4,64,384]{2,1,0:T(8,128)(2,1)S(1)}, bf16[4,64,384]{2,1,0:T(8,128)(2,1)S(1)}, u32[]{:S(2)}, u32[]{:S(2)}) collective-permute-start(bf16[4,64,384]{2,1,0:T(8,128)(2,1)S(1)} %maximum_bitcast_fusion), channel_id=1, source_target_pairs={{0,64},{16,80},{32,96},{48,112},{64,0},{80,16},{96,32},{112,48},{1... | collective-permute-start | bytes 589832 | tf_op jit(solution)/shard_map/ppermute | solution.py:84
  36.8 15.1 %collective-permute-start.5 = (bf16[4,64,384]{2,1,0:T(8,128)(2,1)S(1)}, bf16[4,64,384]{2,1,0:T(8,128)(2,1)S(1)}, u32[]{:S(2)}, u32[]{:S(2)}) collective-permute-start(bf16[4,64,384]{2,1,0:T(8,128)(2,1)S(1)} %maximum_bitcast_fusion), channel_id=1, source_target_pairs={{0,32},{16,48},{32,64},{48,80},{64,96},{80,112},{96,0},{112,16},{1... | collective-permute-start | bytes 589832 | tf_op jit(solution)/shard_map/ppermute | solution.py:84
  60.7 5.4 %collective-permute-start.7 = (f32[1,128,128]{2,1,0:T(8,128)}, f32[1,128,128]{2,1,0:T(8,128)}, u32[]{:S(2)}, u32[]{:S(2)}) collective-permute-start(f32[1,128,128]{2,1,0:T(8,128)} %convolution_bitcast_fusion.1), channel_id=1, source_target_pairs={{0,16},{16,0},{1,17},{17,1},{2,18},{18,2},{3,19},{19,3},{4,20},{20... | collective-permute-start | bytes 196616 | tf_op jit(solution)/shard_map/ppermute | solution.py:21
  67.0 14.6 %collective-permute-start.10 = (f32[1,128,128]{2,1,0:T(8,128)S(1)}, f32[1,128,128]{2,1,0:T(8,128)S(1)}, u32[]{:S(2)}, u32[]{:S(2)}) collective-permute-start(f32[1,128,128]{2,1,0:T(8,128)S(1)} %add.361), channel_id=1, source_target_pairs={{0,96},{32,128},{64,160},{96,192},{128,224},{160,256},{192,288},{2... | collective-permute-start | bytes 196616 | tf_op jit(solution)/shard_map/ppermute | solution.py:35
  72.1 9.4 %collective-permute-start.9 = (f32[1,128,128]{2,1,0:T(8,128)S(1)}, f32[1,128,128]{2,1,0:T(8,128)S(1)}, u32[]{:S(2)}, u32[]{:S(2)}) collective-permute-start(f32[1,128,128]{2,1,0:T(8,128)S(1)} %add.361), channel_id=1, source_target_pairs={{0,64},{32,96},{64,128},{96,160},{128,192},{160,224},{192,256},{22... | collective-permute-start | bytes 196616 | tf_op jit(solution)/shard_map/ppermute | solution.py:35
  77.3 6.2 %collective-permute-start.8 = (f32[1,128,128]{2,1,0:T(8,128)S(1)}, f32[1,128,128]{2,1,0:T(8,128)S(1)}, u32[]{:S(2)}, u32[]{:S(2)}) collective-permute-start(f32[1,128,128]{2,1,0:T(8,128)S(1)} %add.361), channel_id=1, source_target_pairs={{0,32},{32,64},{64,96},{96,128},{128,160},{160,192},{192,224},{224... | collective-permute-start | bytes 196616 | tf_op jit(solution)/shard_map/ppermute | solution.py:35
  83.5 10.3 %collective-permute-start.13 = (f32[1,128,128]{2,1,0:T(8,128)S(1)}, f32[1,128,128]{2,1,0:T(8,128)S(1)}, u32[]{:S(2)}, u32[]{:S(2)}) collective-permute-start(f32[1,128,128]{2,1,0:T(8,128)S(1)} %add_add_fusion.1), channel_id=1, source_target_pairs={{0,384},{32,416},{64,448},{96,480},{1,385},{33,417},{65,449},{97,4... | collective-permute-start | bytes 196616 | tf_op jit(solution)/shard_map/ppermute | solution.py:35
  84.9 9.2 %collective-permute-start.12 = (f32[1,128,128]{2,1,0:T(8,128)S(1)}, f32[1,128,128]{2,1,0:T(8,128)S(1)}, u32[]{:S(2)}, u32[]{:S(2)}) collective-permute-start(f32[1,128,128]{2,1,0:T(8,128)S(1)} %add_add_fusion.1), channel_id=1, source_target_pairs={{0,256},{32,288},{64,320},{96,352},{128,384},{160,416},{192,448},{... | collective-permute-start | bytes 196616 | tf_op jit(solution)/shard_map/ppermute | solution.py:35
  92.2 9.8 %collective-permute-start.11 = (f32[1,128,128]{2,1,0:T(8,128)S(1)}, f32[1,128,128]{2,1,0:T(8,128)S(1)}, u32[]{:S(2)}, u32[]{:S(2)}) collective-permute-start(f32[1,128,128]{2,1,0:T(8,128)S(1)} %add_add_fusion.1), channel_id=1, source_target_pairs={{0,128},{32,160},{64,192},{96,224},{128,256},{160,288},{192,320},{... | collective-permute-start | bytes 196616 | tf_op jit(solution)/shard_map/ppermute | solution.py:35
  106.4 9.3 %collective-permute-start.17 = (f32[1,128,128]{2,1,0:T(8,128)S(1)}, f32[1,128,128]{2,1,0:T(8,128)S(1)}, u32[]{:S(2)}, u32[]{:S(2)}) collective-permute-start(f32[1,128,128]{2,1,0:T(8,128)S(1)} %add.374), channel_id=1, source_target_pairs={{96,0},{128,32},{160,64},{192,96},{224,128},{256,160},{288,192},{3... | collective-permute-start | bytes 196616 | tf_op jit(solution)/shard_map/ppermute | solution.py:35
  108.5 12.6 %collective-permute-start.16 = (f32[1,128,128]{2,1,0:T(8,128)S(1)}, f32[1,128,128]{2,1,0:T(8,128)S(1)}, u32[]{:S(2)}, u32[]{:S(2)}) collective-permute-start(f32[1,128,128]{2,1,0:T(8,128)S(1)} %add.374), channel_id=1, source_target_pairs={{64,0},{96,32},{128,64},{160,96},{192,128},{224,160},{256,192},{28... | collective-permute-start | bytes 196616 | tf_op jit(solution)/shard_map/ppermute | solution.py:35
  110.5 10.7 %collective-permute-start.15 = (f32[1,128,128]{2,1,0:T(8,128)S(1)}, f32[1,128,128]{2,1,0:T(8,128)S(1)}, u32[]{:S(2)}, u32[]{:S(2)}) collective-permute-start(f32[1,128,128]{2,1,0:T(8,128)S(1)} %add.374), channel_id=1, source_target_pairs={{32,0},{64,32},{96,64},{128,96},{160,128},{192,160},{224,192},{256... | collective-permute-start | bytes 196616 | tf_op jit(solution)/shard_map/ppermute | solution.py:35
  121.2 18.8 %collective-permute-start.20 = (f32[1,128,128]{2,1,0:T(8,128)S(1)}, f32[1,128,128]{2,1,0:T(8,128)S(1)}, u32[]{:S(2)}, u32[]{:S(2)}) collective-permute-start(f32[1,128,128]{2,1,0:T(8,128)S(1)} %add_add_fusion), channel_id=1, source_target_pairs={{384,0},{416,32},{448,64},{480,96},{385,1},{417,33},{449,65},{481,... | collective-permute-start | bytes 196616 | tf_op jit(solution)/shard_map/ppermute | solution.py:35
  122.5 22.1 %collective-permute-start.19 = (f32[1,128,128]{2,1,0:T(8,128)S(1)}, f32[1,128,128]{2,1,0:T(8,128)S(1)}, u32[]{:S(2)}, u32[]{:S(2)}) collective-permute-start(f32[1,128,128]{2,1,0:T(8,128)S(1)} %add_add_fusion), channel_id=1, source_target_pairs={{256,0},{288,32},{320,64},{352,96},{384,128},{416,160},{448,192},{... | collective-permute-start | bytes 196616 | tf_op jit(solution)/shard_map/ppermute | solution.py:35
  123.8 20.8 %collective-permute-start.18 = (f32[1,128,128]{2,1,0:T(8,128)S(1)}, f32[1,128,128]{2,1,0:T(8,128)S(1)}, u32[]{:S(2)}, u32[]{:S(2)}) collective-permute-start(f32[1,128,128]{2,1,0:T(8,128)S(1)} %add_add_fusion), channel_id=1, source_target_pairs={{128,0},{160,32},{192,64},{224,96},{256,128},{288,160},{320,192},{... | collective-permute-start | bytes 196616 | tf_op jit(solution)/shard_map/ppermute | solution.py:35
  148.6 15.7 %collective-permute-start.27 = (bf16[16,64,384]{2,1,0:T(8,128)(2,1)}, bf16[16,64,384]{2,1,0:T(8,128)(2,1)}, u32[]{:S(2)}, u32[]{:S(2)}) collective-permute-start(bf16[16,64,384]{2,1,0:T(8,128)(2,1)} %dynamic-slice_bitcast_fusion), channel_id=1, source_target_pairs={{0,16},{16,0},{32,48},{48,32},{64,80},{80,64},{96,112},{112,96},{1... | collective-permute-start | bytes 2359304 | tf_op jit(solution)/shard_map/ppermute | solution.py:117
  153.9 15.8 %collective-permute-start.23 = (bf16[4,128,384]{1,2,0:T(8,128)(2,1)}, bf16[4,128,384]{1,2,0:T(8,128)(2,1)S(1)}, u32[]{:S(2)}, u32[]{:S(2)}) collective-permute-start(bf16[4,128,384]{1,2,0:T(8,128)(2,1)} %bitcast.40), channel_id=1, source_target_pairs={{0,12},{1,13},{2,14},{3,15},{4,0},{5,1},{6,2},{7,3},{8,4},{9,5},{1... | collective-permute-start | bytes 1179656 | tf_op jit(solution)/shard_map/ppermute | solution.py:117
  157.7 17.7 %collective-permute-start.22 = (bf16[4,128,384]{1,2,0:T(8,128)(2,1)}, bf16[4,128,384]{1,2,0:T(8,128)(2,1)S(1)}, u32[]{:S(2)}, u32[]{:S(2)}) collective-permute-start(bf16[4,128,384]{1,2,0:T(8,128)(2,1)} %bitcast.39), channel_id=1, source_target_pairs={{0,8},{1,9},{2,10},{3,11},{4,12},{5,13},{6,14},{7,15},{8,0},{9,1},... | collective-permute-start | bytes 1179656 | tf_op jit(solution)/shard_map/ppermute | solution.py:117
  161.4 19.6 %collective-permute-start.21 = (bf16[4,128,384]{1,2,0:T(8,128)(2,1)}, bf16[4,128,384]{1,2,0:T(8,128)(2,1)S(1)}, u32[]{:S(2)}, u32[]{:S(2)}) collective-permute-start(bf16[4,128,384]{1,2,0:T(8,128)(2,1)} %bitcast.38), channel_id=1, source_target_pairs={{0,4},{1,5},{2,6},{3,7},{4,8},{5,9},{6,10},{7,11},{8,12},{9,13},{1... | collective-permute-start | bytes 1179656 | tf_op jit(solution)/shard_map/ppermute | solution.py:117
  165.8 22.3 %collective-permute-start.30 = (bf16[4,64,384]{2,1,0:T(8,128)(2,1)S(1)}, bf16[4,64,384]{2,1,0:T(8,128)(2,1)S(1)}, u32[]{:S(2)}, u32[]{:S(2)}) collective-permute-start(bf16[4,64,384]{2,1,0:T(8,128)(2,1)S(1)} %get-tuple-element.16), channel_id=1, source_target_pairs={{0,96},{16,112},{32,0},{48,16},{64,32},{80,48},{96,64},{112,80},{1... | collective-permute-start | bytes 589832 | tf_op jit(solution)/shard_map/ppermute | solution.py:117
  167.7 24.2 %collective-permute-start.29 = (bf16[4,64,384]{2,1,0:T(8,128)(2,1)S(1)}, bf16[4,64,384]{2,1,0:T(8,128)(2,1)S(1)}, u32[]{:S(2)}, u32[]{:S(2)}) collective-permute-start(bf16[4,64,384]{2,1,0:T(8,128)(2,1)S(1)} %get-tuple-element.17), channel_id=1, source_target_pairs={{0,64},{16,80},{32,96},{48,112},{64,0},{80,16},{96,32},{112,48},{1... | collective-permute-start | bytes 589832 | tf_op jit(solution)/shard_map/ppermute | solution.py:117
  169.7 22.3 %collective-permute-start.28 = (bf16[4,64,384]{2,1,0:T(8,128)(2,1)S(1)}, bf16[4,64,384]{2,1,0:T(8,128)(2,1)S(1)}, u32[]{:S(2)}, u32[]{:S(2)}) collective-permute-start(bf16[4,64,384]{2,1,0:T(8,128)(2,1)S(1)} %get-tuple-element.15), channel_id=1, source_target_pairs={{0,32},{16,48},{32,64},{48,80},{64,96},{80,112},{96,0},{112,16},{1... | collective-permute-start | bytes 589832 | tf_op jit(solution)/shard_map/ppermute | solution.py:117
  181.2 23.6 %collective-permute-start.26 = (bf16[1,128,384]{1,2,0:T(8,128)(2,1)S(1)}, bf16[1,128,384]{1,2,0:T(8,128)(2,1)S(1)}, u32[]{:S(2)}, u32[]{:S(2)}) collective-permute-start(bf16[1,128,384]{1,2,0:T(8,128)(2,1)S(1)} %get-tuple-element.25), channel_id=1, source_target_pairs={{0,3},{1,0},{2,1},{3,2},{4,7},{5,4},{6,5},{7,6},{8,11},{9,8},{10,9... | collective-permute-start | bytes 294920 | tf_op jit(solution)/shard_map/ppermute | solution.py:117
  185.3 21.4 %collective-permute-start.25 = (bf16[1,128,384]{1,2,0:T(8,128)(2,1)S(1)}, bf16[1,128,384]{1,2,0:T(8,128)(2,1)S(1)}, u32[]{:S(2)}, u32[]{:S(2)}) collective-permute-start(bf16[1,128,384]{1,2,0:T(8,128)(2,1)S(1)} %get-tuple-element.26), channel_id=1, source_target_pairs={{0,2},{1,3},{2,0},{3,1},{4,6},{5,7},{6,4},{7,5},{8,10},{9,11},{10,... | collective-permute-start | bytes 294920 | tf_op jit(solution)/shard_map/ppermute | solution.py:117
  188.1 18.6 %collective-permute-start.24 = (bf16[1,128,384]{1,2,0:T(8,128)(2,1)S(1)}, bf16[1,128,384]{1,2,0:T(8,128)(2,1)S(1)}, u32[]{:S(2)}, u32[]{:S(2)}) collective-permute-start(bf16[1,128,384]{1,2,0:T(8,128)(2,1)S(1)} %get-tuple-element.24), channel_id=1, source_target_pairs={{0,1},{1,2},{2,3},{3,0},{4,5},{5,6},{6,7},{7,4},{8,9},{9,10},{10,1... | collective-permute-start | bytes 294920 | tf_op jit(solution)/shard_map/ppermute | solution.py:117
  192.1 15.4 %collective-permute-start.33 = (bf16[1,64,384]{2,1,0:T(8,128)(2,1)S(1)}, bf16[1,64,384]{2,1,0:T(8,128)(2,1)S(1)}, u32[]{:S(2)}, u32[]{:S(2)}) collective-permute-start(bf16[1,64,384]{2,1,0:T(8,128)(2,1)S(1)} %get-tuple-element.32), channel_id=1, source_target_pairs={{0,384},{16,400},{32,416},{48,432},{64,448},{80,464},{96,480},{112... | collective-permute-start | bytes 147464 | tf_op jit(solution)/shard_map/ppermute | solution.py:117
  194.0 14.7 %collective-permute-start.32 = (bf16[1,64,384]{2,1,0:T(8,128)(2,1)S(1)}, bf16[1,64,384]{2,1,0:T(8,128)(2,1)S(1)}, u32[]{:S(2)}, u32[]{:S(2)}) collective-permute-start(bf16[1,64,384]{2,1,0:T(8,128)(2,1)S(1)} %get-tuple-element.33), channel_id=1, source_target_pairs={{0,256},{16,272},{32,288},{48,304},{64,320},{80,336},{96,352},{112... | collective-permute-start | bytes 147464 | tf_op jit(solution)/shard_map/ppermute | solution.py:117
  204.8 9.9 %collective-permute-start.31 = (bf16[1,64,384]{2,1,0:T(8,128)(2,1)S(1)}, bf16[1,64,384]{2,1,0:T(8,128)(2,1)S(1)}, u32[]{:S(2)}, u32[]{:S(2)}) collective-permute-start(bf16[1,64,384]{2,1,0:T(8,128)(2,1)S(1)} %get-tuple-element.31), channel_id=1, source_target_pairs={{0,128},{16,144},{32,160},{48,176},{64,192},{80,208},{96,224},{112... | collective-permute-start | bytes 147464 | tf_op jit(solution)/shard_map/ppermute | solution.py:117
  (14 other events, 107.0 us)

commit v11 on v10

--- a/solution.py
+++ b/solution.py
@@ -122,6 +122,44 @@
     return current.reshape(rows, cols)
 
 
+def exchange_scatter_columns(term, axis, radices, order):
+    count = math.prod(radices)
+    place = lax.axis_index(axis)
+    rows = term.shape[0]
+    cols = term.shape[1] // math.prod(radices[position] for position in order)
+    current = term
+    for position in order:
+        radix = radices[position]
+        stride = math.prod(radices[:position])
+        digit = (place // stride) % radix
+        split = current.reshape(rows, radix, -1)
+        total = lax.dynamic_index_in_dim(split, digit, 1, False).astype(jnp.float32)
+        for offset in range(1, radix):
+            away = lax.dynamic_index_in_dim(split, (digit + offset) % radix, 1, False)
+            moved = lax.ppermute(
+                away.astype(jnp.bfloat16), axis, digit_pairs(count, stride, radix, offset)
+            )
+            total = total + moved.astype(jnp.float32)
+        current = total
+    return current.reshape(rows, cols)
+
+
+def exchange_scatter_grouped(groups, axis, radices, order):
+    count = math.prod(radices)
+    place = lax.axis_index(axis)
+    radix = radices[order[0]]
+    stride = math.prod(radices[: order[0]])
+    digit = (place // stride) % radix
+    total = lax.dynamic_index_in_dim(groups, digit, 0, False).astype(jnp.float32)
+    for offset in range(1, radix):
+        away = lax.dynamic_index_in_dim(groups, (digit + offset) % radix, 0, False)
+        moved = lax.ppermute(
+            away.astype(jnp.bfloat16), axis, digit_pairs(count, stride, radix, offset)
+        )
+        total = total + moved.astype(jnp.float32)
+    return exchange_scatter_columns(total, axis, radices, order[1:])
+
+
 def halving_scatter(term, axis, count):
     place = lax.axis_index(axis)
     rows = term.shape[0] // count
@@ -214,15 +252,17 @@
         [part.reshape(SEG, columns).astype(jnp.bfloat16) for part in (d_queries, d_keys, d_values)],
         axis=1,
     )
-    input_rows = exchange_scatter(
-        lax.dot_general(
-            weight_cat, grad_cat, (((1,), (1,)), ((), ())), preferred_element_type=jnp.float32
+    fsdp_order = tuple(reversed(range(len(fsdp_radices))))
+    grouped_weights = weight_cat.reshape(fsdp_radices[fsdp_order[0]], -1, weight_cat.shape[1])
+    input_rows = exchange_scatter_grouped(
+        jnp.einsum(
+            "tk,gdk->gtd", grad_cat, grouped_weights, preferred_element_type=jnp.float32
         ).astype(jnp.bfloat16),
         "fsdp",
         fsdp_radices,
-        tuple(reversed(range(len(fsdp_radices)))),
-    )
-    grad_tokens = input_rows.T.astype(jnp.bfloat16)
+        fsdp_order,
+    )
+    grad_tokens = input_rows.astype(jnp.bfloat16)
     seq_order = tuple(range(len(seq_radices)))
     weight_rows = exchange_scatter(
         lax.dot_general(

time: 217 us -> 234 us (1.078)
  the two profiles are of different devices: /device:TPU:104 before, /device:TPU:65 now
where the time goes in v11:
time: 234 us; the launch traced here: 233 us
  starting transfers between devices  128 us (55%)
  waiting for transfers between devices  72.6 us (31%)
  local copies, waits for them, and re-layouts  11 us (5%)
  matrix products  10 us (4%)
  other arithmetic  9.61 us (4%)
    ppermute x7, starting transfers between devices, exchange_gather(): lax.ppermute(current, axis, digit_pairs(count, stride, radix, offset))  36.6 us
    ppermute x12, starting transfers between devices, entering(): parts.append(lax.ppermute(total, 'z', pairs))  35.3 us
    ppermute x7, starting transfers between devices, exchange_scatter(): lax.ppermute(away.astype(jnp.bfloat16), axis, digit_pairs(count, stride,...  33.7 us
    ppermute x12, waiting for transfers between devices, entering(): parts.append(lax.ppermute(total, 'z', pairs))  20.4 us
    ppermute x7, waiting for transfers between devices, exchange_gather(): lax.ppermute(current, axis, digit_pairs(count, stride, radix, offset))  20.4 us
    ppermute x3, waiting for transfers between devices, exchange_scatter_grouped(): lax.ppermute(away.astype(jnp.bfloat16), axis, digit_pairs(count, stride,...  16.6 us
    ppermute x7, waiting for transfers between devices, exchange_scatter(): lax.ppermute(away.astype(jnp.bfloat16), axis, digit_pairs(count, stride,...  14.6 us
    ppermute x3, starting transfers between devices, exchange_scatter_grouped(): lax.ppermute(away.astype(jnp.bfloat16), axis, digit_pairs(count, stride,...  8.46 us
  transfers between devices with their start and end apart: 34, of which 18 were waited for; matrix products, arithmetic and copies ran while one was open for 5% of the time, Pallas kernels for 0%

profile of v11, /device:TPU:65, one launch (start us, length us, event | category | flops | bytes accessed | tf_op | source)
XLA Modules:
  0.0 232.7 jit_solution(4063245024563064848)
XLA Ops:
  1.4 10.6 %collective-permute-start = (bf16[1,64,384]{2,1,0:T(8,128)(2,1)S(1)}, bf16[1,64,384]{2,1,0:T(8,128)(2,1)S(1)}, u32[]{:S(2)}, u32[]{:S(2)}) collective-permute-start(bf16[1,64,384]{2,1,0:T(8,128)(2,1)S(1)} %maximum_bitcast_fusion.1), channel_id=1, source_target_pairs={{0,384},{16,400},{32,416},{48,432},{64,448},{80,464},{96,480},{112... | collective-permute-start | bytes 147464 | tf_op jit(solution)/shard_map/ppermute | solution.py:84
  12.0 5.2 %collective-permute-start.1 = (bf16[1,64,384]{2,1,0:T(8,128)(2,1)S(1)}, bf16[1,64,384]{2,1,0:T(8,128)(2,1)S(1)}, u32[]{:S(2)}, u32[]{:S(2)}) collective-permute-start(bf16[1,64,384]{2,1,0:T(8,128)(2,1)S(1)} %maximum_bitcast_fusion.1), channel_id=1, source_target_pairs={{0,256},{16,272},{32,288},{48,304},{64,320},{80,336},{96,352},{112... | collective-permute-start | bytes 147464 | tf_op jit(solution)/shard_map/ppermute | solution.py:84
  17.2 7.0 %collective-permute-start.2 = (bf16[1,64,384]{2,1,0:T(8,128)(2,1)S(1)}, bf16[1,64,384]{2,1,0:T(8,128)(2,1)S(1)}, u32[]{:S(2)}, u32[]{:S(2)}) collective-permute-start(bf16[1,64,384]{2,1,0:T(8,128)(2,1)S(1)} %maximum_bitcast_fusion.1), channel_id=1, source_target_pairs={{0,128},{16,144},{32,160},{48,176},{64,192},{80,208},{96,224},{112... | collective-permute-start | bytes 147464 | tf_op jit(solution)/shard_map/ppermute | solution.py:84
  25.6 3.6 %collective-permute-done.2 = bf16[1,64,384]{2,1,0:T(8,128)(2,1)S(1)} collective-permute-done((bf16[1,64,384]{2,1,0:T(8,128)(2,1)S(1)}, bf16[1,64,384]{2,1,0:T(8,128)(2,1)S(1)}, u32[]{:S(2)}, u32[]{:S(2)}) %collective-permute-start.2) | collective-permute-done | bytes 49184 | tf_op jit(solution)/shard_map/ppermute | solution.py:84
  30.8 3.8 %collective-permute-start.3 = (bf16[4,64,384]{2,1,0:T(8,128)(2,1)S(1)}, bf16[4,64,384]{2,1,0:T(8,128)(2,1)S(1)}, u32[]{:S(2)}, u32[]{:S(2)}) collective-permute-start(bf16[4,64,384]{2,1,0:T(8,128)(2,1)S(1)} %maximum_bitcast_fusion), channel_id=1, source_target_pairs={{0,96},{16,112},{32,0},{48,16},{64,32},{80,48},{96,64},{112,80},{1... | collective-permute-start | bytes 589832 | tf_op jit(solution)/shard_map/ppermute | solution.py:84
  34.7 5.6 %collective-permute-start.4 = (bf16[4,64,384]{2,1,0:T(8,128)(2,1)S(1)}, bf16[4,64,384]{2,1,0:T(8,128)(2,1)S(1)}, u32[]{:S(2)}, u32[]{:S(2)}) collective-permute-start(bf16[4,64,384]{2,1,0:T(8,128)(2,1)S(1)} %maximum_bitcast_fusion), channel_id=1, source_target_pairs={{0,64},{16,80},{32,96},{48,112},{64,0},{80,16},{96,32},{112,48},{1... | collective-permute-start | bytes 589832 | tf_op jit(solution)/shard_map/ppermute | solution.py:84
  42.4 10.3 %collective-permute-done.4 = bf16[4,64,384]{2,1,0:T(8,128)(2,1)S(1)} collective-permute-done((bf16[4,64,384]{2,1,0:T(8,128)(2,1)S(1)}, bf16[4,64,384]{2,1,0:T(8,128)(2,1)S(1)}, u32[]{:S(2)}, u32[]{:S(2)}) %collective-permute-start.4) | collective-permute-done | bytes 196640 | tf_op jit(solution)/shard_map/ppermute | solution.py:84
  52.7 3.7 %collective-permute-done.5 = bf16[4,64,384]{2,1,0:T(8,128)(2,1)S(1)} collective-permute-done((bf16[4,64,384]{2,1,0:T(8,128)(2,1)S(1)}, bf16[4,64,384]{2,1,0:T(8,128)(2,1)S(1)}, u32[]{:S(2)}, u32[]{:S(2)}) %collective-permute-start.5) | collective-permute-done | bytes 196640 | tf_op jit(solution)/shard_map/ppermute | solution.py:84
  73.2 3.0 %collective-permute-start.9 = (f32[1,128,128]{2,1,0:T(8,128)S(1)}, f32[1,128,128]{2,1,0:T(8,128)S(1)}, u32[]{:S(2)}, u32[]{:S(2)}) collective-permute-start(f32[1,128,128]{2,1,0:T(8,128)S(1)} %add.361), channel_id=1, source_target_pairs={{0,64},{32,96},{64,128},{96,160},{128,192},{160,224},{192,256},{22... | collective-permute-start | bytes 196616 | tf_op jit(solution)/shard_map/ppermute | solution.py:35
  76.2 4.7 %collective-permute-start.8 = (f32[1,128,128]{2,1,0:T(8,128)S(1)}, f32[1,128,128]{2,1,0:T(8,128)S(1)}, u32[]{:S(2)}, u32[]{:S(2)}) collective-permute-start(f32[1,128,128]{2,1,0:T(8,128)S(1)} %add.361), channel_id=1, source_target_pairs={{0,32},{32,64},{64,96},{96,128},{128,160},{160,192},{192,224},{224... | collective-permute-start | bytes 196616 | tf_op jit(solution)/shard_map/ppermute | solution.py:35
  82.3 6.6 %collective-permute-start.13 = (f32[1,128,128]{2,1,0:T(8,128)S(1)}, f32[1,128,128]{2,1,0:T(8,128)S(1)}, u32[]{:S(2)}, u32[]{:S(2)}) collective-permute-start(f32[1,128,128]{2,1,0:T(8,128)S(1)} %add_add_fusion.1), channel_id=1, source_target_pairs={{0,384},{32,416},{64,448},{96,480},{1,385},{33,417},{65,449},{97,4... | collective-permute-start | bytes 196616 | tf_op jit(solution)/shard_map/ppermute | solution.py:35
  88.9 5.0 %collective-permute-start.12 = (f32[1,128,128]{2,1,0:T(8,128)S(1)}, f32[1,128,128]{2,1,0:T(8,128)S(1)}, u32[]{:S(2)}, u32[]{:S(2)}) collective-permute-start(f32[1,128,128]{2,1,0:T(8,128)S(1)} %add_add_fusion.1), channel_id=1, source_target_pairs={{0,256},{32,288},{64,320},{96,352},{128,384},{160,416},{192,448},{... | collective-permute-start | bytes 196616 | tf_op jit(solution)/shard_map/ppermute | solution.py:35
  93.9 3.3 %collective-permute-start.11 = (f32[1,128,128]{2,1,0:T(8,128)S(1)}, f32[1,128,128]{2,1,0:T(8,128)S(1)}, u32[]{:S(2)}, u32[]{:S(2)}) collective-permute-start(f32[1,128,128]{2,1,0:T(8,128)S(1)} %add_add_fusion.1), channel_id=1, source_target_pairs={{0,128},{32,160},{64,192},{96,224},{128,256},{160,288},{192,320},{... | collective-permute-start | bytes 196616 | tf_op jit(solution)/shard_map/ppermute | solution.py:35
  101.2 3.5 %collective-permute-start.14 = (f32[1,128,128]{2,1,0:T(8,128)S(1)}, f32[1,128,128]{2,1,0:T(8,128)S(1)}, u32[]{:S(2)}, u32[]{:S(2)}) collective-permute-start(f32[1,128,128]{2,1,0:T(8,128)S(1)} %convolution_bitcast_fusion), channel_id=1, source_target_pairs={{0,16},{16,0},{1,17},{17,1},{2,18},{18,2},{3,19},{19,3},{4,20},{20... | collective-permute-start | bytes 196616 | tf_op jit(solution)/shard_map/ppermute | solution.py:21
  106.9 4.3 %collective-permute-start.16 = (f32[1,128,128]{2,1,0:T(8,128)S(1)}, f32[1,128,128]{2,1,0:T(8,128)S(1)}, u32[]{:S(2)}, u32[]{:S(2)}) collective-permute-start(f32[1,128,128]{2,1,0:T(8,128)S(1)} %add.374), channel_id=1, source_target_pairs={{64,0},{96,32},{128,64},{160,96},{192,128},{224,160},{256,192},{28... | collective-permute-start | bytes 196616 | tf_op jit(solution)/shard_map/ppermute | solution.py:35
  113.4 7.2 %collective-permute-done.17 = f32[1,128,128]{2,1,0:T(8,128)S(1)} collective-permute-done((f32[1,128,128]{2,1,0:T(8,128)S(1)}, f32[1,128,128]{2,1,0:T(8,128)S(1)}, u32[]{:S(2)}, u32[]{:S(2)}) %collective-permute-start.17) | collective-permute-done | bytes 65568 | tf_op jit(solution)/shard_map/ppermute | solution.py:35
  124.7 6.4 %collective-permute-done.20 = f32[1,128,128]{2,1,0:T(8,128)S(1)} collective-permute-done((f32[1,128,128]{2,1,0:T(8,128)S(1)}, f32[1,128,128]{2,1,0:T(8,128)S(1)}, u32[]{:S(2)}, u32[]{:S(2)}) %collective-permute-start.20) | collective-permute-done | bytes 65568 | tf_op jit(solution)/shard_map/ppermute | solution.py:35
  131.1 5.7 %collective-permute-done.19 = f32[1,128,128]{2,1,0:T(8,128)S(1)} collective-permute-done((f32[1,128,128]{2,1,0:T(8,128)S(1)}, f32[1,128,128]{2,1,0:T(8,128)S(1)}, u32[]{:S(2)}, u32[]{:S(2)}) %collective-permute-start.19) | collective-permute-done | bytes 65568 | tf_op jit(solution)/shard_map/ppermute | solution.py:35
  142.4 5.2 %collective-permute-start.27 = (bf16[16,64,384]{2,1,0:T(8,128)(2,1)}, bf16[16,64,384]{2,1,0:T(8,128)(2,1)}, u32[]{:S(2)}, u32[]{:S(2)}) collective-permute-start(bf16[16,64,384]{2,1,0:T(8,128)(2,1)} %dynamic-slice_bitcast_fusion), channel_id=1, source_target_pairs={{0,16},{16,0},{32,48},{48,32},{64,80},{80,64},{96,112},{112,96},{1... | collective-permute-start | bytes 2359304 | tf_op jit(solution)/shard_map/ppermute | solution.py:117
  148.6 3.7 %collective-permute-start.23 = (bf16[384,512]{0,1:T(8,128)(2,1)}, bf16[384,512]{0,1:T(8,128)(2,1)}, u32[]{:S(2)}, u32[]{:S(2)}) collective-permute-start(bf16[384,512]{0,1:T(8,128)(2,1)} %get-tuple-element.24), channel_id=1, source_target_pairs={{0,12},{1,13},{2,14},{3,15},{4,0},{5,1},{6,2},{7,3},{8,4},{9,5},{1... | collective-permute-start | bytes 1179656 | tf_op jit(solution)/shard_map/ppermute | solution.py:156
  154.6 2.6 %collective-permute-start.21 = (bf16[384,512]{0,1:T(8,128)(2,1)S(1)}, bf16[384,512]{0,1:T(8,128)(2,1)}, u32[]{:S(2)}, u32[]{:S(2)}) collective-permute-start(bf16[384,512]{0,1:T(8,128)(2,1)S(1)} %get-tuple-element.23), channel_id=1, source_target_pairs={{0,4},{1,5},{2,6},{3,7},{4,8},{5,9},{6,10},{7,11},{8,12},{9,13},{1... | collective-permute-start | bytes 1179656 | tf_op jit(solution)/shard_map/ppermute | solution.py:156
  159.0 2.5 %collective-permute-done.23 = bf16[384,512]{0,1:T(8,128)(2,1)} collective-permute-done((bf16[384,512]{0,1:T(8,128)(2,1)}, bf16[384,512]{0,1:T(8,128)(2,1)}, u32[]{:S(2)}, u32[]{:S(2)}) %collective-permute-start.23) | collective-permute-done | bytes 393248 | tf_op jit(solution)/shard_map/ppermute | solution.py:156
  161.5 5.0 %collective-permute-done.22 = bf16[384,512]{0,1:T(8,128)(2,1)} collective-permute-done((bf16[384,512]{0,1:T(8,128)(2,1)}, bf16[384,512]{0,1:T(8,128)(2,1)}, u32[]{:S(2)}, u32[]{:S(2)}) %collective-permute-start.22) | collective-permute-done | bytes 393248 | tf_op jit(solution)/shard_map/ppermute | solution.py:156
  166.5 9.0 %collective-permute-done.21 = bf16[384,512]{0,1:T(8,128)(2,1)} collective-permute-done((bf16[384,512]{0,1:T(8,128)(2,1)S(1)}, bf16[384,512]{0,1:T(8,128)(2,1)}, u32[]{:S(2)}, u32[]{:S(2)}) %collective-permute-start.21) | collective-permute-done | bytes 393248 | tf_op jit(solution)/shard_map/ppermute | solution.py:156
  178.7 2.8 %collective-permute-start.30 = (bf16[4,64,384]{2,1,0:T(8,128)(2,1)S(1)}, bf16[4,64,384]{2,1,0:T(8,128)(2,1)S(1)}, u32[]{:S(2)}, u32[]{:S(2)}) collective-permute-start(bf16[4,64,384]{2,1,0:T(8,128)(2,1)S(1)} %get-tuple-element.21), channel_id=1, source_target_pairs={{0,96},{16,112},{32,0},{48,16},{64,32},{80,48},{96,64},{112,80},{1... | collective-permute-start | bytes 589832 | tf_op jit(solution)/shard_map/ppermute | solution.py:117
  181.5 11.6 %collective-permute-start.29 = (bf16[4,64,384]{2,1,0:T(8,128)(2,1)S(1)}, bf16[4,64,384]{2,1,0:T(8,128)(2,1)S(1)}, u32[]{:S(2)}, u32[]{:S(2)}) collective-permute-start(bf16[4,64,384]{2,1,0:T(8,128)(2,1)S(1)} %get-tuple-element.22), channel_id=1, source_target_pairs={{0,64},{16,80},{32,96},{48,112},{64,0},{80,16},{96,32},{112,48},{1... | collective-permute-start | bytes 589832 | tf_op jit(solution)/shard_map/ppermute | solution.py:117
  196.5 2.8 %collective-permute-start.26 = (bf16[384,128]{1,0:T(8,128)(2,1)S(1)}, bf16[384,128]{1,0:T(8,128)(2,1)S(1)}, u32[]{:S(2)}, u32[]{:S(2)}) collective-permute-start(bf16[384,128]{1,0:T(8,128)(2,1)S(1)} %bitcast.208), channel_id=1, source_target_pairs={{0,3},{1,0},{2,1},{3,2},{4,7},{5,4},{6,5},{7,6},{8,11},{9,8},{10,9... | collective-permute-start | bytes 294920 | tf_op jit(solution)/shard_map/ppermute | solution.py:139
  201.9 2.6 %collective-permute-start.24 = (bf16[384,128]{1,0:T(8,128)(2,1)S(1)}, bf16[384,128]{1,0:T(8,128)(2,1)S(1)}, u32[]{:S(2)}, u32[]{:S(2)}) collective-permute-start(bf16[384,128]{1,0:T(8,128)(2,1)S(1)} %bitcast.209), channel_id=1, source_target_pairs={{0,1},{1,2},{2,3},{3,0},{4,5},{5,6},{6,7},{7,4},{8,9},{9,10},{10,1... | collective-permute-start | bytes 294920 | tf_op jit(solution)/shard_map/ppermute | solution.py:139
  205.5 3.7 %collective-permute-done.28 = bf16[4,64,384]{2,1,0:T(8,128)(2,1)S(1)} collective-permute-done((bf16[4,64,384]{2,1,0:T(8,128)(2,1)S(1)}, bf16[4,64,384]{2,1,0:T(8,128)(2,1)S(1)}, u32[]{:S(2)}, u32[]{:S(2)}) %collective-permute-start.28) | collective-permute-done | bytes 196640 | tf_op jit(solution)/shard_map/ppermute | solution.py:117
  211.2 8.3 %collective-permute-start.32 = (bf16[1,64,384]{2,1,0:T(8,128)(2,1)S(1)}, bf16[1,64,384]{2,1,0:T(8,128)(2,1)S(1)}, u32[]{:S(2)}, u32[]{:S(2)}) collective-permute-start(bf16[1,64,384]{2,1,0:T(8,128)(2,1)S(1)} %get-tuple-element.37), channel_id=1, source_target_pairs={{0,256},{16,272},{32,288},{48,304},{64,320},{80,336},{96,352},{112... | collective-permute-start | bytes 147464 | tf_op jit(solution)/shard_map/ppermute | solution.py:117
  222.2 6.0 %collective-permute-done.32 = bf16[1,64,384]{2,1,0:T(8,128)(2,1)S(1)} collective-permute-done((bf16[1,64,384]{2,1,0:T(8,128)(2,1)S(1)}, bf16[1,64,384]{2,1,0:T(8,128)(2,1)S(1)}, u32[]{:S(2)}, u32[]{:S(2)}) %collective-permute-start.32) | collective-permute-done | bytes 49184 | tf_op jit(solution)/shard_map/ppermute | solution.py:117
  228.2 3.9 %collective-permute-done.31 = bf16[1,64,384]{2,1,0:T(8,128)(2,1)S(1)} collective-permute-done((bf16[1,64,384]{2,1,0:T(8,128)(2,1)S(1)}, bf16[1,64,384]{2,1,0:T(8,128)(2,1)S(1)}, u32[]{:S(2)}, u32[]{:S(2)}) %collective-permute-start.31) | collective-permute-done | bytes 49184 | tf_op jit(solution)/shard_map/ppermute | solution.py:117
  (112 shorter events, 61.4 us)
Async XLA Ops:
  1.4 23.0 %collective-permute-start = (bf16[1,64,384]{2,1,0:T(8,128)(2,1)S(1)}, bf16[1,64,384]{2,1,0:T(8,128)(2,1)S(1)}, u32[]{:S(2)}, u32[]{:S(2)}) collective-permute-start(bf16[1,64,384]{2,1,0:T(8,128)(2,1)S(1)} %maximum_bitcast_fusion.1), channel_id=1, source_target_pairs={{0,384},{16,400},{32,416},{48,432},{64,448},{80,464},{96,480},{112... | collective-permute-start | bytes 147464 | tf_op jit(solution)/shard_map/ppermute | solution.py:84
  12.0 13.6 %collective-permute-start.1 = (bf16[1,64,384]{2,1,0:T(8,128)(2,1)S(1)}, bf16[1,64,384]{2,1,0:T(8,128)(2,1)S(1)}, u32[]{:S(2)}, u32[]{:S(2)}) collective-permute-start(bf16[1,64,384]{2,1,0:T(8,128)(2,1)S(1)} %maximum_bitcast_fusion.1), channel_id=1, source_target_pairs={{0,256},{16,272},{32,288},{48,304},{64,320},{80,336},{96,352},{112... | collective-permute-start | bytes 147464 | tf_op jit(solution)/shard_map/ppermute | solution.py:84
  17.2 12.0 %collective-permute-start.2 = (bf16[1,64,384]{2,1,0:T(8,128)(2,1)S(1)}, bf16[1,64,384]{2,1,0:T(8,128)(2,1)S(1)}, u32[]{:S(2)}, u32[]{:S(2)}) collective-permute-start(bf16[1,64,384]{2,1,0:T(8,128)(2,1)S(1)} %maximum_bitcast_fusion.1), channel_id=1, source_target_pairs={{0,128},{16,144},{32,160},{48,176},{64,192},{80,208},{96,224},{112... | collective-permute-start | bytes 147464 | tf_op jit(solution)/shard_map/ppermute | solution.py:84
  30.8 11.5 %collective-permute-start.3 = (bf16[4,64,384]{2,1,0:T(8,128)(2,1)S(1)}, bf16[4,64,384]{2,1,0:T(8,128)(2,1)S(1)}, u32[]{:S(2)}, u32[]{:S(2)}) collective-permute-start(bf16[4,64,384]{2,1,0:T(8,128)(2,1)S(1)} %maximum_bitcast_fusion), channel_id=1, source_target_pairs={{0,96},{16,112},{32,0},{48,16},{64,32},{80,48},{96,64},{112,80},{1... | collective-permute-start | bytes 589832 | tf_op jit(solution)/shard_map/ppermute | solution.py:84
  34.7 18.0 %collective-permute-start.4 = (bf16[4,64,384]{2,1,0:T(8,128)(2,1)S(1)}, bf16[4,64,384]{2,1,0:T(8,128)(2,1)S(1)}, u32[]{:S(2)}, u32[]{:S(2)}) collective-permute-start(bf16[4,64,384]{2,1,0:T(8,128)(2,1)S(1)} %maximum_bitcast_fusion), channel_id=1, source_target_pairs={{0,64},{16,80},{32,96},{48,112},{64,0},{80,16},{96,32},{112,48},{1... | collective-permute-start | bytes 589832 | tf_op jit(solution)/shard_map/ppermute | solution.py:84
  40.3 16.1 %collective-permute-start.5 = (bf16[4,64,384]{2,1,0:T(8,128)(2,1)S(1)}, bf16[4,64,384]{2,1,0:T(8,128)(2,1)S(1)}, u32[]{:S(2)}, u32[]{:S(2)}) collective-permute-start(bf16[4,64,384]{2,1,0:T(8,128)(2,1)S(1)} %maximum_bitcast_fusion), channel_id=1, source_target_pairs={{0,32},{16,48},{32,64},{48,80},{64,96},{80,112},{96,0},{112,16},{1... | collective-permute-start | bytes 589832 | tf_op jit(solution)/shard_map/ppermute | solution.py:84
  65.3 5.7 %collective-permute-start.7 = (f32[1,128,128]{2,1,0:T(8,128)}, f32[1,128,128]{2,1,0:T(8,128)}, u32[]{:S(2)}, u32[]{:S(2)}) collective-permute-start(f32[1,128,128]{2,1,0:T(8,128)} %convolution_bitcast_fusion.1), channel_id=1, source_target_pairs={{0,16},{16,0},{1,17},{17,1},{2,18},{18,2},{3,19},{19,3},{4,20},{20... | collective-permute-start | bytes 196616 | tf_op jit(solution)/shard_map/ppermute | solution.py:21
  71.9 10.2 %collective-permute-start.10 = (f32[1,128,128]{2,1,0:T(8,128)S(1)}, f32[1,128,128]{2,1,0:T(8,128)S(1)}, u32[]{:S(2)}, u32[]{:S(2)}) collective-permute-start(f32[1,128,128]{2,1,0:T(8,128)S(1)} %add.361), channel_id=1, source_target_pairs={{0,96},{32,128},{64,160},{96,192},{128,224},{160,256},{192,288},{2... | collective-permute-start | bytes 196616 | tf_op jit(solution)/shard_map/ppermute | solution.py:35
  73.2 8.9 %collective-permute-start.9 = (f32[1,128,128]{2,1,0:T(8,128)S(1)}, f32[1,128,128]{2,1,0:T(8,128)S(1)}, u32[]{:S(2)}, u32[]{:S(2)}) collective-permute-start(f32[1,128,128]{2,1,0:T(8,128)S(1)} %add.361), channel_id=1, source_target_pairs={{0,64},{32,96},{64,128},{96,160},{128,192},{160,224},{192,256},{22... | collective-permute-start | bytes 196616 | tf_op jit(solution)/shard_map/ppermute | solution.py:35
  76.2 6.0 %collective-permute-start.8 = (f32[1,128,128]{2,1,0:T(8,128)S(1)}, f32[1,128,128]{2,1,0:T(8,128)S(1)}, u32[]{:S(2)}, u32[]{:S(2)}) collective-permute-start(f32[1,128,128]{2,1,0:T(8,128)S(1)} %add.361), channel_id=1, source_target_pairs={{0,32},{32,64},{64,96},{96,128},{128,160},{160,192},{192,224},{224... | collective-permute-start | bytes 196616 | tf_op jit(solution)/shard_map/ppermute | solution.py:35
  82.3 15.2 %collective-permute-start.13 = (f32[1,128,128]{2,1,0:T(8,128)S(1)}, f32[1,128,128]{2,1,0:T(8,128)S(1)}, u32[]{:S(2)}, u32[]{:S(2)}) collective-permute-start(f32[1,128,128]{2,1,0:T(8,128)S(1)} %add_add_fusion.1), channel_id=1, source_target_pairs={{0,384},{32,416},{64,448},{96,480},{1,385},{33,417},{65,449},{97,4... | collective-permute-start | bytes 196616 | tf_op jit(solution)/shard_map/ppermute | solution.py:35
  88.9 8.6 %collective-permute-start.12 = (f32[1,128,128]{2,1,0:T(8,128)S(1)}, f32[1,128,128]{2,1,0:T(8,128)S(1)}, u32[]{:S(2)}, u32[]{:S(2)}) collective-permute-start(f32[1,128,128]{2,1,0:T(8,128)S(1)} %add_add_fusion.1), channel_id=1, source_target_pairs={{0,256},{32,288},{64,320},{96,352},{128,384},{160,416},{192,448},{... | collective-permute-start | bytes 196616 | tf_op jit(solution)/shard_map/ppermute | solution.py:35
  93.9 4.6 %collective-permute-start.11 = (f32[1,128,128]{2,1,0:T(8,128)S(1)}, f32[1,128,128]{2,1,0:T(8,128)S(1)}, u32[]{:S(2)}, u32[]{:S(2)}) collective-permute-start(f32[1,128,128]{2,1,0:T(8,128)S(1)} %add_add_fusion.1), channel_id=1, source_target_pairs={{0,128},{32,160},{64,192},{96,224},{128,256},{160,288},{192,320},{... | collective-permute-start | bytes 196616 | tf_op jit(solution)/shard_map/ppermute | solution.py:35
  105.6 15.0 %collective-permute-start.17 = (f32[1,128,128]{2,1,0:T(8,128)S(1)}, f32[1,128,128]{2,1,0:T(8,128)S(1)}, u32[]{:S(2)}, u32[]{:S(2)}) collective-permute-start(f32[1,128,128]{2,1,0:T(8,128)S(1)} %add.374), channel_id=1, source_target_pairs={{96,0},{128,32},{160,64},{192,96},{224,128},{256,160},{288,192},{3... | collective-permute-start | bytes 196616 | tf_op jit(solution)/shard_map/ppermute | solution.py:35
  106.9 13.7 %collective-permute-start.16 = (f32[1,128,128]{2,1,0:T(8,128)S(1)}, f32[1,128,128]{2,1,0:T(8,128)S(1)}, u32[]{:S(2)}, u32[]{:S(2)}) collective-permute-start(f32[1,128,128]{2,1,0:T(8,128)S(1)} %add.374), channel_id=1, source_target_pairs={{64,0},{96,32},{128,64},{160,96},{192,128},{224,160},{256,192},{28... | collective-permute-start | bytes 196616 | tf_op jit(solution)/shard_map/ppermute | solution.py:35
  111.2 9.4 %collective-permute-start.15 = (f32[1,128,128]{2,1,0:T(8,128)S(1)}, f32[1,128,128]{2,1,0:T(8,128)S(1)}, u32[]{:S(2)}, u32[]{:S(2)}) collective-permute-start(f32[1,128,128]{2,1,0:T(8,128)S(1)} %add.374), channel_id=1, source_target_pairs={{32,0},{64,32},{96,64},{128,96},{160,128},{192,160},{224,192},{256... | collective-permute-start | bytes 196616 | tf_op jit(solution)/shard_map/ppermute | solution.py:35
  120.6 10.4 %collective-permute-start.20 = (f32[1,128,128]{2,1,0:T(8,128)S(1)}, f32[1,128,128]{2,1,0:T(8,128)S(1)}, u32[]{:S(2)}, u32[]{:S(2)}) collective-permute-start(f32[1,128,128]{2,1,0:T(8,128)S(1)} %add_add_fusion), channel_id=1, source_target_pairs={{384,0},{416,32},{448,64},{480,96},{385,1},{417,33},{449,65},{481,... | collective-permute-start | bytes 196616 | tf_op jit(solution)/shard_map/ppermute | solution.py:35
  121.9 14.8 %collective-permute-start.19 = (f32[1,128,128]{2,1,0:T(8,128)S(1)}, f32[1,128,128]{2,1,0:T(8,128)S(1)}, u32[]{:S(2)}, u32[]{:S(2)}) collective-permute-start(f32[1,128,128]{2,1,0:T(8,128)S(1)} %add_add_fusion), channel_id=1, source_target_pairs={{256,0},{288,32},{320,64},{352,96},{384,128},{416,160},{448,192},{... | collective-permute-start | bytes 196616 | tf_op jit(solution)/shard_map/ppermute | solution.py:35
  123.2 13.5 %collective-permute-start.18 = (f32[1,128,128]{2,1,0:T(8,128)S(1)}, f32[1,128,128]{2,1,0:T(8,128)S(1)}, u32[]{:S(2)}, u32[]{:S(2)}) collective-permute-start(f32[1,128,128]{2,1,0:T(8,128)S(1)} %add_add_fusion), channel_id=1, source_target_pairs={{128,0},{160,32},{192,64},{224,96},{256,128},{288,160},{320,192},{... | collective-permute-start | bytes 196616 | tf_op jit(solution)/shard_map/ppermute | solution.py:35
  142.4 34.6 %collective-permute-start.27 = (bf16[16,64,384]{2,1,0:T(8,128)(2,1)}, bf16[16,64,384]{2,1,0:T(8,128)(2,1)}, u32[]{:S(2)}, u32[]{:S(2)}) collective-permute-start(bf16[16,64,384]{2,1,0:T(8,128)(2,1)} %dynamic-slice_bitcast_fusion), channel_id=1, source_target_pairs={{0,16},{16,0},{32,48},{48,32},{64,80},{80,64},{96,112},{112,96},{1... | collective-permute-start | bytes 2359304 | tf_op jit(solution)/shard_map/ppermute | solution.py:117
  148.6 12.9 %collective-permute-start.23 = (bf16[384,512]{0,1:T(8,128)(2,1)}, bf16[384,512]{0,1:T(8,128)(2,1)}, u32[]{:S(2)}, u32[]{:S(2)}) collective-permute-start(bf16[384,512]{0,1:T(8,128)(2,1)} %get-tuple-element.24), channel_id=1, source_target_pairs={{0,12},{1,13},{2,14},{3,15},{4,0},{5,1},{6,2},{7,3},{8,4},{9,5},{1... | collective-permute-start | bytes 1179656 | tf_op jit(solution)/shard_map/ppermute | solution.py:156
  152.4 14.1 %collective-permute-start.22 = (bf16[384,512]{0,1:T(8,128)(2,1)}, bf16[384,512]{0,1:T(8,128)(2,1)}, u32[]{:S(2)}, u32[]{:S(2)}) collective-permute-start(bf16[384,512]{0,1:T(8,128)(2,1)} %get-tuple-element.25), channel_id=1, source_target_pairs={{0,8},{1,9},{2,10},{3,11},{4,12},{5,13},{6,14},{7,15},{8,0},{9,1},... | collective-permute-start | bytes 1179656 | tf_op jit(solution)/shard_map/ppermute | solution.py:156
  154.6 21.0 %collective-permute-start.21 = (bf16[384,512]{0,1:T(8,128)(2,1)S(1)}, bf16[384,512]{0,1:T(8,128)(2,1)}, u32[]{:S(2)}, u32[]{:S(2)}) collective-permute-start(bf16[384,512]{0,1:T(8,128)(2,1)S(1)} %get-tuple-element.23), channel_id=1, source_target_pairs={{0,4},{1,5},{2,6},{3,7},{4,8},{5,9},{6,10},{7,11},{8,12},{9,13},{1... | collective-permute-start | bytes 1179656 | tf_op jit(solution)/shard_map/ppermute | solution.py:156
  178.7 23.2 %collective-permute-start.30 = (bf16[4,64,384]{2,1,0:T(8,128)(2,1)S(1)}, bf16[4,64,384]{2,1,0:T(8,128)(2,1)S(1)}, u32[]{:S(2)}, u32[]{:S(2)}) collective-permute-start(bf16[4,64,384]{2,1,0:T(8,128)(2,1)S(1)} %get-tuple-element.21), channel_id=1, source_target_pairs={{0,96},{16,112},{32,0},{48,16},{64,32},{80,48},{96,64},{112,80},{1... | collective-permute-start | bytes 589832 | tf_op jit(solution)/shard_map/ppermute | solution.py:117
  181.5 24.0 %collective-permute-start.29 = (bf16[4,64,384]{2,1,0:T(8,128)(2,1)S(1)}, bf16[4,64,384]{2,1,0:T(8,128)(2,1)S(1)}, u32[]{:S(2)}, u32[]{:S(2)}) collective-permute-start(bf16[4,64,384]{2,1,0:T(8,128)(2,1)S(1)} %get-tuple-element.22), channel_id=1, source_target_pairs={{0,64},{16,80},{32,96},{48,112},{64,0},{80,16},{96,32},{112,48},{1... | collective-permute-start | bytes 589832 | tf_op jit(solution)/shard_map/ppermute | solution.py:117
  193.1 16.1 %collective-permute-start.28 = (bf16[4,64,384]{2,1,0:T(8,128)(2,1)S(1)}, bf16[4,64,384]{2,1,0:T(8,128)(2,1)S(1)}, u32[]{:S(2)}, u32[]{:S(2)}) collective-permute-start(bf16[4,64,384]{2,1,0:T(8,128)(2,1)S(1)} %get-tuple-element.20), channel_id=1, source_target_pairs={{0,32},{16,48},{32,64},{48,80},{64,96},{80,112},{96,0},{112,16},{1... | collective-permute-start | bytes 589832 | tf_op jit(solution)/shard_map/ppermute | solution.py:117
  196.5 23.1 %collective-permute-start.26 = (bf16[384,128]{1,0:T(8,128)(2,1)S(1)}, bf16[384,128]{1,0:T(8,128)(2,1)S(1)}, u32[]{:S(2)}, u32[]{:S(2)}) collective-permute-start(bf16[384,128]{1,0:T(8,128)(2,1)S(1)} %bitcast.208), channel_id=1, source_target_pairs={{0,3},{1,0},{2,1},{3,2},{4,7},{5,4},{6,5},{7,6},{8,11},{9,8},{10,9... | collective-permute-start | bytes 294920 | tf_op jit(solution)/shard_map/ppermute | solution.py:139
  199.4 22.1 %collective-permute-start.25 = (bf16[384,128]{1,0:T(8,128)(2,1)S(1)}, bf16[384,128]{1,0:T(8,128)(2,1)S(1)}, u32[]{:S(2)}, u32[]{:S(2)}) collective-permute-start(bf16[384,128]{1,0:T(8,128)(2,1)S(1)} %bitcast.207), channel_id=1, source_target_pairs={{0,2},{1,3},{2,0},{3,1},{4,6},{5,7},{6,4},{7,5},{8,10},{9,11},{10,... | collective-permute-start | bytes 294920 | tf_op jit(solution)/shard_map/ppermute | solution.py:139
  201.9 19.7 %collective-permute-start.24 = (bf16[384,128]{1,0:T(8,128)(2,1)S(1)}, bf16[384,128]{1,0:T(8,128)(2,1)S(1)}, u32[]{:S(2)}, u32[]{:S(2)}) collective-permute-start(bf16[384,128]{1,0:T(8,128)(2,1)S(1)} %bitcast.209), channel_id=1, source_target_pairs={{0,1},{1,2},{2,3},{3,0},{4,5},{5,6},{6,7},{7,4},{8,9},{9,10},{10,1... | collective-permute-start | bytes 294920 | tf_op jit(solution)/shard_map/ppermute | solution.py:139
  209.3 12.9 %collective-permute-start.33 = (bf16[1,64,384]{2,1,0:T(8,128)(2,1)S(1)}, bf16[1,64,384]{2,1,0:T(8,128)(2,1)S(1)}, u32[]{:S(2)}, u32[]{:S(2)}) collective-permute-start(bf16[1,64,384]{2,1,0:T(8,128)(2,1)S(1)} %get-tuple-element.36), channel_id=1, source_target_pairs={{0,384},{16,400},{32,416},{48,432},{64,448},{80,464},{96,480},{112... | collective-permute-start | bytes 147464 | tf_op jit(solution)/shard_map/ppermute | solution.py:117
  211.2 16.9 %collective-permute-start.32 = (bf16[1,64,384]{2,1,0:T(8,128)(2,1)S(1)}, bf16[1,64,384]{2,1,0:T(8,128)(2,1)S(1)}, u32[]{:S(2)}, u32[]{:S(2)}) collective-permute-start(bf16[1,64,384]{2,1,0:T(8,128)(2,1)S(1)} %get-tuple-element.37), channel_id=1, source_target_pairs={{0,256},{16,272},{32,288},{48,304},{64,320},{80,336},{96,352},{112... | collective-permute-start | bytes 147464 | tf_op jit(solution)/shard_map/ppermute | solution.py:117
  219.6 12.5 %collective-permute-start.31 = (bf16[1,64,384]{2,1,0:T(8,128)(2,1)S(1)}, bf16[1,64,384]{2,1,0:T(8,128)(2,1)S(1)}, u32[]{:S(2)}, u32[]{:S(2)}) collective-permute-start(bf16[1,64,384]{2,1,0:T(8,128)(2,1)S(1)} %get-tuple-element.35), channel_id=1, source_target_pairs={{0,128},{16,144},{32,160},{48,176},{64,192},{80,208},{96,224},{112... | collective-permute-start | bytes 147464 | tf_op jit(solution)/shard_map/ppermute | solution.py:117
  (10 other events, 123.8 us)
